TPU v7x, 128 devices: a whole 4x4x4 slice. The times are simulated.
128 devices in a mesh: dp: 8 (over y_lo, x), ctx: 16 (over z, y_hi, core).
Axes of the slice: x: 4, y: 4 (y_hi: 2, y_lo: 2; y = y_hi * 2 + y_lo), z: 4, core: 2. Of those that a mesh axis runs over, the one named last changes fastest.
Arguments:
- stream: bfloat16 [32768, 2, 1024], P(('dp', 'ctx')), parts along dimension 0, may hold values from -6 to 6
- w_gate: bfloat16 [1024, 2048], replicated, may hold values from -0.1875 to 0.1875
- w_xbc: bfloat16 [1024, 2176], replicated, may hold values from -0.1875 to 0.1875
- w_dt: bfloat16 [1024, 32], replicated, may hold values from -0.1875 to 0.1875
- dt_bias: float32 [2, 32], replicated, may hold values from -1 to 1
- decay_log: float32 [2, 32], replicated, may hold values from -16 to -3, as said below
- conv_w: float32 [2, 4, 2176], replicated, may hold values from -3 to 3
- conv_b: float32 [2, 2176], replicated, may hold values from -3 to 3
- skip_gain: float32 [2, 32], replicated, may hold values from 0.5 to 1.5
- norm_gain: float32 [2048], replicated, may hold values from 0.1 to 1.9
- w_out: bfloat16 [2048, 1024], replicated, may hold values from -0.125 to 0.125
Outputs:
- mixed: bfloat16 [32768, 2, 1024], P(('dp', 'ctx')), parts along dimension 0
There are 8 independent parts, one for each index of `dp`. A program takes and returns all parts, laid end to end along the dimension named above; an argument that names none is the same for every part. Nothing has to cross between parts.
Inputs may be any that keep to these rules, and one draw needn't show every extreme that they name: `decay_log`: logarithms of per-step decay rates, one row per direction.
All inputs are finite; a program needn't handle non-finite values.
Results may differ from a plain program's by a relative error of at most 0.0095.
Values may be sent and summed in bfloat16 or wider, within the bound.
No kernel may reach another device: no remote copies, remote signals or barrier semaphores. Data moves between devices by JAX's collectives and lax.ppermute only.
A program may use at most 256 MiB of HBM per device.

v0:
```python
import jax
import jax.numpy as jnp
from jax import lax
from jax.sharding import PartitionSpec as P

NS = 64
K = 4
Q = 256


def shifted(value, distance):
    size = lax.axis_size("ctx")
    if abs(distance) >= size:
        return jax.tree.map(jnp.zeros_like, value)
    if distance > 0:
        pairs = [(i, i + distance) for i in range(size - distance)]
    else:
        pairs = [(i - distance, i) for i in range(size + distance)]
    return lax.ppermute(value, "ctx", pairs)


def combine(earlier, later):
    return (earlier[0] * later[0], later[0][..., None, None] * earlier[1] + later[1])


def exclusive_chain(element, sense):
    size = lax.axis_size("ctx")
    cover = 1
    gathered = element
    while 2 * cover < size:
        gathered = combine(shifted(gathered, sense * cover), gathered)
        cover *= 2
    near = shifted(gathered, sense)
    far = shifted(gathered, sense * (cover + 1))
    return combine(far, near)[1]


def group_terms(window, dt_raw, dt_shift, log_rate, weights, offset, skip_heads, falling):
    runs, length = dt_raw.shape[0], dt_raw.shape[1]
    heads = dt_raw.shape[2]
    if falling:
        taps = [window[:, K - 1 - k : K - 1 - k + length] for k in range(K)]
    else:
        taps = [window[:, k : k + length] for k in range(K)]
    total = offset[:, None, :] + weights[:, 0][:, None, :] * taps[0].astype(jnp.float32)
    for k in range(1, K):
        total = total + weights[:, k][:, None, :] * taps[k].astype(jnp.float32)
    conv = jax.nn.silu(total).astype(jnp.bfloat16)
    inner = conv.shape[2] - 2 * NS
    head_size = inner // heads
    values = conv[:, :, :inner].reshape(runs, length, heads, head_size)
    keys_in = conv[:, :, inner : inner + NS]
    reads = conv[:, :, inner + NS :]
    step = jax.nn.softplus(dt_raw.astype(jnp.float32) + dt_shift[:, None, :])
    rate = -jnp.exp(log_rate)
    cum = lax.cumsum(step * rate[:, None, :], axis=1, reverse=falling)
    by_head = jnp.transpose(cum, (0, 2, 1))
    rows = jnp.arange(length)
    if falling:
        keep = rows[:, None] <= rows[None, :]
    else:
        keep = rows[:, None] >= rows[None, :]
    decay = jnp.exp(
        jnp.where(keep[None, None], by_head[:, :, :, None] - by_head[:, :, None, :], -1e30)
    )
    scores = jnp.einsum("rtn,rsn->rts", reads, keys_in, preferred_element_type=jnp.float32)
    mixing = (scores[:, None] * decay).astype(jnp.bfloat16)
    values32 = values.astype(jnp.float32)
    scaled = (values32 * step[..., None]).astype(jnp.bfloat16)
    diagonal = jnp.einsum("rhts,rshp->rthp", mixing, scaled, preferred_element_type=jnp.float32)
    last = cum[:, 0] if falling else cum[:, -1]
    to_end = jnp.exp(last[:, None, :] - cum)
    weighted = (values32 * (step * to_end)[..., None]).astype(jnp.bfloat16)
    block_state = jnp.einsum(
        "rshp,rsn->rhpn", weighted, keys_in, preferred_element_type=jnp.float32
    )
    block_decay = jnp.exp(last)
    local = diagonal + skip_heads[:, None, :, None] * values32
    return local, cum, reads, (block_decay, block_state)


def finish(local, cum, reads, entering):
    product = jnp.einsum(
        "rtn,rhpn->rthp", reads.astype(jnp.float32), entering, precision=lax.Precision.HIGHEST
    )
    result = local + product * jnp.exp(cum)[..., None]
    return result.reshape(result.shape[0], result.shape[1], -1)


def body(
    stream, w_gate, w_xbc, w_dt, dt_bias, decay_log, conv_w, conv_b, skip_gain, norm_gain, w_out
):
    length = stream.shape[0]
    rows = jnp.concatenate([stream[:, 0, :], stream[:, 1, :]], axis=0)
    gate = jnp.dot(rows, w_gate, preferred_element_type=jnp.float32).astype(jnp.bfloat16)
    projected = jnp.dot(rows, w_xbc, preferred_element_type=jnp.float32).astype(jnp.bfloat16)
    projected = projected.reshape(2, length, projected.shape[1])
    dt_raw = jnp.dot(rows, w_dt, preferred_element_type=jnp.float32).astype(jnp.bfloat16)
    dt_raw = dt_raw.reshape(2, length, dt_raw.shape[1])
    before = shifted(projected[:, length - (K - 1) :], 1)
    after = shifted(projected[:, : K - 1], -1)
    rising = group_terms(
        jnp.concatenate([before, projected], axis=1),
        dt_raw,
        dt_bias,
        decay_log,
        conv_w,
        conv_b,
        skip_gain,
        False,
    )
    falling = group_terms(
        jnp.concatenate([projected, after], axis=1),
        dt_raw,
        dt_bias[::-1],
        decay_log[::-1],
        conv_w[::-1],
        conv_b[::-1],
        skip_gain[::-1],
        True,
    )
    rising_in = exclusive_chain(rising[3], 1)
    falling_in = exclusive_chain(falling[3], -1)
    combined = finish(*rising[:3], rising_in) + finish(*falling[:3], falling_in)
    gated = combined * jax.nn.silu(gate.reshape(2, length, gate.shape[1]).astype(jnp.float32))
    normed = (
        gated * lax.rsqrt(jnp.mean(gated * gated, axis=-1, keepdims=True) + 1e-05) * norm_gain
    ).astype(jnp.bfloat16)
    projected_out = jnp.dot(
        normed.reshape(2 * length, normed.shape[2]), w_out, preferred_element_type=jnp.float32
    )
    final_rows = (rows.astype(jnp.float32) + projected_out).astype(jnp.bfloat16)
    return jnp.stack([final_rows[:length], final_rows[length:]], axis=1)


def solution(mesh):
    placed = (P(("dp", "ctx"), None, None), P(), P(), P(), P(), P(), P(), P(), P(), P(), P())
    return jax.shard_map(
        body, mesh=mesh, in_specs=placed, out_specs=P(("dp", "ctx"), None, None), check_vma=False
    )
```

profile of v0, /device:TPU:1, one launch (start us, length us, event | category | flops | bytes accessed | tf_op | source)
XLA Modules:
  0.0 387.6 jit_solution(9608624524281306969)
XLA Ops:
  0.0 3.4 fusion.67
  3.9 3.4 convolution_convert_fusion
  8.0 3.3 collective-permute-start.10
  11.9 4.8 %collective-permute-start = (bf16[2,3,2176]{2,0,1:T(2,128)(2,1)}, bf16[2,3,2176]{2,0,1:T(2,128)(2,1)}, u32[]{:S(2)}, u32[]{:S(2)}) collective-permute-start(bf16[2,3,2176]{2,0,1:T(2,128)(2,1)} %copy.111), channel_id=1, source_target_pairs={{0,1},{1,2},{2,3},{3,4},{4,5},{5,6},{6,7},{7,8},{8,9},{9,10},{10,1... | collective-permute-start | bytes 78344 | tf_op jit(solution)/shard_map/ppermute | solution.py:19
  18.9 5.0 %reduce-window.16 = f32[2,32,2,128]{3,1,2,0:T(8,128)S(1)} reduce-window(f32[2,32,2,128]{3,1,2,0:T(8,128)S(1)} %bitcast.126, f32[]{:T(128)} %constant.18.clone.1), window={size=1x1x1x128 pad=0_0x0_0x0_0x0_127}, to_apply=%region_2.3 | reduce-window | flops 2080768 | bytes 131076 | tf_op jit(solution)/shard_map/reduce-window.2
  24.9 1.9 collective-permute-start.11
  29.1 5.1 %collective-permute-start.1 = (f32[2,32]{1,0:T(2,128)S(1)}, f32[2,32]{1,0:T(2,128)}, u32[]{:S(2)}, u32[]{:S(2)}) collective-permute-start(f32[2,32]{1,0:T(2,128)S(1)} %exp.72), channel_id=1, source_target_pairs={{0,1},{1,2},{2,3},{3,4},{4,5},{5,6},{6,7},{7,8},{8,9},{9,10},{10,1... | collective-permute-start | bytes 776 | tf_op jit(solution)/shard_map/ppermute | solution.py:19
  38.3 2.4 copy.76
  40.7 5.3 %rev.13 = f32[2,2176]{1,0:T(2,128)} reverse(f32[2,2176]{1,0:T(2,128)S(1)} %copy-done.14), dimensions={0} | reverse | bytes 34816 | tf_op jit(solution)/shard_map/rev | solution.py:118
  46.0 1.4 copy.83
  47.4 2.2 copy.75
  49.5 19.5 %multiply_convert_fusion.4 = (bf16[2,256,2176]{1,2,0:T(8,128)(2,1)S(1)}, bf16[2,256,2176]{1,2,0:T(8,128)(2,1)S(1)}) fusion(bf16[2,256,2176]{1,2,0:T(8,128)(2,1)} %copy.76, bf16[2,3,2176]{1,2,0:T(8,128)(2,1)S(1)} %copy.83, f32[2,2176]{1,0:T(2,128)} %get-tuple-element.41, f32[2,2176]{1,0:T(2,128)} %get-tuple-element.42, f32[2,2176]{1,0:T(2,128)} %get-tuple-element.43, ...), kind=kLoop, calls=%fused_computation.25 | loop fusion | flops 56819712 | bytes 6910976 | tf_op jit(solution)/shard_map/convert_element_type | solution.py:48
  70.1 3.0 collective-permute-start.5
  73.9 2.1 collective-permute-start.15
  76.0 4.4 %fusion.23 = f32[512,2048]{1,0:T(8,128)} fusion(bf16[1024,2048]{1,0:T(8,128)(2,1)S(1)} %copy-done.26, bf16[256,1024]{1,0:T(8,128)(2,1)S(1)} %copy-done.9, bf16[256,1024]{1,0:T(8,128)(2,1)S(1)} %copy-done.11), kind=kOutput, calls=%fused_computation.47 | convolution fusion | flops 2151677952 | bytes 9437184 | tf_op jit(solution)/shard_map/dot_general | solution.py:95
  81.8 6.0 %collective-permute-start.2 = (f32[2,32]{1,0:T(2,128)S(1)}, f32[2,32]{1,0:T(2,128)S(1)}, u32[]{:S(2)}, u32[]{:S(2)}) collective-permute-start(f32[2,32]{1,0:T(2,128)S(1)} %exponential_multiply_fusion.3), channel_id=1, source_target_pairs={{0,2},{1,3},{2,4},{3,5},{4,6},{5,7},{6,8},{7,9},{8,10},{9,11},{10,... | collective-permute-start | bytes 776 | tf_op jit(solution)/shard_map/ppermute | solution.py:19
  87.8 8.3 %collective-permute-done.5 = f32[2,32,64,64]{3,2,1,0:T(8,128)S(1)} collective-permute-done((f32[2,32,64,64]{3,2,1,0:T(8,128)S(1)}, f32[2,32,64,64]{3,2,1,0:T(8,128)S(1)}, u32[]{:S(2)}, u32[]{:S(2)}) %collective-permute-start.5) | collective-permute-done | bytes 1048608 | tf_op jit(solution)/shard_map/ppermute | solution.py:19
  96.1 1.7 multiply_add_fusion.5
  97.8 26.2 %collective-permute-start.6 = (f32[2,32,64,64]{3,2,1,0:T(8,128)}, f32[2,32,64,64]{3,2,1,0:T(8,128)}, u32[]{:S(2)}, u32[]{:S(2)}) collective-permute-start(f32[2,32,64,64]{3,2,1,0:T(8,128)} %multiply_add_fusion.5), channel_id=1, source_target_pairs={{0,2},{1,3},{2,4},{3,5},{4,6},{5,7},{6,8},{7,9},{8,10},{9,11},{10,... | collective-permute-start | bytes 3145736 | tf_op jit(solution)/shard_map/ppermute | solution.py:19
  124.0 1.6 multiply_add_fusion.2
  128.8 7.9 %reshape.195 = f32[2,256,32,64]{3,2,1,0:T(8,128)} reshape(f32[512,2048]{1,0:T(8,128)} %fusion.23) | data formatting | bytes 8388608 | tf_op jit(solution)/shard_map/convert_element_type | solution.py:125
  136.7 7.8 %copy.91 = f32[2,256,32,64]{1,3,2,0:T(8,128)} copy(f32[2,256,32,64]{3,2,1,0:T(8,128)} %reshape.195) | data formatting | bytes 8388608 | tf_op jit(solution)/shard_map/convert_element_type | solution.py:125
  144.6 7.3 %collective-permute-start.3 = (f32[2,32]{1,0:T(2,128)S(1)}, f32[2,32]{1,0:T(2,128)S(1)}, u32[]{:S(2)}, u32[]{:S(2)}) collective-permute-start(f32[2,32]{1,0:T(2,128)S(1)} %mul.330), channel_id=1, source_target_pairs={{0,4},{1,5},{2,6},{3,7},{4,8},{5,9},{6,10},{7,11},{8,12},{9,13},{1... | collective-permute-start | bytes 776 | tf_op jit(solution)/shard_map/ppermute | solution.py:19
  151.8 56.9 %collective-permute-done.12 = f32[2,32]{1,0:T(2,128)S(1)} collective-permute-done((f32[2,32]{1,0:T(2,128)S(1)}, f32[2,32]{1,0:T(2,128)S(1)}, u32[]{:S(2)}, u32[]{:S(2)}) %collective-permute-start.12) | collective-permute-done | bytes 288 | tf_op jit(solution)/shard_map/ppermute | solution.py:19
  210.6 11.9 %collective-permute-start.4 = (f32[2,32]{1,0:T(2,128)S(1)}, f32[2,32]{1,0:T(2,128)S(1)}, u32[]{:S(2)}, u32[]{:S(2)}) collective-permute-start(f32[2,32]{1,0:T(2,128)S(1)} %mul.331), channel_id=1, source_target_pairs={{0,1},{1,2},{2,3},{3,4},{4,5},{5,6},{6,7},{7,8},{8,9},{9,10},{10,1... | collective-permute-start | bytes 776 | tf_op jit(solution)/shard_map/ppermute | solution.py:19
  224.0 2.5 multiply_add_fusion.4
  226.5 4.5 %collective-permute-start.7 = (f32[2,32,64,64]{3,2,1,0:T(8,128)S(1)}, f32[2,32,64,64]{3,2,1,0:T(8,128)S(1)}, u32[]{:S(2)}, u32[]{:S(2)}) collective-permute-start(f32[2,32,64,64]{3,2,1,0:T(8,128)S(1)} %multiply_add_fusion.4), channel_id=1, source_target_pairs={{0,4},{1,5},{2,6},{3,7},{4,8},{5,9},{6,10},{7,11},{8,12},{9,13},{1... | collective-permute-start | bytes 3145736 | tf_op jit(solution)/shard_map/ppermute | solution.py:19
  231.1 2.5 multiply_add_fusion.1
  233.6 1.3 collective-permute-start.17
  234.9 5.7 %fusion.1 = f32[2,32,64,256]{3,2,1,0:T(8,128)} fusion(f32[2,32,256]{2,1,0:T(8,128)S(1)} %copy-done.17, f32[2,256,256]{2,1,0:T(8,128)S(1)} %fusion.52, pred[256,256]{1,0:T(8,128)(4,1)S(1)} %copy-done.18, bf16[2,256,32,64]{1,3,2,0:T(8,128)(2,1)S(1)} %bitcast.119, f32[2,256,32]{1,2,0:T(8,128)S(1)} %copy-done.13), kind=kOutput, calls=%fused_computation.3 | convolution fusion | flops 556793856 | bytes 7012352 | tf_op jit(solution)/shard_map/rhts,rshp->rthp/dot_general | solution.py:70
  240.6 32.9 %collective-permute-done.7 = f32[2,32,64,64]{3,2,1,0:T(8,128)S(1)} collective-permute-done((f32[2,32,64,64]{3,2,1,0:T(8,128)S(1)}, f32[2,32,64,64]{3,2,1,0:T(8,128)S(1)}, u32[]{:S(2)}, u32[]{:S(2)}) %collective-permute-start.7) | collective-permute-done | bytes 1048608 | tf_op jit(solution)/shard_map/ppermute | solution.py:19
  273.8 5.2 %collective-permute-start.9 = (f32[2,32,64,64]{3,2,1,0:T(8,128)S(1)}, f32[2,32,64,64]{3,2,1,0:T(8,128)S(1)}, u32[]{:S(2)}, u32[]{:S(2)}) collective-permute-start(f32[2,32,64,64]{3,2,1,0:T(8,128)S(1)} %multiply_add_fusion.3), channel_id=1, source_target_pairs={{0,1},{1,2},{2,3},{3,4},{4,5},{5,6},{6,7},{7,8},{8,9},{9,10},{10,1... | collective-permute-start | bytes 3145736 | tf_op jit(solution)/shard_map/ppermute | solution.py:19
  279.0 5.9 %collective-permute-start.8 = (f32[2,32,64,64]{3,2,1,0:T(8,128)S(1)}, f32[2,32,64,64]{3,2,1,0:T(8,128)S(1)}, u32[]{:S(2)}, u32[]{:S(2)}) collective-permute-start(f32[2,32,64,64]{3,2,1,0:T(8,128)S(1)} %multiply_add_fusion.3), channel_id=1, source_target_pairs={{0,9},{1,10},{2,11},{3,12},{4,13},{5,14},{6,15},{16,25},{17,26},{1... | collective-permute-start | bytes 3145736 | tf_op jit(solution)/shard_map/ppermute | solution.py:19
  285.2 2.6 collective-permute-start.19
  287.8 1.3 collective-permute-start.18
  289.1 5.7 %fusion = f32[2,32,64,256]{3,2,1,0:T(8,128)} fusion(f32[2,32,256]{2,1,0:T(8,128)S(1)} %copy-done.16, f32[2,256,256]{2,1,0:T(8,128)S(1)} %fusion.57, pred[256,256]{1,0:T(8,128)(4,1)S(1)} %iota_compare_fusion.1, bf16[2,256,32,64]{1,3,2,0:T(8,128)(2,1)S(1)} %bitcast.122, f32[2,256,32]{1,2,0:T(8,128)S(1)} %get-tuple-element.6), kind=kOutput, calls=%fused_computation.2 | convolution fusion | flops 556793856 | bytes 7012352 | tf_op jit(solution)/shard_map/rhts,rshp->rthp/dot_general | solution.py:70
  294.9 2.4 collective-permute-start.14
  297.3 4.7 %collective-permute-done.9 = f32[2,32,64,64]{3,2,1,0:T(8,128)S(1)} collective-permute-done((f32[2,32,64,64]{3,2,1,0:T(8,128)S(1)}, f32[2,32,64,64]{3,2,1,0:T(8,128)S(1)}, u32[]{:S(2)}, u32[]{:S(2)}) %collective-permute-start.9) | collective-permute-done | bytes 1048608 | tf_op jit(solution)/shard_map/ppermute | solution.py:19
  302.0 22.5 %collective-permute-done.8 = f32[2,32,64,64]{3,2,1,0:T(8,128)S(1)} collective-permute-done((f32[2,32,64,64]{3,2,1,0:T(8,128)S(1)}, f32[2,32,64,64]{3,2,1,0:T(8,128)S(1)}, u32[]{:S(2)}, u32[]{:S(2)}) %collective-permute-start.8) | collective-permute-done | bytes 1048608 | tf_op jit(solution)/shard_map/ppermute | solution.py:19
  324.4 1.9 fusion.38
  326.3 10.5 %collective-permute-done.14 = f32[2,32]{1,0:T(2,128)S(1)} collective-permute-done((f32[2,32]{1,0:T(2,128)S(1)}, f32[2,32]{1,0:T(2,128)S(1)}, u32[]{:S(2)}, u32[]{:S(2)}) %collective-permute-start.14) | collective-permute-done | bytes 288 | tf_op jit(solution)/shard_map/ppermute | solution.py:19
  336.9 13.6 %collective-permute-done.18 = f32[2,32,64,64]{3,2,1,0:T(8,128)S(1)} collective-permute-done((f32[2,32,64,64]{3,2,1,0:T(8,128)S(1)}, f32[2,32,64,64]{3,2,1,0:T(8,128)S(1)}, u32[]{:S(2)}, u32[]{:S(2)}) %collective-permute-start.18) | collective-permute-done | bytes 1048608 | tf_op jit(solution)/shard_map/ppermute | solution.py:19
  350.5 1.4 copy-done.28
  351.9 9.0 %multiply_reduce_fusion = (f32[2,256]{1,0:T(2,128)S(1)}, f32[2,256,32,64]{1,3,2,0:T(8,128)}) fusion(f32[2,256,32,64]{1,3,2,0:T(8,128)S(1)} %copy-done.7, f32[2,256,32]{1,2,0:T(8,128)S(1)} %copy-done.19, f32[2,32,64,64]{3,2,1,0:T(8,128)} %copy-done.27, f32[2,32,64,64]{3,2,1,0:T(8,128)} %copy-done.28, f32[2,32]{1,0:T(2,128)S(1)} %collective-permute-done.14, ...), kind=kOutput, calls=%fused_computation.37 | convolution fusion | flops 824704512 | bytes 29559552 | tf_op jit(solution)/shard_map/rtn,rhpn->rthp/dot_general | solution.py:83
  360.9 9.2 %copy.97 = f32[2,256,32,64]{3,2,1,0:T(8,128)} copy(f32[2,256,32,64]{1,3,2,0:T(8,128)} %get-tuple-element.32) | data formatting | bytes 8388608 | tf_op jit(solution)/shard_map/add | solution.py:124
  370.1 7.8 %reshape.194 = f32[512,2048]{1,0:T(8,128)} reshape(f32[2,256,32,64]{3,2,1,0:T(8,128)} %copy.97) | data formatting | bytes 8388608 | tf_op jit(solution)/shard_map/add | solution.py:124
  377.9 7.5 %add_convert_fusion = bf16[512,1024]{1,0:T(8,128)(2,1)S(1)} fusion(bf16[2048,1024]{1,0:T(8,128)(2,1)} %param.21, f32[512,2048]{1,0:T(8,128)} %reshape.194, f32[512,2048]{1,0:T(8,128)} %fusion.23, f32[2048]{0:T(1024)S(1)} %copy-done.29, f32[512]{0:T(512)S(1)} %bitcast.129, bf16[256,1024]{1,0:T(8,128)(2,1)S(1)} %copy-done.9, bf16[256,1024]{1,0:T(8,128)(2,1)S(1)} %copy-done.11), kind=kOutput, calls=%fused_computation.56 | convolution fusion | flops 2159017984 | bytes 14690304 | tf_op jit(solution)/shard_map/dot_general | solution.py:129
  385.6 2.0 copy.92
  (131 shorter events, 21.4 us)
Async XLA Ops:
  0.0 16.8 %copy-start = (bf16[1024,32]{0,1:T(8,128)(2,1)S(1)}, bf16[1024,32]{0,1:T(8,128)(2,1)}, u32[]{:S(2)}) copy-start(bf16[1024,32]{0,1:T(8,128)(2,1)} %param.14) | copy-start | bytes 196612
  3.8 13.0 %copy-start.8 = (bf16[256,1024]{1,0:T(8,128)(2,1)}, bf16[256,1024]{1,0:T(8,128)(2,1)S(1)}, u32[]{:S(2)}) copy-start(bf16[256,1024]{1,0:T(8,128)(2,1)S(1)} %get-tuple-element.33) | copy-start | bytes 1572868
  3.8 13.0 %copy-start.10 = (bf16[256,1024]{1,0:T(8,128)(2,1)}, bf16[256,1024]{1,0:T(8,128)(2,1)S(1)}, u32[]{:S(2)}) copy-start(bf16[256,1024]{1,0:T(8,128)(2,1)S(1)} %get-tuple-element.34) | copy-start | bytes 1572868
  3.9 12.9 %copy-start.21 = (f32[2,32]{1,0:T(2,128)S(1)}, f32[2,32]{1,0:T(2,128)}, u32[]{:S(2)}) copy-start(f32[2,32]{1,0:T(2,128)} %param.16) | copy-start | bytes 772
  3.9 14.0 %copy-start.22 = (f32[2,32]{1,0:T(2,128)S(1)}, f32[2,32]{1,0:T(2,128)}, u32[]{:S(2)}) copy-start(f32[2,32]{1,0:T(2,128)} %param.15) | copy-start | bytes 772
  3.9 30.4 %copy-start.15 = (f32[2,4,2176]{2,1,0:T(4,128)S(1)}, f32[2,4,2176]{2,1,0:T(4,128)}, u32[]{:S(2)}) copy-start(f32[2,4,2176]{2,1,0:T(4,128)} %param.17) | copy-start | bytes 208900
  8.0 38.0 %collective-permute-start.10 = (bf16[2,3,2176]{2,0,1:T(2,128)(2,1)}, bf16[2,3,2176]{2,0,1:T(2,128)(2,1)}, u32[]{:S(2)}, u32[]{:S(2)}) collective-permute-start(bf16[2,3,2176]{2,0,1:T(2,128)(2,1)} %copy.112), channel_id=1, source_target_pairs={{1,0},{2,1},{3,2},{4,3},{5,4},{6,5},{7,6},{8,7},{9,8},{10,9},{11,1... | collective-permute-start | bytes 78344 | tf_op jit(solution)/shard_map/ppermute | solution.py:19
  11.9 35.5 %collective-permute-start = (bf16[2,3,2176]{2,0,1:T(2,128)(2,1)}, bf16[2,3,2176]{2,0,1:T(2,128)(2,1)}, u32[]{:S(2)}, u32[]{:S(2)}) collective-permute-start(bf16[2,3,2176]{2,0,1:T(2,128)(2,1)} %copy.111), channel_id=1, source_target_pairs={{0,1},{1,2},{2,3},{3,4},{4,5},{5,6},{6,7},{7,8},{8,9},{9,10},{10,1... | collective-permute-start | bytes 78344 | tf_op jit(solution)/shard_map/ppermute | solution.py:19
  16.8 23.9 %copy-start.14 = (f32[2,2176]{1,0:T(2,128)S(1)}, f32[2,2176]{1,0:T(2,128)}, u32[]{:S(2)}) copy-start(f32[2,2176]{1,0:T(2,128)} %param.18) | copy-start | bytes 52228
  18.9 27.1 %copy-start.12 = (f32[2,256,32]{1,2,0:T(8,128)}, f32[2,256,32]{1,2,0:T(8,128)S(1)}, u32[]{:S(2)}) copy-start(f32[2,256,32]{1,2,0:T(8,128)S(1)} %get-tuple-element.30) | copy-start | bytes 196612
  24.9 102.0 %collective-permute-start.11 = (f32[2,32]{1,0:T(2,128)S(1)}, f32[2,32]{1,0:T(2,128)}, u32[]{:S(2)}, u32[]{:S(2)}) collective-permute-start(f32[2,32]{1,0:T(2,128)S(1)} %exp.79), channel_id=1, source_target_pairs={{1,0},{2,1},{3,2},{4,3},{5,4},{6,5},{7,6},{8,7},{9,8},{10,9},{11,1... | collective-permute-start | bytes 776 | tf_op jit(solution)/shard_map/ppermute | solution.py:19
  29.1 52.0 %collective-permute-start.1 = (f32[2,32]{1,0:T(2,128)S(1)}, f32[2,32]{1,0:T(2,128)}, u32[]{:S(2)}, u32[]{:S(2)}) collective-permute-start(f32[2,32]{1,0:T(2,128)S(1)} %exp.72), channel_id=1, source_target_pairs={{0,1},{1,2},{2,3},{3,4},{4,5},{5,6},{6,7},{7,8},{8,9},{9,10},{10,1... | collective-permute-start | bytes 776 | tf_op jit(solution)/shard_map/ppermute | solution.py:19
  69.0 4.1 %copy-start.2 = (bf16[2,256,2176]{1,2,0:T(8,128)(2,1)}, bf16[2,256,2176]{1,2,0:T(8,128)(2,1)S(1)}, u32[]{:S(2)}) copy-start(bf16[2,256,2176]{1,2,0:T(8,128)(2,1)S(1)} %get-tuple-element.9) | copy-start | bytes 6684676
  69.2 4.0 %copy-start.3 = (bf16[2,256,2048]{1,2,0:T(8,128)(2,1)}, bf16[2,256,2048]{1,2,0:T(8,128)(2,1)S(1)}, u32[]{:S(2)}) copy-start(bf16[2,256,2048]{1,2,0:T(8,128)(2,1)S(1)} %slice.148) | copy-start | bytes 6291460
  69.3 4.5 %copy-start.5 = (bf16[2,256,2048]{1,2,0:T(8,128)(2,1)}, bf16[2,256,2048]{1,2,0:T(8,128)(2,1)S(1)}, u32[]{:S(2)}) copy-start(bf16[2,256,2048]{1,2,0:T(8,128)(2,1)S(1)} %slice.137) | copy-start | bytes 6291460
  69.3 6.6 %copy-start.9 = (bf16[256,1024]{1,0:T(8,128)(2,1)S(1)}, bf16[256,1024]{1,0:T(8,128)(2,1)}, u32[]{:S(2)}) copy-start(bf16[256,1024]{1,0:T(8,128)(2,1)} %copy-done.8) | copy-start | bytes 1572868
  69.4 6.6 %copy-start.11 = (bf16[256,1024]{1,0:T(8,128)(2,1)S(1)}, bf16[256,1024]{1,0:T(8,128)(2,1)}, u32[]{:S(2)}) copy-start(bf16[256,1024]{1,0:T(8,128)(2,1)} %copy-done.10) | copy-start | bytes 1572868
  69.4 6.6 %copy-start.26 = (bf16[1024,2048]{1,0:T(8,128)(2,1)S(1)}, bf16[1024,2048]{1,0:T(8,128)(2,1)}, u32[]{:S(2)}) copy-start(bf16[1024,2048]{1,0:T(8,128)(2,1)} %param.12) | copy-start | bytes 12582916
  70.1 26.0 %collective-permute-start.5 = (f32[2,32,64,64]{3,2,1,0:T(8,128)S(1)}, f32[2,32,64,64]{3,2,1,0:T(8,128)S(1)}, u32[]{:S(2)}, u32[]{:S(2)}) collective-permute-start(f32[2,32,64,64]{3,2,1,0:T(8,128)S(1)} %fusion.31), channel_id=1, source_target_pairs={{0,1},{1,2},{2,3},{3,4},{4,5},{5,6},{6,7},{7,8},{8,9},{9,10},{10,1... | collective-permute-start | bytes 3145736 | tf_op jit(solution)/shard_map/ppermute | solution.py:19
  73.9 50.1 %collective-permute-start.15 = (f32[2,32,64,64]{3,2,1,0:T(8,128)S(1)}, f32[2,32,64,64]{3,2,1,0:T(8,128)S(1)}, u32[]{:S(2)}, u32[]{:S(2)}) collective-permute-start(f32[2,32,64,64]{3,2,1,0:T(8,128)S(1)} %fusion.28), channel_id=1, source_target_pairs={{1,0},{2,1},{3,2},{4,3},{5,4},{6,5},{7,6},{8,7},{9,8},{10,9},{11,1... | collective-permute-start | bytes 3145736 | tf_op jit(solution)/shard_map/ppermute | solution.py:19
  81.8 62.8 %collective-permute-start.2 = (f32[2,32]{1,0:T(2,128)S(1)}, f32[2,32]{1,0:T(2,128)S(1)}, u32[]{:S(2)}, u32[]{:S(2)}) collective-permute-start(f32[2,32]{1,0:T(2,128)S(1)} %exponential_multiply_fusion.3), channel_id=1, source_target_pairs={{0,2},{1,3},{2,4},{3,5},{4,6},{5,7},{6,8},{7,9},{8,10},{9,11},{10,... | collective-permute-start | bytes 776 | tf_op jit(solution)/shard_map/ppermute | solution.py:19
  97.8 126.2 %collective-permute-start.6 = (f32[2,32,64,64]{3,2,1,0:T(8,128)}, f32[2,32,64,64]{3,2,1,0:T(8,128)}, u32[]{:S(2)}, u32[]{:S(2)}) collective-permute-start(f32[2,32,64,64]{3,2,1,0:T(8,128)} %multiply_add_fusion.5), channel_id=1, source_target_pairs={{0,2},{1,3},{2,4},{3,5},{4,6},{5,7},{6,8},{7,9},{8,10},{9,11},{10,... | collective-permute-start | bytes 3145736 | tf_op jit(solution)/shard_map/ppermute | solution.py:19
  125.6 105.5 %collective-permute-start.16 = (f32[2,32,64,64]{3,2,1,0:T(8,128)}, f32[2,32,64,64]{3,2,1,0:T(8,128)}, u32[]{:S(2)}, u32[]{:S(2)}) collective-permute-start(f32[2,32,64,64]{3,2,1,0:T(8,128)} %multiply_add_fusion.2), channel_id=1, source_target_pairs={{2,0},{3,1},{4,2},{5,3},{6,4},{7,5},{8,6},{9,7},{10,8},{11,9},{12,... | collective-permute-start | bytes 3145736 | tf_op jit(solution)/shard_map/ppermute | solution.py:19
  127.5 81.2 %collective-permute-start.12 = (f32[2,32]{1,0:T(2,128)S(1)}, f32[2,32]{1,0:T(2,128)S(1)}, u32[]{:S(2)}, u32[]{:S(2)}) collective-permute-start(f32[2,32]{1,0:T(2,128)S(1)} %exponential_multiply_fusion.2), channel_id=1, source_target_pairs={{2,0},{3,1},{4,2},{5,3},{6,4},{7,5},{8,6},{9,7},{10,8},{11,9},{12,... | collective-permute-start | bytes 776 | tf_op jit(solution)/shard_map/ppermute | solution.py:19
  136.7 73.3 %copy-start.23 = (f32[2,32]{1,0:T(2,128)S(1)}, f32[2,32]{1,0:T(2,128)}, u32[]{:S(2)}) copy-start(f32[2,32]{1,0:T(2,128)} %param.19) | copy-start | bytes 772
  144.6 66.1 %collective-permute-start.3 = (f32[2,32]{1,0:T(2,128)S(1)}, f32[2,32]{1,0:T(2,128)S(1)}, u32[]{:S(2)}, u32[]{:S(2)}) collective-permute-start(f32[2,32]{1,0:T(2,128)S(1)} %mul.330), channel_id=1, source_target_pairs={{0,4},{1,5},{2,6},{3,7},{4,8},{5,9},{6,10},{7,11},{8,12},{9,13},{1... | collective-permute-start | bytes 776 | tf_op jit(solution)/shard_map/ppermute | solution.py:19
  208.7 13.9 %collective-permute-start.13 = (f32[2,32]{1,0:T(2,128)S(1)}, f32[2,32]{1,0:T(2,128)S(1)}, u32[]{:S(2)}, u32[]{:S(2)}) collective-permute-start(f32[2,32]{1,0:T(2,128)S(1)} %mul.367), channel_id=1, source_target_pairs={{4,0},{5,1},{6,2},{7,3},{8,4},{9,5},{10,6},{11,7},{12,8},{13,9},{1... | collective-permute-start | bytes 776 | tf_op jit(solution)/shard_map/ppermute | solution.py:19
  210.6 84.2 %collective-permute-start.4 = (f32[2,32]{1,0:T(2,128)S(1)}, f32[2,32]{1,0:T(2,128)S(1)}, u32[]{:S(2)}, u32[]{:S(2)}) collective-permute-start(f32[2,32]{1,0:T(2,128)S(1)} %mul.331), channel_id=1, source_target_pairs={{0,1},{1,2},{2,3},{3,4},{4,5},{5,6},{6,7},{7,8},{8,9},{9,10},{10,1... | collective-permute-start | bytes 776 | tf_op jit(solution)/shard_map/ppermute | solution.py:19
  226.5 8.4 %copy-start.4 = (bf16[2,256,2048]{1,2,0:T(8,128)(2,1)S(1)}, bf16[2,256,2048]{1,2,0:T(8,128)(2,1)}, u32[]{:S(2)}) copy-start(bf16[2,256,2048]{1,2,0:T(8,128)(2,1)} %copy-done.3) | copy-start | bytes 6291460
  226.5 8.4 %copy-start.13 = (f32[2,256,32]{1,2,0:T(8,128)S(1)}, f32[2,256,32]{1,2,0:T(8,128)}, u32[]{:S(2)}) copy-start(f32[2,256,32]{1,2,0:T(8,128)} %copy-done.12) | copy-start | bytes 196612
  226.5 8.4 %copy-start.17 = (f32[2,32,256]{2,1,0:T(8,128)S(1)}, f32[2,32,256]{2,1,0:T(8,128)}, u32[]{:S(2)}) copy-start(f32[2,32,256]{2,1,0:T(8,128)} %get-tuple-element.26) | copy-start | bytes 196612
  226.5 8.4 %copy-start.18 = (pred[256,256]{1,0:T(8,128)(4,1)S(1)}, pred[256,256]{1,0:T(8,128)(4,1)}, u32[]{:S(2)}) copy-start(pred[256,256]{1,0:T(8,128)(4,1)} %iota_compare_fusion) | copy-start | bytes 196612
  226.5 47.0 %collective-permute-start.7 = (f32[2,32,64,64]{3,2,1,0:T(8,128)S(1)}, f32[2,32,64,64]{3,2,1,0:T(8,128)S(1)}, u32[]{:S(2)}, u32[]{:S(2)}) collective-permute-start(f32[2,32,64,64]{3,2,1,0:T(8,128)S(1)} %multiply_add_fusion.4), channel_id=1, source_target_pairs={{0,4},{1,5},{2,6},{3,7},{4,8},{5,9},{6,10},{7,11},{8,12},{9,13},{1... | collective-permute-start | bytes 3145736 | tf_op jit(solution)/shard_map/ppermute | solution.py:19
  233.6 51.4 %collective-permute-start.17 = (f32[2,32,64,64]{3,2,1,0:T(8,128)S(1)}, f32[2,32,64,64]{3,2,1,0:T(8,128)S(1)}, u32[]{:S(2)}, u32[]{:S(2)}) collective-permute-start(f32[2,32,64,64]{3,2,1,0:T(8,128)S(1)} %multiply_add_fusion.1), channel_id=1, source_target_pairs={{4,0},{5,1},{6,2},{7,3},{8,4},{9,5},{10,6},{11,7},{12,8},{13,9},{1... | collective-permute-start | bytes 3145736 | tf_op jit(solution)/shard_map/ppermute | solution.py:19
  273.8 15.3 %copy-start.6 = (bf16[2,256,2048]{1,2,0:T(8,128)(2,1)S(1)}, bf16[2,256,2048]{1,2,0:T(8,128)(2,1)}, u32[]{:S(2)}) copy-start(bf16[2,256,2048]{1,2,0:T(8,128)(2,1)} %copy-done.5) | copy-start | bytes 6291460
  273.8 15.3 %copy-start.16 = (f32[2,32,256]{2,1,0:T(8,128)S(1)}, f32[2,32,256]{2,1,0:T(8,128)}, u32[]{:S(2)}) copy-start(f32[2,32,256]{2,1,0:T(8,128)} %get-tuple-element.28) | copy-start | bytes 196612
  273.8 28.2 %collective-permute-start.9 = (f32[2,32,64,64]{3,2,1,0:T(8,128)S(1)}, f32[2,32,64,64]{3,2,1,0:T(8,128)S(1)}, u32[]{:S(2)}, u32[]{:S(2)}) collective-permute-start(f32[2,32,64,64]{3,2,1,0:T(8,128)S(1)} %multiply_add_fusion.3), channel_id=1, source_target_pairs={{0,1},{1,2},{2,3},{3,4},{4,5},{5,6},{6,7},{7,8},{8,9},{9,10},{10,1... | collective-permute-start | bytes 3145736 | tf_op jit(solution)/shard_map/ppermute | solution.py:19
  279.0 45.4 %collective-permute-start.8 = (f32[2,32,64,64]{3,2,1,0:T(8,128)S(1)}, f32[2,32,64,64]{3,2,1,0:T(8,128)S(1)}, u32[]{:S(2)}, u32[]{:S(2)}) collective-permute-start(f32[2,32,64,64]{3,2,1,0:T(8,128)S(1)} %multiply_add_fusion.3), channel_id=1, source_target_pairs={{0,9},{1,10},{2,11},{3,12},{4,13},{5,14},{6,15},{16,25},{17,26},{1... | collective-permute-start | bytes 3145736 | tf_op jit(solution)/shard_map/ppermute | solution.py:19
  285.2 51.6 %collective-permute-start.19 = (f32[2,32,64,64]{3,2,1,0:T(8,128)S(1)}, f32[2,32,64,64]{3,2,1,0:T(8,128)S(1)}, u32[]{:S(2)}, u32[]{:S(2)}) collective-permute-start(f32[2,32,64,64]{3,2,1,0:T(8,128)S(1)} %multiply_add_fusion), channel_id=1, source_target_pairs={{1,0},{2,1},{3,2},{4,3},{5,4},{6,5},{7,6},{8,7},{9,8},{10,9},{11,1... | collective-permute-start | bytes 3145736 | tf_op jit(solution)/shard_map/ppermute | solution.py:19
  287.8 62.7 %collective-permute-start.18 = (f32[2,32,64,64]{3,2,1,0:T(8,128)S(1)}, f32[2,32,64,64]{3,2,1,0:T(8,128)S(1)}, u32[]{:S(2)}, u32[]{:S(2)}) collective-permute-start(f32[2,32,64,64]{3,2,1,0:T(8,128)S(1)} %multiply_add_fusion), channel_id=1, source_target_pairs={{9,0},{10,1},{11,2},{12,3},{13,4},{14,5},{15,6},{25,16},{26,17},{2... | collective-permute-start | bytes 3145736 | tf_op jit(solution)/shard_map/ppermute | solution.py:19
  294.8 57.0 %copy-start.7 = (f32[2,256,32,64]{1,3,2,0:T(8,128)S(1)}, f32[2,256,32,64]{1,3,2,0:T(8,128)}, u32[]{:S(2)}) copy-start(f32[2,256,32,64]{1,3,2,0:T(8,128)} %copy.91) | copy-start | bytes 12582916
  294.8 57.0 %copy-start.19 = (f32[2,256,32]{1,2,0:T(8,128)S(1)}, f32[2,256,32]{1,2,0:T(8,128)}, u32[]{:S(2)}) copy-start(f32[2,256,32]{1,2,0:T(8,128)} %get-tuple-element.24) | copy-start | bytes 196612
  294.8 57.0 %copy-start.20 = (f32[2,256,32]{1,2,0:T(8,128)S(1)}, f32[2,256,32]{1,2,0:T(8,128)}, u32[]{:S(2)}) copy-start(f32[2,256,32]{1,2,0:T(8,128)} %get-tuple-element.21) | copy-start | bytes 196612
  294.8 57.0 %copy-start.24 = (f32[2,32]{1,0:T(2,128)S(1)}, f32[2,32]{1,0:T(2,128)}, u32[]{:S(2)}) copy-start(f32[2,32]{1,0:T(2,128)} %rev.16) | copy-start | bytes 772
  294.9 42.0 %collective-permute-start.14 = (f32[2,32]{1,0:T(2,128)S(1)}, f32[2,32]{1,0:T(2,128)S(1)}, u32[]{:S(2)}, u32[]{:S(2)}) collective-permute-start(f32[2,32]{1,0:T(2,128)S(1)} %mul.368), channel_id=1, source_target_pairs={{1,0},{2,1},{3,2},{4,3},{5,4},{6,5},{7,6},{8,7},{9,8},{10,9},{11,1... | collective-permute-start | bytes 776 | tf_op jit(solution)/shard_map/ppermute | solution.py:19
  336.9 13.6 %copy-start.27 = (f32[2,32,64,64]{3,2,1,0:T(8,128)}, f32[2,32,64,64]{3,2,1,0:T(8,128)S(1)}, u32[]{:S(2)}) copy-start(f32[2,32,64,64]{3,2,1,0:T(8,128)S(1)} %collective-permute-done.19) | copy-start | bytes 3145732
  370.0 7.9 %copy-start.29 = (f32[2048]{0:T(1024)S(1)}, f32[2048]{0:T(1024)}, u32[]{:S(2)}) copy-start(f32[2048]{0:T(1024)} %param.20) | copy-start | bytes 24580
  377.9 9.7 %copy-start.1 = (bf16[1024,32]{0,1:T(8,128)(2,1)S(1)}, bf16[1024,32]{0,1:T(8,128)(2,1)}, u32[]{:S(2)}) copy-start(bf16[1024,32]{0,1:T(8,128)(2,1)} %param.14) | copy-start | bytes 196612
  (2 other events, 5.2 us)
where the time goes:
time: 389 us; the launch traced here: 388 us
  waiting for transfers between devices  149 us (38%)
  starting transfers between devices  98.8 us (25%)
  local copies, waits for them, and re-layouts  56.8 us (15%)
  matrix products  41.4 us (11%)
  other arithmetic  40.5 us (10%)
    ppermute x20, waiting for transfers between devices, shifted(): return lax.ppermute(value, 'ctx', pairs)  149 us
    ppermute x20, starting transfers between devices, shifted(): return lax.ppermute(value, 'ctx', pairs)  98.8 us
    convert_element_type x1, other arithmetic, group_terms(): conv = jax.nn.silu(total).astype(jnp.bfloat16)  19.5 us
    add x2, local copies, waits for them, and re-layouts, body(): combined = finish(*rising[:3], rising_in) + finish(*falling[:3], falling_in)  17 us
    convert_element_type x2, local copies, waits for them, and re-layouts, body(): gate.reshape(2, length, gate.shape[1]).astype(jnp.float32)  15.7 us
    dot_general x2, matrix products, group_terms(): jnp.einsum('rhts,rshp->rthp', mixing, scaled, preferred_element_type=jnp....  11.4 us
    dot_general x2, matrix products, finish(): jnp.einsum('rtn,rhpn->rthp', reads.astype(jnp.float32), entering, precisi...  10.9 us
    add x6, other arithmetic, combine(): later[0][..., None, None] * earlier[1] + later[1]  8.8 us
  transfers between devices with their start and end apart: 20, of which 7 were waited for; matrix products, arithmetic and copies ran while one was open for 24% of the time, Pallas kernels for 0%

commit v1 on v0

--- a/solution.py
+++ b/solution.py
@@ -6,6 +6,7 @@
 NS = 64
 K = 4
 Q = 256
+DECAY_LANES = 128
 
 
 def shifted(value, distance):
@@ -20,7 +21,9 @@
 
 
 def combine(earlier, later):
-    return (earlier[0] * later[0], later[0][..., None, None] * earlier[1] + later[1])
+    width = later.shape[-1] - DECAY_LANES
+    lanes = lax.broadcasted_iota(jnp.int32, later.shape, later.ndim - 1)
+    return later[..., width : width + 1] * earlier + jnp.where(lanes < width, later, 0.0)
 
 
 def exclusive_chain(element, sense):
@@ -32,7 +35,8 @@
         cover *= 2
     near = shifted(gathered, sense)
     far = shifted(gathered, sense * (cover + 1))
-    return combine(far, near)[1]
+    chained = combine(far, near)
+    return chained[..., : chained.shape[-1] - DECAY_LANES]
 
 
 def group_terms(window, dt_raw, dt_shift, log_rate, weights, offset, skip_heads, falling):
@@ -75,11 +79,19 @@
         "rshp,rsn->rhpn", weighted, keys_in, preferred_element_type=jnp.float32
     )
     block_decay = jnp.exp(last)
+    message = jnp.concatenate(
+        [
+            block_state.reshape(runs, heads, head_size * NS),
+            jnp.broadcast_to(block_decay[..., None], (runs, heads, DECAY_LANES)),
+        ],
+        axis=-1,
+    )
     local = diagonal + skip_heads[:, None, :, None] * values32
-    return local, cum, reads, (block_decay, block_state)
+    return local, cum, reads, message
 
 
 def finish(local, cum, reads, entering):
+    entering = entering.reshape(local.shape[0], local.shape[2], local.shape[3], NS)
     product = jnp.einsum(
         "rtn,rhpn->rthp", reads.astype(jnp.float32), entering, precision=lax.Precision.HIGHEST
     )

time: 389 us -> 269 us (0.69)
  the two profiles are of different devices: /device:TPU:1 before, /device:TPU:0 now
where the time goes in v1:
time: 269 us; the launch traced here: 268 us
  local copies, waits for them, and re-layouts  72.9 us (27%)
  waiting for transfers between devices  67.6 us (25%)
  matrix products  44.7 us (17%)
  starting transfers between devices  44.6 us (17%)
  other arithmetic  37.8 us (14%)
    ppermute x12, waiting for transfers between devices, shifted(): return lax.ppermute(value, 'ctx', pairs)  67.6 us
    ppermute x12, starting transfers between devices, shifted(): return lax.ppermute(value, 'ctx', pairs)  44.6 us
    convert_element_type x1, other arithmetic, group_terms(): conv = jax.nn.silu(total).astype(jnp.bfloat16)  19.4 us
    add x2, local copies, waits for them, and re-layouts, body(): combined = finish(*rising[:3], rising_in) + finish(*falling[:3], falling_in)  17.1 us
    convert_element_type x2, local copies, waits for them, and re-layouts, body(): gate.reshape(2, length, gate.shape[1]).astype(jnp.float32)  15.7 us
    dot_general x2, matrix products, finish(): jnp.einsum('rtn,rhpn->rthp', reads.astype(jnp.float32), entering, precisi...  12.1 us
    dot_general x2, matrix products, group_terms(): jnp.einsum('rhts,rshp->rthp', mixing, scaled, preferred_element_type=jnp....  11.5 us
    unnamed x77, local copies, waits for them, and re-layouts  7.81 us
  transfers between devices with their start and end apart: 12, of which 3 were waited for; matrix products, arithmetic and copies ran while one was open for 25% of the time, Pallas kernels for 0%

profile of v1, /device:TPU:0, one launch (start us, length us, event | category | flops | bytes accessed | tf_op | source)
XLA Modules:
  0.0 268.2 jit_solution(10923935605412144256)
XLA Ops:
  0.0 3.4 %fusion.63 = (bf16[256,1,1024]{2,1,0:T(2,128)(2,1)S(1)}, bf16[256,1,1024]{2,1,0:T(2,128)(2,1)S(1)}) fusion(bf16[256,2,1024]{2,1,0:T(2,128)(2,1)} %param.11), kind=kLoop, calls=%fused_computation.145 | loop fusion | bytes 2097152 | tf_op jit(solution)/shard_map/slice | solution.py:106
  3.9 3.4 %convolution_convert_fusion = bf16[512,2176]{1,0:T(8,128)(2,1)S(1)} fusion(bf16[1024,2176]{1,0:T(8,128)(2,1)S(1)} %copy-done.32, bf16[256,1024]{1,0:T(8,128)(2,1)S(1)} %get-tuple-element.39, bf16[256,1024]{1,0:T(8,128)(2,1)S(1)} %get-tuple-element.40), kind=kOutput, calls=%fused_computation.22 | convolution fusion | flops 2284912640 | bytes 7733248 | tf_op jit(solution)/shard_map/dot_general | solution.py:108
  7.9 1.3 collective-permute-start.6
  9.9 3.6 %collective-permute-start = (bf16[2,3,2176]{2,0,1:T(2,128)(2,1)}, bf16[2,3,2176]{2,0,1:T(2,128)(2,1)}, u32[]{:S(2)}, u32[]{:S(2)}) collective-permute-start(bf16[2,3,2176]{2,0,1:T(2,128)(2,1)} %copy.144), channel_id=1, source_target_pairs={{0,1},{1,2},{2,3},{3,4},{4,5},{5,6},{6,7},{7,8},{8,9},{9,10},{10,1... | collective-permute-start | bytes 78344 | tf_op jit(solution)/shard_map/ppermute | solution.py:20
  17.9 5.0 %reduce-window.16 = f32[2,32,2,128]{3,1,2,0:T(8,128)S(1)} reduce-window(f32[2,32,2,128]{3,1,2,0:T(8,128)S(1)} %bitcast.132, f32[]{:T(128)} %constant.13.clone.1), window={size=1x1x1x128 pad=0_0x0_0x0_0x0_127}, to_apply=%region_2.3 | reduce-window | flops 2080768 | bytes 131076 | tf_op jit(solution)/shard_map/reduce-window.2
  27.3 1.3 copy_bitcast_fusion.8
  28.8 2.5 copy.109
  31.3 5.2 %rev.13 = f32[2,2176]{1,0:T(2,128)} reverse(f32[2,2176]{1,0:T(2,128)S(1)} %copy-done.20), dimensions={0} | reverse | bytes 34816 | tf_op jit(solution)/shard_map/rev | solution.py:130
  36.5 1.4 copy.116
  37.9 2.2 copy.108
  40.1 19.4 %multiply_convert_fusion.4 = (bf16[2,256,2176]{1,2,0:T(8,128)(2,1)S(1)}, bf16[2,256,2176]{1,2,0:T(8,128)(2,1)S(1)}) fusion(bf16[2,256,2176]{1,2,0:T(8,128)(2,1)} %copy.109, bf16[2,3,2176]{1,2,0:T(8,128)(2,1)S(1)} %copy.116, f32[2,2176]{1,0:T(2,128)} %get-tuple-element.47, f32[2,2176]{1,0:T(2,128)} %get-tuple-element.48, f32[2,2176]{1,0:T(2,128)} %get-tuple-element.49, ...), kind=kLoop, calls=%fused_computation.25 | loop fusion | flops 56819712 | bytes 6910976 | tf_op jit(solution)/shard_map/convert_element_type | solution.py:52
  59.6 1.2 copy-done.3
  61.5 2.1 fusion.28
  63.5 2.1 reshape.198
  66.8 1.3 collective-permute-start.7
  69.0 1.4 copy-done.7
  70.3 2.0 fusion.31
  72.4 2.9 %reshape.194 = f32[2,32,4096]{2,1,0:T(8,128)} reshape(f32[2,32,64,64]{3,2,1,0:T(8,128)} %fusion.31) | data formatting | bytes 2097152 | tf_op jit(solution)/shard_map/reshape | solution.py:84
  75.3 1.4 pad_maximum_fusion.2
  76.7 4.9 %collective-permute-start.1 = (f32[2,32,4224]{2,1,0:T(8,128)S(1)}, f32[2,32,4224]{2,1,0:T(8,128)S(1)}, u32[]{:S(2)}, u32[]{:S(2)}) collective-permute-start(f32[2,32,4224]{2,1,0:T(8,128)S(1)} %pad_maximum_fusion.2), channel_id=1, source_target_pairs={{0,1},{1,2},{2,3},{3,4},{4,5},{5,6},{6,7},{7,8},{8,9},{9,10},{10,1... | collective-permute-start | bytes 3244040 | tf_op jit(solution)/shard_map/ppermute | solution.py:20
  81.7 1.4 select_add_fusion.2
  83.1 1.7 collective-permute-start.8
  84.9 30.5 %collective-permute-done.8 = f32[2,32,4224]{2,1,0:T(8,128)S(1)} collective-permute-done((f32[2,32,4224]{2,1,0:T(8,128)S(1)}, f32[2,32,4224]{2,1,0:T(8,128)S(1)}, u32[]{:S(2)}, u32[]{:S(2)}) %collective-permute-start.8) | collective-permute-done | bytes 1081376 | tf_op jit(solution)/shard_map/ppermute | solution.py:20
  115.5 1.3 select_add_fusion.1
  116.8 1.3 collective-permute-start.9
  118.0 9.4 %collective-permute-start.2 = (f32[2,32,4224]{2,1,0:T(8,128)}, f32[2,32,4224]{2,1,0:T(8,128)}, u32[]{:S(2)}, u32[]{:S(2)}) collective-permute-start(f32[2,32,4224]{2,1,0:T(8,128)} %get-tuple-element.34), channel_id=1, source_target_pairs={{0,2},{1,3},{2,4},{3,5},{4,6},{5,7},{6,8},{7,9},{8,10},{9,11},{10,... | collective-permute-start | bytes 3244040 | tf_op jit(solution)/shard_map/ppermute | solution.py:20
  127.4 4.4 %fusion.23 = f32[512,2048]{1,0:T(8,128)} fusion(bf16[1024,2048]{1,0:T(8,128)(2,1)S(1)} %copy-done.33, bf16[256,1024]{1,0:T(8,128)(2,1)S(1)} %copy-done.12, bf16[256,1024]{1,0:T(8,128)(2,1)S(1)} %copy-done.15), kind=kOutput, calls=%fused_computation.47 | convolution fusion | flops 2151677952 | bytes 9437184 | tf_op jit(solution)/shard_map/dot_general | solution.py:107
  131.8 7.9 %reshape.209 = f32[2,256,32,64]{3,2,1,0:T(8,128)} reshape(f32[512,2048]{1,0:T(8,128)} %fusion.23) | data formatting | bytes 8388608 | tf_op jit(solution)/shard_map/convert_element_type | solution.py:137
  139.7 7.8 %copy.124 = f32[2,256,32,64]{1,3,2,0:T(8,128)} copy(f32[2,256,32,64]{3,2,1,0:T(8,128)} %reshape.209) | data formatting | bytes 8388608 | tf_op jit(solution)/shard_map/convert_element_type | solution.py:137
  148.6 2.3 select_add_fusion
  150.9 6.9 %collective-permute-start.3 = (f32[2,32,4224]{2,1,0:T(8,128)S(1)}, f32[2,32,4224]{2,1,0:T(8,128)S(1)}, u32[]{:S(2)}, u32[]{:S(2)}) collective-permute-start(f32[2,32,4224]{2,1,0:T(8,128)S(1)} %get-tuple-element.32), channel_id=1, source_target_pairs={{0,4},{1,5},{2,6},{3,7},{4,8},{5,9},{6,10},{7,11},{8,12},{9,13},{1... | collective-permute-start | bytes 3244040 | tf_op jit(solution)/shard_map/ppermute | solution.py:20
  158.9 5.7 %fusion.1 = f32[2,32,64,256]{3,2,1,0:T(8,128)} fusion(f32[2,32,256]{2,1,0:T(8,128)S(1)} %copy-done.26, f32[2,256,256]{2,1,0:T(8,128)S(1)} %fusion.48, pred[256,256]{1,0:T(8,128)(4,1)S(1)} %iota_compare_fusion, bf16[2,256,32,64]{1,3,2,0:T(8,128)(2,1)S(1)} %bitcast.125, f32[2,256,32]{1,2,0:T(8,128)S(1)} %copy-done.18), kind=kOutput, calls=%fused_computation.3 | convolution fusion | flops 556793856 | bytes 7012352 | tf_op jit(solution)/shard_map/rhts,rshp->rthp/dot_general | solution.py:74
  164.6 1.4 collective-permute-start.10
  166.1 1.3 collective-permute-start.11
  167.4 12.2 %collective-permute-done.3 = f32[2,32,4224]{2,1,0:T(8,128)S(1)} collective-permute-done((f32[2,32,4224]{2,1,0:T(8,128)S(1)}, f32[2,32,4224]{2,1,0:T(8,128)S(1)}, u32[]{:S(2)}, u32[]{:S(2)}) %collective-permute-start.3) | collective-permute-done | bytes 1081376 | tf_op jit(solution)/shard_map/ppermute | solution.py:20
  179.8 4.4 %collective-permute-start.4 = (f32[2,32,4224]{2,1,0:T(8,128)S(1)}, f32[2,32,4224]{2,1,0:T(8,128)S(1)}, u32[]{:S(2)}, u32[]{:S(2)}) collective-permute-start(f32[2,32,4224]{2,1,0:T(8,128)S(1)} %select_add_fusion.3), channel_id=1, source_target_pairs={{0,1},{1,2},{2,3},{3,4},{4,5},{5,6},{6,7},{7,8},{8,9},{9,10},{10,1... | collective-permute-start | bytes 3244040 | tf_op jit(solution)/shard_map/ppermute | solution.py:20
  184.2 7.1 %collective-permute-start.5 = (f32[2,32,4224]{2,1,0:T(8,128)S(1)}, f32[2,32,4224]{2,1,0:T(8,128)S(1)}, u32[]{:S(2)}, u32[]{:S(2)}) collective-permute-start(f32[2,32,4224]{2,1,0:T(8,128)S(1)} %select_add_fusion.3), channel_id=1, source_target_pairs={{0,9},{1,10},{2,11},{3,12},{4,13},{5,14},{6,15},{16,25},{17,26},{1... | collective-permute-start | bytes 3244040 | tf_op jit(solution)/shard_map/ppermute | solution.py:20
  191.6 5.8 %fusion = f32[2,32,64,256]{3,2,1,0:T(8,128)} fusion(f32[2,32,256]{2,1,0:T(8,128)S(1)} %copy-done.25, f32[2,256,256]{2,1,0:T(8,128)S(1)} %fusion.53, pred[256,256]{1,0:T(8,128)(4,1)S(1)} %iota_compare_fusion.1, bf16[2,256,32,64]{1,3,2,0:T(8,128)(2,1)S(1)} %bitcast.128, f32[2,256,32]{1,2,0:T(8,128)S(1)} %get-tuple-element.6), kind=kOutput, calls=%fused_computation.2 | convolution fusion | flops 556793856 | bytes 7012352 | tf_op jit(solution)/shard_map/rhts,rshp->rthp/dot_general | solution.py:74
  197.6 24.9 %collective-permute-done.11 = f32[2,32,4224]{2,1,0:T(8,128)S(1)} collective-permute-done((f32[2,32,4224]{2,1,0:T(8,128)S(1)}, f32[2,32,4224]{2,1,0:T(8,128)S(1)}, u32[]{:S(2)}, u32[]{:S(2)}) %collective-permute-start.11) | collective-permute-done | bytes 1081376 | tf_op jit(solution)/shard_map/ppermute | solution.py:20
  222.5 1.4 fusion.40
  223.8 3.2 %reshape.199 = f32[2,32,64,64]{3,2,1,0:T(8,128)} reshape(f32[2,32,4096]{2,1,0:T(8,128)} %get-tuple-element.35) | data formatting | bytes 2097152 | tf_op jit(solution)/shard_map/reshape | solution.py:94
  227.0 2.2 reshape.195
  229.2 3.5 %fusion.45 = f32[2,256,32,64]{1,3,2,0:T(8,128)S(1)} fusion(f32[2,32,64,64]{3,2,1,0:T(8,128)} %reshape.195, bf16[2,256,2176]{1,2,0:T(8,128)(2,1)S(1)} %get-tuple-element.10), kind=kOutput, calls=%fused_computation.99 | convolution fusion | flops 805306368 | bytes 5308416 | tf_op jit(solution)/shard_map/rtn,rhpn->rthp/dot_general | solution.py:95
  232.8 8.6 %multiply_reduce_fusion = (f32[2,256]{1,0:T(2,128)S(1)}, f32[2,256,32,64]{1,3,2,0:T(8,128)}) fusion(f32[2,256,32,64]{1,3,2,0:T(8,128)} %copy.124, f32[2,256,32]{1,2,0:T(8,128)S(1)} %copy-done.27, f32[2,32,64,64]{3,2,1,0:T(8,128)S(1)} %copy-done.10, bf16[2,256,2176]{1,2,0:T(8,128)(2,1)} %copy-done.3, bf16[2,256,32,64]{1,3,2,0:T(8,128)(2,1)S(1)} %bitcast.126, ...), kind=kOutput, calls=%fused_computation.37 | convolution fusion | flops 824180224 | bytes 26413568 | tf_op jit(solution)/shard_map/rtn,rhpn->rthp/dot_general | solution.py:95
  241.3 9.1 %copy.130 = f32[2,256,32,64]{3,2,1,0:T(8,128)} copy(f32[2,256,32,64]{1,3,2,0:T(8,128)} %get-tuple-element.38) | data formatting | bytes 8388608 | tf_op jit(solution)/shard_map/add | solution.py:136
  250.5 7.9 %reshape.208 = f32[512,2048]{1,0:T(8,128)} reshape(f32[2,256,32,64]{3,2,1,0:T(8,128)} %copy.130) | data formatting | bytes 8388608 | tf_op jit(solution)/shard_map/add | solution.py:136
  258.5 7.5 %add_convert_fusion = bf16[512,1024]{1,0:T(8,128)(2,1)S(1)} fusion(bf16[2048,1024]{1,0:T(8,128)(2,1)} %param.21, f32[512,2048]{1,0:T(8,128)} %reshape.208, f32[512,2048]{1,0:T(8,128)} %fusion.23, f32[2048]{0:T(1024)S(1)} %copy-done.34, f32[512]{0:T(512)S(1)} %bitcast.135, bf16[256,1024]{1,0:T(8,128)(2,1)S(1)} %copy-done.13, bf16[256,1024]{1,0:T(8,128)(2,1)S(1)} %copy-done.16), kind=kOutput, calls=%fused_computation.56 | convolution fusion | flops 2159017984 | bytes 14690304 | tf_op jit(solution)/shard_map/dot_general | solution.py:141
  266.1 2.0 copy.125
  (135 shorter events, 16.7 us)
Async XLA Ops:
  0.0 17.2 %copy-start = (bf16[1024,32]{0,1:T(8,128)(2,1)S(1)}, bf16[1024,32]{0,1:T(8,128)(2,1)}, u32[]{:S(2)}) copy-start(bf16[1024,32]{0,1:T(8,128)(2,1)} %param.14) | copy-start | bytes 196612
  0.0 3.8 %copy-start.32 = (bf16[1024,2176]{1,0:T(8,128)(2,1)S(1)}, bf16[1024,2176]{1,0:T(8,128)(2,1)}, u32[]{:S(2)}) copy-start(bf16[1024,2176]{1,0:T(8,128)(2,1)} %param.13) | copy-start | bytes 13369348
  3.8 13.4 %copy-start.11 = (bf16[256,1024]{1,0:T(8,128)(2,1)}, bf16[256,1024]{1,0:T(8,128)(2,1)S(1)}, u32[]{:S(2)}) copy-start(bf16[256,1024]{1,0:T(8,128)(2,1)S(1)} %get-tuple-element.39) | copy-start | bytes 1572868
  3.8 13.4 %copy-start.14 = (bf16[256,1024]{1,0:T(8,128)(2,1)}, bf16[256,1024]{1,0:T(8,128)(2,1)S(1)}, u32[]{:S(2)}) copy-start(bf16[256,1024]{1,0:T(8,128)(2,1)S(1)} %get-tuple-element.40) | copy-start | bytes 1572868
  3.8 9.7 %copy-start.21 = (f32[2,4,2176]{2,1,0:T(4,128)S(1)}, f32[2,4,2176]{2,1,0:T(4,128)}, u32[]{:S(2)}) copy-start(f32[2,4,2176]{2,1,0:T(4,128)} %param.17) | copy-start | bytes 208900
  3.8 13.4 %copy-start.29 = (f32[2,32]{1,0:T(2,128)S(1)}, f32[2,32]{1,0:T(2,128)}, u32[]{:S(2)}) copy-start(f32[2,32]{1,0:T(2,128)} %param.16) | copy-start | bytes 772
  3.9 13.8 %copy-start.30 = (f32[2,32]{1,0:T(2,128)S(1)}, f32[2,32]{1,0:T(2,128)}, u32[]{:S(2)}) copy-start(f32[2,32]{1,0:T(2,128)} %param.15) | copy-start | bytes 772
  7.9 28.6 %collective-permute-start.6 = (bf16[2,3,2176]{2,0,1:T(2,128)(2,1)}, bf16[2,3,2176]{2,0,1:T(2,128)(2,1)}, u32[]{:S(2)}, u32[]{:S(2)}) collective-permute-start(bf16[2,3,2176]{2,0,1:T(2,128)(2,1)} %copy.145), channel_id=1, source_target_pairs={{1,0},{2,1},{3,2},{4,3},{5,4},{6,5},{7,6},{8,7},{9,8},{10,9},{11,1... | collective-permute-start | bytes 78344 | tf_op jit(solution)/shard_map/ppermute | solution.py:20
  9.9 28.0 %collective-permute-start = (bf16[2,3,2176]{2,0,1:T(2,128)(2,1)}, bf16[2,3,2176]{2,0,1:T(2,128)(2,1)}, u32[]{:S(2)}, u32[]{:S(2)}) collective-permute-start(bf16[2,3,2176]{2,0,1:T(2,128)(2,1)} %copy.144), channel_id=1, source_target_pairs={{0,1},{1,2},{2,3},{3,4},{4,5},{5,6},{6,7},{7,8},{8,9},{9,10},{10,1... | collective-permute-start | bytes 78344 | tf_op jit(solution)/shard_map/ppermute | solution.py:20
  15.4 11.3 %copy-start.22 = (f32[2,1,2176]{2,1,0:T(1,128)S(1)}, f32[2,1,2176]{2,1,0:T(1,128)}, u32[]{:S(2)}) copy-start(f32[2,1,2176]{2,1,0:T(1,128)} %slice.153) | copy-start | bytes 52228
  17.2 9.5 %copy-start.23 = (f32[2,1,2176]{2,1,0:T(1,128)S(1)}, f32[2,1,2176]{2,1,0:T(1,128)}, u32[]{:S(2)}) copy-start(f32[2,1,2176]{2,1,0:T(1,128)} %slice.151) | copy-start | bytes 52228
  17.2 10.1 %copy-start.24 = (f32[2,1,2176]{2,1,0:T(1,128)S(1)}, f32[2,1,2176]{2,1,0:T(1,128)}, u32[]{:S(2)}) copy-start(f32[2,1,2176]{2,1,0:T(1,128)} %slice.149) | copy-start | bytes 52228
  17.7 13.6 %copy-start.20 = (f32[2,2176]{1,0:T(2,128)S(1)}, f32[2,2176]{1,0:T(2,128)}, u32[]{:S(2)}) copy-start(f32[2,2176]{1,0:T(2,128)} %param.18) | copy-start | bytes 52228
  17.9 18.6 %copy-start.17 = (f32[2,256,32]{1,2,0:T(8,128)}, f32[2,256,32]{1,2,0:T(8,128)S(1)}, u32[]{:S(2)}) copy-start(f32[2,256,32]{1,2,0:T(8,128)S(1)} %get-tuple-element.30) | copy-start | bytes 196612
  59.5 1.4 copy-start.3
  59.6 1.8 copy-start.4
  66.8 14.8 %collective-permute-start.7 = (f32[2,32,4224]{2,1,0:T(8,128)}, f32[2,32,4224]{2,1,0:T(8,128)}, u32[]{:S(2)}, u32[]{:S(2)}) collective-permute-start(f32[2,32,4224]{2,1,0:T(8,128)} %pad_maximum_fusion.3), channel_id=1, source_target_pairs={{1,0},{2,1},{3,2},{4,3},{5,4},{6,5},{7,6},{8,7},{9,8},{10,9},{11,1... | collective-permute-start | bytes 3244040 | tf_op jit(solution)/shard_map/ppermute | solution.py:20
  68.8 110.8 %copy-start.19 = (pred[4224]{0:T(1024)(128)(4,1)}, pred[4224]{0:T(1024)(128)(4,1)S(1)}, u32[]{:S(2)}) copy-start(pred[4224]{0:T(1024)(128)(4,1)S(1)} %iota_compare_fusion.2) | copy-start | bytes 12676
  69.0 1.4 copy-start.7
  75.3 40.2 %copy-start.2 = (f32[2,32,4096]{2,1,0:T(8,128)S(1)}, f32[2,32,4096]{2,1,0:T(8,128)}, u32[]{:S(2)}) copy-start(f32[2,32,4096]{2,1,0:T(8,128)} %reshape.194) | copy-start | bytes 3145732
  76.7 8.2 %collective-permute-start.1 = (f32[2,32,4224]{2,1,0:T(8,128)S(1)}, f32[2,32,4224]{2,1,0:T(8,128)S(1)}, u32[]{:S(2)}, u32[]{:S(2)}) collective-permute-start(f32[2,32,4224]{2,1,0:T(8,128)S(1)} %pad_maximum_fusion.2), channel_id=1, source_target_pairs={{0,1},{1,2},{2,3},{3,4},{4,5},{5,6},{6,7},{7,8},{8,9},{9,10},{10,1... | collective-permute-start | bytes 3244040 | tf_op jit(solution)/shard_map/ppermute | solution.py:20
  83.1 44.4 %copy-start.12 = (bf16[256,1024]{1,0:T(8,128)(2,1)S(1)}, bf16[256,1024]{1,0:T(8,128)(2,1)}, u32[]{:S(2)}) copy-start(bf16[256,1024]{1,0:T(8,128)(2,1)} %copy-done.11) | copy-start | bytes 1572868
  83.1 44.4 %copy-start.15 = (bf16[256,1024]{1,0:T(8,128)(2,1)S(1)}, bf16[256,1024]{1,0:T(8,128)(2,1)}, u32[]{:S(2)}) copy-start(bf16[256,1024]{1,0:T(8,128)(2,1)} %copy-done.14) | copy-start | bytes 1572868
  83.1 44.3 %copy-start.33 = (bf16[1024,2048]{1,0:T(8,128)(2,1)S(1)}, bf16[1024,2048]{1,0:T(8,128)(2,1)}, u32[]{:S(2)}) copy-start(bf16[1024,2048]{1,0:T(8,128)(2,1)} %param.12) | copy-start | bytes 12582916
  83.1 32.4 %collective-permute-start.8 = (f32[2,32,4224]{2,1,0:T(8,128)S(1)}, f32[2,32,4224]{2,1,0:T(8,128)S(1)}, u32[]{:S(2)}, u32[]{:S(2)}) collective-permute-start(f32[2,32,4224]{2,1,0:T(8,128)S(1)} %select_add_fusion.2), channel_id=1, source_target_pairs={{2,0},{3,1},{4,2},{5,3},{6,4},{7,5},{8,6},{9,7},{10,8},{11,9},{12,... | collective-permute-start | bytes 3244040 | tf_op jit(solution)/shard_map/ppermute | solution.py:20
  116.8 31.8 %collective-permute-start.9 = (f32[2,32,4224]{2,1,0:T(8,128)S(1)}, f32[2,32,4224]{2,1,0:T(8,128)}, u32[]{:S(2)}, u32[]{:S(2)}) collective-permute-start(f32[2,32,4224]{2,1,0:T(8,128)S(1)} %get-tuple-element.33), channel_id=1, source_target_pairs={{4,0},{5,1},{6,2},{7,3},{8,4},{9,5},{10,6},{11,7},{12,8},{13,9},{1... | collective-permute-start | bytes 3244040 | tf_op jit(solution)/shard_map/ppermute | solution.py:20
  118.0 30.5 %collective-permute-start.2 = (f32[2,32,4224]{2,1,0:T(8,128)}, f32[2,32,4224]{2,1,0:T(8,128)}, u32[]{:S(2)}, u32[]{:S(2)}) collective-permute-start(f32[2,32,4224]{2,1,0:T(8,128)} %get-tuple-element.34), channel_id=1, source_target_pairs={{0,2},{1,3},{2,4},{3,5},{4,6},{5,7},{6,8},{7,9},{8,10},{9,11},{10,... | collective-permute-start | bytes 3244040 | tf_op jit(solution)/shard_map/ppermute | solution.py:20
  139.7 7.8 %copy-start.31 = (f32[2,32]{1,0:T(2,128)S(1)}, f32[2,32]{1,0:T(2,128)}, u32[]{:S(2)}) copy-start(f32[2,32]{1,0:T(2,128)} %param.19) | copy-start | bytes 772
  148.5 10.4 %copy-start.5 = (bf16[2,256,2048]{1,2,0:T(8,128)(2,1)S(1)}, bf16[2,256,2048]{1,2,0:T(8,128)(2,1)}, u32[]{:S(2)}) copy-start(bf16[2,256,2048]{1,2,0:T(8,128)(2,1)} %copy-done.4) | copy-start | bytes 6291460
  148.5 10.4 %copy-start.18 = (f32[2,256,32]{1,2,0:T(8,128)S(1)}, f32[2,256,32]{1,2,0:T(8,128)}, u32[]{:S(2)}) copy-start(f32[2,256,32]{1,2,0:T(8,128)} %copy-done.17) | copy-start | bytes 196612
  148.5 10.4 %copy-start.26 = (f32[2,32,256]{2,1,0:T(8,128)S(1)}, f32[2,32,256]{2,1,0:T(8,128)}, u32[]{:S(2)}) copy-start(f32[2,32,256]{2,1,0:T(8,128)} %get-tuple-element.26) | copy-start | bytes 196612
  150.9 28.7 %collective-permute-start.3 = (f32[2,32,4224]{2,1,0:T(8,128)S(1)}, f32[2,32,4224]{2,1,0:T(8,128)S(1)}, u32[]{:S(2)}, u32[]{:S(2)}) collective-permute-start(f32[2,32,4224]{2,1,0:T(8,128)S(1)} %get-tuple-element.32), channel_id=1, source_target_pairs={{0,4},{1,5},{2,6},{3,7},{4,8},{5,9},{6,10},{7,11},{8,12},{9,13},{1... | collective-permute-start | bytes 3244040 | tf_op jit(solution)/shard_map/ppermute | solution.py:20
  164.6 26.9 %copy-start.8 = (bf16[2,256,2048]{1,2,0:T(8,128)(2,1)S(1)}, bf16[2,256,2048]{1,2,0:T(8,128)(2,1)}, u32[]{:S(2)}) copy-start(bf16[2,256,2048]{1,2,0:T(8,128)(2,1)} %copy-done.7) | copy-start | bytes 6291460
  164.6 26.9 %copy-start.25 = (f32[2,32,256]{2,1,0:T(8,128)S(1)}, f32[2,32,256]{2,1,0:T(8,128)}, u32[]{:S(2)}) copy-start(f32[2,32,256]{2,1,0:T(8,128)} %get-tuple-element.28) | copy-start | bytes 196612
  164.6 32.7 %collective-permute-start.10 = (f32[2,32,4224]{2,1,0:T(8,128)S(1)}, f32[2,32,4224]{2,1,0:T(8,128)S(1)}, u32[]{:S(2)}, u32[]{:S(2)}) collective-permute-start(f32[2,32,4224]{2,1,0:T(8,128)S(1)} %get-tuple-element.31), channel_id=1, source_target_pairs={{1,0},{2,1},{3,2},{4,3},{5,4},{6,5},{7,6},{8,7},{9,8},{10,9},{11,1... | collective-permute-start | bytes 3244040 | tf_op jit(solution)/shard_map/ppermute | solution.py:20
  166.1 56.4 %collective-permute-start.11 = (f32[2,32,4224]{2,1,0:T(8,128)S(1)}, f32[2,32,4224]{2,1,0:T(8,128)S(1)}, u32[]{:S(2)}, u32[]{:S(2)}) collective-permute-start(f32[2,32,4224]{2,1,0:T(8,128)S(1)} %get-tuple-element.31), channel_id=1, source_target_pairs={{9,0},{10,1},{11,2},{12,3},{13,4},{14,5},{15,6},{25,16},{26,17},{2... | collective-permute-start | bytes 3244040 | tf_op jit(solution)/shard_map/ppermute | solution.py:20
  179.8 17.7 %collective-permute-start.4 = (f32[2,32,4224]{2,1,0:T(8,128)S(1)}, f32[2,32,4224]{2,1,0:T(8,128)S(1)}, u32[]{:S(2)}, u32[]{:S(2)}) collective-permute-start(f32[2,32,4224]{2,1,0:T(8,128)S(1)} %select_add_fusion.3), channel_id=1, source_target_pairs={{0,1},{1,2},{2,3},{3,4},{4,5},{5,6},{6,7},{7,8},{8,9},{9,10},{10,1... | collective-permute-start | bytes 3244040 | tf_op jit(solution)/shard_map/ppermute | solution.py:20
  184.2 38.2 %collective-permute-start.5 = (f32[2,32,4224]{2,1,0:T(8,128)S(1)}, f32[2,32,4224]{2,1,0:T(8,128)S(1)}, u32[]{:S(2)}, u32[]{:S(2)}) collective-permute-start(f32[2,32,4224]{2,1,0:T(8,128)S(1)} %select_add_fusion.3), channel_id=1, source_target_pairs={{0,9},{1,10},{2,11},{3,12},{4,13},{5,14},{6,15},{16,25},{17,26},{1... | collective-permute-start | bytes 3244040 | tf_op jit(solution)/shard_map/ppermute | solution.py:20
  191.6 30.9 %slice-start = ((pred[4224]{0:T(1024)(128)(4,1)}), pred[4096]{0:T(1024)(128)(4,1)S(1)}, s32[]{:S(2)}) async-start(pred[4224]{0:T(1024)(128)(4,1)} %copy-done.19), calls=%async_computation | async-start | bytes 8192 | tf_op jit(solution)/shard_map/slice | solution.py:39
  227.0 5.8 %copy-start.28 = (f32[2,256,32]{1,2,0:T(8,128)S(1)}, f32[2,256,32]{1,2,0:T(8,128)}, u32[]{:S(2)}) copy-start(f32[2,256,32]{1,2,0:T(8,128)} %get-tuple-element.21) | copy-start | bytes 196612
  229.2 3.5 %copy-start.6 = (bf16[2,256,2048]{1,2,0:T(8,128)(2,1)S(1)}, bf16[2,256,2048]{1,2,0:T(8,128)(2,1)}, u32[]{:S(2)}) copy-start(bf16[2,256,2048]{1,2,0:T(8,128)(2,1)} %copy-done.4) | copy-start | bytes 6291460
  229.2 3.6 %copy-start.9 = (bf16[2,256,2048]{1,2,0:T(8,128)(2,1)S(1)}, bf16[2,256,2048]{1,2,0:T(8,128)(2,1)}, u32[]{:S(2)}) copy-start(bf16[2,256,2048]{1,2,0:T(8,128)(2,1)} %copy-done.7) | copy-start | bytes 6291460
  229.2 3.6 %copy-start.10 = (f32[2,32,64,64]{3,2,1,0:T(8,128)S(1)}, f32[2,32,64,64]{3,2,1,0:T(8,128)}, u32[]{:S(2)}) copy-start(f32[2,32,64,64]{3,2,1,0:T(8,128)} %reshape.199) | copy-start | bytes 3145732
  229.2 3.6 %copy-start.27 = (f32[2,256,32]{1,2,0:T(8,128)S(1)}, f32[2,256,32]{1,2,0:T(8,128)}, u32[]{:S(2)}) copy-start(f32[2,256,32]{1,2,0:T(8,128)} %get-tuple-element.23) | copy-start | bytes 196612
  250.5 7.9 %copy-start.13 = (bf16[256,1024]{1,0:T(8,128)(2,1)S(1)}, bf16[256,1024]{1,0:T(8,128)(2,1)}, u32[]{:S(2)}) copy-start(bf16[256,1024]{1,0:T(8,128)(2,1)} %copy-done.11) | copy-start | bytes 1572868
  250.5 7.9 %copy-start.16 = (bf16[256,1024]{1,0:T(8,128)(2,1)S(1)}, bf16[256,1024]{1,0:T(8,128)(2,1)}, u32[]{:S(2)}) copy-start(bf16[256,1024]{1,0:T(8,128)(2,1)} %copy-done.14) | copy-start | bytes 1572868
  250.5 8.0 %copy-start.34 = (f32[2048]{0:T(1024)S(1)}, f32[2048]{0:T(1024)}, u32[]{:S(2)}) copy-start(f32[2048]{0:T(1024)} %param.20) | copy-start | bytes 24580
  258.4 9.7 %copy-start.1 = (bf16[1024,32]{0,1:T(8,128)(2,1)S(1)}, bf16[1024,32]{0,1:T(8,128)(2,1)}, u32[]{:S(2)}) copy-start(bf16[1024,32]{0,1:T(8,128)(2,1)} %param.14) | copy-start | bytes 196612

commit v2 on v1

--- a/solution.py
+++ b/solution.py
@@ -28,14 +28,31 @@
 
 def exclusive_chain(element, sense):
     size = lax.axis_size("ctx")
-    cover = 1
-    gathered = element
-    while 2 * cover < size:
-        gathered = combine(shifted(gathered, sense * cover), gathered)
-        cover *= 2
-    near = shifted(gathered, sense)
-    far = shifted(gathered, sense * (cover + 1))
-    chained = combine(far, near)
+    group = 4
+    assert size == group * group
+    here = lax.axis_index("ctx")
+    spot = here if sense == 1 else size - 1 - here
+    slot = spot % group
+
+    def place(position):
+        return position if sense == 1 else size - 1 - position
+
+    def send(value, moves):
+        return lax.ppermute(value, "ctx", [(place(a), place(b)) for a, b in moves])
+
+    tops = range(0, size, group)
+    first = send(element, [(t + k, t + k + 1) for t in tops for k in (0, 2)])
+    pair = combine(first, element)
+    other = send(pair, [(t + a, t + b) for t in tops for a, b in ((1, 3), (3, 1))])
+    whole = jnp.where(slot == 1, combine(pair, other), combine(other, pair))
+    ends = [t + k for t in tops for k in (1, 3)]
+    previous = send(whole, [(a, a + group) for a in ends if a + group < size])
+    two = combine(previous, whole)
+    further = send(two, [(a, a + 2 * group) for a in ends if a + 2 * group < size])
+    entering = combine(further, previous)
+    handed = jnp.where(slot == 1, entering, combine(entering, other))
+    below = send(handed, [(t + k + 1, t + k) for t in tops for k in (0, 2)])
+    chained = jnp.where(slot % 2 == 1, combine(handed, first), below)
     return chained[..., : chained.shape[-1] - DECAY_LANES]
 
 

time: 269 us -> 243 us (0.903)
  the two profiles are of different devices: /device:TPU:0 before, /device:TPU:1 now
where the time goes in v2:
time: 243 us; the launch traced here: 242 us
  local copies, waits for them, and re-layouts  74.3 us (31%)
  starting transfers between devices  57.3 us (24%)
  matrix products  47 us (19%)
  other arithmetic  46.7 us (19%)
  waiting for transfers between devices  16 us (7%)
    ppermute x10, starting transfers between devices, send(): return lax.ppermute(value, 'ctx', [(place(a), place(b)) for a, b in moves])  49.1 us
    convert_element_type x1, other arithmetic, group_terms(): conv = jax.nn.silu(total).astype(jnp.bfloat16)  18.9 us
    add x2, local copies, waits for them, and re-layouts, body(): combined = finish(*rising[:3], rising_in) + finish(*falling[:3], falling_in)  17 us
    ppermute x10, waiting for transfers between devices, send(): return lax.ppermute(value, 'ctx', [(place(a), place(b)) for a, b in moves])  15.9 us
    convert_element_type x2, local copies, waits for them, and re-layouts, body(): gate.reshape(2, length, gate.shape[1]).astype(jnp.float32)  15.6 us
    dot_general x2, matrix products, finish(): jnp.einsum('rtn,rhpn->rthp', reads.astype(jnp.float32), entering, precisi...  12 us
    dot_general x2, matrix products, group_terms(): jnp.einsum('rhts,rshp->rthp', mixing, scaled, preferred_element_type=jnp....  11.4 us
    ppermute x2, starting transfers between devices, shifted(): return lax.ppermute(value, 'ctx', pairs)  8.13 us
  transfers between devices with their start and end apart: 12, of which 3 were waited for; matrix products, arithmetic and copies ran while one was open for 30% of the time, Pallas kernels for 0%

profile of v2, /device:TPU:1, one launch (start us, length us, event | category | flops | bytes accessed | tf_op | source)
XLA Modules:
  0.0 241.9 jit_solution(11941891644330070298)
XLA Ops:
  0.0 3.4 %fusion.63 = (bf16[256,1,1024]{2,1,0:T(2,128)(2,1)S(1)}, bf16[256,1,1024]{2,1,0:T(2,128)(2,1)S(1)}) fusion(bf16[256,2,1024]{2,1,0:T(2,128)(2,1)} %param.11), kind=kLoop, calls=%fused_computation.153 | loop fusion | bytes 2097152 | tf_op jit(solution)/shard_map/slice | solution.py:123
  3.9 3.4 %convolution_convert_fusion = bf16[512,2176]{1,0:T(8,128)(2,1)S(1)} fusion(bf16[1024,2176]{1,0:T(8,128)(2,1)S(1)} %copy-done.32, bf16[256,1024]{1,0:T(8,128)(2,1)S(1)} %get-tuple-element.39, bf16[256,1024]{1,0:T(8,128)(2,1)S(1)} %get-tuple-element.40), kind=kOutput, calls=%fused_computation.22 | convolution fusion | flops 2284912640 | bytes 7733248 | tf_op jit(solution)/shard_map/dot_general | solution.py:125
  7.3 1.4 copy-done.13
  8.7 3.3 %collective-permute-start.6 = (bf16[2,3,2176]{2,0,1:T(2,128)(2,1)S(1)}, bf16[2,3,2176]{2,0,1:T(2,128)(2,1)S(1)}, u32[]{:S(2)}, u32[]{:S(2)}) collective-permute-start(bf16[2,3,2176]{2,0,1:T(2,128)(2,1)S(1)} %copy.145), channel_id=1, source_target_pairs={{1,0},{2,1},{3,2},{4,3},{5,4},{6,5},{7,6},{8,7},{9,8},{10,9},{11,1... | collective-permute-start | bytes 78344 | tf_op jit(solution)/shard_map/ppermute | solution.py:20
  12.1 4.8 %collective-permute-start = (bf16[2,3,2176]{2,0,1:T(2,128)(2,1)S(1)}, bf16[2,3,2176]{2,0,1:T(2,128)(2,1)S(1)}, u32[]{:S(2)}, u32[]{:S(2)}) collective-permute-start(bf16[2,3,2176]{2,0,1:T(2,128)(2,1)S(1)} %copy.144), channel_id=1, source_target_pairs={{0,1},{1,2},{2,3},{3,4},{4,5},{5,6},{6,7},{7,8},{8,9},{9,10},{10,1... | collective-permute-start | bytes 78344 | tf_op jit(solution)/shard_map/ppermute | solution.py:20
  19.0 5.0 %reduce-window.16 = f32[2,32,2,128]{3,1,2,0:T(8,128)S(1)} reduce-window(f32[2,32,2,128]{3,1,2,0:T(8,128)S(1)} %bitcast.132, f32[]{:T(128)} %constant.50.clone.1), window={size=1x1x1x128 pad=0_0x0_0x0_0x0_127}, to_apply=%region_2.3 | reduce-window | flops 2080768 | bytes 131076 | tf_op jit(solution)/shard_map/reduce-window.2
  27.5 4.1 %copy.109 = bf16[2,256,2176]{1,2,0:T(8,128)(2,1)} copy(bf16[2,256,2176]{2,1,0:T(8,128)(2,1)} %bitcast.131) | data formatting | bytes 4456448 | tf_op jit(solution)/shard_map/reshape | solution.py:126
  31.6 5.3 %rev.13 = f32[2,2176]{1,0:T(2,128)} reverse(f32[2,2176]{1,0:T(2,128)S(1)} %copy-done.23), dimensions={0} | reverse | bytes 34816 | tf_op jit(solution)/shard_map/rev | solution.py:147
  37.5 1.4 copy.108
  39.0 18.9 %multiply_convert_fusion.4 = (bf16[2,256,2176]{1,2,0:T(8,128)(2,1)S(1)}, bf16[2,256,2176]{1,2,0:T(8,128)(2,1)S(1)}) fusion(bf16[2,256,2176]{1,2,0:T(8,128)(2,1)} %copy.109, bf16[2,3,2176]{1,2,0:T(8,128)(2,1)S(1)} %copy.116, f32[2,2176]{1,0:T(2,128)} %get-tuple-element.47, f32[2,2176]{1,0:T(2,128)} %get-tuple-element.48, f32[2,2176]{1,0:T(2,128)} %get-tuple-element.49, ...), kind=kLoop, calls=%fused_computation.25 | loop fusion | flops 56819712 | bytes 6910976 | tf_op jit(solution)/shard_map/convert_element_type | solution.py:69
  59.8 2.0 fusion.28
  61.9 2.1 reshape.198
  65.2 2.3 collective-permute-start.7
  69.1 2.4 %select_add_fusion.1 = f32[2,32,4224]{2,1,0:T(8,128)} fusion(f32[2,32,4224]{2,1,0:T(8,128)} %collective-permute-done.7, f32[2,32]{1,0:T(2,128)S(1)} %copy-done.28, pred[4224]{0:T(1024)(128)(4,1)S(1)} %iota_compare_fusion.2, f32[2,32,128]{2,1,0:T(8,128)S(1)} %broadcast_in_dim.44, f32[2,32,4096]{2,1,0:T(8,128)S(1)} %reshape.198), kind=kLoop, calls=%fused_computation.69 | loop fusion | flops 1081344 | bytes 3248512 | tf_op jit(solution)/shard_map/add | solution.py:26
  71.5 1.6 collective-permute-start.8
  73.2 1.6 bitcast_exponential_fusion.1
  74.9 1.3 copy-done.6
  76.2 2.0 fusion.31
  78.3 2.1 reshape.194
  80.6 1.3 collective-permute-start.1
  83.6 1.9 add_select_fusion.1
  86.4 2.1 collective-permute-done.1
  88.5 2.0 select_add_fusion
  90.6 3.4 %collective-permute-start.2 = (f32[2,32,4224]{2,1,0:T(8,128)}, f32[2,32,4224]{2,1,0:T(8,128)S(1)}, u32[]{:S(2)}, u32[]{:S(2)}) collective-permute-start(f32[2,32,4224]{2,1,0:T(8,128)} %get-tuple-element.34), channel_id=1, source_target_pairs={{1,3},{3,1},{5,7},{7,5},{9,11},{11,9},{13,15},{15,13},{17,19},{19,... | collective-permute-start | bytes 3244040 | tf_op jit(solution)/shard_map/ppermute | solution.py:41
  94.0 1.7 collective-permute-start.10
  97.4 10.8 %collective-permute-done.2 = f32[2,32,4224]{2,1,0:T(8,128)S(1)} collective-permute-done((f32[2,32,4224]{2,1,0:T(8,128)}, f32[2,32,4224]{2,1,0:T(8,128)S(1)}, u32[]{:S(2)}, u32[]{:S(2)}) %collective-permute-start.2) | collective-permute-done | bytes 1081376 | tf_op jit(solution)/shard_map/ppermute | solution.py:41
  108.3 4.2 %add_select_fusion = (f32[2,32,4224]{2,1,0:T(8,128)}, f32[2,32,4224]{2,1,0:T(8,128)}) fusion(f32[2,32,4224]{2,1,0:T(8,128)} %copy-done.9, f32[2,32,4224]{2,1,0:T(8,128)} %collective-permute-done.10, f32[2,32,4224]{2,1,0:T(8,128)} %collective-permute-done.8, f32[2,32]{1,0:T(2,128)S(1)} %slice_reduce_fusion.3, f32[2,32]{1,0:T(2,128)S(1)} %slice_reduce_fusion.5, ...), kind=kLoop, calls=%fused_computation.66 | loop fusion | flops 3784704 | bytes 7574658 | tf_op jit(solution)/shard_map/jit(_where)/select_n | solution.py:53
  112.5 4.5 %collective-permute-start.3 = (f32[2,32,4224]{2,1,0:T(8,128)}, f32[2,32,4224]{2,1,0:T(8,128)}, u32[]{:S(2)}, u32[]{:S(2)}) collective-permute-start(f32[2,32,4224]{2,1,0:T(8,128)} %get-tuple-element.32), channel_id=1, source_target_pairs={{1,5},{3,7},{5,9},{7,11},{9,13},{11,15},{17,21},{19,23},{21,25},{2... | collective-permute-start | bytes 3244040 | tf_op jit(solution)/shard_map/ppermute | solution.py:41
  117.0 6.8 %fusion.23 = f32[512,2048]{1,0:T(8,128)} fusion(bf16[1024,2048]{1,0:T(8,128)(2,1)} %param.12, bf16[256,1024]{1,0:T(8,128)(2,1)} %copy-done.15, bf16[256,1024]{1,0:T(8,128)(2,1)} %copy-done.17), kind=kOutput, calls=%fused_computation.47 | convolution fusion | flops 2151677952 | bytes 9437184 | tf_op jit(solution)/shard_map/dot_general | solution.py:124
  123.9 7.8 %reshape.209 = f32[2,256,32,64]{3,2,1,0:T(8,128)} reshape(f32[512,2048]{1,0:T(8,128)} %fusion.23) | data formatting | bytes 8388608 | tf_op jit(solution)/shard_map/convert_element_type | solution.py:154
  131.7 7.8 %copy.124 = f32[2,256,32,64]{1,3,2,0:T(8,128)} copy(f32[2,256,32,64]{3,2,1,0:T(8,128)} %reshape.209) | data formatting | bytes 8388608 | tf_op jit(solution)/shard_map/convert_element_type | solution.py:154
  140.6 1.7 select_add_fusion.2
  142.4 3.0 %collective-permute-start.4 = (f32[2,32,4224]{2,1,0:T(8,128)S(1)}, f32[2,32,4224]{2,1,0:T(8,128)S(1)}, u32[]{:S(2)}, u32[]{:S(2)}) collective-permute-start(f32[2,32,4224]{2,1,0:T(8,128)S(1)} %select_add_fusion.2), channel_id=1, source_target_pairs={{1,9},{3,11},{5,13},{7,15},{17,25},{19,27},{21,29},{23,31},{33,41}... | collective-permute-start | bytes 3244040 | tf_op jit(solution)/shard_map/ppermute | solution.py:41
  146.6 5.7 %fusion.1 = f32[2,32,64,256]{3,2,1,0:T(8,128)} fusion(f32[2,32,256]{2,1,0:T(8,128)S(1)} %copy-done.25, f32[2,256,256]{2,1,0:T(8,128)S(1)} %fusion.48, pred[256,256]{1,0:T(8,128)(4,1)S(1)} %iota_compare_fusion, bf16[2,256,32,64]{1,3,2,0:T(8,128)(2,1)S(1)} %bitcast.125, f32[2,256,32]{1,2,0:T(8,128)S(1)} %copy-done.22), kind=kOutput, calls=%fused_computation.3 | convolution fusion | flops 556793856 | bytes 7012352 | tf_op jit(solution)/shard_map/rhts,rshp->rthp/dot_general | solution.py:91
  152.3 1.3 collective-permute-start.11
  154.4 3.0 %collective-permute-done.4 = f32[2,32,4224]{2,1,0:T(8,128)S(1)} collective-permute-done((f32[2,32,4224]{2,1,0:T(8,128)S(1)}, f32[2,32,4224]{2,1,0:T(8,128)S(1)}, u32[]{:S(2)}, u32[]{:S(2)}) %collective-permute-start.4) | collective-permute-done | bytes 1081376 | tf_op jit(solution)/shard_map/ppermute | solution.py:41
  157.4 1.6 add_select_fusion.2
  159.0 29.1 %collective-permute-start.5 = (f32[2,32,4224]{2,1,0:T(8,128)S(1)}, f32[2,32,4224]{2,1,0:T(8,128)S(1)}, u32[]{:S(2)}, u32[]{:S(2)}) collective-permute-start(f32[2,32,4224]{2,1,0:T(8,128)S(1)} %add_select_fusion.2), channel_id=1, source_target_pairs={{1,0},{3,2},{5,4},{7,6},{9,8},{11,10},{13,12},{15,14},{17,16},{19,... | collective-permute-start | bytes 3244040 | tf_op jit(solution)/shard_map/ppermute | solution.py:41
  188.4 5.7 %fusion = f32[2,32,64,256]{3,2,1,0:T(8,128)} fusion(f32[2,32,256]{2,1,0:T(8,128)S(1)} %get-tuple-element.28, f32[2,256,256]{2,1,0:T(8,128)S(1)} %fusion.53, pred[256,256]{1,0:T(8,128)(4,1)S(1)} %iota_compare_fusion.1, bf16[2,256,32,64]{1,3,2,0:T(8,128)(2,1)S(1)} %bitcast.128, f32[2,256,32]{1,2,0:T(8,128)S(1)} %copy-done.20), kind=kOutput, calls=%fused_computation.2 | convolution fusion | flops 556793856 | bytes 7012352 | tf_op jit(solution)/shard_map/rhts,rshp->rthp/dot_general | solution.py:91
  195.1 2.6 %slice_select_fusion = (f32[2,32,4096]{2,1,0:T(8,128)}, f32[2,32,4096]{2,1,0:T(8,128)S(1)}) fusion(f32[2,32,4224]{2,1,0:T(8,128)S(1)} %collective-permute-done.11, f32[2,32,4224]{2,1,0:T(8,128)} %collective-permute-done.7, f32[2,32,4224]{2,1,0:T(8,128)S(1)} %copy-done.12, f32[2,32]{1,0:T(2,128)S(1)} %slice_reduce_fusion.6, pred[]{:T(512)S(6)} %eq.21, ...), kind=kLoop, calls=%fused_computation.74 | loop fusion | flops 2097152 | bytes 8393218 | tf_op jit(solution)/shard_map/jit(_where)/select_n | solution.py:55
  197.7 3.1 %reshape.199 = f32[2,32,64,64]{3,2,1,0:T(8,128)} reshape(f32[2,32,4096]{2,1,0:T(8,128)} %get-tuple-element.35) | data formatting | bytes 2097152 | tf_op jit(solution)/shard_map/reshape | solution.py:111
  200.8 2.2 reshape.195
  203.0 3.5 %fusion.45 = f32[2,256,32,64]{1,3,2,0:T(8,128)S(1)} fusion(f32[2,32,64,64]{3,2,1,0:T(8,128)} %reshape.195, bf16[2,256,2176]{1,2,0:T(8,128)(2,1)S(1)} %get-tuple-element.10), kind=kOutput, calls=%fused_computation.103 | convolution fusion | flops 805306368 | bytes 5308416 | tf_op jit(solution)/shard_map/rtn,rhpn->rthp/dot_general | solution.py:112
  206.6 8.5 %multiply_reduce_fusion = (f32[2,256]{1,0:T(2,128)S(1)}, f32[2,256,32,64]{1,3,2,0:T(8,128)}) fusion(f32[2,256,32,64]{1,3,2,0:T(8,128)} %copy.124, f32[2,256,32]{1,2,0:T(8,128)S(1)} %copy-done.26, f32[2,32,64,64]{3,2,1,0:T(8,128)S(1)} %copy-done.14, bf16[2,256,2176]{1,2,0:T(8,128)(2,1)} %copy-done.2, bf16[2,256,32,64]{1,3,2,0:T(8,128)(2,1)S(1)} %bitcast.126, ...), kind=kOutput, calls=%fused_computation.37 | convolution fusion | flops 824180224 | bytes 26413568 | tf_op jit(solution)/shard_map/rtn,rhpn->rthp/dot_general | solution.py:112
  215.1 9.1 %copy.130 = f32[2,256,32,64]{3,2,1,0:T(8,128)} copy(f32[2,256,32,64]{1,3,2,0:T(8,128)} %get-tuple-element.38) | data formatting | bytes 8388608 | tf_op jit(solution)/shard_map/add | solution.py:153
  224.3 7.9 %reshape.208 = f32[512,2048]{1,0:T(8,128)} reshape(f32[2,256,32,64]{3,2,1,0:T(8,128)} %copy.130) | data formatting | bytes 8388608 | tf_op jit(solution)/shard_map/add | solution.py:153
  232.2 7.5 %add_convert_fusion = bf16[512,1024]{1,0:T(8,128)(2,1)S(1)} fusion(bf16[2048,1024]{1,0:T(8,128)(2,1)} %param.21, f32[512,2048]{1,0:T(8,128)} %reshape.208, f32[512,2048]{1,0:T(8,128)} %fusion.23, f32[2048]{0:T(1024)S(1)} %copy-done.33, f32[512]{0:T(512)S(1)} %bitcast.135, bf16[256,1024]{1,0:T(8,128)(2,1)S(1)} %copy-done.16, bf16[256,1024]{1,0:T(8,128)(2,1)S(1)} %copy-done.18), kind=kOutput, calls=%fused_computation.56 | convolution fusion | flops 2159017984 | bytes 14690304 | tf_op jit(solution)/shard_map/dot_general | solution.py:158
  239.9 2.0 copy.125
  (139 shorter events, 20.7 us)
Async XLA Ops:
  0.0 17.7 %copy-start = (bf16[1024,32]{0,1:T(8,128)(2,1)S(1)}, bf16[1024,32]{0,1:T(8,128)(2,1)}, u32[]{:S(2)}) copy-start(bf16[1024,32]{0,1:T(8,128)(2,1)} %param.14) | copy-start | bytes 196612
  0.0 3.8 %copy-start.32 = (bf16[1024,2176]{1,0:T(8,128)(2,1)S(1)}, bf16[1024,2176]{1,0:T(8,128)(2,1)}, u32[]{:S(2)}) copy-start(bf16[1024,2176]{1,0:T(8,128)(2,1)} %param.13) | copy-start | bytes 13369348
  3.8 13.9 %copy-start.15 = (bf16[256,1024]{1,0:T(8,128)(2,1)}, bf16[256,1024]{1,0:T(8,128)(2,1)S(1)}, u32[]{:S(2)}) copy-start(bf16[256,1024]{1,0:T(8,128)(2,1)S(1)} %get-tuple-element.39) | copy-start | bytes 1572868
  3.8 13.9 %copy-start.17 = (bf16[256,1024]{1,0:T(8,128)(2,1)}, bf16[256,1024]{1,0:T(8,128)(2,1)S(1)}, u32[]{:S(2)}) copy-start(bf16[256,1024]{1,0:T(8,128)(2,1)S(1)} %get-tuple-element.40) | copy-start | bytes 1572868
  3.8 13.1 %copy-start.24 = (f32[2,4,2176]{2,1,0:T(4,128)S(1)}, f32[2,4,2176]{2,1,0:T(4,128)}, u32[]{:S(2)}) copy-start(f32[2,4,2176]{2,1,0:T(4,128)} %param.17) | copy-start | bytes 208900
  3.8 13.8 %copy-start.29 = (f32[2,32]{1,0:T(2,128)S(1)}, f32[2,32]{1,0:T(2,128)}, u32[]{:S(2)}) copy-start(f32[2,32]{1,0:T(2,128)} %param.16) | copy-start | bytes 772
  7.3 1.4 copy-start.13
  7.3 10.9 %copy-start.30 = (f32[2,32]{1,0:T(2,128)S(1)}, f32[2,32]{1,0:T(2,128)}, u32[]{:S(2)}) copy-start(f32[2,32]{1,0:T(2,128)} %param.15) | copy-start | bytes 772
  8.7 28.1 %collective-permute-start.6 = (bf16[2,3,2176]{2,0,1:T(2,128)(2,1)S(1)}, bf16[2,3,2176]{2,0,1:T(2,128)(2,1)S(1)}, u32[]{:S(2)}, u32[]{:S(2)}) collective-permute-start(bf16[2,3,2176]{2,0,1:T(2,128)(2,1)S(1)} %copy.145), channel_id=1, source_target_pairs={{1,0},{2,1},{3,2},{4,3},{5,4},{6,5},{7,6},{8,7},{9,8},{10,9},{11,1... | collective-permute-start | bytes 78344 | tf_op jit(solution)/shard_map/ppermute | solution.py:20
  12.1 25.5 %collective-permute-start = (bf16[2,3,2176]{2,0,1:T(2,128)(2,1)S(1)}, bf16[2,3,2176]{2,0,1:T(2,128)(2,1)S(1)}, u32[]{:S(2)}, u32[]{:S(2)}) collective-permute-start(bf16[2,3,2176]{2,0,1:T(2,128)(2,1)S(1)} %copy.144), channel_id=1, source_target_pairs={{0,1},{1,2},{2,3},{3,4},{4,5},{5,6},{6,7},{7,8},{8,9},{9,10},{10,1... | collective-permute-start | bytes 78344 | tf_op jit(solution)/shard_map/ppermute | solution.py:20
  19.0 12.6 %copy-start.21 = (f32[2,256,32]{1,2,0:T(8,128)}, f32[2,256,32]{1,2,0:T(8,128)S(1)}, u32[]{:S(2)}) copy-start(f32[2,256,32]{1,2,0:T(8,128)S(1)} %get-tuple-element.30) | copy-start | bytes 196612
  27.5 4.1 %copy-start.23 = (f32[2,2176]{1,0:T(2,128)S(1)}, f32[2,2176]{1,0:T(2,128)}, u32[]{:S(2)}) copy-start(f32[2,2176]{1,0:T(2,128)} %param.18) | copy-start | bytes 52228
  57.8 1.4 copy-start.2
  58.0 1.8 copy-start.3
  61.9 2.1 copy-start.28
  65.2 3.9 %collective-permute-start.7 = (f32[2,32,4224]{2,1,0:T(8,128)}, f32[2,32,4224]{2,1,0:T(8,128)}, u32[]{:S(2)}, u32[]{:S(2)}) collective-permute-start(f32[2,32,4224]{2,1,0:T(8,128)} %pad_maximum_fusion.3), channel_id=1, source_target_pairs={{15,14},{13,12},{11,10},{9,8},{7,6},{5,4},{3,2},{1,0},{31,30},{29,... | collective-permute-start | bytes 3244040 | tf_op jit(solution)/shard_map/ppermute | solution.py:41
  68.8 88.6 %copy-start.19 = (pred[4224]{0:T(1024)(128)(4,1)}, pred[4224]{0:T(1024)(128)(4,1)S(1)}, u32[]{:S(2)}) copy-start(pred[4224]{0:T(1024)(128)(4,1)S(1)} %iota_compare_fusion.2) | copy-start | bytes 12676
  71.5 11.2 %collective-permute-start.8 = (f32[2,32,4224]{2,1,0:T(8,128)}, f32[2,32,4224]{2,1,0:T(8,128)}, u32[]{:S(2)}, u32[]{:S(2)}) collective-permute-start(f32[2,32,4224]{2,1,0:T(8,128)} %select_add_fusion.1), channel_id=1, source_target_pairs={{14,12},{12,14},{10,8},{8,10},{6,4},{4,6},{2,0},{0,2},{30,28},{28,... | collective-permute-start | bytes 3244040 | tf_op jit(solution)/shard_map/ppermute | solution.py:41
  74.9 1.4 copy-start.6
  80.6 8.0 %collective-permute-start.1 = (f32[2,32,4224]{2,1,0:T(8,128)S(1)}, f32[2,32,4224]{2,1,0:T(8,128)S(1)}, u32[]{:S(2)}, u32[]{:S(2)}) collective-permute-start(f32[2,32,4224]{2,1,0:T(8,128)S(1)} %pad_maximum_fusion.2), channel_id=1, source_target_pairs={{0,1},{2,3},{4,5},{6,7},{8,9},{10,11},{12,13},{14,15},{16,17},{18,... | collective-permute-start | bytes 3244040 | tf_op jit(solution)/shard_map/ppermute | solution.py:41
  85.4 3.1 %collective-permute-start.9 = (f32[2,32,4224]{2,1,0:T(8,128)S(1)}, f32[2,32,4224]{2,1,0:T(8,128)S(1)}, u32[]{:S(2)}, u32[]{:S(2)}) collective-permute-start(f32[2,32,4224]{2,1,0:T(8,128)S(1)} %add_select_fusion.1), channel_id=1, source_target_pairs={{14,10},{12,8},{10,6},{8,4},{6,2},{4,0},{30,26},{28,24},{26,22},{2... | collective-permute-start | bytes 3244040 | tf_op jit(solution)/shard_map/ppermute | solution.py:41
  88.5 2.0 copy-start.10
  88.5 2.1 copy-start.9
  90.6 17.6 %collective-permute-start.2 = (f32[2,32,4224]{2,1,0:T(8,128)}, f32[2,32,4224]{2,1,0:T(8,128)S(1)}, u32[]{:S(2)}, u32[]{:S(2)}) collective-permute-start(f32[2,32,4224]{2,1,0:T(8,128)} %get-tuple-element.34), channel_id=1, source_target_pairs={{1,3},{3,1},{5,7},{7,5},{9,11},{11,9},{13,15},{15,13},{17,19},{19,... | collective-permute-start | bytes 3244040 | tf_op jit(solution)/shard_map/ppermute | solution.py:41
  94.0 14.3 %collective-permute-start.10 = (f32[2,32,4224]{2,1,0:T(8,128)}, f32[2,32,4224]{2,1,0:T(8,128)}, u32[]{:S(2)}, u32[]{:S(2)}) collective-permute-start(f32[2,32,4224]{2,1,0:T(8,128)} %get-tuple-element.33), channel_id=1, source_target_pairs={{14,6},{12,4},{10,2},{8,0},{30,22},{28,20},{26,18},{24,16},{46,38}... | collective-permute-start | bytes 3244040 | tf_op jit(solution)/shard_map/ppermute | solution.py:41
  112.5 28.1 %collective-permute-start.3 = (f32[2,32,4224]{2,1,0:T(8,128)}, f32[2,32,4224]{2,1,0:T(8,128)}, u32[]{:S(2)}, u32[]{:S(2)}) collective-permute-start(f32[2,32,4224]{2,1,0:T(8,128)} %get-tuple-element.32), channel_id=1, source_target_pairs={{1,5},{3,7},{5,9},{7,11},{9,13},{11,15},{17,21},{19,23},{21,25},{2... | collective-permute-start | bytes 3244040 | tf_op jit(solution)/shard_map/ppermute | solution.py:41
  131.7 7.8 %copy-start.31 = (f32[2,32]{1,0:T(2,128)S(1)}, f32[2,32]{1,0:T(2,128)}, u32[]{:S(2)}) copy-start(f32[2,32]{1,0:T(2,128)} %param.19) | copy-start | bytes 772
  139.5 7.0 %copy-start.22 = (f32[2,256,32]{1,2,0:T(8,128)S(1)}, f32[2,256,32]{1,2,0:T(8,128)}, u32[]{:S(2)}) copy-start(f32[2,256,32]{1,2,0:T(8,128)} %copy-done.21) | copy-start | bytes 196612
  139.5 7.0 %copy-start.25 = (f32[2,32,256]{2,1,0:T(8,128)S(1)}, f32[2,32,256]{2,1,0:T(8,128)}, u32[]{:S(2)}) copy-start(f32[2,32,256]{2,1,0:T(8,128)} %get-tuple-element.26) | copy-start | bytes 196612
  139.5 7.0 %copy-start.4 = (bf16[2,256,2048]{1,2,0:T(8,128)(2,1)S(1)}, bf16[2,256,2048]{1,2,0:T(8,128)(2,1)}, u32[]{:S(2)}) copy-start(bf16[2,256,2048]{1,2,0:T(8,128)(2,1)} %copy-done.3) | copy-start | bytes 6291460
  142.4 15.0 %collective-permute-start.4 = (f32[2,32,4224]{2,1,0:T(8,128)S(1)}, f32[2,32,4224]{2,1,0:T(8,128)S(1)}, u32[]{:S(2)}, u32[]{:S(2)}) collective-permute-start(f32[2,32,4224]{2,1,0:T(8,128)S(1)} %select_add_fusion.2), channel_id=1, source_target_pairs={{1,9},{3,11},{5,13},{7,15},{17,25},{19,27},{21,29},{23,31},{33,41}... | collective-permute-start | bytes 3244040 | tf_op jit(solution)/shard_map/ppermute | solution.py:41
  146.6 5.7 %copy-start.12 = (f32[2,32,4224]{2,1,0:T(8,128)S(1)}, f32[2,32,4224]{2,1,0:T(8,128)}, u32[]{:S(2)}) copy-start(f32[2,32,4224]{2,1,0:T(8,128)} %get-tuple-element.31) | copy-start | bytes 3244036
  152.3 42.8 %collective-permute-start.11 = (f32[2,32,4224]{2,1,0:T(8,128)S(1)}, f32[2,32,4224]{2,1,0:T(8,128)S(1)}, u32[]{:S(2)}, u32[]{:S(2)}) collective-permute-start(f32[2,32,4224]{2,1,0:T(8,128)S(1)} %copy-done.12), channel_id=1, source_target_pairs={{14,15},{12,13},{10,11},{8,9},{6,7},{4,5},{2,3},{0,1},{30,31},{28,... | collective-permute-start | bytes 3244040 | tf_op jit(solution)/shard_map/ppermute | solution.py:41
  154.4 34.0 %copy-start.7 = (bf16[2,256,2048]{1,2,0:T(8,128)(2,1)S(1)}, bf16[2,256,2048]{1,2,0:T(8,128)(2,1)}, u32[]{:S(2)}) copy-start(bf16[2,256,2048]{1,2,0:T(8,128)(2,1)} %copy-done.6) | copy-start | bytes 6291460
  154.4 34.0 %copy-start.20 = (f32[2,256,32]{1,2,0:T(8,128)S(1)}, f32[2,256,32]{1,2,0:T(8,128)}, u32[]{:S(2)}) copy-start(f32[2,256,32]{1,2,0:T(8,128)} %get-tuple-element.6) | copy-start | bytes 196612
  159.0 36.1 %collective-permute-start.5 = (f32[2,32,4224]{2,1,0:T(8,128)S(1)}, f32[2,32,4224]{2,1,0:T(8,128)S(1)}, u32[]{:S(2)}, u32[]{:S(2)}) collective-permute-start(f32[2,32,4224]{2,1,0:T(8,128)S(1)} %add_select_fusion.2), channel_id=1, source_target_pairs={{1,0},{3,2},{5,4},{7,6},{9,8},{11,10},{13,12},{15,14},{17,16},{19,... | collective-permute-start | bytes 3244040 | tf_op jit(solution)/shard_map/ppermute | solution.py:41
  188.4 6.6 %copy-start.11 = (f32[2,32,4224]{2,1,0:T(8,128)S(1)}, f32[2,32,4224]{2,1,0:T(8,128)}, u32[]{:S(2)}) copy-start(f32[2,32,4224]{2,1,0:T(8,128)} %copy-done.10) | copy-start | bytes 3244036
  188.4 6.7 %slice-start = ((pred[4224]{0:T(1024)(128)(4,1)}), pred[4096]{0:T(1024)(128)(4,1)S(1)}, s32[]{:S(2)}) async-start(pred[4224]{0:T(1024)(128)(4,1)} %copy-done.19), calls=%async_computation | async-start | bytes 8192 | tf_op jit(solution)/shard_map/slice | solution.py:56
  200.8 5.8 %copy-start.27 = (f32[2,256,32]{1,2,0:T(8,128)S(1)}, f32[2,256,32]{1,2,0:T(8,128)}, u32[]{:S(2)}) copy-start(f32[2,256,32]{1,2,0:T(8,128)} %get-tuple-element.21) | copy-start | bytes 196612
  203.0 3.5 %copy-start.5 = (bf16[2,256,2048]{1,2,0:T(8,128)(2,1)S(1)}, bf16[2,256,2048]{1,2,0:T(8,128)(2,1)}, u32[]{:S(2)}) copy-start(bf16[2,256,2048]{1,2,0:T(8,128)(2,1)} %copy-done.3) | copy-start | bytes 6291460
  203.0 3.6 %copy-start.8 = (bf16[2,256,2048]{1,2,0:T(8,128)(2,1)S(1)}, bf16[2,256,2048]{1,2,0:T(8,128)(2,1)}, u32[]{:S(2)}) copy-start(bf16[2,256,2048]{1,2,0:T(8,128)(2,1)} %copy-done.6) | copy-start | bytes 6291460
  203.0 3.6 %copy-start.14 = (f32[2,32,64,64]{3,2,1,0:T(8,128)S(1)}, f32[2,32,64,64]{3,2,1,0:T(8,128)}, u32[]{:S(2)}) copy-start(f32[2,32,64,64]{3,2,1,0:T(8,128)} %reshape.199) | copy-start | bytes 3145732
  203.0 3.6 %copy-start.26 = (f32[2,256,32]{1,2,0:T(8,128)S(1)}, f32[2,256,32]{1,2,0:T(8,128)}, u32[]{:S(2)}) copy-start(f32[2,256,32]{1,2,0:T(8,128)} %get-tuple-element.23) | copy-start | bytes 196612
  224.3 7.9 %copy-start.16 = (bf16[256,1024]{1,0:T(8,128)(2,1)S(1)}, bf16[256,1024]{1,0:T(8,128)(2,1)}, u32[]{:S(2)}) copy-start(bf16[256,1024]{1,0:T(8,128)(2,1)} %copy-done.15) | copy-start | bytes 1572868
  224.3 7.9 %copy-start.18 = (bf16[256,1024]{1,0:T(8,128)(2,1)S(1)}, bf16[256,1024]{1,0:T(8,128)(2,1)}, u32[]{:S(2)}) copy-start(bf16[256,1024]{1,0:T(8,128)(2,1)} %copy-done.17) | copy-start | bytes 1572868
  224.3 7.9 %copy-start.33 = (f32[2048]{0:T(1024)S(1)}, f32[2048]{0:T(1024)}, u32[]{:S(2)}) copy-start(f32[2048]{0:T(1024)} %param.20) | copy-start | bytes 24580
  239.7 2.2 copy-start.1

commit v3 on v2

--- a/solution.py
+++ b/solution.py
@@ -38,7 +38,9 @@
         return position if sense == 1 else size - 1 - position
 
     def send(value, moves):
-        return lax.ppermute(value, "ctx", [(place(a), place(b)) for a, b in moves])
+        pairs = [(place(a), place(b)) for a, b in moves]
+        moved = lax.ppermute(value.astype(jnp.bfloat16), "ctx", pairs)
+        return moved.astype(jnp.float32)
 
     tops = range(0, size, group)
     first = send(element, [(t + k, t + k + 1) for t in tops for k in (0, 2)])

time: 243 us -> 200 us (0.82)
  starting transfers between devices: 57.3 us -> 34.4 us
  waiting for transfers between devices: 16 us -> 5.79 us
  other arithmetic: 46.7 us -> 41.1 us
  local copies, waits for them, and re-layouts: 74.3 us -> 70.8 us
    ppermute x10, starting transfers between devices: 49.1 us -> 26.3 us  [send(): moved = lax.ppermute(value.astype(jnp.bfloat16), 'ctx', pairs)]
    convert_element_type x0 -> x14, other arithmetic: none -> 10.9 us  [the longest x8 8.4 us: send(): moved = lax.ppermute(value.astype(jnp.bfloat16), 'ctx', pairs)]
    ppermute x10, waiting for transfers between devices: 15.9 us -> 5.78 us  [send(): moved = lax.ppermute(value.astype(jnp.bfloat16), 'ctx', pairs)]
    select_n x3 -> x0, other arithmetic: 7.67 us -> none  [the longest x2 5.8 us: exclusive_chain(): handed = jnp.where(slot == 1, entering, combine(entering, other))]
    add x3 -> x0, other arithmetic: 6.2 us -> none  [combine(): later[..., width:width + 1] * earlier + jnp.where(lanes < width, later, 0.0)]
    slice x10, local copies, waits for them, and re-layouts: 6.33 us -> 1.74 us  [combine(): later[..., width:width + 1] * earlier + jnp.where(lanes < width, later, 0.0)]
    dot_general x1, matrix products: 6.82 us -> 4.34 us  [body(): jnp.dot(rows, w_gate, preferred_element_type=jnp.float32)]
    unnamed x75 -> x93, local copies, waits for them, and re-layouts: 6.66 us -> 7.57 us
  transfers between devices with their start and end apart: 12 -> 12, of which waited for: 3 -> 2; matrix products, arithmetic and copies ran while one was open for 30% -> 34% of each run, Pallas kernels for 0% -> 0%
where the time goes in v3:
time: 200 us; the launch traced here: 197 us
  local copies, waits for them, and re-layouts  70.8 us (35%)
  matrix products  44.6 us (22%)
  other arithmetic  41.1 us (21%)
  starting transfers between devices  34.4 us (17%)
  waiting for transfers between devices  5.79 us (3%)
    ppermute x10, starting transfers between devices, send(): moved = lax.ppermute(value.astype(jnp.bfloat16), 'ctx', pairs)  26.3 us
    convert_element_type x1, other arithmetic, group_terms(): conv = jax.nn.silu(total).astype(jnp.bfloat16)  19.3 us
    add x2, local copies, waits for them, and re-layouts, body(): combined = finish(*rising[:3], rising_in) + finish(*falling[:3], falling_in)  17.1 us
    convert_element_type x2, local copies, waits for them, and re-layouts, body(): gate.reshape(2, length, gate.shape[1]).astype(jnp.float32)  15.7 us
    dot_general x2, matrix products, finish(): jnp.einsum('rtn,rhpn->rthp', reads.astype(jnp.float32), entering, precisi...  12.1 us
    dot_general x2, matrix products, group_terms(): jnp.einsum('rhts,rshp->rthp', mixing, scaled, preferred_element_type=jnp....  11.4 us
    convert_element_type x8, other arithmetic, send(): moved = lax.ppermute(value.astype(jnp.bfloat16), 'ctx', pairs)  8.4 us
    ppermute x2, starting transfers between devices, shifted(): return lax.ppermute(value, 'ctx', pairs)  8.13 us
  transfers between devices with their start and end apart: 12, of which 2 were waited for; matrix products, arithmetic and copies ran while one was open for 34% of the time, Pallas kernels for 0%

profile of v3, /device:TPU:1, one launch (start us, length us, event | category | flops | bytes accessed | tf_op | source)
XLA Modules:
  0.0 197.5 jit_solution(9939358060454545818)
XLA Ops:
  0.0 3.4 %fusion.73 = (bf16[256,1,1024]{2,1,0:T(2,128)(2,1)S(1)}, bf16[256,1,1024]{2,1,0:T(2,128)(2,1)S(1)}) fusion(bf16[256,2,1024]{2,1,0:T(2,128)(2,1)} %param.11), kind=kLoop, calls=%fused_computation.161 | loop fusion | bytes 2097152 | tf_op jit(solution)/shard_map/slice | solution.py:125
  3.9 3.4 %convolution_convert_fusion = bf16[512,2176]{1,0:T(8,128)(2,1)S(1)} fusion(bf16[1024,2176]{1,0:T(8,128)(2,1)S(1)} %copy-done.40, bf16[256,1024]{1,0:T(8,128)(2,1)S(1)} %get-tuple-element.50, bf16[256,1024]{1,0:T(8,128)(2,1)S(1)} %get-tuple-element.51), kind=kOutput, calls=%fused_computation.22 | convolution fusion | flops 2284912640 | bytes 7733248 | tf_op jit(solution)/shard_map/dot_general | solution.py:127
  7.3 1.4 copy-done.15
  8.7 3.3 %collective-permute-start.6 = (bf16[2,3,2176]{2,0,1:T(2,128)(2,1)S(1)}, bf16[2,3,2176]{2,0,1:T(2,128)(2,1)S(1)}, u32[]{:S(2)}, u32[]{:S(2)}) collective-permute-start(bf16[2,3,2176]{2,0,1:T(2,128)(2,1)S(1)} %copy.145), channel_id=1, source_target_pairs={{1,0},{2,1},{3,2},{4,3},{5,4},{6,5},{7,6},{8,7},{9,8},{10,9},{11,1... | collective-permute-start | bytes 78344 | tf_op jit(solution)/shard_map/ppermute | solution.py:20
  12.1 4.8 %collective-permute-start = (bf16[2,3,2176]{2,0,1:T(2,128)(2,1)S(1)}, bf16[2,3,2176]{2,0,1:T(2,128)(2,1)S(1)}, u32[]{:S(2)}, u32[]{:S(2)}) collective-permute-start(bf16[2,3,2176]{2,0,1:T(2,128)(2,1)S(1)} %copy.144), channel_id=1, source_target_pairs={{0,1},{1,2},{2,3},{3,4},{4,5},{5,6},{6,7},{7,8},{8,9},{9,10},{10,1... | collective-permute-start | bytes 78344 | tf_op jit(solution)/shard_map/ppermute | solution.py:20
  19.0 5.0 %reduce-window.16 = f32[2,32,2,128]{3,1,2,0:T(8,128)S(1)} reduce-window(f32[2,32,2,128]{3,1,2,0:T(8,128)S(1)} %bitcast.132, f32[]{:T(128)} %constant.50.clone.1), window={size=1x1x1x128 pad=0_0x0_0x0_0x0_127}, to_apply=%region_2.3 | reduce-window | flops 2080768 | bytes 131076 | tf_op jit(solution)/shard_map/reduce-window.2
  24.9 1.2 reduce-window.14
  29.7 4.1 %copy.109 = bf16[2,256,2176]{1,2,0:T(8,128)(2,1)} copy(bf16[2,256,2176]{2,1,0:T(8,128)(2,1)} %bitcast.131) | data formatting | bytes 4456448 | tf_op jit(solution)/shard_map/reshape | solution.py:128
  33.8 5.3 %rev.13 = f32[2,2176]{1,0:T(2,128)} reverse(f32[2,2176]{1,0:T(2,128)S(1)} %copy-done.28), dimensions={0} | reverse | bytes 34816 | tf_op jit(solution)/shard_map/rev | solution.py:149
  39.8 1.5 copy.108
  41.3 19.3 %multiply_convert_fusion.4 = (bf16[2,256,2176]{1,2,0:T(8,128)(2,1)S(1)}, bf16[2,256,2176]{1,2,0:T(8,128)(2,1)S(1)}) fusion(bf16[2,256,2176]{1,2,0:T(8,128)(2,1)} %copy.109, bf16[2,3,2176]{1,2,0:T(8,128)(2,1)S(1)} %copy.116, f32[2,2176]{1,0:T(2,128)} %get-tuple-element.58, f32[2,2176]{1,0:T(2,128)} %get-tuple-element.59, f32[2,2176]{1,0:T(2,128)} %get-tuple-element.60, ...), kind=kLoop, calls=%fused_computation.25 | loop fusion | flops 56819712 | bytes 6910976 | tf_op jit(solution)/shard_map/convert_element_type | solution.py:71
  60.7 1.2 copy-done.3
  62.6 2.0 %fusion.28 = f32[2,32,64,64]{3,2,1,0:T(8,128)} fusion(bf16[2,256,32,64]{1,3,2,0:T(8,128)(2,1)S(1)} %bitcast.124, f32[2,256,32]{1,2,0:T(8,128)S(1)} %get-tuple-element.36, bf16[2,256,2176]{1,2,0:T(8,128)(2,1)S(1)} %get-tuple-element.21), kind=kOutput, calls=%fused_computation.54 | convolution fusion | flops 137363456 | bytes 3276800 | tf_op jit(solution)/shard_map/rshp,rsn->rhpn/dot_general | solution.py:97
  64.6 2.1 %reshape.198 = f32[2,32,4096]{2,1,0:T(8,128)S(1)} reshape(f32[2,32,64,64]{3,2,1,0:T(8,128)} %fusion.28) | data formatting | bytes 2097152 | tf_op jit(solution)/shard_map/reshape | solution.py:103
  66.8 1.1 fusion.44
  67.9 2.1 %collective-permute-start.7 = (bf16[2,32,4224]{2,1,0:T(8,128)(2,1)}, bf16[2,32,4224]{2,1,0:T(8,128)(2,1)}, u32[]{:S(2)}, u32[]{:S(2)}) collective-permute-start(bf16[2,32,4224]{2,1,0:T(8,128)(2,1)} %fusion.44), channel_id=1, source_target_pairs={{15,14},{13,12},{11,10},{9,8},{7,6},{5,4},{3,2},{1,0},{31,30},{29,... | collective-permute-start | bytes 1622024 | tf_op jit(solution)/shard_map/ppermute | solution.py:42
  70.9 1.4 copy-done.7
  72.2 2.0 %fusion.31 = f32[2,32,64,64]{3,2,1,0:T(8,128)} fusion(bf16[2,256,32,64]{1,3,2,0:T(8,128)(2,1)S(1)} %bitcast.127, f32[2,256,32]{1,2,0:T(8,128)S(1)} %get-tuple-element.34, bf16[2,256,2176]{1,2,0:T(8,128)(2,1)S(1)} %get-tuple-element.22), kind=kOutput, calls=%fused_computation.55 | convolution fusion | flops 137363456 | bytes 3276800 | tf_op jit(solution)/shard_map/rshp,rsn->rhpn/dot_general | solution.py:97
  74.3 2.1 %reshape.194 = f32[2,32,4096]{2,1,0:T(8,128)S(1)} reshape(f32[2,32,64,64]{3,2,1,0:T(8,128)} %fusion.31) | data formatting | bytes 2097152 | tf_op jit(solution)/shard_map/reshape | solution.py:103
  76.4 1.6 fusion.68
  78.9 1.5 collective-permute-start.1
  82.8 1.6 fusion.71
  84.5 1.6 collective-permute-start.10
  86.1 5.3 %collective-permute-start.2 = (bf16[2,32,4224]{2,1,0:T(8,128)(2,1)}, bf16[2,32,4224]{2,1,0:T(8,128)(2,1)}, u32[]{:S(2)}, u32[]{:S(2)}) collective-permute-start(bf16[2,32,4224]{2,1,0:T(8,128)(2,1)} %get-tuple-element.15), channel_id=1, source_target_pairs={{1,3},{3,1},{5,7},{7,5},{9,11},{11,9},{13,15},{15,13},{17,19},{19,... | collective-permute-start | bytes 1622024 | tf_op jit(solution)/shard_map/ppermute | solution.py:42
  91.4 4.3 %fusion.23 = f32[512,2048]{1,0:T(8,128)} fusion(bf16[1024,2048]{1,0:T(8,128)(2,1)S(1)} %copy-done.41, bf16[256,1024]{1,0:T(8,128)(2,1)S(1)} %copy-done.20, bf16[256,1024]{1,0:T(8,128)(2,1)S(1)} %copy-done.23), kind=kOutput, calls=%fused_computation.47 | convolution fusion | flops 2151677952 | bytes 9437184 | tf_op jit(solution)/shard_map/dot_general | solution.py:126
  95.8 7.9 %reshape.209 = f32[2,256,32,64]{3,2,1,0:T(8,128)} reshape(f32[512,2048]{1,0:T(8,128)} %fusion.23) | data formatting | bytes 8388608 | tf_op jit(solution)/shard_map/convert_element_type | solution.py:156
  103.7 7.9 %copy.124 = f32[2,256,32,64]{1,3,2,0:T(8,128)} copy(f32[2,256,32,64]{3,2,1,0:T(8,128)} %reshape.209) | data formatting | bytes 8388608 | tf_op jit(solution)/shard_map/convert_element_type | solution.py:156
  112.7 1.1 convert_element_type.181
  113.9 2.0 %fusion.66 = (bf16[2,32,4224]{2,1,0:T(8,128)(2,1)S(1)}, f32[2,32,4224]{2,1,0:T(8,128)S(1)}, bf16[2,32,4224]{2,1,0:T(8,128)(2,1)S(1)}, f32[2,32,4224]{2,1,0:T(8,128)S(1)}) fusion(bf16[2,32,4224]{2,1,0:T(8,128)(2,1)S(1)} %copy-done.13, f32[2,32]{1,0:T(2,128)S(1)} %slice_reduce_fusion.5, bf16[2,32,4224]{2,1,0:T(8,128)(2,1)S(1)} %copy-done.11, ...), kind=kLoop, calls=%fused_computation.154 | loop fusion | flops 5406720 | bytes 6493314 | tf_op jit(solution)/shard_map/convert_element_type | solution.py:42
  116.0 3.7 %collective-permute-start.3 = (bf16[2,32,4224]{2,1,0:T(8,128)(2,1)S(1)}, bf16[2,32,4224]{2,1,0:T(8,128)(2,1)S(1)}, u32[]{:S(2)}, u32[]{:S(2)}) collective-permute-start(bf16[2,32,4224]{2,1,0:T(8,128)(2,1)S(1)} %get-tuple-element.43), channel_id=1, source_target_pairs={{1,5},{3,7},{5,9},{7,11},{9,13},{11,15},{17,21},{19,23},{21,25},{2... | collective-permute-start | bytes 1622024 | tf_op jit(solution)/shard_map/ppermute | solution.py:42
  119.7 1.1 fusion.52
  121.0 4.9 %collective-permute-done.3 = bf16[2,32,4224]{2,1,0:T(8,128)(2,1)S(1)} collective-permute-done((bf16[2,32,4224]{2,1,0:T(8,128)(2,1)S(1)}, bf16[2,32,4224]{2,1,0:T(8,128)(2,1)S(1)}, u32[]{:S(2)}, u32[]{:S(2)}) %collective-permute-start.3) | collective-permute-done | bytes 540704 | tf_op jit(solution)/shard_map/ppermute | solution.py:42
  126.1 5.8 %collective-permute-start.4 = (bf16[2,32,4224]{2,1,0:T(8,128)(2,1)S(1)}, bf16[2,32,4224]{2,1,0:T(8,128)(2,1)S(1)}, u32[]{:S(2)}, u32[]{:S(2)}) collective-permute-start(bf16[2,32,4224]{2,1,0:T(8,128)(2,1)S(1)} %add_convert_fusion.2), channel_id=1, source_target_pairs={{1,9},{3,11},{5,13},{7,15},{17,25},{19,27},{21,29},{23,31},{33,41}... | collective-permute-start | bytes 1622024 | tf_op jit(solution)/shard_map/ppermute | solution.py:42
  132.0 5.7 %fusion.1 = f32[2,32,64,256]{3,2,1,0:T(8,128)} fusion(f32[2,32,256]{2,1,0:T(8,128)S(1)} %copy-done.31, f32[2,256,256]{2,1,0:T(8,128)S(1)} %fusion.52, pred[256,256]{1,0:T(8,128)(4,1)S(1)} %iota_compare_fusion, bf16[2,256,32,64]{1,3,2,0:T(8,128)(2,1)S(1)} %bitcast.125, f32[2,256,32]{1,2,0:T(8,128)S(1)} %copy-done.27), kind=kOutput, calls=%fused_computation.3 | convolution fusion | flops 556793856 | bytes 7012352 | tf_op jit(solution)/shard_map/rhts,rshp->rthp/dot_general | solution.py:93
  138.0 1.4 collective-permute-start.11
  139.6 1.5 fusion.69
  141.1 3.5 %collective-permute-start.5 = (bf16[2,32,4224]{2,1,0:T(8,128)(2,1)S(1)}, bf16[2,32,4224]{2,1,0:T(8,128)(2,1)S(1)}, u32[]{:S(2)}, u32[]{:S(2)}) collective-permute-start(bf16[2,32,4224]{2,1,0:T(8,128)(2,1)S(1)} %get-tuple-element.11), channel_id=1, source_target_pairs={{1,0},{3,2},{5,4},{7,6},{9,8},{11,10},{13,12},{15,14},{17,16},{19,... | collective-permute-start | bytes 1622024 | tf_op jit(solution)/shard_map/ppermute | solution.py:42
  144.6 5.8 %fusion = f32[2,32,64,256]{3,2,1,0:T(8,128)} fusion(f32[2,32,256]{2,1,0:T(8,128)S(1)} %copy-done.30, f32[2,256,256]{2,1,0:T(8,128)S(1)} %fusion.57, pred[256,256]{1,0:T(8,128)(4,1)S(1)} %iota_compare_fusion.1, bf16[2,256,32,64]{1,3,2,0:T(8,128)(2,1)S(1)} %bitcast.128, f32[2,256,32]{1,2,0:T(8,128)S(1)} %get-tuple-element.18), kind=kOutput, calls=%fused_computation.2 | convolution fusion | flops 556793856 | bytes 7012352 | tf_op jit(solution)/shard_map/rhts,rshp->rthp/dot_general | solution.py:93
  150.3 1.1 convert_element_type.198
  151.8 1.4 fusion.41
  153.2 3.2 %reshape.199 = f32[2,32,64,64]{3,2,1,0:T(8,128)} reshape(f32[2,32,4096]{2,1,0:T(8,128)} %get-tuple-element.46) | data formatting | bytes 2097152 | tf_op jit(solution)/shard_map/reshape | solution.py:113
  156.3 2.2 %reshape.195 = f32[2,32,64,64]{3,2,1,0:T(8,128)} reshape(f32[2,32,4096]{2,1,0:T(8,128)S(1)} %get-tuple-element.47) | data formatting | bytes 2097152 | tf_op jit(solution)/shard_map/reshape | solution.py:113
  158.5 3.5 %fusion.49 = f32[2,256,32,64]{1,3,2,0:T(8,128)S(1)} fusion(f32[2,32,64,64]{3,2,1,0:T(8,128)} %reshape.195, bf16[2,256,2176]{1,2,0:T(8,128)(2,1)S(1)} %get-tuple-element.22), kind=kOutput, calls=%fused_computation.105 | convolution fusion | flops 805306368 | bytes 5308416 | tf_op jit(solution)/shard_map/rtn,rhpn->rthp/dot_general | solution.py:114
  162.1 8.5 %multiply_reduce_fusion = (f32[2,256]{1,0:T(2,128)S(1)}, f32[2,256,32,64]{1,3,2,0:T(8,128)}) fusion(f32[2,256,32,64]{1,3,2,0:T(8,128)} %copy.124, f32[2,256,32]{1,2,0:T(8,128)S(1)} %copy-done.32, f32[2,32,64,64]{3,2,1,0:T(8,128)S(1)} %copy-done.18, bf16[2,256,2176]{1,2,0:T(8,128)(2,1)} %copy-done.3, bf16[2,256,32,64]{1,3,2,0:T(8,128)(2,1)S(1)} %bitcast.126, ...), kind=kOutput, calls=%fused_computation.37 | convolution fusion | flops 824180224 | bytes 26413568 | tf_op jit(solution)/shard_map/rtn,rhpn->rthp/dot_general | solution.py:114
  170.7 9.2 %copy.130 = f32[2,256,32,64]{3,2,1,0:T(8,128)} copy(f32[2,256,32,64]{1,3,2,0:T(8,128)} %get-tuple-element.49) | data formatting | bytes 8388608 | tf_op jit(solution)/shard_map/add | solution.py:155
  179.8 7.9 %reshape.208 = f32[512,2048]{1,0:T(8,128)} reshape(f32[2,256,32,64]{3,2,1,0:T(8,128)} %copy.130) | data formatting | bytes 8388608 | tf_op jit(solution)/shard_map/add | solution.py:155
  187.8 7.4 %add_convert_fusion = bf16[512,1024]{1,0:T(8,128)(2,1)S(1)} fusion(bf16[2048,1024]{1,0:T(8,128)(2,1)} %param.21, f32[512,2048]{1,0:T(8,128)} %reshape.208, f32[512,2048]{1,0:T(8,128)} %fusion.23, f32[2048]{0:T(1024)S(1)} %copy-done.42, f32[512]{0:T(512)S(1)} %bitcast.135, bf16[256,1024]{1,0:T(8,128)(2,1)S(1)} %copy-done.21, bf16[256,1024]{1,0:T(8,128)(2,1)S(1)} %copy-done.24), kind=kOutput, calls=%fused_computation.56 | convolution fusion | flops 2159017984 | bytes 14690304 | tf_op jit(solution)/shard_map/dot_general | solution.py:160
  195.4 2.0 %copy.125 = bf16[256,2,1024]{2,1,0:T(2,128)(2,1)} copy(bf16[256,2,1024]{2,0,1:T(8,128)(2,1)S(1)} %pad_maximum_fusion.5) | data formatting | bytes 2097152 | tf_op jit(solution)/shard_map/stack | solution.py:164
  (163 shorter events, 15.3 us)
Async XLA Ops:
  0.0 18.3 %copy-start = (bf16[1024,32]{0,1:T(8,128)(2,1)S(1)}, bf16[1024,32]{0,1:T(8,128)(2,1)}, u32[]{:S(2)}) copy-start(bf16[1024,32]{0,1:T(8,128)(2,1)} %param.14) | copy-start | bytes 196612
  0.0 3.8 %copy-start.40 = (bf16[1024,2176]{1,0:T(8,128)(2,1)S(1)}, bf16[1024,2176]{1,0:T(8,128)(2,1)}, u32[]{:S(2)}) copy-start(bf16[1024,2176]{1,0:T(8,128)(2,1)} %param.13) | copy-start | bytes 13369348
  3.8 14.5 %copy-start.19 = (bf16[256,1024]{1,0:T(8,128)(2,1)}, bf16[256,1024]{1,0:T(8,128)(2,1)S(1)}, u32[]{:S(2)}) copy-start(bf16[256,1024]{1,0:T(8,128)(2,1)S(1)} %get-tuple-element.50) | copy-start | bytes 1572868
  3.8 14.5 %copy-start.22 = (bf16[256,1024]{1,0:T(8,128)(2,1)}, bf16[256,1024]{1,0:T(8,128)(2,1)S(1)}, u32[]{:S(2)}) copy-start(bf16[256,1024]{1,0:T(8,128)(2,1)S(1)} %get-tuple-element.51) | copy-start | bytes 1572868
  3.8 13.1 %copy-start.29 = (f32[2,4,2176]{2,1,0:T(4,128)S(1)}, f32[2,4,2176]{2,1,0:T(4,128)}, u32[]{:S(2)}) copy-start(f32[2,4,2176]{2,1,0:T(4,128)} %param.17) | copy-start | bytes 208900
  3.8 14.4 %copy-start.37 = (f32[2,32]{1,0:T(2,128)S(1)}, f32[2,32]{1,0:T(2,128)}, u32[]{:S(2)}) copy-start(f32[2,32]{1,0:T(2,128)} %param.16) | copy-start | bytes 772
  7.3 11.5 %copy-start.38 = (f32[2,32]{1,0:T(2,128)S(1)}, f32[2,32]{1,0:T(2,128)}, u32[]{:S(2)}) copy-start(f32[2,32]{1,0:T(2,128)} %param.15) | copy-start | bytes 772
  8.7 30.4 %collective-permute-start.6 = (bf16[2,3,2176]{2,0,1:T(2,128)(2,1)S(1)}, bf16[2,3,2176]{2,0,1:T(2,128)(2,1)S(1)}, u32[]{:S(2)}, u32[]{:S(2)}) collective-permute-start(bf16[2,3,2176]{2,0,1:T(2,128)(2,1)S(1)} %copy.145), channel_id=1, source_target_pairs={{1,0},{2,1},{3,2},{4,3},{5,4},{6,5},{7,6},{8,7},{9,8},{10,9},{11,1... | collective-permute-start | bytes 78344 | tf_op jit(solution)/shard_map/ppermute | solution.py:20
  12.1 27.7 %collective-permute-start = (bf16[2,3,2176]{2,0,1:T(2,128)(2,1)S(1)}, bf16[2,3,2176]{2,0,1:T(2,128)(2,1)S(1)}, u32[]{:S(2)}, u32[]{:S(2)}) collective-permute-start(bf16[2,3,2176]{2,0,1:T(2,128)(2,1)S(1)} %copy.144), channel_id=1, source_target_pairs={{0,1},{1,2},{2,3},{3,4},{4,5},{5,6},{6,7},{7,8},{8,9},{9,10},{10,1... | collective-permute-start | bytes 78344 | tf_op jit(solution)/shard_map/ppermute | solution.py:20
  18.9 14.9 %copy-start.26 = (f32[2,256,32]{1,2,0:T(8,128)}, f32[2,256,32]{1,2,0:T(8,128)S(1)}, u32[]{:S(2)}) copy-start(f32[2,256,32]{1,2,0:T(8,128)S(1)} %get-tuple-element.42) | copy-start | bytes 196612
  27.2 11.9 %copy-start.34 = (f32[2,32]{1,0:T(2,128)}, f32[2,32]{1,0:T(2,128)S(1)}, u32[]{:S(2)}) copy-start(f32[2,32]{1,0:T(2,128)S(1)} %slice_reduce_fusion.13) | copy-start | bytes 772
  29.1 110.4 %copy-start.25 = (pred[4224]{0:T(1024)(128)(4,1)}, pred[4224]{0:T(1024)(128)(4,1)S(1)}, u32[]{:S(2)}) copy-start(pred[4224]{0:T(1024)(128)(4,1)S(1)} %iota_compare_fusion.2) | copy-start | bytes 12676
  29.7 4.1 %copy-start.28 = (f32[2,2176]{1,0:T(2,128)S(1)}, f32[2,2176]{1,0:T(2,128)}, u32[]{:S(2)}) copy-start(f32[2,2176]{1,0:T(2,128)} %param.18) | copy-start | bytes 52228
  64.6 2.1 %copy-start.36 = (f32[2,32]{1,0:T(2,128)S(1)}, f32[2,32]{1,0:T(2,128)}, u32[]{:S(2)}) copy-start(f32[2,32]{1,0:T(2,128)} %exp.80) | copy-start | bytes 772
  64.6 5.4 %copy-start.35 = (f32[2,32]{1,0:T(2,128)S(1)}, f32[2,32]{1,0:T(2,128)}, u32[]{:S(2)}) copy-start(f32[2,32]{1,0:T(2,128)} %copy-done.34) | copy-start | bytes 772
  66.7 4.1 %copy-start.2 = (f32[2,32,4096]{2,1,0:T(8,128)}, f32[2,32,4096]{2,1,0:T(8,128)S(1)}, u32[]{:S(2)}) copy-start(f32[2,32,4096]{2,1,0:T(8,128)S(1)} %reshape.198) | copy-start | bytes 3145732
  67.9 8.5 %collective-permute-start.7 = (bf16[2,32,4224]{2,1,0:T(8,128)(2,1)}, bf16[2,32,4224]{2,1,0:T(8,128)(2,1)}, u32[]{:S(2)}, u32[]{:S(2)}) collective-permute-start(bf16[2,32,4224]{2,1,0:T(8,128)(2,1)} %fusion.44), channel_id=1, source_target_pairs={{15,14},{13,12},{11,10},{9,8},{7,6},{5,4},{3,2},{1,0},{31,30},{29,... | collective-permute-start | bytes 1622024 | tf_op jit(solution)/shard_map/ppermute | solution.py:42
  78.0 2.4 %collective-permute-start.8 = (bf16[2,32,4224]{2,1,0:T(8,128)(2,1)S(1)}, bf16[2,32,4224]{2,1,0:T(8,128)(2,1)S(1)}, u32[]{:S(2)}, u32[]{:S(2)}) collective-permute-start(bf16[2,32,4224]{2,1,0:T(8,128)(2,1)S(1)} %get-tuple-element.9), channel_id=1, source_target_pairs={{14,12},{12,14},{10,8},{8,10},{6,4},{4,6},{2,0},{0,2},{30,28},{28,... | collective-permute-start | bytes 1622024 | tf_op jit(solution)/shard_map/ppermute | solution.py:42
  78.9 4.0 %collective-permute-start.1 = (bf16[2,32,4224]{2,1,0:T(8,128)(2,1)S(1)}, bf16[2,32,4224]{2,1,0:T(8,128)(2,1)S(1)}, u32[]{:S(2)}, u32[]{:S(2)}) collective-permute-start(bf16[2,32,4224]{2,1,0:T(8,128)(2,1)S(1)} %fusion.45), channel_id=1, source_target_pairs={{0,1},{2,3},{4,5},{6,7},{8,9},{10,11},{12,13},{14,15},{16,17},{18,... | collective-permute-start | bytes 1622024 | tf_op jit(solution)/shard_map/ppermute | solution.py:42
  81.2 1.6 collective-permute-start.9
  82.0 9.4 %copy-start.20 = (bf16[256,1024]{1,0:T(8,128)(2,1)S(1)}, bf16[256,1024]{1,0:T(8,128)(2,1)}, u32[]{:S(2)}) copy-start(bf16[256,1024]{1,0:T(8,128)(2,1)} %copy-done.19) | copy-start | bytes 1572868
  82.0 9.4 %copy-start.23 = (bf16[256,1024]{1,0:T(8,128)(2,1)S(1)}, bf16[256,1024]{1,0:T(8,128)(2,1)}, u32[]{:S(2)}) copy-start(bf16[256,1024]{1,0:T(8,128)(2,1)} %copy-done.22) | copy-start | bytes 1572868
  82.0 9.4 %copy-start.41 = (bf16[1024,2048]{1,0:T(8,128)(2,1)S(1)}, bf16[1024,2048]{1,0:T(8,128)(2,1)}, u32[]{:S(2)}) copy-start(bf16[1024,2048]{1,0:T(8,128)(2,1)} %param.12) | copy-start | bytes 12582916
  84.5 29.4 %collective-permute-start.10 = (bf16[2,32,4224]{2,1,0:T(8,128)(2,1)}, bf16[2,32,4224]{2,1,0:T(8,128)(2,1)}, u32[]{:S(2)}, u32[]{:S(2)}) collective-permute-start(bf16[2,32,4224]{2,1,0:T(8,128)(2,1)} %get-tuple-element.45), channel_id=1, source_target_pairs={{14,6},{12,4},{10,2},{8,0},{30,22},{28,20},{26,18},{24,16},{46,38}... | collective-permute-start | bytes 1622024 | tf_op jit(solution)/shard_map/ppermute | solution.py:42
  86.1 26.6 %collective-permute-start.2 = (bf16[2,32,4224]{2,1,0:T(8,128)(2,1)}, bf16[2,32,4224]{2,1,0:T(8,128)(2,1)}, u32[]{:S(2)}, u32[]{:S(2)}) collective-permute-start(bf16[2,32,4224]{2,1,0:T(8,128)(2,1)} %get-tuple-element.15), channel_id=1, source_target_pairs={{1,3},{3,1},{5,7},{7,5},{9,11},{11,9},{13,15},{15,13},{17,19},{19,... | collective-permute-start | bytes 1622024 | tf_op jit(solution)/shard_map/ppermute | solution.py:42
  103.7 7.9 %copy-start.39 = (f32[2,32]{1,0:T(2,128)S(1)}, f32[2,32]{1,0:T(2,128)}, u32[]{:S(2)}) copy-start(f32[2,32]{1,0:T(2,128)} %param.19) | copy-start | bytes 772
  103.7 7.9 %copy-start.11 = (bf16[2,32,4224]{2,1,0:T(8,128)(2,1)S(1)}, bf16[2,32,4224]{2,1,0:T(8,128)(2,1)}, u32[]{:S(2)}) copy-start(bf16[2,32,4224]{2,1,0:T(8,128)(2,1)} %copy-done.10) | copy-start | bytes 1622020
  111.5 2.4 %copy-start.13 = (bf16[2,32,4224]{2,1,0:T(8,128)(2,1)S(1)}, bf16[2,32,4224]{2,1,0:T(8,128)(2,1)}, u32[]{:S(2)}) copy-start(bf16[2,32,4224]{2,1,0:T(8,128)(2,1)} %copy-done.12) | copy-start | bytes 1622020
  111.6 2.4 %copy-start.14 = (f32[2,32,4224]{2,1,0:T(8,128)S(1)}, f32[2,32,4224]{2,1,0:T(8,128)}, u32[]{:S(2)}) copy-start(f32[2,32,4224]{2,1,0:T(8,128)} %get-tuple-element.16) | copy-start | bytes 3244036
  115.9 16.1 %copy-start.5 = (bf16[2,256,2048]{1,2,0:T(8,128)(2,1)S(1)}, bf16[2,256,2048]{1,2,0:T(8,128)(2,1)}, u32[]{:S(2)}) copy-start(bf16[2,256,2048]{1,2,0:T(8,128)(2,1)} %copy-done.4) | copy-start | bytes 6291460
  115.9 16.1 %copy-start.27 = (f32[2,256,32]{1,2,0:T(8,128)S(1)}, f32[2,256,32]{1,2,0:T(8,128)}, u32[]{:S(2)}) copy-start(f32[2,256,32]{1,2,0:T(8,128)} %copy-done.26) | copy-start | bytes 196612
  115.9 16.1 %copy-start.31 = (f32[2,32,256]{2,1,0:T(8,128)S(1)}, f32[2,32,256]{2,1,0:T(8,128)}, u32[]{:S(2)}) copy-start(f32[2,32,256]{2,1,0:T(8,128)} %get-tuple-element.38) | copy-start | bytes 196612
  116.0 10.0 %collective-permute-start.3 = (bf16[2,32,4224]{2,1,0:T(8,128)(2,1)S(1)}, bf16[2,32,4224]{2,1,0:T(8,128)(2,1)S(1)}, u32[]{:S(2)}, u32[]{:S(2)}) collective-permute-start(bf16[2,32,4224]{2,1,0:T(8,128)(2,1)S(1)} %get-tuple-element.43), channel_id=1, source_target_pairs={{1,5},{3,7},{5,9},{7,11},{9,13},{11,15},{17,21},{19,23},{21,25},{2... | collective-permute-start | bytes 1622024 | tf_op jit(solution)/shard_map/ppermute | solution.py:42
  126.1 13.4 %collective-permute-start.4 = (bf16[2,32,4224]{2,1,0:T(8,128)(2,1)S(1)}, bf16[2,32,4224]{2,1,0:T(8,128)(2,1)S(1)}, u32[]{:S(2)}, u32[]{:S(2)}) collective-permute-start(bf16[2,32,4224]{2,1,0:T(8,128)(2,1)S(1)} %add_convert_fusion.2), channel_id=1, source_target_pairs={{1,9},{3,11},{5,13},{7,15},{17,25},{19,27},{21,29},{23,31},{33,41}... | collective-permute-start | bytes 1622024 | tf_op jit(solution)/shard_map/ppermute | solution.py:42
  138.0 6.6 %copy-start.8 = (bf16[2,256,2048]{1,2,0:T(8,128)(2,1)S(1)}, bf16[2,256,2048]{1,2,0:T(8,128)(2,1)}, u32[]{:S(2)}) copy-start(bf16[2,256,2048]{1,2,0:T(8,128)(2,1)} %copy-done.7) | copy-start | bytes 6291460
  138.0 6.6 %copy-start.30 = (f32[2,32,256]{2,1,0:T(8,128)S(1)}, f32[2,32,256]{2,1,0:T(8,128)}, u32[]{:S(2)}) copy-start(f32[2,32,256]{2,1,0:T(8,128)} %get-tuple-element.40) | copy-start | bytes 196612
  138.0 13.8 %collective-permute-start.11 = (bf16[2,32,4224]{2,1,0:T(8,128)(2,1)S(1)}, bf16[2,32,4224]{2,1,0:T(8,128)(2,1)S(1)}, u32[]{:S(2)}, u32[]{:S(2)}) collective-permute-start(bf16[2,32,4224]{2,1,0:T(8,128)(2,1)S(1)} %get-tuple-element.5), channel_id=1, source_target_pairs={{14,15},{12,13},{10,11},{8,9},{6,7},{4,5},{2,3},{0,1},{30,31},{28,... | collective-permute-start | bytes 1622024 | tf_op jit(solution)/shard_map/ppermute | solution.py:42
  141.1 10.7 %collective-permute-start.5 = (bf16[2,32,4224]{2,1,0:T(8,128)(2,1)S(1)}, bf16[2,32,4224]{2,1,0:T(8,128)(2,1)S(1)}, u32[]{:S(2)}, u32[]{:S(2)}) collective-permute-start(bf16[2,32,4224]{2,1,0:T(8,128)(2,1)S(1)} %get-tuple-element.11), channel_id=1, source_target_pairs={{1,0},{3,2},{5,4},{7,6},{9,8},{11,10},{13,12},{15,14},{17,16},{19,... | collective-permute-start | bytes 1622024 | tf_op jit(solution)/shard_map/ppermute | solution.py:42
  144.6 6.9 %copy-start.17 = (bf16[2,32,4224]{2,1,0:T(8,128)(2,1)S(1)}, bf16[2,32,4224]{2,1,0:T(8,128)(2,1)}, u32[]{:S(2)}) copy-start(bf16[2,32,4224]{2,1,0:T(8,128)(2,1)} %copy-done.16) | copy-start | bytes 1622020
  156.3 5.8 %copy-start.33 = (f32[2,256,32]{1,2,0:T(8,128)S(1)}, f32[2,256,32]{1,2,0:T(8,128)}, u32[]{:S(2)}) copy-start(f32[2,256,32]{1,2,0:T(8,128)} %get-tuple-element.33) | copy-start | bytes 196612
  158.5 3.5 %copy-start.6 = (bf16[2,256,2048]{1,2,0:T(8,128)(2,1)S(1)}, bf16[2,256,2048]{1,2,0:T(8,128)(2,1)}, u32[]{:S(2)}) copy-start(bf16[2,256,2048]{1,2,0:T(8,128)(2,1)} %copy-done.4) | copy-start | bytes 6291460
  158.5 3.6 %copy-start.9 = (bf16[2,256,2048]{1,2,0:T(8,128)(2,1)S(1)}, bf16[2,256,2048]{1,2,0:T(8,128)(2,1)}, u32[]{:S(2)}) copy-start(bf16[2,256,2048]{1,2,0:T(8,128)(2,1)} %copy-done.7) | copy-start | bytes 6291460
  158.5 3.6 %copy-start.18 = (f32[2,32,64,64]{3,2,1,0:T(8,128)S(1)}, f32[2,32,64,64]{3,2,1,0:T(8,128)}, u32[]{:S(2)}) copy-start(f32[2,32,64,64]{3,2,1,0:T(8,128)} %reshape.199) | copy-start | bytes 3145732
  158.5 3.6 %copy-start.32 = (f32[2,256,32]{1,2,0:T(8,128)S(1)}, f32[2,256,32]{1,2,0:T(8,128)}, u32[]{:S(2)}) copy-start(f32[2,256,32]{1,2,0:T(8,128)} %get-tuple-element.35) | copy-start | bytes 196612
  179.8 7.9 %copy-start.21 = (bf16[256,1024]{1,0:T(8,128)(2,1)S(1)}, bf16[256,1024]{1,0:T(8,128)(2,1)}, u32[]{:S(2)}) copy-start(bf16[256,1024]{1,0:T(8,128)(2,1)} %copy-done.19) | copy-start | bytes 1572868
  179.8 7.9 %copy-start.24 = (bf16[256,1024]{1,0:T(8,128)(2,1)S(1)}, bf16[256,1024]{1,0:T(8,128)(2,1)}, u32[]{:S(2)}) copy-start(bf16[256,1024]{1,0:T(8,128)(2,1)} %copy-done.22) | copy-start | bytes 1572868
  179.8 7.9 %copy-start.42 = (f32[2048]{0:T(1024)S(1)}, f32[2048]{0:T(1024)}, u32[]{:S(2)}) copy-start(f32[2048]{0:T(1024)} %param.20) | copy-start | bytes 24580
  195.2 2.2 %copy-start.1 = (bf16[1024,32]{0,1:T(8,128)(2,1)S(1)}, bf16[1024,32]{0,1:T(8,128)(2,1)}, u32[]{:S(2)}) copy-start(bf16[1024,32]{0,1:T(8,128)(2,1)} %param.14) | copy-start | bytes 196612
  (8 other events, 11.5 us)

commit v4 on v3

--- a/solution.py
+++ b/solution.py
@@ -114,8 +114,11 @@
     product = jnp.einsum(
         "rtn,rhpn->rthp", reads.astype(jnp.float32), entering, precision=lax.Precision.HIGHEST
     )
-    result = local + product * jnp.exp(cum)[..., None]
-    return result.reshape(result.shape[0], result.shape[1], -1)
+    return local + product * jnp.exp(cum)[..., None]
+
+
+def swapped(pair):
+    return jnp.concatenate([pair[1:2], pair[0:1]], axis=0)
 
 
 def body(
@@ -143,25 +146,33 @@
     falling = group_terms(
         jnp.concatenate([projected, after], axis=1),
         dt_raw,
-        dt_bias[::-1],
-        decay_log[::-1],
-        conv_w[::-1],
-        conv_b[::-1],
-        skip_gain[::-1],
+        swapped(dt_bias),
+        swapped(decay_log),
+        swapped(conv_w),
+        swapped(conv_b),
+        swapped(skip_gain),
         True,
     )
     rising_in = exclusive_chain(rising[3], 1)
     falling_in = exclusive_chain(falling[3], -1)
     combined = finish(*rising[:3], rising_in) + finish(*falling[:3], falling_in)
-    gated = combined * jax.nn.silu(gate.reshape(2, length, gate.shape[1]).astype(jnp.float32))
+    heads, head_size = combined.shape[2], combined.shape[3]
+    gate_heads = gate.reshape(2, length, heads, head_size).astype(jnp.float32)
+    gated = combined * jax.nn.silu(gate_heads)
+    mean_square = jnp.mean(gated * gated, axis=(2, 3), keepdims=True)
     normed = (
-        gated * lax.rsqrt(jnp.mean(gated * gated, axis=-1, keepdims=True) + 1e-05) * norm_gain
+        gated * lax.rsqrt(mean_square + 1e-05) * norm_gain.reshape(heads, head_size)
     ).astype(jnp.bfloat16)
-    projected_out = jnp.dot(
-        normed.reshape(2 * length, normed.shape[2]), w_out, preferred_element_type=jnp.float32
+    projected_out = jnp.einsum(
+        "rthp,hpd->rtd",
+        normed,
+        w_out.reshape(heads, head_size, w_out.shape[1]),
+        preferred_element_type=jnp.float32,
     )
-    final_rows = (rows.astype(jnp.float32) + projected_out).astype(jnp.bfloat16)
-    return jnp.stack([final_rows[:length], final_rows[length:]], axis=1)
+    final_rows = (rows.reshape(2, length, -1).astype(jnp.float32) + projected_out).astype(
+        jnp.bfloat16
+    )
+    return jnp.stack([final_rows[0], final_rows[1]], axis=1)
 
 
 def solution(mesh):

time: 200 us -> 183 us (0.915)
  local copies, waits for them, and re-layouts: 70.8 us -> 47.9 us
  starting transfers between devices: 34.4 us -> 46 us
  matrix products: 44.6 us -> 38.4 us
  other arithmetic: 41.1 us -> 43.8 us
    add x2 -> x0, local copies, waits for them, and re-layouts: 17.1 us -> none  [body(): combined = finish(*rising[:3], rising_in) + finish(*falling[:3], falling_in)]
    ppermute x10, starting transfers between devices: 26.3 us -> 37.8 us  [send(): moved = lax.ppermute(value.astype(jnp.bfloat16), 'ctx', pairs)]
    rev x4 -> x0, local copies, waits for them, and re-layouts: 5.36 us -> none  [the longest x1 5.28 us: body(): conv_b[::-1]]
    dot_general x1, matrix products: 7.45 us -> 2.44 us  [body(): jnp.einsum('rthp,hpd->rtd', normed, w_out.reshape(heads, head_size, w_out...]
    concatenate x0 -> x5, other arithmetic: none -> 3.08 us  [the longest x1 2.39 us: body(): rows = jnp.concatenate([stream[:, 0, :], stream[:, 1, :]], axis=0)]
    unnamed x93 -> x86, local copies, waits for them, and re-layouts: 7.57 us -> 6.83 us
  transfers between devices with their start and end apart: 12 -> 12, of which waited for: 2 -> 1; matrix products, arithmetic and copies ran while one was open for 34% -> 35% of each run, Pallas kernels for 0% -> 0%
where the time goes in v4:
time: 183 us; the launch traced here: 182 us
  local copies, waits for them, and re-layouts  47.9 us (26%)
  starting transfers between devices  46 us (25%)
  other arithmetic  43.8 us (24%)
  matrix products  38.4 us (21%)
  waiting for transfers between devices  5.13 us (3%)
    ppermute x10, starting transfers between devices, send(): moved = lax.ppermute(value.astype(jnp.bfloat16), 'ctx', pairs)  37.8 us
    convert_element_type x1, other arithmetic, group_terms(): conv = jax.nn.silu(total).astype(jnp.bfloat16)  19.4 us
    convert_element_type x2, local copies, waits for them, and re-layouts, body(): gate_heads = gate.reshape(2, length, heads, head_size).astype(jnp.float32)  15.7 us
    dot_general x2, matrix products, group_terms(): jnp.einsum('rhts,rshp->rthp', mixing, scaled, preferred_element_type=jnp....  11.4 us
    dot_general x2, matrix products, finish(): jnp.einsum('rtn,rhpn->rthp', reads.astype(jnp.float32), entering, precisi...  10.9 us
    ppermute x2, starting transfers between devices, shifted(): return lax.ppermute(value, 'ctx', pairs)  8.11 us
    another operation x6, other arithmetic  7.69 us
    convert_element_type x8, other arithmetic, send(): moved = lax.ppermute(value.astype(jnp.bfloat16), 'ctx', pairs)  7.48 us
  transfers between devices with their start and end apart: 12, of which 1 were waited for; matrix products, arithmetic and copies ran while one was open for 35% of the time, Pallas kernels for 0%

profile of v4, /device:TPU:1, one launch (start us, length us, event | category | flops | bytes accessed | tf_op | source)
XLA Modules:
  0.0 182.1 jit_solution(12995853507329536465)
XLA Ops:
  0.0 3.4 %fusion.80 = (bf16[256,1,1024]{2,1,0:T(2,128)(2,1)S(1)}, bf16[256,1,1024]{2,1,0:T(2,128)(2,1)S(1)}) fusion(bf16[256,2,1024]{2,1,0:T(2,128)(2,1)} %param.11), kind=kLoop, calls=%fused_computation.178 | loop fusion | bytes 2097152 | tf_op jit(solution)/shard_map/slice | solution.py:128
  3.8 3.4 %convolution_convert_fusion = bf16[512,2176]{1,0:T(8,128)(2,1)S(1)} fusion(bf16[1024,2176]{1,0:T(8,128)(2,1)S(1)} %copy-done.38, bf16[256,1024]{1,0:T(8,128)(2,1)S(1)} %get-tuple-element.64, bf16[256,1024]{1,0:T(8,128)(2,1)S(1)} %get-tuple-element.65), kind=kOutput, calls=%fused_computation.22 | convolution fusion | flops 2284912640 | bytes 7733248 | tf_op jit(solution)/shard_map/dot_general | solution.py:130
  7.4 3.3 %collective-permute-start.6 = (bf16[2,3,2176]{2,0,1:T(2,128)(2,1)S(1)}, bf16[2,3,2176]{2,0,1:T(2,128)(2,1)}, u32[]{:S(2)}, u32[]{:S(2)}) collective-permute-start(bf16[2,3,2176]{2,0,1:T(2,128)(2,1)S(1)} %copy.135), channel_id=1, source_target_pairs={{1,0},{2,1},{3,2},{4,3},{5,4},{6,5},{7,6},{8,7},{9,8},{10,9},{11,1... | collective-permute-start | bytes 78344 | tf_op jit(solution)/shard_map/ppermute | solution.py:20
  11.3 4.8 %collective-permute-start = (bf16[2,3,2176]{2,0,1:T(2,128)(2,1)}, bf16[2,3,2176]{2,0,1:T(2,128)(2,1)}, u32[]{:S(2)}, u32[]{:S(2)}) collective-permute-start(bf16[2,3,2176]{2,0,1:T(2,128)(2,1)} %copy.134), channel_id=1, source_target_pairs={{0,1},{1,2},{2,3},{3,4},{4,5},{5,6},{6,7},{7,8},{8,9},{9,10},{10,1... | collective-permute-start | bytes 78344 | tf_op jit(solution)/shard_map/ppermute | solution.py:20
  17.6 5.0 %reduce-window.16 = f32[2,32,2,128]{3,1,2,0:T(8,128)S(1)} reduce-window(f32[2,32,2,128]{3,1,2,0:T(8,128)S(1)} %bitcast.137, f32[]{:T(128)} %constant.50.clone.1), window={size=1x1x1x128 pad=0_0x0_0x0_0x0_127}, to_apply=%region_2.3 | reduce-window | flops 2080768 | bytes 131076 | tf_op jit(solution)/shard_map/reduce-window.2
  22.7 0.7 fusion.72
  23.5 1.2 reduce-window.14
  24.9 0.7 fusion.71
  25.8 0.7 bitcast_exponential_fusion
  30.3 2.4 %copy.102 = bf16[2,256,2176]{1,2,0:T(8,128)(2,1)} copy(bf16[2,256,2176]{2,1,0:T(8,128)(2,1)S(1)} %bitcast.136) | data formatting | bytes 4456448 | tf_op jit(solution)/shard_map/reshape | solution.py:131
  33.3 1.4 copy.109
  34.7 2.2 %copy.101 = bf16[2,3,2176]{1,2,0:T(8,128)(2,1)} copy(bf16[2,3,2176]{2,0,1:T(2,128)(2,1)} %collective-permute-done) | data formatting | bytes 52224 | tf_op jit(solution)/shard_map/ppermute | solution.py:20
  36.9 19.4 %multiply_convert_fusion.4 = (bf16[2,256,2176]{1,2,0:T(8,128)(2,1)S(1)}, bf16[2,256,2176]{1,2,0:T(8,128)(2,1)S(1)}) fusion(bf16[2,256,2176]{1,2,0:T(8,128)(2,1)} %copy.102, bf16[2,3,2176]{1,2,0:T(8,128)(2,1)S(1)} %copy.109, f32[2,2176]{1,0:T(2,128)} %get-tuple-element.68, f32[2,2176]{1,0:T(2,128)} %get-tuple-element.69, f32[2,2176]{1,0:T(2,128)} %get-tuple-element.70, ...), kind=kLoop, calls=%fused_computation.25 | loop fusion | flops 56819712 | bytes 6910976 | tf_op jit(solution)/shard_map/convert_element_type | solution.py:71
  56.5 1.2 copy-done.3
  58.3 2.0 %fusion.30 = f32[2,32,64,64]{3,2,1,0:T(8,128)} fusion(bf16[2,256,32,64]{1,3,2,0:T(8,128)(2,1)S(1)} %bitcast.127, f32[2,256,32]{1,2,0:T(8,128)S(1)} %get-tuple-element.42, bf16[2,256,2176]{1,2,0:T(8,128)(2,1)S(1)} %get-tuple-element.21), kind=kOutput, calls=%fused_computation.56 | convolution fusion | flops 137363456 | bytes 3276800 | tf_op jit(solution)/shard_map/rshp,rsn->rhpn/dot_general | solution.py:97
  60.3 2.1 %reshape.204 = f32[2,32,4096]{2,1,0:T(8,128)S(1)} reshape(f32[2,32,64,64]{3,2,1,0:T(8,128)} %fusion.30) | data formatting | bytes 2097152 | tf_op jit(solution)/shard_map/reshape | solution.py:103
  62.6 1.0 fusion.48
  63.6 2.1 %collective-permute-start.7 = (bf16[2,32,4224]{2,1,0:T(8,128)(2,1)}, bf16[2,32,4224]{2,1,0:T(8,128)(2,1)}, u32[]{:S(2)}, u32[]{:S(2)}) collective-permute-start(bf16[2,32,4224]{2,1,0:T(8,128)(2,1)} %fusion.48), channel_id=1, source_target_pairs={{15,14},{13,12},{11,10},{9,8},{7,6},{5,4},{3,2},{1,0},{31,30},{29,... | collective-permute-start | bytes 1622024 | tf_op jit(solution)/shard_map/ppermute | solution.py:42
  65.6 0.7 bitcast_exponential_fusion.1
  66.5 1.3 copy-done.7
  67.9 2.0 %fusion.33 = f32[2,32,64,64]{3,2,1,0:T(8,128)} fusion(bf16[2,256,32,64]{1,3,2,0:T(8,128)(2,1)S(1)} %bitcast.130, f32[2,256,32]{1,2,0:T(8,128)S(1)} %get-tuple-element.40, bf16[2,256,2176]{1,2,0:T(8,128)(2,1)S(1)} %get-tuple-element.22), kind=kOutput, calls=%fused_computation.57 | convolution fusion | flops 137363456 | bytes 3276800 | tf_op jit(solution)/shard_map/rshp,rsn->rhpn/dot_general | solution.py:97
  69.9 2.1 %reshape.200 = f32[2,32,4096]{2,1,0:T(8,128)S(1)} reshape(f32[2,32,64,64]{3,2,1,0:T(8,128)} %fusion.33) | data formatting | bytes 2097152 | tf_op jit(solution)/shard_map/reshape | solution.py:103
  72.0 1.6 fusion.75
  74.5 1.7 collective-permute-start.1
  77.7 4.3 %fusion.24 = f32[512,2048]{1,0:T(8,128)} fusion(bf16[1024,2048]{1,0:T(8,128)(2,1)S(1)} %copy-done.39, bf16[256,1024]{1,0:T(8,128)(2,1)S(1)} %copy-done.17, bf16[256,1024]{1,0:T(8,128)(2,1)S(1)} %copy-done.19), kind=kOutput, calls=%fused_computation.48 | convolution fusion | flops 2151677952 | bytes 9437184 | tf_op jit(solution)/shard_map/dot_general | solution.py:129
  82.9 5.5 %collective-permute-start.2 = (bf16[2,32,4224]{2,1,0:T(8,128)(2,1)S(1)}, bf16[2,32,4224]{2,1,0:T(8,128)(2,1)S(1)}, u32[]{:S(2)}, u32[]{:S(2)}) collective-permute-start(bf16[2,32,4224]{2,1,0:T(8,128)(2,1)S(1)} %get-tuple-element.15), channel_id=1, source_target_pairs={{1,3},{3,1},{5,7},{7,5},{9,11},{11,9},{13,15},{15,13},{17,19},{19,... | collective-permute-start | bytes 1622024 | tf_op jit(solution)/shard_map/ppermute | solution.py:42
  90.0 5.1 %collective-permute-done.2 = bf16[2,32,4224]{2,1,0:T(8,128)(2,1)S(1)} collective-permute-done((bf16[2,32,4224]{2,1,0:T(8,128)(2,1)S(1)}, bf16[2,32,4224]{2,1,0:T(8,128)(2,1)S(1)}, u32[]{:S(2)}, u32[]{:S(2)}) %collective-permute-start.2) | collective-permute-done | bytes 540704 | tf_op jit(solution)/shard_map/ppermute | solution.py:42
  95.3 2.1 %fusion.73 = (bf16[2,32,4224]{2,1,0:T(8,128)(2,1)}, f32[2,32,4224]{2,1,0:T(8,128)}, bf16[2,32,4224]{2,1,0:T(8,128)(2,1)}, f32[2,32,4224]{2,1,0:T(8,128)}) fusion(bf16[2,32,4224]{2,1,0:T(8,128)(2,1)S(1)} %collective-permute-done.8, f32[2,32]{1,0:T(2,128)S(1)} %slice_reduce_fusion.5, bf16[2,32,4224]{2,1,0:T(8,128)(2,1)S(1)} %collective-permute-done.9, ...), kind=kLoop, calls=%fused_computation.171 | loop fusion | flops 5406720 | bytes 6493314 | tf_op jit(solution)/shard_map/convert_element_type | solution.py:42
  97.4 3.6 %collective-permute-start.3 = (bf16[2,32,4224]{2,1,0:T(8,128)(2,1)}, bf16[2,32,4224]{2,1,0:T(8,128)(2,1)S(1)}, u32[]{:S(2)}, u32[]{:S(2)}) collective-permute-start(bf16[2,32,4224]{2,1,0:T(8,128)(2,1)} %get-tuple-element.51), channel_id=1, source_target_pairs={{1,5},{3,7},{5,9},{7,11},{9,13},{11,15},{17,21},{19,23},{21,25},{2... | collective-permute-start | bytes 1622024 | tf_op jit(solution)/shard_map/ppermute | solution.py:42
  101.0 7.9 %reshape.218 = f32[2,256,32,64]{3,2,1,0:T(8,128)} reshape(f32[512,2048]{1,0:T(8,128)} %fusion.24) | data formatting | bytes 8388608 | tf_op jit(solution)/shard_map/convert_element_type | solution.py:160
  108.9 7.8 %copy.115 = f32[2,256,32,64]{1,3,2,0:T(8,128)} copy(f32[2,256,32,64]{3,2,1,0:T(8,128)} %reshape.218) | data formatting | bytes 8388608 | tf_op jit(solution)/shard_map/convert_element_type | solution.py:160
  116.8 2.4 %pad_maximum_fusion.4 = bf16[512,1024]{1,0:T(8,128)(2,1)} fusion(bf16[256,1024]{1,0:T(8,128)(2,1)} %copy-done.16, bf16[256,1024]{1,0:T(8,128)(2,1)} %copy-done.18), kind=kLoop, calls=%fused_computation.86 | loop fusion | flops 2097152 | bytes 2097152 | tf_op jit(solution)/shard_map/concatenate | solution.py:128
  119.2 1.1 fusion.56
  120.4 0.8 slice_reduce_fusion.8
  121.2 1.5 add_convert_fusion.1
  122.7 4.9 %collective-permute-start.4 = (bf16[2,32,4224]{2,1,0:T(8,128)(2,1)S(1)}, bf16[2,32,4224]{2,1,0:T(8,128)(2,1)S(1)}, u32[]{:S(2)}, u32[]{:S(2)}) collective-permute-start(bf16[2,32,4224]{2,1,0:T(8,128)(2,1)S(1)} %add_convert_fusion.1), channel_id=1, source_target_pairs={{1,9},{3,11},{5,13},{7,15},{17,25},{19,27},{21,29},{23,31},{33,41}... | collective-permute-start | bytes 1622024 | tf_op jit(solution)/shard_map/ppermute | solution.py:42
  127.6 5.7 %fusion.1 = f32[2,32,64,256]{3,2,1,0:T(8,128)} fusion(f32[2,32,256]{2,1,0:T(8,128)S(1)} %copy-done.27, f32[2,256,256]{2,1,0:T(8,128)S(1)} %fusion.56, pred[256,256]{1,0:T(8,128)(4,1)S(1)} %copy-done.28, bf16[2,256,32,64]{1,3,2,0:T(8,128)(2,1)S(1)} %bitcast.128, f32[2,256,32]{1,2,0:T(8,128)S(1)} %copy-done.24), kind=kOutput, calls=%fused_computation.3 | convolution fusion | flops 556793856 | bytes 7012352 | tf_op jit(solution)/shard_map/rhts,rshp->rthp/dot_general | solution.py:93
  133.6 1.4 collective-permute-start.11
  135.6 16.6 %collective-permute-start.5 = (bf16[2,32,4224]{2,1,0:T(8,128)(2,1)S(1)}, bf16[2,32,4224]{2,1,0:T(8,128)(2,1)S(1)}, u32[]{:S(2)}, u32[]{:S(2)}) collective-permute-start(bf16[2,32,4224]{2,1,0:T(8,128)(2,1)S(1)} %get-tuple-element.11), channel_id=1, source_target_pairs={{1,0},{3,2},{5,4},{7,6},{9,8},{11,10},{13,12},{15,14},{17,16},{19,... | collective-permute-start | bytes 1622024 | tf_op jit(solution)/shard_map/ppermute | solution.py:42
  152.3 5.8 %fusion = f32[2,32,64,256]{3,2,1,0:T(8,128)} fusion(f32[2,32,256]{2,1,0:T(8,128)S(1)} %copy-done.26, f32[2,256,256]{2,1,0:T(8,128)S(1)} %fusion.61, pred[256,256]{1,0:T(8,128)(4,1)S(1)} %copy-done.29, bf16[2,256,32,64]{1,3,2,0:T(8,128)(2,1)S(1)} %bitcast.131, f32[2,256,32]{1,2,0:T(8,128)S(1)} %get-tuple-element.18), kind=kOutput, calls=%fused_computation.2 | convolution fusion | flops 556793856 | bytes 7012352 | tf_op jit(solution)/shard_map/rhts,rshp->rthp/dot_general | solution.py:93
  158.0 1.2 convert_element_type.197
  159.6 1.5 fusion.45
  161.0 3.1 %reshape.205 = f32[2,32,64,64]{3,2,1,0:T(8,128)} reshape(f32[2,32,4096]{2,1,0:T(8,128)} %get-tuple-element.54) | data formatting | bytes 2097152 | tf_op jit(solution)/shard_map/reshape | solution.py:113
  164.1 2.2 %reshape.201 = f32[2,32,64,64]{3,2,1,0:T(8,128)} reshape(f32[2,32,4096]{2,1,0:T(8,128)S(1)} %get-tuple-element.55) | data formatting | bytes 2097152 | tf_op jit(solution)/shard_map/reshape | solution.py:113
  166.4 3.5 %fusion.53 = f32[2,256,32,64]{1,3,2,0:T(8,128)S(1)} fusion(f32[2,32,64,64]{3,2,1,0:T(8,128)} %reshape.201, bf16[2,256,2176]{1,2,0:T(8,128)(2,1)S(1)} %get-tuple-element.22), kind=kOutput, calls=%fused_computation.115 | convolution fusion | flops 805306368 | bytes 5308416 | tf_op jit(solution)/shard_map/rtn,rhpn->rthp/dot_general | solution.py:114
  170.0 7.4 %multiply_reduce_fusion = (f32[2,256]{1,0:T(2,128)S(1)}, f32[2,256,32,64]{1,3,2,0:T(8,128)S(1)}) fusion(f32[2,256,32,64]{1,3,2,0:T(8,128)} %copy.115, f32[2,256,32]{1,2,0:T(8,128)S(1)} %copy-done.30, f32[2,32,64,64]{3,2,1,0:T(8,128)S(1)} %copy-done.15, bf16[2,256,2176]{1,2,0:T(8,128)(2,1)} %copy-done.3, bf16[2,256,32,64]{1,3,2,0:T(8,128)(2,1)S(1)} %bitcast.129, ...), kind=kOutput, calls=%fused_computation.38 | convolution fusion | flops 824180224 | bytes 26413568 | tf_op jit(solution)/shard_map/rtn,rhpn->rthp/dot_general | solution.py:114
  177.4 2.4 %fusion.36 = bf16[2,256,1024]{2,1,0:T(8,128)(2,1)S(1)} fusion(bf16[2,256,1024]{2,1,0:T(8,128)(2,1)S(1)} %bitcast.134, bf16[32,64,1024,1]{2,1,0,3:T(8,128)(2,1)S(1)} %bitcast.133, f32[2,256,32,64]{1,3,2,0:T(8,128)S(1)} %get-tuple-element.63, f32[32,64]{1,0:T(8,128)S(1)} %mul.438, f32[2,256]{1,0:T(2,128)S(1)} %add_rsqrt_fusion), kind=kOutput, calls=%fused_computation.59 | convolution fusion | flops 2152202240 | bytes 10496000 | tf_op jit(solution)/shard_map/rthp,hpd->rtd/dot_general | solution.py:166
  180.0 2.0 %copy.116 = bf16[256,2,1024]{2,1,0:T(2,128)(2,1)} copy(bf16[256,2,1024]{2,0,1:T(8,128)(2,1)S(1)} %pad_maximum_fusion.5) | data formatting | bytes 2097152 | tf_op jit(solution)/shard_map/stack | solution.py:175
  (157 shorter events, 14.6 us)
Async XLA Ops:
  0.0 16.9 %copy-start = (bf16[1024,32]{0,1:T(8,128)(2,1)S(1)}, bf16[1024,32]{0,1:T(8,128)(2,1)}, u32[]{:S(2)}) copy-start(bf16[1024,32]{0,1:T(8,128)(2,1)} %param.14) | copy-start | bytes 196612
  0.0 3.8 %copy-start.38 = (bf16[1024,2176]{1,0:T(8,128)(2,1)S(1)}, bf16[1024,2176]{1,0:T(8,128)(2,1)}, u32[]{:S(2)}) copy-start(bf16[1024,2176]{1,0:T(8,128)(2,1)} %param.13) | copy-start | bytes 13369348
  3.8 13.1 %copy-start.16 = (bf16[256,1024]{1,0:T(8,128)(2,1)}, bf16[256,1024]{1,0:T(8,128)(2,1)S(1)}, u32[]{:S(2)}) copy-start(bf16[256,1024]{1,0:T(8,128)(2,1)S(1)} %get-tuple-element.64) | copy-start | bytes 1572868
  3.8 13.1 %copy-start.18 = (bf16[256,1024]{1,0:T(8,128)(2,1)}, bf16[256,1024]{1,0:T(8,128)(2,1)S(1)}, u32[]{:S(2)}) copy-start(bf16[256,1024]{1,0:T(8,128)(2,1)S(1)} %get-tuple-element.65) | copy-start | bytes 1572868
  3.8 12.3 %copy-start.35 = (f32[2,32]{1,0:T(2,128)S(1)}, f32[2,32]{1,0:T(2,128)}, u32[]{:S(2)}) copy-start(f32[2,32]{1,0:T(2,128)} %param.16) | copy-start | bytes 772
  3.8 12.3 %copy-start.22 = (f32[2,4,2176]{2,1,0:T(4,128)S(1)}, f32[2,4,2176]{2,1,0:T(4,128)}, u32[]{:S(2)}) copy-start(f32[2,4,2176]{2,1,0:T(4,128)} %param.17) | copy-start | bytes 208900
  7.3 10.1 %copy-start.36 = (f32[2,32]{1,0:T(2,128)S(1)}, f32[2,32]{1,0:T(2,128)}, u32[]{:S(2)}) copy-start(f32[2,32]{1,0:T(2,128)} %param.15) | copy-start | bytes 772
  7.3 16.2 %copy-start.25 = (f32[2,2176]{1,0:T(2,128)S(1)}, f32[2,2176]{1,0:T(2,128)}, u32[]{:S(2)}) copy-start(f32[2,2176]{1,0:T(2,128)} %param.18) | copy-start | bytes 52228
  7.4 25.9 %collective-permute-start.6 = (bf16[2,3,2176]{2,0,1:T(2,128)(2,1)S(1)}, bf16[2,3,2176]{2,0,1:T(2,128)(2,1)}, u32[]{:S(2)}, u32[]{:S(2)}) collective-permute-start(bf16[2,3,2176]{2,0,1:T(2,128)(2,1)S(1)} %copy.135), channel_id=1, source_target_pairs={{1,0},{2,1},{3,2},{4,3},{5,4},{6,5},{7,6},{8,7},{9,8},{10,9},{11,1... | collective-permute-start | bytes 78344 | tf_op jit(solution)/shard_map/ppermute | solution.py:20
  11.3 23.4 %collective-permute-start = (bf16[2,3,2176]{2,0,1:T(2,128)(2,1)}, bf16[2,3,2176]{2,0,1:T(2,128)(2,1)}, u32[]{:S(2)}, u32[]{:S(2)}) collective-permute-start(bf16[2,3,2176]{2,0,1:T(2,128)(2,1)} %copy.134), channel_id=1, source_target_pairs={{0,1},{1,2},{2,3},{3,4},{4,5},{5,6},{6,7},{7,8},{8,9},{9,10},{10,1... | collective-permute-start | bytes 78344 | tf_op jit(solution)/shard_map/ppermute | solution.py:20
  17.5 15.2 %copy-start.23 = (f32[2,256,32]{1,2,0:T(8,128)}, f32[2,256,32]{1,2,0:T(8,128)S(1)}, u32[]{:S(2)}) copy-start(f32[2,256,32]{1,2,0:T(8,128)S(1)} %get-tuple-element.48) | copy-start | bytes 196612
  29.7 105.5 %copy-start.21 = (pred[4224]{0:T(1024)(128)(4,1)}, pred[4224]{0:T(1024)(128)(4,1)S(1)}, u32[]{:S(2)}) copy-start(pred[4224]{0:T(1024)(128)(4,1)S(1)} %iota_compare_fusion.2) | copy-start | bytes 12676
  56.5 1.8 copy-start.4
  60.3 2.1 %copy-start.33 = (f32[2,32]{1,0:T(2,128)S(1)}, f32[2,32]{1,0:T(2,128)}, u32[]{:S(2)}) copy-start(f32[2,32]{1,0:T(2,128)} %exp.80) | copy-start | bytes 772
  62.5 4.0 %copy-start.2 = (f32[2,32,4096]{2,1,0:T(8,128)}, f32[2,32,4096]{2,1,0:T(8,128)S(1)}, u32[]{:S(2)}) copy-start(f32[2,32,4096]{2,1,0:T(8,128)S(1)} %reshape.204) | copy-start | bytes 3145732
  63.6 8.5 %collective-permute-start.7 = (bf16[2,32,4224]{2,1,0:T(8,128)(2,1)}, bf16[2,32,4224]{2,1,0:T(8,128)(2,1)}, u32[]{:S(2)}, u32[]{:S(2)}) collective-permute-start(bf16[2,32,4224]{2,1,0:T(8,128)(2,1)} %fusion.48), channel_id=1, source_target_pairs={{15,14},{13,12},{11,10},{9,8},{7,6},{5,4},{3,2},{1,0},{31,30},{29,... | collective-permute-start | bytes 1622024 | tf_op jit(solution)/shard_map/ppermute | solution.py:42
  72.0 2.3 %copy-start.32 = (f32[2,32]{1,0:T(2,128)S(1)}, f32[2,32]{1,0:T(2,128)}, u32[]{:S(2)}) copy-start(f32[2,32]{1,0:T(2,128)} %exp.73) | copy-start | bytes 772
  73.6 2.7 %collective-permute-start.8 = (bf16[2,32,4224]{2,1,0:T(8,128)(2,1)S(1)}, bf16[2,32,4224]{2,1,0:T(8,128)(2,1)S(1)}, u32[]{:S(2)}, u32[]{:S(2)}) collective-permute-start(bf16[2,32,4224]{2,1,0:T(8,128)(2,1)S(1)} %get-tuple-element.9), channel_id=1, source_target_pairs={{14,12},{12,14},{10,8},{8,10},{6,4},{4,6},{2,0},{0,2},{30,28},{28,... | collective-permute-start | bytes 1622024 | tf_op jit(solution)/shard_map/ppermute | solution.py:42
  74.4 3.2 %copy-start.39 = (bf16[1024,2048]{1,0:T(8,128)(2,1)S(1)}, bf16[1024,2048]{1,0:T(8,128)(2,1)}, u32[]{:S(2)}) copy-start(bf16[1024,2048]{1,0:T(8,128)(2,1)} %param.12) | copy-start | bytes 12582916
  74.5 7.6 %collective-permute-start.1 = (bf16[2,32,4224]{2,1,0:T(8,128)(2,1)S(1)}, bf16[2,32,4224]{2,1,0:T(8,128)(2,1)S(1)}, u32[]{:S(2)}, u32[]{:S(2)}) collective-permute-start(bf16[2,32,4224]{2,1,0:T(8,128)(2,1)S(1)} %fusion.49), channel_id=1, source_target_pairs={{0,1},{2,3},{4,5},{6,7},{8,9},{10,11},{12,13},{14,15},{16,17},{18,... | collective-permute-start | bytes 1622024 | tf_op jit(solution)/shard_map/ppermute | solution.py:42
  76.9 5.2 %collective-permute-start.9 = (bf16[2,32,4224]{2,1,0:T(8,128)(2,1)S(1)}, bf16[2,32,4224]{2,1,0:T(8,128)(2,1)S(1)}, u32[]{:S(2)}, u32[]{:S(2)}) collective-permute-start(bf16[2,32,4224]{2,1,0:T(8,128)(2,1)S(1)} %get-tuple-element.7), channel_id=1, source_target_pairs={{14,10},{12,8},{10,6},{8,4},{6,2},{4,0},{30,26},{28,24},{26,22},{2... | collective-permute-start | bytes 1622024 | tf_op jit(solution)/shard_map/ppermute | solution.py:42
  82.1 7.7 %copy-start.37 = (f32[2,32]{1,0:T(2,128)S(1)}, f32[2,32]{1,0:T(2,128)}, u32[]{:S(2)}) copy-start(f32[2,32]{1,0:T(2,128)} %param.19) | copy-start | bytes 772
  82.9 12.2 %collective-permute-start.2 = (bf16[2,32,4224]{2,1,0:T(8,128)(2,1)S(1)}, bf16[2,32,4224]{2,1,0:T(8,128)(2,1)S(1)}, u32[]{:S(2)}, u32[]{:S(2)}) collective-permute-start(bf16[2,32,4224]{2,1,0:T(8,128)(2,1)S(1)} %get-tuple-element.15), channel_id=1, source_target_pairs={{1,3},{3,1},{5,7},{7,5},{9,11},{11,9},{13,15},{15,13},{17,19},{19,... | collective-permute-start | bytes 1622024 | tf_op jit(solution)/shard_map/ppermute | solution.py:42
  89.1 6.2 %collective-permute-start.10 = (bf16[2,32,4224]{2,1,0:T(8,128)(2,1)S(1)}, bf16[2,32,4224]{2,1,0:T(8,128)(2,1)S(1)}, u32[]{:S(2)}, u32[]{:S(2)}) collective-permute-start(bf16[2,32,4224]{2,1,0:T(8,128)(2,1)S(1)} %get-tuple-element.53), channel_id=1, source_target_pairs={{14,6},{12,4},{10,2},{8,0},{30,22},{28,20},{26,18},{24,16},{46,38}... | collective-permute-start | bytes 1622024 | tf_op jit(solution)/shard_map/ppermute | solution.py:42
  97.4 23.8 %collective-permute-start.3 = (bf16[2,32,4224]{2,1,0:T(8,128)(2,1)}, bf16[2,32,4224]{2,1,0:T(8,128)(2,1)S(1)}, u32[]{:S(2)}, u32[]{:S(2)}) collective-permute-start(bf16[2,32,4224]{2,1,0:T(8,128)(2,1)} %get-tuple-element.51), channel_id=1, source_target_pairs={{1,5},{3,7},{5,9},{7,11},{9,13},{11,15},{17,21},{19,23},{21,25},{2... | collective-permute-start | bytes 1622024 | tf_op jit(solution)/shard_map/ppermute | solution.py:42
  108.9 7.8 %copy-start.34 = (f32[2048]{0:T(1024)S(1)}, f32[2048]{0:T(1024)}, u32[]{:S(2)}) copy-start(f32[2048]{0:T(1024)} %param.20) | copy-start | bytes 24580
  116.8 10.8 %copy-start.5 = (bf16[2,256,2048]{1,2,0:T(8,128)(2,1)S(1)}, bf16[2,256,2048]{1,2,0:T(8,128)(2,1)}, u32[]{:S(2)}) copy-start(bf16[2,256,2048]{1,2,0:T(8,128)(2,1)} %copy-done.4) | copy-start | bytes 6291460
  116.8 10.8 %copy-start.24 = (f32[2,256,32]{1,2,0:T(8,128)S(1)}, f32[2,256,32]{1,2,0:T(8,128)}, u32[]{:S(2)}) copy-start(f32[2,256,32]{1,2,0:T(8,128)} %copy-done.23) | copy-start | bytes 196612
  116.8 10.8 %copy-start.27 = (f32[2,32,256]{2,1,0:T(8,128)S(1)}, f32[2,32,256]{2,1,0:T(8,128)}, u32[]{:S(2)}) copy-start(f32[2,32,256]{2,1,0:T(8,128)} %get-tuple-element.44) | copy-start | bytes 196612
  116.8 10.8 %copy-start.28 = (pred[256,256]{1,0:T(8,128)(4,1)S(1)}, pred[256,256]{1,0:T(8,128)(4,1)}, u32[]{:S(2)}) copy-start(pred[256,256]{1,0:T(8,128)(4,1)} %iota_compare_fusion) | copy-start | bytes 196612
  122.7 12.5 %collective-permute-start.4 = (bf16[2,32,4224]{2,1,0:T(8,128)(2,1)S(1)}, bf16[2,32,4224]{2,1,0:T(8,128)(2,1)S(1)}, u32[]{:S(2)}, u32[]{:S(2)}) collective-permute-start(bf16[2,32,4224]{2,1,0:T(8,128)(2,1)S(1)} %add_convert_fusion.1), channel_id=1, source_target_pairs={{1,9},{3,11},{5,13},{7,15},{17,25},{19,27},{21,29},{23,31},{33,41}... | collective-permute-start | bytes 1622024 | tf_op jit(solution)/shard_map/ppermute | solution.py:42
  127.6 5.9 %copy-start.20 = (bf16[2,32,4224]{2,1,0:T(8,128)(2,1)S(1)}, bf16[2,32,4224]{2,1,0:T(8,128)(2,1)}, u32[]{:S(2)}) copy-start(bf16[2,32,4224]{2,1,0:T(8,128)(2,1)} %get-tuple-element.5) | copy-start | bytes 1622020
  133.6 18.7 %copy-start.8 = (bf16[2,256,2048]{1,2,0:T(8,128)(2,1)S(1)}, bf16[2,256,2048]{1,2,0:T(8,128)(2,1)}, u32[]{:S(2)}) copy-start(bf16[2,256,2048]{1,2,0:T(8,128)(2,1)} %copy-done.7) | copy-start | bytes 6291460
  133.6 18.7 %copy-start.26 = (f32[2,32,256]{2,1,0:T(8,128)S(1)}, f32[2,32,256]{2,1,0:T(8,128)}, u32[]{:S(2)}) copy-start(f32[2,32,256]{2,1,0:T(8,128)} %get-tuple-element.46) | copy-start | bytes 196612
  133.6 18.7 %copy-start.29 = (pred[256,256]{1,0:T(8,128)(4,1)S(1)}, pred[256,256]{1,0:T(8,128)(4,1)}, u32[]{:S(2)}) copy-start(pred[256,256]{1,0:T(8,128)(4,1)} %iota_compare_fusion.1) | copy-start | bytes 196612
  133.6 25.9 %collective-permute-start.11 = (bf16[2,32,4224]{2,1,0:T(8,128)(2,1)S(1)}, bf16[2,32,4224]{2,1,0:T(8,128)(2,1)S(1)}, u32[]{:S(2)}, u32[]{:S(2)}) collective-permute-start(bf16[2,32,4224]{2,1,0:T(8,128)(2,1)S(1)} %copy-done.20), channel_id=1, source_target_pairs={{14,15},{12,13},{10,11},{8,9},{6,7},{4,5},{2,3},{0,1},{30,31},{28,... | collective-permute-start | bytes 1622024 | tf_op jit(solution)/shard_map/ppermute | solution.py:42
  135.6 23.9 %collective-permute-start.5 = (bf16[2,32,4224]{2,1,0:T(8,128)(2,1)S(1)}, bf16[2,32,4224]{2,1,0:T(8,128)(2,1)S(1)}, u32[]{:S(2)}, u32[]{:S(2)}) collective-permute-start(bf16[2,32,4224]{2,1,0:T(8,128)(2,1)S(1)} %get-tuple-element.11), channel_id=1, source_target_pairs={{1,0},{3,2},{5,4},{7,6},{9,8},{11,10},{13,12},{15,14},{17,16},{19,... | collective-permute-start | bytes 1622024 | tf_op jit(solution)/shard_map/ppermute | solution.py:42
  152.3 7.0 %copy-start.14 = (bf16[2,32,4224]{2,1,0:T(8,128)(2,1)S(1)}, bf16[2,32,4224]{2,1,0:T(8,128)(2,1)}, u32[]{:S(2)}) copy-start(bf16[2,32,4224]{2,1,0:T(8,128)(2,1)} %copy-done.13) | copy-start | bytes 1622020
  158.0 1.5 copy-start.11
  158.0 1.5 slice-start
  164.1 5.8 %copy-start.31 = (f32[2,256,32]{1,2,0:T(8,128)S(1)}, f32[2,256,32]{1,2,0:T(8,128)}, u32[]{:S(2)}) copy-start(f32[2,256,32]{1,2,0:T(8,128)} %get-tuple-element.39) | copy-start | bytes 196612
  166.4 3.5 %copy-start.6 = (bf16[2,256,2048]{1,2,0:T(8,128)(2,1)S(1)}, bf16[2,256,2048]{1,2,0:T(8,128)(2,1)}, u32[]{:S(2)}) copy-start(bf16[2,256,2048]{1,2,0:T(8,128)(2,1)} %copy-done.4) | copy-start | bytes 6291460
  166.4 3.6 %copy-start.9 = (bf16[2,256,2048]{1,2,0:T(8,128)(2,1)S(1)}, bf16[2,256,2048]{1,2,0:T(8,128)(2,1)}, u32[]{:S(2)}) copy-start(bf16[2,256,2048]{1,2,0:T(8,128)(2,1)} %copy-done.7) | copy-start | bytes 6291460
  166.4 3.6 %copy-start.15 = (f32[2,32,64,64]{3,2,1,0:T(8,128)S(1)}, f32[2,32,64,64]{3,2,1,0:T(8,128)}, u32[]{:S(2)}) copy-start(f32[2,32,64,64]{3,2,1,0:T(8,128)} %reshape.205) | copy-start | bytes 3145732
  166.4 3.6 %copy-start.30 = (f32[2,256,32]{1,2,0:T(8,128)S(1)}, f32[2,256,32]{1,2,0:T(8,128)}, u32[]{:S(2)}) copy-start(f32[2,256,32]{1,2,0:T(8,128)} %get-tuple-element.41) | copy-start | bytes 196612
  169.9 7.4 %copy-start.10 = (bf16[2048,1024]{1,0:T(8,128)(2,1)S(1)}, bf16[2048,1024]{1,0:T(8,128)(2,1)}, u32[]{:S(2)}) copy-start(bf16[2048,1024]{1,0:T(8,128)(2,1)} %param.21) | copy-start | bytes 12582916
  170.0 7.4 %copy-start.12 = (bf16[512,1024]{1,0:T(8,128)(2,1)S(1)}, bf16[512,1024]{1,0:T(8,128)(2,1)}, u32[]{:S(2)}) copy-start(bf16[512,1024]{1,0:T(8,128)(2,1)} %pad_maximum_fusion.4) | copy-start | bytes 3145732
  179.8 2.2 %copy-start.1 = (bf16[1024,32]{0,1:T(8,128)(2,1)S(1)}, bf16[1024,32]{0,1:T(8,128)(2,1)}, u32[]{:S(2)}) copy-start(bf16[1024,32]{0,1:T(8,128)(2,1)} %param.14) | copy-start | bytes 196612
  (5 other events, 6.2 us)

commit v5 on v4

--- a/solution.py
+++ b/solution.py
@@ -1,6 +1,7 @@
 import jax
 import jax.numpy as jnp
 from jax import lax
+from jax.experimental.layout import Layout, with_layout_constraint
 from jax.sharding import PartitionSpec as P
 
 NS = 64
@@ -68,7 +69,7 @@
     total = offset[:, None, :] + weights[:, 0][:, None, :] * taps[0].astype(jnp.float32)
     for k in range(1, K):
         total = total + weights[:, k][:, None, :] * taps[k].astype(jnp.float32)
-    conv = jax.nn.silu(total).astype(jnp.bfloat16)
+    conv = with_layout_constraint(jax.nn.silu(total).astype(jnp.bfloat16), Layout((0, 1, 2)))
     inner = conv.shape[2] - 2 * NS
     head_size = inner // heads
     values = conv[:, :, :inner].reshape(runs, length, heads, head_size)

time: 183 us -> 194 us (1.060)
  matrix products: 38.4 us -> 46 us
  other arithmetic: 43.8 us -> 46.4 us
  starting transfers between devices: 46 us -> 48.2 us
    convert_element_type x0 -> x2, local copies, waits for them, and re-layouts: none -> 10.7 us  [group_terms(): values32 = values.astype(jnp.float32)]
    unnamed x86 -> x72, local copies, waits for them, and re-layouts: 6.83 us -> 1.92 us
    dot_general x2, matrix products: 4.06 us -> 8.51 us  [group_terms(): jnp.einsum('rshp,rsn->rhpn', weighted, keys_in, preferred_element_type=jn...]
    convert_element_type x1 -> x3, other arithmetic: 19.4 us -> 23.2 us  [the longest x1 16.7 us: group_terms(): jax.nn.silu(total).astype(jnp.bfloat16)]
    ppermute x2 -> x0, local copies, waits for them, and re-layouts: 3.58 us -> none  [shifted(): return lax.ppermute(value, 'ctx', pairs)]
    reshape x2 -> x1, local copies, waits for them, and re-layouts: 2.44 us -> 0.01 us  [the longest x1 2.44 us: body(): projected = projected.reshape(2, length, projected.shape[1])]
    ppermute x10, starting transfers between devices: 37.8 us -> 40.1 us  [send(): moved = lax.ppermute(value.astype(jnp.bfloat16), 'ctx', pairs)]
    dot_general x1, matrix products: 2.44 us -> 4.69 us  [body(): jnp.einsum('rthp,hpd->rtd', normed, w_out.reshape(heads, head_size, w_out...]
  transfers between devices with their start and end apart: 12 -> 12, of which waited for: 1 -> 1; matrix products, arithmetic and copies ran while one was open for 35% -> 34% of each run, Pallas kernels for 0% -> 0%
where the time goes in v5:
time: 194 us; the launch traced here: 193 us
  starting transfers between devices  48.2 us (25%)
  local copies, waits for them, and re-layouts  46.4 us (24%)
  other arithmetic  46.4 us (24%)
  matrix products  46 us (24%)
  waiting for transfers between devices  5.13 us (3%)
    ppermute x10, starting transfers between devices, send(): moved = lax.ppermute(value.astype(jnp.bfloat16), 'ctx', pairs)  40.1 us
    convert_element_type x1, other arithmetic, group_terms(): jax.nn.silu(total).astype(jnp.bfloat16)  16.7 us
    convert_element_type x2, local copies, waits for them, and re-layouts, body(): gate_heads = gate.reshape(2, length, heads, head_size).astype(jnp.float32)  15.7 us
    dot_general x2, matrix products, finish(): jnp.einsum('rtn,rhpn->rthp', reads.astype(jnp.float32), entering, precisi...  11.9 us
    dot_general x2, matrix products, group_terms(): jnp.einsum('rhts,rshp->rthp', mixing, scaled, preferred_element_type=jnp....  11.3 us
    convert_element_type x2, local copies, waits for them, and re-layouts, group_terms(): values32 = values.astype(jnp.float32)  10.7 us
    dot_general x2, matrix products, group_terms(): jnp.einsum('rshp,rsn->rhpn', weighted, keys_in, preferred_element_type=jn...  8.51 us
    ppermute x2, starting transfers between devices, shifted(): return lax.ppermute(value, 'ctx', pairs)  8.12 us
  transfers between devices with their start and end apart: 12, of which 1 were waited for; matrix products, arithmetic and copies ran while one was open for 34% of the time, Pallas kernels for 0%

profile of v5, /device:TPU:1, one launch (start us, length us, event | category | flops | bytes accessed | tf_op | source)
XLA Modules:
  0.0 193.1 jit_solution(15830254142927333685)
XLA Ops:
  0.0 3.4 %fusion.70 = (bf16[256,1,1024]{2,1,0:T(2,128)(2,1)S(1)}, bf16[256,1,1024]{2,1,0:T(2,128)(2,1)S(1)}) fusion(bf16[256,2,1024]{2,1,0:T(2,128)(2,1)} %param.11), kind=kLoop, calls=%fused_computation.170 | loop fusion | bytes 2097152 | tf_op jit(solution)/shard_map/slice | solution.py:129
  3.9 3.4 %convolution_convert_fusion = bf16[512,2176]{1,0:T(8,128)(2,1)S(1)} fusion(bf16[1024,2176]{1,0:T(8,128)(2,1)S(1)} %copy-done.32, bf16[256,1024]{1,0:T(8,128)(2,1)S(1)} %get-tuple-element.64, bf16[256,1024]{1,0:T(8,128)(2,1)S(1)} %get-tuple-element.65), kind=kOutput, calls=%fused_computation.16 | convolution fusion | flops 2284912640 | bytes 7733248 | tf_op jit(solution)/shard_map/dot_general | solution.py:131
  7.3 1.3 copy-done.9
  8.7 6.2 %collective-permute-start = (bf16[2,3,2176]{2,1,0:T(4,128)(2,1)S(1)}, bf16[2,3,2176]{2,1,0:T(4,128)(2,1)S(1)}, u32[]{:S(2)}, u32[]{:S(2)}) collective-permute-start(bf16[2,3,2176]{2,1,0:T(4,128)(2,1)S(1)} %get-tuple-element.23), channel_id=1, source_target_pairs={{0,1},{1,2},{2,3},{3,4},{4,5},{5,6},{6,7},{7,8},{8,9},{9,10},{10,1... | collective-permute-start | bytes 78344 | tf_op jit(solution)/shard_map/ppermute | solution.py:21
  14.9 1.9 collective-permute-start.6
  18.3 5.0 %reduce-window.16 = f32[2,32,2,128]{3,1,2,0:T(8,128)S(1)} reduce-window(f32[2,32,2,128]{3,1,2,0:T(8,128)S(1)} %bitcast.145, f32[]{:T(128)} %constant.50.clone.1), window={size=1x1x1x128 pad=0_0x0_0x0_0x0_127}, to_apply=%region_2.3 | reduce-window | flops 2080768 | bytes 131076 | tf_op jit(solution)/shard_map/reduce-window.2
  23.4 0.7 fusion.62
  24.3 1.2 reduce-window.14
  25.7 0.7 fusion.61
  26.8 0.7 bitcast_exponential_fusion.1
  27.7 16.7 %multiply_convert_fusion.5 = (bf16[2,256,2176]{2,1,0:T(8,128)(2,1)}, bf16[2,256,2176]{2,1,0:T(8,128)(2,1)S(1)}) fusion(bf16[2,256,2176]{2,1,0:T(8,128)(2,1)} %bitcast.144, bf16[2,3,2176]{2,1,0:T(4,128)(2,1)S(1)} %collective-permute-done, f32[2,2176]{1,0:T(2,128)S(1)} %get-tuple-element.68, f32[2,2176]{1,0:T(2,128)S(1)} %get-tuple-element.69, ...), kind=kLoop, calls=%fused_computation.20 | loop fusion | flops 56819712 | bytes 6910976 | tf_op jit(solution)/shard_map/convert_element_type | solution.py:72
  44.3 2.5 %slice_convert_fusion = f32[2,256,2048]{2,1,0:T(8,128)} fusion(bf16[2,256,2176]{2,1,0:T(8,128)(2,1)S(1)} %get-tuple-element.22), kind=kLoop, calls=%fused_computation.48 | loop fusion | flops 1048576 | bytes 6291456 | tf_op jit(solution)/shard_map/convert_element_type | solution.py:92
  46.8 5.4 %copy.122 = f32[2,256,2048]{1,2,0:T(8,128)} copy(f32[2,256,2048]{2,1,0:T(8,128)} %slice_convert_fusion) | data formatting | bytes 8388608 | tf_op jit(solution)/shard_map/convert_element_type | solution.py:92
  52.2 4.2 %fusion.24 = f32[2,32,64,64]{3,2,1,0:T(8,128)} fusion(f32[2,256,32,64]{1,3,2,0:T(8,128)} %bitcast.135, f32[2,256,32]{1,2,0:T(8,128)S(1)} %get-tuple-element.42, bf16[2,256,2176]{2,1,0:T(8,128)(2,1)S(1)} %get-tuple-element.22), kind=kOutput, calls=%fused_computation.46 | convolution fusion | flops 136314880 | bytes 5439488 | tf_op jit(solution)/shard_map/rshp,rsn->rhpn/dot_general | solution.py:98
  56.4 2.1 %reshape.204 = f32[2,32,4096]{2,1,0:T(8,128)S(1)} reshape(f32[2,32,64,64]{3,2,1,0:T(8,128)} %fusion.24) | data formatting | bytes 2097152 | tf_op jit(solution)/shard_map/reshape | solution.py:104
  58.6 1.0 fusion.38
  59.6 2.2 %collective-permute-start.7 = (bf16[2,32,4224]{2,1,0:T(8,128)(2,1)}, bf16[2,32,4224]{2,1,0:T(8,128)(2,1)}, u32[]{:S(2)}, u32[]{:S(2)}) collective-permute-start(bf16[2,32,4224]{2,1,0:T(8,128)(2,1)} %fusion.38), channel_id=1, source_target_pairs={{15,14},{13,12},{11,10},{9,8},{7,6},{5,4},{3,2},{1,0},{31,30},{29,... | collective-permute-start | bytes 1622024 | tf_op jit(solution)/shard_map/ppermute | solution.py:43
  61.8 4.1 %slice_convert_fusion.1 = f32[2,256,2048]{2,1,0:T(8,128)} fusion(bf16[2,256,2176]{2,1,0:T(8,128)(2,1)} %get-tuple-element.21), kind=kLoop, calls=%fused_computation.49 | loop fusion | flops 1048576 | bytes 6291456 | tf_op jit(solution)/shard_map/convert_element_type | solution.py:92
  65.9 5.4 %copy.114 = f32[2,256,2048]{1,2,0:T(8,128)} copy(f32[2,256,2048]{2,1,0:T(8,128)} %slice_convert_fusion.1) | data formatting | bytes 8388608 | tf_op jit(solution)/shard_map/convert_element_type | solution.py:92
  71.2 4.3 %fusion.23 = f32[2,32,64,64]{3,2,1,0:T(8,128)} fusion(f32[2,256,32,64]{1,3,2,0:T(8,128)} %bitcast.138, f32[2,256,32]{1,2,0:T(8,128)} %get-tuple-element.40, bf16[2,256,2176]{2,1,0:T(8,128)(2,1)} %get-tuple-element.21), kind=kOutput, calls=%fused_computation.45 | convolution fusion | flops 136314880 | bytes 5439488 | tf_op jit(solution)/shard_map/rshp,rsn->rhpn/dot_general | solution.py:98
  75.5 2.1 %reshape.200 = f32[2,32,4096]{2,1,0:T(8,128)S(1)} reshape(f32[2,32,64,64]{3,2,1,0:T(8,128)} %fusion.23) | data formatting | bytes 2097152 | tf_op jit(solution)/shard_map/reshape | solution.py:104
  77.7 1.6 fusion.65
  79.3 0.7 collective-permute-start.8
  80.1 1.6 collective-permute-start.1
  83.1 4.3 %fusion.18 = f32[512,2048]{1,0:T(8,128)} fusion(bf16[1024,2048]{1,0:T(8,128)(2,1)S(1)} %copy-done.33, bf16[256,1024]{1,0:T(8,128)(2,1)S(1)} %copy-done.13, bf16[256,1024]{1,0:T(8,128)(2,1)S(1)} %copy-done.15), kind=kOutput, calls=%fused_computation.38 | convolution fusion | flops 2151677952 | bytes 9437184 | tf_op jit(solution)/shard_map/dot_general | solution.py:130
  88.3 5.9 %collective-permute-start.2 = (bf16[2,32,4224]{2,1,0:T(8,128)(2,1)S(1)}, bf16[2,32,4224]{2,1,0:T(8,128)(2,1)S(1)}, u32[]{:S(2)}, u32[]{:S(2)}) collective-permute-start(bf16[2,32,4224]{2,1,0:T(8,128)(2,1)S(1)} %get-tuple-element.15), channel_id=1, source_target_pairs={{1,3},{3,1},{5,7},{7,5},{9,11},{11,9},{13,15},{15,13},{17,19},{19,... | collective-permute-start | bytes 1622024 | tf_op jit(solution)/shard_map/ppermute | solution.py:43
  95.8 5.1 %collective-permute-done.2 = bf16[2,32,4224]{2,1,0:T(8,128)(2,1)S(1)} collective-permute-done((bf16[2,32,4224]{2,1,0:T(8,128)(2,1)S(1)}, bf16[2,32,4224]{2,1,0:T(8,128)(2,1)S(1)}, u32[]{:S(2)}, u32[]{:S(2)}) %collective-permute-start.2) | collective-permute-done | bytes 540704 | tf_op jit(solution)/shard_map/ppermute | solution.py:43
  101.0 2.2 %fusion.63 = (bf16[2,32,4224]{2,1,0:T(8,128)(2,1)}, f32[2,32,4224]{2,1,0:T(8,128)}, bf16[2,32,4224]{2,1,0:T(8,128)(2,1)}, f32[2,32,4224]{2,1,0:T(8,128)}) fusion(bf16[2,32,4224]{2,1,0:T(8,128)(2,1)S(1)} %collective-permute-done.8, f32[2,32]{1,0:T(2,128)S(1)} %slice_reduce_fusion.5, bf16[2,32,4224]{2,1,0:T(8,128)(2,1)S(1)} %collective-permute-done.9, ...), kind=kLoop, calls=%fused_computation.163 | loop fusion | flops 5406720 | bytes 6493314 | tf_op jit(solution)/shard_map/convert_element_type | solution.py:43
  103.2 4.5 %collective-permute-start.3 = (bf16[2,32,4224]{2,1,0:T(8,128)(2,1)}, bf16[2,32,4224]{2,1,0:T(8,128)(2,1)S(1)}, u32[]{:S(2)}, u32[]{:S(2)}) collective-permute-start(bf16[2,32,4224]{2,1,0:T(8,128)(2,1)} %get-tuple-element.51), channel_id=1, source_target_pairs={{1,5},{3,7},{5,9},{7,11},{9,13},{11,15},{17,21},{19,23},{21,25},{2... | collective-permute-start | bytes 1622024 | tf_op jit(solution)/shard_map/ppermute | solution.py:43
  107.8 7.9 %reshape.218 = f32[2,256,32,64]{3,2,1,0:T(8,128)} reshape(f32[512,2048]{1,0:T(8,128)} %fusion.18) | data formatting | bytes 8388608 | tf_op jit(solution)/shard_map/convert_element_type | solution.py:161
  115.6 7.8 %copy.132 = f32[2,256,32,64]{1,3,2,0:T(8,128)} copy(f32[2,256,32,64]{3,2,1,0:T(8,128)} %reshape.218) | data formatting | bytes 8388608 | tf_op jit(solution)/shard_map/convert_element_type | solution.py:161
  123.5 2.4 %pad_maximum_fusion.4 = bf16[512,1024]{1,0:T(8,128)(2,1)} fusion(bf16[256,1024]{1,0:T(8,128)(2,1)} %copy-done.12, bf16[256,1024]{1,0:T(8,128)(2,1)} %copy-done.14), kind=kLoop, calls=%fused_computation.78 | loop fusion | flops 2097152 | bytes 2097152 | tf_op jit(solution)/shard_map/concatenate | solution.py:129
  126.2 0.8 slice_reduce_fusion.8
  127.1 1.5 add_convert_fusion.1
  128.5 5.2 %collective-permute-start.4 = (bf16[2,32,4224]{2,1,0:T(8,128)(2,1)S(1)}, bf16[2,32,4224]{2,1,0:T(8,128)(2,1)S(1)}, u32[]{:S(2)}, u32[]{:S(2)}) collective-permute-start(bf16[2,32,4224]{2,1,0:T(8,128)(2,1)S(1)} %add_convert_fusion.1), channel_id=1, source_target_pairs={{1,9},{3,11},{5,13},{7,15},{17,25},{19,27},{21,29},{23,31},{33,41}... | collective-permute-start | bytes 1622024 | tf_op jit(solution)/shard_map/ppermute | solution.py:43
  133.8 5.6 %fusion.1 = f32[2,32,64,256]{3,2,1,0:T(8,128)} fusion(f32[2,32,256]{2,1,0:T(8,128)S(1)} %copy-done.25, f32[2,256,256]{2,1,0:T(8,128)S(1)} %fusion.46, pred[256,256]{1,0:T(8,128)(4,1)S(1)} %copy-done.26, f32[2,256,32,64]{1,3,2,0:T(8,128)S(1)} %bitcast.136, f32[2,256,32]{1,2,0:T(8,128)S(1)} %copy-done.22), kind=kOutput, calls=%fused_computation.3 | convolution fusion | flops 555745280 | bytes 9109504 | tf_op jit(solution)/shard_map/rhts,rshp->rthp/dot_general | solution.py:94
  139.4 1.2 fusion.51
  140.7 1.6 collective-permute-start.11
  142.9 17.2 %collective-permute-start.5 = (bf16[2,32,4224]{2,1,0:T(8,128)(2,1)S(1)}, bf16[2,32,4224]{2,1,0:T(8,128)(2,1)S(1)}, u32[]{:S(2)}, u32[]{:S(2)}) collective-permute-start(bf16[2,32,4224]{2,1,0:T(8,128)(2,1)S(1)} %get-tuple-element.11), channel_id=1, source_target_pairs={{1,0},{3,2},{5,4},{7,6},{9,8},{11,10},{13,12},{15,14},{17,16},{19,... | collective-permute-start | bytes 1622024 | tf_op jit(solution)/shard_map/ppermute | solution.py:43
  160.2 5.7 %fusion = f32[2,32,64,256]{3,2,1,0:T(8,128)} fusion(f32[2,32,256]{2,1,0:T(8,128)S(1)} %copy-done.24, f32[2,256,256]{2,1,0:T(8,128)S(1)} %fusion.51, pred[256,256]{1,0:T(8,128)(4,1)S(1)} %copy-done.27, f32[2,256,32,64]{1,3,2,0:T(8,128)S(1)} %bitcast.140, f32[2,256,32]{1,2,0:T(8,128)S(1)} %copy-done.20), kind=kOutput, calls=%fused_computation.2 | convolution fusion | flops 555745280 | bytes 9109504 | tf_op jit(solution)/shard_map/rhts,rshp->rthp/dot_general | solution.py:94
  165.8 1.2 convert_element_type.197
  167.3 1.5 fusion.35
  168.8 3.2 %reshape.205 = f32[2,32,64,64]{3,2,1,0:T(8,128)} reshape(f32[2,32,4096]{2,1,0:T(8,128)} %get-tuple-element.54) | data formatting | bytes 2097152 | tf_op jit(solution)/shard_map/reshape | solution.py:114
  172.0 2.2 %reshape.201 = f32[2,32,64,64]{3,2,1,0:T(8,128)} reshape(f32[2,32,4096]{2,1,0:T(8,128)S(1)} %get-tuple-element.55) | data formatting | bytes 2097152 | tf_op jit(solution)/shard_map/reshape | solution.py:114
  174.3 3.8 %fusion.43 = f32[2,256,32,64]{1,3,2,0:T(8,128)S(1)} fusion(f32[2,32,64,64]{3,2,1,0:T(8,128)} %reshape.201, bf16[2,256,2176]{2,1,0:T(8,128)(2,1)} %get-tuple-element.21), kind=kOutput, calls=%fused_computation.93 | convolution fusion | flops 805306368 | bytes 6422528 | tf_op jit(solution)/shard_map/rtn,rhpn->rthp/dot_general | solution.py:115
  178.0 8.1 %multiply_reduce_fusion = (f32[2,256]{1,0:T(2,128)S(1)}, f32[2,256,32,64]{1,3,2,0:T(8,128)S(1)}) fusion(f32[2,256,32,64]{1,3,2,0:T(8,128)} %copy.132, f32[2,256,32]{1,2,0:T(8,128)S(1)} %get-tuple-element.41, f32[2,32,64,64]{3,2,1,0:T(8,128)S(1)} %copy-done.6, bf16[2,256,2176]{2,1,0:T(8,128)(2,1)S(1)} %get-tuple-element.22, ...), kind=kOutput, calls=%fused_computation.28 | convolution fusion | flops 822083072 | bytes 31723520 | tf_op jit(solution)/shard_map/rtn,rhpn->rthp/dot_general | solution.py:115
  186.2 4.7 %fusion.26 = bf16[2,256,1024]{2,1,0:T(8,128)(2,1)S(1)} fusion(bf16[2,256,1024]{2,1,0:T(8,128)(2,1)S(1)} %bitcast.142, bf16[32,64,1024,1]{2,1,0,3:T(8,128)(2,1)} %bitcast.141, f32[2,256,32,64]{1,3,2,0:T(8,128)S(1)} %get-tuple-element.63, f32[32,64]{1,0:T(8,128)S(1)} %mul.438, f32[2,256]{1,0:T(2,128)S(1)} %add_rsqrt_fusion), kind=kOutput, calls=%fused_computation.51 | convolution fusion | flops 2152202240 | bytes 10496000 | tf_op jit(solution)/shard_map/rthp,hpd->rtd/dot_general | solution.py:167
  191.1 2.0 %copy.133 = bf16[256,2,1024]{2,1,0:T(2,128)(2,1)} copy(bf16[256,2,1024]{2,0,1:T(8,128)(2,1)S(1)} %pad_maximum_fusion.5) | data formatting | bytes 2097152 | tf_op jit(solution)/shard_map/stack | solution.py:176
  (142 shorter events, 8.3 us)
Async XLA Ops:
  0.0 17.6 %copy-start = (bf16[1024,32]{0,1:T(8,128)(2,1)S(1)}, bf16[1024,32]{0,1:T(8,128)(2,1)}, u32[]{:S(2)}) copy-start(bf16[1024,32]{0,1:T(8,128)(2,1)} %param.14) | copy-start | bytes 196612
  0.0 3.8 %copy-start.32 = (bf16[1024,2176]{1,0:T(8,128)(2,1)S(1)}, bf16[1024,2176]{1,0:T(8,128)(2,1)}, u32[]{:S(2)}) copy-start(bf16[1024,2176]{1,0:T(8,128)(2,1)} %param.13) | copy-start | bytes 13369348
  3.8 13.8 %copy-start.12 = (bf16[256,1024]{1,0:T(8,128)(2,1)}, bf16[256,1024]{1,0:T(8,128)(2,1)S(1)}, u32[]{:S(2)}) copy-start(bf16[256,1024]{1,0:T(8,128)(2,1)S(1)} %get-tuple-element.64) | copy-start | bytes 1572868
  3.8 13.8 %copy-start.14 = (bf16[256,1024]{1,0:T(8,128)(2,1)}, bf16[256,1024]{1,0:T(8,128)(2,1)S(1)}, u32[]{:S(2)}) copy-start(bf16[256,1024]{1,0:T(8,128)(2,1)S(1)} %get-tuple-element.65) | copy-start | bytes 1572868
  3.8 13.0 %copy-start.30 = (f32[2,32]{1,0:T(2,128)S(1)}, f32[2,32]{1,0:T(2,128)}, u32[]{:S(2)}) copy-start(f32[2,32]{1,0:T(2,128)} %param.16) | copy-start | bytes 772
  3.8 13.0 %copy-start.18 = (f32[2,4,2176]{2,1,0:T(4,128)S(1)}, f32[2,4,2176]{2,1,0:T(4,128)}, u32[]{:S(2)}) copy-start(f32[2,4,2176]{2,1,0:T(4,128)} %param.17) | copy-start | bytes 208900
  7.3 1.4 copy-start.9
  7.3 10.7 %copy-start.31 = (f32[2,32]{1,0:T(2,128)S(1)}, f32[2,32]{1,0:T(2,128)}, u32[]{:S(2)}) copy-start(f32[2,32]{1,0:T(2,128)} %param.15) | copy-start | bytes 772
  7.3 16.9 %copy-start.23 = (f32[2,2176]{1,0:T(2,128)S(1)}, f32[2,2176]{1,0:T(2,128)}, u32[]{:S(2)}) copy-start(f32[2,2176]{1,0:T(2,128)} %param.18) | copy-start | bytes 52228
  8.7 18.9 %collective-permute-start = (bf16[2,3,2176]{2,1,0:T(4,128)(2,1)S(1)}, bf16[2,3,2176]{2,1,0:T(4,128)(2,1)S(1)}, u32[]{:S(2)}, u32[]{:S(2)}) collective-permute-start(bf16[2,3,2176]{2,1,0:T(4,128)(2,1)S(1)} %get-tuple-element.23), channel_id=1, source_target_pairs={{0,1},{1,2},{2,3},{3,4},{4,5},{5,6},{6,7},{7,8},{8,9},{9,10},{10,1... | collective-permute-start | bytes 78344 | tf_op jit(solution)/shard_map/ppermute | solution.py:21
  14.9 12.7 %collective-permute-start.6 = (bf16[2,3,2176]{2,1,0:T(4,128)(2,1)S(1)}, bf16[2,3,2176]{2,1,0:T(4,128)(2,1)S(1)}, u32[]{:S(2)}, u32[]{:S(2)}) collective-permute-start(bf16[2,3,2176]{2,1,0:T(4,128)(2,1)S(1)} %get-tuple-element.24), channel_id=1, source_target_pairs={{1,0},{2,1},{3,2},{4,3},{5,4},{6,5},{7,6},{8,7},{9,8},{10,9},{11,1... | collective-permute-start | bytes 78344 | tf_op jit(solution)/shard_map/ppermute | solution.py:21
  18.2 26.1 %copy-start.19 = (f32[2,256,32]{1,2,0:T(8,128)}, f32[2,256,32]{1,2,0:T(8,128)S(1)}, u32[]{:S(2)}) copy-start(f32[2,256,32]{1,2,0:T(8,128)S(1)} %get-tuple-element.18) | copy-start | bytes 196612
  18.2 26.1 %copy-start.21 = (f32[2,256,32]{1,2,0:T(8,128)}, f32[2,256,32]{1,2,0:T(8,128)S(1)}, u32[]{:S(2)}) copy-start(f32[2,256,32]{1,2,0:T(8,128)S(1)} %get-tuple-element.48) | copy-start | bytes 196612
  27.6 114.9 %copy-start.17 = (pred[4224]{0:T(1024)(128)(4,1)}, pred[4224]{0:T(1024)(128)(4,1)S(1)}, u32[]{:S(2)}) copy-start(pred[4224]{0:T(1024)(128)(4,1)S(1)} %iota_compare_fusion.2) | copy-start | bytes 12676
  58.5 7.3 %copy-start.5 = (f32[2,32,4096]{2,1,0:T(8,128)}, f32[2,32,4096]{2,1,0:T(8,128)S(1)}, u32[]{:S(2)}) copy-start(f32[2,32,4096]{2,1,0:T(8,128)S(1)} %reshape.204) | copy-start | bytes 3145732
  59.6 18.0 %collective-permute-start.7 = (bf16[2,32,4224]{2,1,0:T(8,128)(2,1)}, bf16[2,32,4224]{2,1,0:T(8,128)(2,1)}, u32[]{:S(2)}, u32[]{:S(2)}) collective-permute-start(bf16[2,32,4224]{2,1,0:T(8,128)(2,1)} %fusion.38), channel_id=1, source_target_pairs={{15,14},{13,12},{11,10},{9,8},{7,6},{5,4},{3,2},{1,0},{31,30},{29,... | collective-permute-start | bytes 1622024 | tf_op jit(solution)/shard_map/ppermute | solution.py:43
  79.3 2.5 %collective-permute-start.8 = (bf16[2,32,4224]{2,1,0:T(8,128)(2,1)S(1)}, bf16[2,32,4224]{2,1,0:T(8,128)(2,1)S(1)}, u32[]{:S(2)}, u32[]{:S(2)}) collective-permute-start(bf16[2,32,4224]{2,1,0:T(8,128)(2,1)S(1)} %get-tuple-element.9), channel_id=1, source_target_pairs={{14,12},{12,14},{10,8},{8,10},{6,4},{4,6},{2,0},{0,2},{30,28},{28,... | collective-permute-start | bytes 1622024 | tf_op jit(solution)/shard_map/ppermute | solution.py:43
  80.0 3.0 %copy-start.33 = (bf16[1024,2048]{1,0:T(8,128)(2,1)S(1)}, bf16[1024,2048]{1,0:T(8,128)(2,1)}, u32[]{:S(2)}) copy-start(bf16[1024,2048]{1,0:T(8,128)(2,1)} %param.12) | copy-start | bytes 12582916
  80.1 7.4 %collective-permute-start.1 = (bf16[2,32,4224]{2,1,0:T(8,128)(2,1)S(1)}, bf16[2,32,4224]{2,1,0:T(8,128)(2,1)S(1)}, u32[]{:S(2)}, u32[]{:S(2)}) collective-permute-start(bf16[2,32,4224]{2,1,0:T(8,128)(2,1)S(1)} %fusion.39), channel_id=1, source_target_pairs={{0,1},{2,3},{4,5},{6,7},{8,9},{10,11},{12,13},{14,15},{16,17},{18,... | collective-permute-start | bytes 1622024 | tf_op jit(solution)/shard_map/ppermute | solution.py:43
  81.7 1.3 copy-start.13
  81.7 1.3 copy-start.15
  82.3 5.1 %collective-permute-start.9 = (bf16[2,32,4224]{2,1,0:T(8,128)(2,1)S(1)}, bf16[2,32,4224]{2,1,0:T(8,128)(2,1)S(1)}, u32[]{:S(2)}, u32[]{:S(2)}) collective-permute-start(bf16[2,32,4224]{2,1,0:T(8,128)(2,1)S(1)} %get-tuple-element.7), channel_id=1, source_target_pairs={{14,10},{12,8},{10,6},{8,4},{6,2},{4,0},{30,26},{28,24},{26,22},{2... | collective-permute-start | bytes 1622024 | tf_op jit(solution)/shard_map/ppermute | solution.py:43
  87.5 8.0 %copy-start.28 = (f32[2,32]{1,0:T(2,128)S(1)}, f32[2,32]{1,0:T(2,128)}, u32[]{:S(2)}) copy-start(f32[2,32]{1,0:T(2,128)} %param.19) | copy-start | bytes 772
  87.5 0.8 copy-start.10
  88.3 12.6 %collective-permute-start.2 = (bf16[2,32,4224]{2,1,0:T(8,128)(2,1)S(1)}, bf16[2,32,4224]{2,1,0:T(8,128)(2,1)S(1)}, u32[]{:S(2)}, u32[]{:S(2)}) collective-permute-start(bf16[2,32,4224]{2,1,0:T(8,128)(2,1)S(1)} %get-tuple-element.15), channel_id=1, source_target_pairs={{1,3},{3,1},{5,7},{7,5},{9,11},{11,9},{13,15},{15,13},{17,19},{19,... | collective-permute-start | bytes 1622024 | tf_op jit(solution)/shard_map/ppermute | solution.py:43
  94.8 6.2 %collective-permute-start.10 = (bf16[2,32,4224]{2,1,0:T(8,128)(2,1)S(1)}, bf16[2,32,4224]{2,1,0:T(8,128)(2,1)S(1)}, u32[]{:S(2)}, u32[]{:S(2)}) collective-permute-start(bf16[2,32,4224]{2,1,0:T(8,128)(2,1)S(1)} %get-tuple-element.53), channel_id=1, source_target_pairs={{14,6},{12,4},{10,2},{8,0},{30,22},{28,20},{26,18},{24,16},{46,38}... | collective-permute-start | bytes 1622024 | tf_op jit(solution)/shard_map/ppermute | solution.py:43
  103.2 23.8 %collective-permute-start.3 = (bf16[2,32,4224]{2,1,0:T(8,128)(2,1)}, bf16[2,32,4224]{2,1,0:T(8,128)(2,1)S(1)}, u32[]{:S(2)}, u32[]{:S(2)}) collective-permute-start(bf16[2,32,4224]{2,1,0:T(8,128)(2,1)} %get-tuple-element.51), channel_id=1, source_target_pairs={{1,5},{3,7},{5,9},{7,11},{9,13},{11,15},{17,21},{19,23},{21,25},{2... | collective-permute-start | bytes 1622024 | tf_op jit(solution)/shard_map/ppermute | solution.py:43
  115.6 7.8 %copy-start.29 = (f32[2048]{0:T(1024)S(1)}, f32[2048]{0:T(1024)}, u32[]{:S(2)}) copy-start(f32[2048]{0:T(1024)} %param.20) | copy-start | bytes 24580
  123.5 10.2 %copy-start.2 = (f32[2,256,2048]{1,2,0:T(8,128)S(1)}, f32[2,256,2048]{1,2,0:T(8,128)}, u32[]{:S(2)}) copy-start(f32[2,256,2048]{1,2,0:T(8,128)} %copy.122) | copy-start | bytes 12582916
  123.5 10.2 %copy-start.22 = (f32[2,256,32]{1,2,0:T(8,128)S(1)}, f32[2,256,32]{1,2,0:T(8,128)}, u32[]{:S(2)}) copy-start(f32[2,256,32]{1,2,0:T(8,128)} %copy-done.21) | copy-start | bytes 196612
  123.5 10.2 %copy-start.25 = (f32[2,32,256]{2,1,0:T(8,128)S(1)}, f32[2,32,256]{2,1,0:T(8,128)}, u32[]{:S(2)}) copy-start(f32[2,32,256]{2,1,0:T(8,128)} %get-tuple-element.44) | copy-start | bytes 196612
  123.5 10.2 %copy-start.26 = (pred[256,256]{1,0:T(8,128)(4,1)S(1)}, pred[256,256]{1,0:T(8,128)(4,1)}, u32[]{:S(2)}) copy-start(pred[256,256]{1,0:T(8,128)(4,1)} %iota_compare_fusion) | copy-start | bytes 196612
  128.5 13.9 %collective-permute-start.4 = (bf16[2,32,4224]{2,1,0:T(8,128)(2,1)S(1)}, bf16[2,32,4224]{2,1,0:T(8,128)(2,1)S(1)}, u32[]{:S(2)}, u32[]{:S(2)}) collective-permute-start(bf16[2,32,4224]{2,1,0:T(8,128)(2,1)S(1)} %add_convert_fusion.1), channel_id=1, source_target_pairs={{1,9},{3,11},{5,13},{7,15},{17,25},{19,27},{21,29},{23,31},{33,41}... | collective-permute-start | bytes 1622024 | tf_op jit(solution)/shard_map/ppermute | solution.py:43
  133.8 6.9 %copy-start.16 = (bf16[2,32,4224]{2,1,0:T(8,128)(2,1)S(1)}, bf16[2,32,4224]{2,1,0:T(8,128)(2,1)}, u32[]{:S(2)}) copy-start(bf16[2,32,4224]{2,1,0:T(8,128)(2,1)} %get-tuple-element.5) | copy-start | bytes 1622020
  140.7 19.4 %copy-start.4 = (f32[2,256,2048]{1,2,0:T(8,128)S(1)}, f32[2,256,2048]{1,2,0:T(8,128)}, u32[]{:S(2)}) copy-start(f32[2,256,2048]{1,2,0:T(8,128)} %copy.114) | copy-start | bytes 12582916
  140.7 19.4 %copy-start.20 = (f32[2,256,32]{1,2,0:T(8,128)S(1)}, f32[2,256,32]{1,2,0:T(8,128)}, u32[]{:S(2)}) copy-start(f32[2,256,32]{1,2,0:T(8,128)} %copy-done.19) | copy-start | bytes 196612
  140.7 19.4 %copy-start.24 = (f32[2,32,256]{2,1,0:T(8,128)S(1)}, f32[2,32,256]{2,1,0:T(8,128)}, u32[]{:S(2)}) copy-start(f32[2,32,256]{2,1,0:T(8,128)} %get-tuple-element.46) | copy-start | bytes 196612
  140.7 19.4 %copy-start.27 = (pred[256,256]{1,0:T(8,128)(4,1)S(1)}, pred[256,256]{1,0:T(8,128)(4,1)}, u32[]{:S(2)}) copy-start(pred[256,256]{1,0:T(8,128)(4,1)} %iota_compare_fusion.1) | copy-start | bytes 196612
  140.7 26.6 %collective-permute-start.11 = (bf16[2,32,4224]{2,1,0:T(8,128)(2,1)S(1)}, bf16[2,32,4224]{2,1,0:T(8,128)(2,1)S(1)}, u32[]{:S(2)}, u32[]{:S(2)}) collective-permute-start(bf16[2,32,4224]{2,1,0:T(8,128)(2,1)S(1)} %copy-done.16), channel_id=1, source_target_pairs={{14,15},{12,13},{10,11},{8,9},{6,7},{4,5},{2,3},{0,1},{30,31},{28,... | collective-permute-start | bytes 1622024 | tf_op jit(solution)/shard_map/ppermute | solution.py:43
  142.9 24.4 %collective-permute-start.5 = (bf16[2,32,4224]{2,1,0:T(8,128)(2,1)S(1)}, bf16[2,32,4224]{2,1,0:T(8,128)(2,1)S(1)}, u32[]{:S(2)}, u32[]{:S(2)}) collective-permute-start(bf16[2,32,4224]{2,1,0:T(8,128)(2,1)S(1)} %get-tuple-element.11), channel_id=1, source_target_pairs={{1,0},{3,2},{5,4},{7,6},{9,8},{11,10},{13,12},{15,14},{17,16},{19,... | collective-permute-start | bytes 1622024 | tf_op jit(solution)/shard_map/ppermute | solution.py:43
  160.1 6.9 %copy-start.11 = (bf16[2,32,4224]{2,1,0:T(8,128)(2,1)S(1)}, bf16[2,32,4224]{2,1,0:T(8,128)(2,1)}, u32[]{:S(2)}) copy-start(bf16[2,32,4224]{2,1,0:T(8,128)(2,1)} %copy-done.10) | copy-start | bytes 1622020
  165.8 1.5 copy-start.7
  165.8 1.5 slice-start
  174.2 3.8 %copy-start.3 = (f32[2,256,2048]{1,2,0:T(8,128)S(1)}, f32[2,256,2048]{1,2,0:T(8,128)}, u32[]{:S(2)}) copy-start(f32[2,256,2048]{1,2,0:T(8,128)} %copy.122) | copy-start | bytes 12582916
  174.3 3.8 %copy-start.6 = (f32[2,32,64,64]{3,2,1,0:T(8,128)S(1)}, f32[2,32,64,64]{3,2,1,0:T(8,128)}, u32[]{:S(2)}) copy-start(f32[2,32,64,64]{3,2,1,0:T(8,128)} %reshape.205) | copy-start | bytes 3145732
  178.0 8.1 %copy-start.8 = (bf16[512,1024]{1,0:T(8,128)(2,1)S(1)}, bf16[512,1024]{1,0:T(8,128)(2,1)}, u32[]{:S(2)}) copy-start(bf16[512,1024]{1,0:T(8,128)(2,1)} %pad_maximum_fusion.4) | copy-start | bytes 3145732
  190.9 2.2 %copy-start.1 = (bf16[1024,32]{0,1:T(8,128)(2,1)S(1)}, bf16[1024,32]{0,1:T(8,128)(2,1)}, u32[]{:S(2)}) copy-start(bf16[1024,32]{0,1:T(8,128)(2,1)} %param.14) | copy-start | bytes 196612

commit v6 on v4

--- a/solution.py
+++ b/solution.py
@@ -76,13 +76,18 @@
     reads = conv[:, :, inner + NS :]
     step = jax.nn.softplus(dt_raw.astype(jnp.float32) + dt_shift[:, None, :])
     rate = -jnp.exp(log_rate)
-    cum = lax.cumsum(step * rate[:, None, :], axis=1, reverse=falling)
-    by_head = jnp.transpose(cum, (0, 2, 1))
     rows = jnp.arange(length)
     if falling:
         keep = rows[:, None] <= rows[None, :]
     else:
         keep = rows[:, None] >= rows[None, :]
+    cum = jnp.einsum(
+        "ts,rsh->rth",
+        keep.astype(jnp.float32),
+        step * rate[:, None, :],
+        precision=lax.Precision.HIGHEST,
+    )
+    by_head = jnp.transpose(cum, (0, 2, 1))
     decay = jnp.exp(
         jnp.where(keep[None, None], by_head[:, :, :, None] - by_head[:, :, None, :], -1e30)
     )

time: 183 us -> 175 us (0.956)
  other arithmetic: 43.8 us -> 36 us
    another operation x6 -> x0, other arithmetic: 7.69 us -> none
    unnamed x86 -> x84, local copies, waits for them, and re-layouts: 6.83 us -> 6.79 us
  transfers between devices with their start and end apart: 12 -> 12, of which waited for: 1 -> 1; matrix products, arithmetic and copies ran while one was open for 35% -> 32% of each run, Pallas kernels for 0% -> 0%
where the time goes in v6:
time: 175 us; the launch traced here: 174 us
  local copies, waits for them, and re-layouts  47 us (27%)
  starting transfers between devices  46.1 us (26%)
  matrix products  39.1 us (22%)
  other arithmetic  36 us (21%)
  waiting for transfers between devices  5.15 us (3%)
    ppermute x10, starting transfers between devices, send(): moved = lax.ppermute(value.astype(jnp.bfloat16), 'ctx', pairs)  38 us
    convert_element_type x1, other arithmetic, group_terms(): conv = jax.nn.silu(total).astype(jnp.bfloat16)  19.5 us
    convert_element_type x2, local copies, waits for them, and re-layouts, body(): gate_heads = gate.reshape(2, length, heads, head_size).astype(jnp.float32)  15.8 us
    dot_general x2, matrix products, group_terms(): jnp.einsum('rhts,rshp->rthp', mixing, scaled, preferred_element_type=jnp....  11.5 us
    dot_general x2, matrix products, finish(): jnp.einsum('rtn,rhpn->rthp', reads.astype(jnp.float32), entering, precisi...  10.9 us
    ppermute x2, starting transfers between devices, shifted(): return lax.ppermute(value, 'ctx', pairs)  8.11 us
    convert_element_type x8, other arithmetic, send(): moved = lax.ppermute(value.astype(jnp.bfloat16), 'ctx', pairs)  7.47 us
    unnamed x84, local copies, waits for them, and re-layouts  6.79 us
  transfers between devices with their start and end apart: 12, of which 1 were waited for; matrix products, arithmetic and copies ran while one was open for 32% of the time, Pallas kernels for 0%

profile of v6, /device:TPU:1, one launch (start us, length us, event | category | flops | bytes accessed | tf_op | source)
XLA Modules:
  0.0 174.3 jit_solution(10042827766057429209)
XLA Ops:
  0.0 3.4 %fusion.86 = (bf16[256,1,1024]{2,1,0:T(2,128)(2,1)S(1)}, bf16[256,1,1024]{2,1,0:T(2,128)(2,1)S(1)}) fusion(bf16[256,2,1024]{2,1,0:T(2,128)(2,1)} %param.11), kind=kLoop, calls=%fused_computation.174 | loop fusion | bytes 2097152 | tf_op jit(solution)/shard_map/slice | solution.py:133
  3.8 3.4 %convolution_convert_fusion = bf16[512,2176]{1,0:T(8,128)(2,1)S(1)} fusion(bf16[1024,2176]{1,0:T(8,128)(2,1)S(1)} %copy-done.37, bf16[256,1024]{1,0:T(8,128)(2,1)S(1)} %get-tuple-element.56, bf16[256,1024]{1,0:T(8,128)(2,1)S(1)} %get-tuple-element.57), kind=kOutput, calls=%fused_computation.22 | convolution fusion | flops 2284912640 | bytes 7733248 | tf_op jit(solution)/shard_map/dot_general | solution.py:135
  7.4 3.3 %collective-permute-start.6 = (bf16[2,3,2176]{2,0,1:T(2,128)(2,1)S(1)}, bf16[2,3,2176]{2,0,1:T(2,128)(2,1)}, u32[]{:S(2)}, u32[]{:S(2)}) collective-permute-start(bf16[2,3,2176]{2,0,1:T(2,128)(2,1)S(1)} %copy.90), channel_id=1, source_target_pairs={{1,0},{2,1},{3,2},{4,3},{5,4},{6,5},{7,6},{8,7},{9,8},{10,9},{11,1... | collective-permute-start | bytes 78344 | tf_op jit(solution)/shard_map/ppermute | solution.py:20
  11.3 4.8 %collective-permute-start = (bf16[2,3,2176]{2,0,1:T(2,128)(2,1)}, bf16[2,3,2176]{2,0,1:T(2,128)(2,1)}, u32[]{:S(2)}, u32[]{:S(2)}) collective-permute-start(bf16[2,3,2176]{2,0,1:T(2,128)(2,1)} %copy.89), channel_id=1, source_target_pairs={{0,1},{1,2},{2,3},{3,4},{4,5},{5,6},{6,7},{7,8},{8,9},{9,10},{10,1... | collective-permute-start | bytes 78344 | tf_op jit(solution)/shard_map/ppermute | solution.py:20
  16.3 0.7 iota_compare_fusion
  17.9 0.7 bitcast_exponential_fusion
  22.9 2.4 %copy.61 = bf16[2,256,2176]{1,2,0:T(8,128)(2,1)} copy(bf16[2,256,2176]{2,1,0:T(8,128)(2,1)S(1)} %bitcast.102) | data formatting | bytes 4456448 | tf_op jit(solution)/shard_map/reshape | solution.py:136
  25.3 1.4 copy.66
  26.7 2.2 %copy.60 = bf16[2,3,2176]{1,2,0:T(8,128)(2,1)} copy(bf16[2,3,2176]{2,0,1:T(2,128)(2,1)} %collective-permute-done) | data formatting | bytes 52224 | tf_op jit(solution)/shard_map/ppermute | solution.py:20
  28.9 19.5 %multiply_convert_fusion.4 = (bf16[2,256,2176]{1,2,0:T(8,128)(2,1)S(1)}, bf16[2,256,2176]{1,2,0:T(8,128)(2,1)S(1)}) fusion(bf16[2,256,2176]{1,2,0:T(8,128)(2,1)} %copy.61, bf16[2,3,2176]{1,2,0:T(8,128)(2,1)S(1)} %copy.66, f32[2,2176]{1,0:T(2,128)} %get-tuple-element.58, f32[2,2176]{1,0:T(2,128)} %get-tuple-element.59, f32[2,2176]{1,0:T(2,128)} %get-tuple-element.60, ...), kind=kLoop, calls=%fused_computation.25 | loop fusion | flops 56819712 | bytes 6910976 | tf_op jit(solution)/shard_map/convert_element_type | solution.py:71
  48.6 1.2 copy-done.3
  50.4 2.1 %fusion.30 = f32[2,32,64,64]{3,2,1,0:T(8,128)} fusion(bf16[2,256,32,64]{1,3,2,0:T(8,128)(2,1)S(1)} %bitcast.93, f32[2,256,32]{1,2,0:T(8,128)S(1)} %copy-done.25, bf16[2,256,2176]{1,2,0:T(8,128)(2,1)S(1)} %get-tuple-element.17), kind=kOutput, calls=%fused_computation.56 | convolution fusion | flops 137363456 | bytes 3276800 | tf_op jit(solution)/shard_map/rshp,rsn->rhpn/dot_general | solution.py:102
  52.4 2.1 %reshape.142 = f32[2,32,4096]{2,1,0:T(8,128)S(1)} reshape(f32[2,32,64,64]{3,2,1,0:T(8,128)} %fusion.30) | data formatting | bytes 2097152 | tf_op jit(solution)/shard_map/reshape | solution.py:108
  54.7 1.0 fusion.48
  55.6 2.1 %collective-permute-start.7 = (bf16[2,32,4224]{2,1,0:T(8,128)(2,1)}, bf16[2,32,4224]{2,1,0:T(8,128)(2,1)}, u32[]{:S(2)}, u32[]{:S(2)}) collective-permute-start(bf16[2,32,4224]{2,1,0:T(8,128)(2,1)} %fusion.48), channel_id=1, source_target_pairs={{15,14},{13,12},{11,10},{9,8},{7,6},{5,4},{3,2},{1,0},{31,30},{29,... | collective-permute-start | bytes 1622024 | tf_op jit(solution)/shard_map/ppermute | solution.py:42
  58.5 1.3 copy-done.7
  59.9 2.1 %fusion.33 = f32[2,32,64,64]{3,2,1,0:T(8,128)} fusion(bf16[2,256,32,64]{1,3,2,0:T(8,128)(2,1)S(1)} %bitcast.96, f32[2,256,32]{1,2,0:T(8,128)S(1)} %get-tuple-element.36, bf16[2,256,2176]{1,2,0:T(8,128)(2,1)S(1)} %get-tuple-element.18), kind=kOutput, calls=%fused_computation.57 | convolution fusion | flops 137363456 | bytes 3276800 | tf_op jit(solution)/shard_map/rshp,rsn->rhpn/dot_general | solution.py:102
  61.9 2.1 %reshape.140 = f32[2,32,4096]{2,1,0:T(8,128)S(1)} reshape(f32[2,32,64,64]{3,2,1,0:T(8,128)} %fusion.33) | data formatting | bytes 2097152 | tf_op jit(solution)/shard_map/reshape | solution.py:108
  64.1 1.6 fusion.81
  65.7 0.7 collective-permute-start.8
  66.5 1.6 collective-permute-start.1
  68.7 0.9 collective-permute-start.9
  69.7 4.4 %fusion.24 = f32[512,2048]{1,0:T(8,128)} fusion(bf16[1024,2048]{1,0:T(8,128)(2,1)S(1)} %copy-done.38, bf16[256,1024]{1,0:T(8,128)(2,1)S(1)} %copy-done.17, bf16[256,1024]{1,0:T(8,128)(2,1)S(1)} %copy-done.19), kind=kOutput, calls=%fused_computation.48 | convolution fusion | flops 2151677952 | bytes 9437184 | tf_op jit(solution)/shard_map/dot_general | solution.py:134
  75.0 5.5 %collective-permute-start.2 = (bf16[2,32,4224]{2,1,0:T(8,128)(2,1)S(1)}, bf16[2,32,4224]{2,1,0:T(8,128)(2,1)S(1)}, u32[]{:S(2)}, u32[]{:S(2)}) collective-permute-start(bf16[2,32,4224]{2,1,0:T(8,128)(2,1)S(1)} %get-tuple-element.15), channel_id=1, source_target_pairs={{1,3},{3,1},{5,7},{7,5},{9,11},{11,9},{13,15},{15,13},{17,19},{19,... | collective-permute-start | bytes 1622024 | tf_op jit(solution)/shard_map/ppermute | solution.py:42
  80.4 0.6 iota_compare_fusion.1
  81.1 0.7 collective-permute-start.10
  82.1 5.1 %collective-permute-done.2 = bf16[2,32,4224]{2,1,0:T(8,128)(2,1)S(1)} collective-permute-done((bf16[2,32,4224]{2,1,0:T(8,128)(2,1)S(1)}, bf16[2,32,4224]{2,1,0:T(8,128)(2,1)S(1)}, u32[]{:S(2)}, u32[]{:S(2)}) %collective-permute-start.2) | collective-permute-done | bytes 540704 | tf_op jit(solution)/shard_map/ppermute | solution.py:42
  87.3 2.1 %fusion.79 = (bf16[2,32,4224]{2,1,0:T(8,128)(2,1)}, f32[2,32,4224]{2,1,0:T(8,128)}, bf16[2,32,4224]{2,1,0:T(8,128)(2,1)}, f32[2,32,4224]{2,1,0:T(8,128)}) fusion(bf16[2,32,4224]{2,1,0:T(8,128)(2,1)S(1)} %collective-permute-done.8, f32[2,32]{1,0:T(2,128)S(1)} %slice_reduce_fusion.3, bf16[2,32,4224]{2,1,0:T(8,128)(2,1)S(1)} %collective-permute-done.9, ...), kind=kLoop, calls=%fused_computation.167 | loop fusion | flops 5406720 | bytes 6493314 | tf_op jit(solution)/shard_map/convert_element_type | solution.py:42
  89.4 3.6 %collective-permute-start.3 = (bf16[2,32,4224]{2,1,0:T(8,128)(2,1)}, bf16[2,32,4224]{2,1,0:T(8,128)(2,1)S(1)}, u32[]{:S(2)}, u32[]{:S(2)}) collective-permute-start(bf16[2,32,4224]{2,1,0:T(8,128)(2,1)} %get-tuple-element.43), channel_id=1, source_target_pairs={{1,5},{3,7},{5,9},{7,11},{9,13},{11,15},{17,21},{19,23},{21,25},{2... | collective-permute-start | bytes 1622024 | tf_op jit(solution)/shard_map/ppermute | solution.py:42
  93.1 7.9 %reshape.158 = f32[2,256,32,64]{3,2,1,0:T(8,128)} reshape(f32[512,2048]{1,0:T(8,128)} %fusion.24) | data formatting | bytes 8388608 | tf_op jit(solution)/shard_map/convert_element_type | solution.py:165
  101.0 7.9 %copy.70 = f32[2,256,32,64]{1,3,2,0:T(8,128)} copy(f32[2,256,32,64]{3,2,1,0:T(8,128)} %reshape.158) | data formatting | bytes 8388608 | tf_op jit(solution)/shard_map/convert_element_type | solution.py:165
  108.9 2.4 %pad_maximum_fusion.4 = bf16[512,1024]{1,0:T(8,128)(2,1)} fusion(bf16[256,1024]{1,0:T(8,128)(2,1)} %copy-done.16, bf16[256,1024]{1,0:T(8,128)(2,1)} %copy-done.18), kind=kLoop, calls=%fused_computation.86 | loop fusion | flops 2097152 | bytes 2097152 | tf_op jit(solution)/shard_map/concatenate | solution.py:133
  111.3 1.1 fusion.62
  112.4 0.8 slice_reduce_fusion.6
  113.3 1.5 add_convert_fusion.1
  114.8 5.0 %collective-permute-start.4 = (bf16[2,32,4224]{2,1,0:T(8,128)(2,1)S(1)}, bf16[2,32,4224]{2,1,0:T(8,128)(2,1)S(1)}, u32[]{:S(2)}, u32[]{:S(2)}) collective-permute-start(bf16[2,32,4224]{2,1,0:T(8,128)(2,1)S(1)} %add_convert_fusion.1), channel_id=1, source_target_pairs={{1,9},{3,11},{5,13},{7,15},{17,25},{19,27},{21,29},{23,31},{33,41}... | collective-permute-start | bytes 1622024 | tf_op jit(solution)/shard_map/ppermute | solution.py:42
  119.8 5.7 %fusion.1 = f32[2,32,64,256]{3,2,1,0:T(8,128)} fusion(f32[2,32,256]{2,1,0:T(8,128)S(1)} %copy-done.22, f32[2,256,256]{2,1,0:T(8,128)S(1)} %fusion.62, pred[256,256]{1,0:T(8,128)(4,1)S(1)} %copy-done.27, bf16[2,256,32,64]{1,3,2,0:T(8,128)(2,1)S(1)} %bitcast.94, f32[2,256,32]{1,2,0:T(8,128)S(1)} %get-tuple-element.40), kind=kOutput, calls=%fused_computation.3 | convolution fusion | flops 556793856 | bytes 7012352 | tf_op jit(solution)/shard_map/rhts,rshp->rthp/dot_general | solution.py:98
  125.8 1.4 collective-permute-start.11
  127.9 16.7 %collective-permute-start.5 = (bf16[2,32,4224]{2,1,0:T(8,128)(2,1)S(1)}, bf16[2,32,4224]{2,1,0:T(8,128)(2,1)S(1)}, u32[]{:S(2)}, u32[]{:S(2)}) collective-permute-start(bf16[2,32,4224]{2,1,0:T(8,128)(2,1)S(1)} %get-tuple-element.11), channel_id=1, source_target_pairs={{1,0},{3,2},{5,4},{7,6},{9,8},{11,10},{13,12},{15,14},{17,16},{19,... | collective-permute-start | bytes 1622024 | tf_op jit(solution)/shard_map/ppermute | solution.py:42
  144.6 5.8 %fusion = f32[2,32,64,256]{3,2,1,0:T(8,128)} fusion(f32[2,32,256]{2,1,0:T(8,128)S(1)} %fusion.52, f32[2,256,256]{2,1,0:T(8,128)S(1)} %fusion.67, pred[256,256]{1,0:T(8,128)(4,1)S(1)} %copy-done.28, bf16[2,256,32,64]{1,3,2,0:T(8,128)(2,1)S(1)} %bitcast.97, f32[2,256,32]{1,2,0:T(8,128)S(1)} %get-tuple-element.39), kind=kOutput, calls=%fused_computation.2 | convolution fusion | flops 556793856 | bytes 7012352 | tf_op jit(solution)/shard_map/rhts,rshp->rthp/dot_general | solution.py:98
  150.3 1.2 convert_element_type.199
  151.8 1.4 fusion.45
  153.3 3.1 %reshape.143 = f32[2,32,64,64]{3,2,1,0:T(8,128)} reshape(f32[2,32,4096]{2,1,0:T(8,128)} %get-tuple-element.46) | data formatting | bytes 2097152 | tf_op jit(solution)/shard_map/reshape | solution.py:118
  156.4 2.2 %reshape.141 = f32[2,32,64,64]{3,2,1,0:T(8,128)} reshape(f32[2,32,4096]{2,1,0:T(8,128)S(1)} %get-tuple-element.47) | data formatting | bytes 2097152 | tf_op jit(solution)/shard_map/reshape | solution.py:118
  158.6 3.5 %fusion.57 = f32[2,256,32,64]{1,3,2,0:T(8,128)S(1)} fusion(f32[2,32,64,64]{3,2,1,0:T(8,128)} %reshape.141, bf16[2,256,2176]{1,2,0:T(8,128)(2,1)S(1)} %get-tuple-element.18), kind=kOutput, calls=%fused_computation.113 | convolution fusion | flops 805306368 | bytes 5308416 | tf_op jit(solution)/shard_map/rtn,rhpn->rthp/dot_general | solution.py:119
  162.2 7.3 %multiply_reduce_fusion = (f32[2,256]{1,0:T(2,128)S(1)}, f32[2,256,32,64]{1,3,2,0:T(8,128)S(1)}) fusion(f32[2,256,32,64]{1,3,2,0:T(8,128)} %copy.70, f32[2,256,32]{1,2,0:T(8,128)S(1)} %copy-done.29, f32[2,32,64,64]{3,2,1,0:T(8,128)S(1)} %copy-done.15, bf16[2,256,2176]{1,2,0:T(8,128)(2,1)} %copy-done.3, bf16[2,256,32,64]{1,3,2,0:T(8,128)(2,1)S(1)} %bitcast.95, ...), kind=kOutput, calls=%fused_computation.38 | convolution fusion | flops 824180224 | bytes 26413568 | tf_op jit(solution)/shard_map/rtn,rhpn->rthp/dot_general | solution.py:119
  169.6 2.4 %fusion.36 = bf16[2,256,1024]{2,1,0:T(8,128)(2,1)S(1)} fusion(bf16[2,256,1024]{2,1,0:T(8,128)(2,1)S(1)} %bitcast.100, bf16[32,64,1024,1]{2,1,0,3:T(8,128)(2,1)S(1)} %bitcast.99, f32[2,256,32,64]{1,3,2,0:T(8,128)S(1)} %get-tuple-element.55, f32[32,64]{1,0:T(8,128)S(1)} %mul.438, f32[2,256]{1,0:T(2,128)S(1)} %add_rsqrt_fusion), kind=kOutput, calls=%fused_computation.59 | convolution fusion | flops 2152202240 | bytes 10496000 | tf_op jit(solution)/shard_map/rthp,hpd->rtd/dot_general | solution.py:171
  172.2 2.0 %copy.71 = bf16[256,2,1024]{2,1,0:T(2,128)(2,1)} copy(bf16[256,2,1024]{2,0,1:T(8,128)(2,1)S(1)} %pad_maximum_fusion.5) | data formatting | bytes 2097152 | tf_op jit(solution)/shard_map/stack | solution.py:180
  (146 shorter events, 11.5 us)
Async XLA Ops:
  0.0 16.9 %copy-start = (bf16[1024,32]{0,1:T(8,128)(2,1)S(1)}, bf16[1024,32]{0,1:T(8,128)(2,1)}, u32[]{:S(2)}) copy-start(bf16[1024,32]{0,1:T(8,128)(2,1)} %param.14) | copy-start | bytes 196612
  0.0 3.8 %copy-start.37 = (bf16[1024,2176]{1,0:T(8,128)(2,1)S(1)}, bf16[1024,2176]{1,0:T(8,128)(2,1)}, u32[]{:S(2)}) copy-start(bf16[1024,2176]{1,0:T(8,128)(2,1)} %param.13) | copy-start | bytes 13369348
  3.8 13.1 %copy-start.16 = (bf16[256,1024]{1,0:T(8,128)(2,1)}, bf16[256,1024]{1,0:T(8,128)(2,1)S(1)}, u32[]{:S(2)}) copy-start(bf16[256,1024]{1,0:T(8,128)(2,1)S(1)} %get-tuple-element.56) | copy-start | bytes 1572868
  3.8 13.1 %copy-start.18 = (bf16[256,1024]{1,0:T(8,128)(2,1)}, bf16[256,1024]{1,0:T(8,128)(2,1)S(1)}, u32[]{:S(2)}) copy-start(bf16[256,1024]{1,0:T(8,128)(2,1)S(1)} %get-tuple-element.57) | copy-start | bytes 1572868
  3.8 12.3 %copy-start.24 = (f32[2,4,2176]{2,1,0:T(4,128)S(1)}, f32[2,4,2176]{2,1,0:T(4,128)}, u32[]{:S(2)}) copy-start(f32[2,4,2176]{2,1,0:T(4,128)} %param.17) | copy-start | bytes 208900
  3.8 12.4 %copy-start.34 = (f32[2,32]{1,0:T(2,128)S(1)}, f32[2,32]{1,0:T(2,128)}, u32[]{:S(2)}) copy-start(f32[2,32]{1,0:T(2,128)} %param.16) | copy-start | bytes 772
  7.3 10.1 %copy-start.33 = (f32[2,32]{1,0:T(2,128)S(1)}, f32[2,32]{1,0:T(2,128)}, u32[]{:S(2)}) copy-start(f32[2,32]{1,0:T(2,128)} %param.15) | copy-start | bytes 772
  7.3 11.4 %copy-start.26 = (f32[2,2176]{1,0:T(2,128)S(1)}, f32[2,2176]{1,0:T(2,128)}, u32[]{:S(2)}) copy-start(f32[2,2176]{1,0:T(2,128)} %param.18) | copy-start | bytes 52228
  7.4 18.0 %collective-permute-start.6 = (bf16[2,3,2176]{2,0,1:T(2,128)(2,1)S(1)}, bf16[2,3,2176]{2,0,1:T(2,128)(2,1)}, u32[]{:S(2)}, u32[]{:S(2)}) collective-permute-start(bf16[2,3,2176]{2,0,1:T(2,128)(2,1)S(1)} %copy.90), channel_id=1, source_target_pairs={{1,0},{2,1},{3,2},{4,3},{5,4},{6,5},{7,6},{8,7},{9,8},{10,9},{11,1... | collective-permute-start | bytes 78344 | tf_op jit(solution)/shard_map/ppermute | solution.py:20
  11.3 15.4 %collective-permute-start = (bf16[2,3,2176]{2,0,1:T(2,128)(2,1)}, bf16[2,3,2176]{2,0,1:T(2,128)(2,1)}, u32[]{:S(2)}, u32[]{:S(2)}) collective-permute-start(bf16[2,3,2176]{2,0,1:T(2,128)(2,1)} %copy.89), channel_id=1, source_target_pairs={{0,1},{1,2},{2,3},{3,4},{4,5},{5,6},{6,7},{7,8},{8,9},{9,10},{10,1... | collective-permute-start | bytes 78344 | tf_op jit(solution)/shard_map/ppermute | solution.py:20
  17.8 7.5 %copy-start.21 = (f32[2,32,256]{2,1,0:T(8,128)}, f32[2,32,256]{2,1,0:T(8,128)S(1)}, u32[]{:S(2)}) copy-start(f32[2,32,256]{2,1,0:T(8,128)S(1)} %fusion.50) | copy-start | bytes 196612
  22.3 105.1 %copy-start.23 = (pred[4224]{0:T(1024)(128)(4,1)}, pred[4224]{0:T(1024)(128)(4,1)S(1)}, u32[]{:S(2)}) copy-start(pred[4224]{0:T(1024)(128)(4,1)S(1)} %iota_compare_fusion.4) | copy-start | bytes 12676
  48.4 2.0 %copy-start.25 = (f32[2,256,32]{1,2,0:T(8,128)S(1)}, f32[2,256,32]{1,2,0:T(8,128)}, u32[]{:S(2)}) copy-start(f32[2,256,32]{1,2,0:T(8,128)} %get-tuple-element.38) | copy-start | bytes 196612
  48.6 1.8 %copy-start.4 = (bf16[2,256,2048]{1,2,0:T(8,128)(2,1)}, bf16[2,256,2048]{1,2,0:T(8,128)(2,1)S(1)}, u32[]{:S(2)}) copy-start(bf16[2,256,2048]{1,2,0:T(8,128)(2,1)S(1)} %slice.233) | copy-start | bytes 6291460
  52.4 2.1 %copy-start.31 = (f32[2,32]{1,0:T(2,128)S(1)}, f32[2,32]{1,0:T(2,128)}, u32[]{:S(2)}) copy-start(f32[2,32]{1,0:T(2,128)} %exp.80) | copy-start | bytes 772
  54.6 3.9 %copy-start.2 = (f32[2,32,4096]{2,1,0:T(8,128)}, f32[2,32,4096]{2,1,0:T(8,128)S(1)}, u32[]{:S(2)}) copy-start(f32[2,32,4096]{2,1,0:T(8,128)S(1)} %reshape.142) | copy-start | bytes 3145732
  55.6 8.4 %collective-permute-start.7 = (bf16[2,32,4224]{2,1,0:T(8,128)(2,1)}, bf16[2,32,4224]{2,1,0:T(8,128)(2,1)}, u32[]{:S(2)}, u32[]{:S(2)}) collective-permute-start(bf16[2,32,4224]{2,1,0:T(8,128)(2,1)} %fusion.48), channel_id=1, source_target_pairs={{15,14},{13,12},{11,10},{9,8},{7,6},{5,4},{3,2},{1,0},{31,30},{29,... | collective-permute-start | bytes 1622024 | tf_op jit(solution)/shard_map/ppermute | solution.py:42
  65.7 2.5 %collective-permute-start.8 = (bf16[2,32,4224]{2,1,0:T(8,128)(2,1)S(1)}, bf16[2,32,4224]{2,1,0:T(8,128)(2,1)S(1)}, u32[]{:S(2)}, u32[]{:S(2)}) collective-permute-start(bf16[2,32,4224]{2,1,0:T(8,128)(2,1)S(1)} %get-tuple-element.9), channel_id=1, source_target_pairs={{14,12},{12,14},{10,8},{8,10},{6,4},{4,6},{2,0},{0,2},{30,28},{28,... | collective-permute-start | bytes 1622024 | tf_op jit(solution)/shard_map/ppermute | solution.py:42
  66.4 3.2 %copy-start.38 = (bf16[1024,2048]{1,0:T(8,128)(2,1)S(1)}, bf16[1024,2048]{1,0:T(8,128)(2,1)}, u32[]{:S(2)}) copy-start(bf16[1024,2048]{1,0:T(8,128)(2,1)} %param.12) | copy-start | bytes 12582916
  66.5 7.6 %collective-permute-start.1 = (bf16[2,32,4224]{2,1,0:T(8,128)(2,1)S(1)}, bf16[2,32,4224]{2,1,0:T(8,128)(2,1)S(1)}, u32[]{:S(2)}, u32[]{:S(2)}) collective-permute-start(bf16[2,32,4224]{2,1,0:T(8,128)(2,1)S(1)} %fusion.49), channel_id=1, source_target_pairs={{0,1},{2,3},{4,5},{6,7},{8,9},{10,11},{12,13},{14,15},{16,17},{18,... | collective-permute-start | bytes 1622024 | tf_op jit(solution)/shard_map/ppermute | solution.py:42
  68.2 1.5 copy-start.19
  68.7 5.4 %collective-permute-start.9 = (bf16[2,32,4224]{2,1,0:T(8,128)(2,1)S(1)}, bf16[2,32,4224]{2,1,0:T(8,128)(2,1)S(1)}, u32[]{:S(2)}, u32[]{:S(2)}) collective-permute-start(bf16[2,32,4224]{2,1,0:T(8,128)(2,1)S(1)} %get-tuple-element.7), channel_id=1, source_target_pairs={{14,10},{12,8},{10,6},{8,4},{6,2},{4,0},{30,26},{28,24},{26,22},{2... | collective-permute-start | bytes 1622024 | tf_op jit(solution)/shard_map/ppermute | solution.py:42
  74.1 7.6 %copy-start.35 = (f32[2,32]{1,0:T(2,128)S(1)}, f32[2,32]{1,0:T(2,128)}, u32[]{:S(2)}) copy-start(f32[2,32]{1,0:T(2,128)} %param.19) | copy-start | bytes 772
  75.0 12.2 %collective-permute-start.2 = (bf16[2,32,4224]{2,1,0:T(8,128)(2,1)S(1)}, bf16[2,32,4224]{2,1,0:T(8,128)(2,1)S(1)}, u32[]{:S(2)}, u32[]{:S(2)}) collective-permute-start(bf16[2,32,4224]{2,1,0:T(8,128)(2,1)S(1)} %get-tuple-element.15), channel_id=1, source_target_pairs={{1,3},{3,1},{5,7},{7,5},{9,11},{11,9},{13,15},{15,13},{17,19},{19,... | collective-permute-start | bytes 1622024 | tf_op jit(solution)/shard_map/ppermute | solution.py:42
  81.1 6.2 %collective-permute-start.10 = (bf16[2,32,4224]{2,1,0:T(8,128)(2,1)S(1)}, bf16[2,32,4224]{2,1,0:T(8,128)(2,1)S(1)}, u32[]{:S(2)}, u32[]{:S(2)}) collective-permute-start(bf16[2,32,4224]{2,1,0:T(8,128)(2,1)S(1)} %get-tuple-element.45), channel_id=1, source_target_pairs={{14,6},{12,4},{10,2},{8,0},{30,22},{28,20},{26,18},{24,16},{46,38}... | collective-permute-start | bytes 1622024 | tf_op jit(solution)/shard_map/ppermute | solution.py:42
  89.4 23.8 %collective-permute-start.3 = (bf16[2,32,4224]{2,1,0:T(8,128)(2,1)}, bf16[2,32,4224]{2,1,0:T(8,128)(2,1)S(1)}, u32[]{:S(2)}, u32[]{:S(2)}) collective-permute-start(bf16[2,32,4224]{2,1,0:T(8,128)(2,1)} %get-tuple-element.43), channel_id=1, source_target_pairs={{1,5},{3,7},{5,9},{7,11},{9,13},{11,15},{17,21},{19,23},{21,25},{2... | collective-permute-start | bytes 1622024 | tf_op jit(solution)/shard_map/ppermute | solution.py:42
  101.0 7.9 %copy-start.32 = (f32[2048]{0:T(1024)S(1)}, f32[2048]{0:T(1024)}, u32[]{:S(2)}) copy-start(f32[2048]{0:T(1024)} %param.20) | copy-start | bytes 24580
  108.9 10.9 %copy-start.5 = (bf16[2,256,2048]{1,2,0:T(8,128)(2,1)S(1)}, bf16[2,256,2048]{1,2,0:T(8,128)(2,1)}, u32[]{:S(2)}) copy-start(bf16[2,256,2048]{1,2,0:T(8,128)(2,1)} %copy-done.4) | copy-start | bytes 6291460
  108.9 10.9 %copy-start.22 = (f32[2,32,256]{2,1,0:T(8,128)S(1)}, f32[2,32,256]{2,1,0:T(8,128)}, u32[]{:S(2)}) copy-start(f32[2,32,256]{2,1,0:T(8,128)} %copy-done.21) | copy-start | bytes 196612
  108.9 10.9 %copy-start.27 = (pred[256,256]{1,0:T(8,128)(4,1)S(1)}, pred[256,256]{1,0:T(8,128)(4,1)}, u32[]{:S(2)}) copy-start(pred[256,256]{1,0:T(8,128)(4,1)} %iota_compare_fusion) | copy-start | bytes 196612
  114.8 11.0 %copy-start.20 = (bf16[2,32,4224]{2,1,0:T(8,128)(2,1)S(1)}, bf16[2,32,4224]{2,1,0:T(8,128)(2,1)}, u32[]{:S(2)}) copy-start(bf16[2,32,4224]{2,1,0:T(8,128)(2,1)} %get-tuple-element.5) | copy-start | bytes 1622020
  114.8 12.7 %collective-permute-start.4 = (bf16[2,32,4224]{2,1,0:T(8,128)(2,1)S(1)}, bf16[2,32,4224]{2,1,0:T(8,128)(2,1)S(1)}, u32[]{:S(2)}, u32[]{:S(2)}) collective-permute-start(bf16[2,32,4224]{2,1,0:T(8,128)(2,1)S(1)} %add_convert_fusion.1), channel_id=1, source_target_pairs={{1,9},{3,11},{5,13},{7,15},{17,25},{19,27},{21,29},{23,31},{33,41}... | collective-permute-start | bytes 1622024 | tf_op jit(solution)/shard_map/ppermute | solution.py:42
  125.8 18.7 %copy-start.8 = (bf16[2,256,2048]{1,2,0:T(8,128)(2,1)S(1)}, bf16[2,256,2048]{1,2,0:T(8,128)(2,1)}, u32[]{:S(2)}) copy-start(bf16[2,256,2048]{1,2,0:T(8,128)(2,1)} %copy-done.7) | copy-start | bytes 6291460
  125.8 18.7 %copy-start.28 = (pred[256,256]{1,0:T(8,128)(4,1)S(1)}, pred[256,256]{1,0:T(8,128)(4,1)}, u32[]{:S(2)}) copy-start(pred[256,256]{1,0:T(8,128)(4,1)} %iota_compare_fusion.1) | copy-start | bytes 196612
  125.8 26.0 %collective-permute-start.11 = (bf16[2,32,4224]{2,1,0:T(8,128)(2,1)S(1)}, bf16[2,32,4224]{2,1,0:T(8,128)(2,1)S(1)}, u32[]{:S(2)}, u32[]{:S(2)}) collective-permute-start(bf16[2,32,4224]{2,1,0:T(8,128)(2,1)S(1)} %copy-done.20), channel_id=1, source_target_pairs={{14,15},{12,13},{10,11},{8,9},{6,7},{4,5},{2,3},{0,1},{30,31},{28,... | collective-permute-start | bytes 1622024 | tf_op jit(solution)/shard_map/ppermute | solution.py:42
  127.9 23.7 %copy-start.14 = (bf16[2,32,4224]{2,1,0:T(8,128)(2,1)S(1)}, bf16[2,32,4224]{2,1,0:T(8,128)(2,1)}, u32[]{:S(2)}) copy-start(bf16[2,32,4224]{2,1,0:T(8,128)(2,1)} %copy-done.13) | copy-start | bytes 1622020
  127.9 23.9 %collective-permute-start.5 = (bf16[2,32,4224]{2,1,0:T(8,128)(2,1)S(1)}, bf16[2,32,4224]{2,1,0:T(8,128)(2,1)S(1)}, u32[]{:S(2)}, u32[]{:S(2)}) collective-permute-start(bf16[2,32,4224]{2,1,0:T(8,128)(2,1)S(1)} %get-tuple-element.11), channel_id=1, source_target_pairs={{1,0},{3,2},{5,4},{7,6},{9,8},{11,10},{13,12},{15,14},{17,16},{19,... | collective-permute-start | bytes 1622024 | tf_op jit(solution)/shard_map/ppermute | solution.py:42
  150.3 1.5 copy-start.11
  150.3 1.5 slice-start
  156.4 5.7 %copy-start.30 = (f32[2,256,32]{1,2,0:T(8,128)S(1)}, f32[2,256,32]{1,2,0:T(8,128)}, u32[]{:S(2)}) copy-start(f32[2,256,32]{1,2,0:T(8,128)} %get-tuple-element.35) | copy-start | bytes 196612
  158.6 3.6 %copy-start.6 = (bf16[2,256,2048]{1,2,0:T(8,128)(2,1)S(1)}, bf16[2,256,2048]{1,2,0:T(8,128)(2,1)}, u32[]{:S(2)}) copy-start(bf16[2,256,2048]{1,2,0:T(8,128)(2,1)} %copy-done.4) | copy-start | bytes 6291460
  158.6 3.6 %copy-start.9 = (bf16[2,256,2048]{1,2,0:T(8,128)(2,1)S(1)}, bf16[2,256,2048]{1,2,0:T(8,128)(2,1)}, u32[]{:S(2)}) copy-start(bf16[2,256,2048]{1,2,0:T(8,128)(2,1)} %copy-done.7) | copy-start | bytes 6291460
  158.6 3.6 %copy-start.15 = (f32[2,32,64,64]{3,2,1,0:T(8,128)S(1)}, f32[2,32,64,64]{3,2,1,0:T(8,128)}, u32[]{:S(2)}) copy-start(f32[2,32,64,64]{3,2,1,0:T(8,128)} %reshape.143) | copy-start | bytes 3145732
  158.6 3.6 %copy-start.29 = (f32[2,256,32]{1,2,0:T(8,128)S(1)}, f32[2,256,32]{1,2,0:T(8,128)}, u32[]{:S(2)}) copy-start(f32[2,256,32]{1,2,0:T(8,128)} %get-tuple-element.37) | copy-start | bytes 196612
  158.6 3.6 %copy-start.36 = (f32[2,32]{1,0:T(2,128)S(1)}, f32[2,32]{1,0:T(2,128)}, u32[]{:S(2)}) copy-start(f32[2,32]{1,0:T(2,128)} %param.19) | copy-start | bytes 772
  162.2 7.4 %copy-start.10 = (bf16[2048,1024]{1,0:T(8,128)(2,1)S(1)}, bf16[2048,1024]{1,0:T(8,128)(2,1)}, u32[]{:S(2)}) copy-start(bf16[2048,1024]{1,0:T(8,128)(2,1)} %param.21) | copy-start | bytes 12582916
  162.2 7.4 %copy-start.12 = (bf16[512,1024]{1,0:T(8,128)(2,1)S(1)}, bf16[512,1024]{1,0:T(8,128)(2,1)}, u32[]{:S(2)}) copy-start(bf16[512,1024]{1,0:T(8,128)(2,1)} %pad_maximum_fusion.4) | copy-start | bytes 3145732
  172.0 2.2 %copy-start.1 = (bf16[1024,32]{0,1:T(8,128)(2,1)S(1)}, bf16[1024,32]{0,1:T(8,128)(2,1)}, u32[]{:S(2)}) copy-start(bf16[1024,32]{0,1:T(8,128)(2,1)} %param.14) | copy-start | bytes 196612
  (4 other events, 5.0 us)

commit v7 on v6

--- a/solution.py
+++ b/solution.py
@@ -131,7 +131,9 @@
 ):
     length = stream.shape[0]
     rows = jnp.concatenate([stream[:, 0, :], stream[:, 1, :]], axis=0)
-    gate = jnp.dot(rows, w_gate, preferred_element_type=jnp.float32).astype(jnp.bfloat16)
+    gate = jnp.einsum(
+        "rtd,de->ret", rows.reshape(2, length, -1), w_gate, preferred_element_type=jnp.float32
+    ).astype(jnp.bfloat16)
     projected = jnp.dot(rows, w_xbc, preferred_element_type=jnp.float32).astype(jnp.bfloat16)
     projected = projected.reshape(2, length, projected.shape[1])
     dt_raw = jnp.dot(rows, w_dt, preferred_element_type=jnp.float32).astype(jnp.bfloat16)
@@ -162,7 +164,9 @@
     falling_in = exclusive_chain(falling[3], -1)
     combined = finish(*rising[:3], rising_in) + finish(*falling[:3], falling_in)
     heads, head_size = combined.shape[2], combined.shape[3]
-    gate_heads = gate.reshape(2, length, heads, head_size).astype(jnp.float32)
+    gate_heads = jnp.transpose(
+        gate.reshape(2, heads, head_size, length).astype(jnp.float32), (0, 3, 1, 2)
+    )
     gated = combined * jax.nn.silu(gate_heads)
     mean_square = jnp.mean(gated * gated, axis=(2, 3), keepdims=True)
     normed = (

time: 175 us -> 159 us (0.909)
  starting transfers between devices: 46.1 us -> 34.6 us
  local copies, waits for them, and re-layouts: 47 us -> 36.3 us
  waiting for transfers between devices: 5.15 us -> 9.67 us
    convert_element_type x2 -> x0, local copies, waits for them, and re-layouts: 15.8 us -> none  [body(): gate_heads = gate.reshape(2, length, heads, head_size).astype(jnp.float32)]
    ppermute x10, starting transfers between devices: 38 us -> 26.2 us  [send(): moved = lax.ppermute(value.astype(jnp.bfloat16), 'ctx', pairs)]
    transpose x0 -> x1, local copies, waits for them, and re-layouts: none -> 5.36 us  [body(): jnp.transpose(gate.reshape(2, heads, head_size, length).astype(jnp.float3...]
    ppermute x10, waiting for transfers between devices: 5.14 us -> 9.66 us  [send(): moved = lax.ppermute(value.astype(jnp.bfloat16), 'ctx', pairs)]
    convert_element_type x6, other arithmetic: 1.57 us -> 3.58 us  [send(): return moved.astype(jnp.float32)]
    convert_element_type x8, other arithmetic: 7.47 us -> 9.37 us  [send(): moved = lax.ppermute(value.astype(jnp.bfloat16), 'ctx', pairs)]
    unnamed x84 -> x68, local copies, waits for them, and re-layouts: 6.79 us -> 6.44 us
  transfers between devices with their start and end apart: 12 -> 12, of which waited for: 1 -> 2; matrix products, arithmetic and copies ran while one was open for 32% -> 30% of each run, Pallas kernels for 0% -> 0%
where the time goes in v7:
time: 159 us; the launch traced here: 158 us
  matrix products  39.1 us (25%)
  other arithmetic  37.4 us (24%)
  local copies, waits for them, and re-layouts  36.3 us (23%)
  starting transfers between devices  34.6 us (22%)
  waiting for transfers between devices  9.67 us (6%)
    ppermute x10, starting transfers between devices, send(): moved = lax.ppermute(value.astype(jnp.bfloat16), 'ctx', pairs)  26.2 us
    convert_element_type x1, other arithmetic, group_terms(): conv = jax.nn.silu(total).astype(jnp.bfloat16)  19.5 us
    dot_general x2, matrix products, group_terms(): jnp.einsum('rhts,rshp->rthp', mixing, scaled, preferred_element_type=jnp....  11.5 us
    dot_general x2, matrix products, finish(): jnp.einsum('rtn,rhpn->rthp', reads.astype(jnp.float32), entering, precisi...  10.9 us
    ppermute x10, waiting for transfers between devices, send(): moved = lax.ppermute(value.astype(jnp.bfloat16), 'ctx', pairs)  9.66 us
    convert_element_type x8, other arithmetic, send(): moved = lax.ppermute(value.astype(jnp.bfloat16), 'ctx', pairs)  9.37 us
    ppermute x2, starting transfers between devices, shifted(): return lax.ppermute(value, 'ctx', pairs)  8.37 us
    unnamed x68, local copies, waits for them, and re-layouts  6.44 us
  transfers between devices with their start and end apart: 12, of which 2 were waited for; matrix products, arithmetic and copies ran while one was open for 30% of the time, Pallas kernels for 0%

profile of v7, /device:TPU:1, one launch (start us, length us, event | category | flops | bytes accessed | tf_op | source)
XLA Modules:
  0.0 157.8 jit_solution(2147844978243863127)
XLA Ops:
  0.0 3.4 %fusion.92 = (bf16[256,1,1024]{2,1,0:T(2,128)(2,1)S(1)}, bf16[256,1,1024]{2,1,0:T(2,128)(2,1)S(1)}) fusion(bf16[256,2,1024]{2,1,0:T(2,128)(2,1)} %param.11), kind=kLoop, calls=%fused_computation.176 | loop fusion | bytes 2097152 | tf_op jit(solution)/shard_map/slice | solution.py:133
  3.8 3.4 %convolution_convert_fusion = bf16[512,2176]{1,0:T(8,128)(2,1)S(1)} fusion(bf16[1024,2176]{1,0:T(8,128)(2,1)S(1)} %copy-done.29, bf16[256,1024]{1,0:T(8,128)(2,1)S(1)} %get-tuple-element.56, bf16[256,1024]{1,0:T(8,128)(2,1)S(1)} %get-tuple-element.57), kind=kOutput, calls=%fused_computation.22 | convolution fusion | flops 2284912640 | bytes 7733248 | tf_op jit(solution)/shard_map/dot_general | solution.py:137
  7.3 3.4 %collective-permute-start.6 = (bf16[2,3,2176]{2,0,1:T(2,128)(2,1)S(1)}, bf16[2,3,2176]{2,0,1:T(2,128)(2,1)}, u32[]{:S(2)}, u32[]{:S(2)}) collective-permute-start(bf16[2,3,2176]{2,0,1:T(2,128)(2,1)S(1)} %copy.83), channel_id=1, source_target_pairs={{1,0},{2,1},{3,2},{4,3},{5,4},{6,5},{7,6},{8,7},{9,8},{10,9},{11,1... | collective-permute-start | bytes 78344 | tf_op jit(solution)/shard_map/ppermute | solution.py:20
  11.4 5.0 %collective-permute-start = (bf16[2,3,2176]{2,0,1:T(2,128)(2,1)}, bf16[2,3,2176]{2,0,1:T(2,128)(2,1)}, u32[]{:S(2)}, u32[]{:S(2)}) collective-permute-start(bf16[2,3,2176]{2,0,1:T(2,128)(2,1)} %copy.82), channel_id=1, source_target_pairs={{0,1},{1,2},{2,3},{3,4},{4,5},{5,6},{6,7},{7,8},{8,9},{9,10},{10,1... | collective-permute-start | bytes 78344 | tf_op jit(solution)/shard_map/ppermute | solution.py:20
  16.3 1.0 pad_maximum_fusion.4
  18.5 0.7 bitcast_exponential_fusion
  22.9 2.5 %copy.58 = bf16[2,256,2176]{1,2,0:T(8,128)(2,1)} copy(bf16[2,256,2176]{2,1,0:T(8,128)(2,1)S(1)} %bitcast.117) | data formatting | bytes 4456448 | tf_op jit(solution)/shard_map/reshape | solution.py:138
  25.9 1.4 copy.63
  27.3 2.2 %copy.57 = bf16[2,3,2176]{1,2,0:T(8,128)(2,1)} copy(bf16[2,3,2176]{2,0,1:T(2,128)(2,1)} %collective-permute-done) | data formatting | bytes 52224 | tf_op jit(solution)/shard_map/ppermute | solution.py:20
  29.5 19.5 %multiply_convert_fusion.4 = (bf16[2,256,2176]{1,2,0:T(8,128)(2,1)S(1)}, bf16[2,256,2176]{1,2,0:T(8,128)(2,1)S(1)}) fusion(bf16[2,256,2176]{1,2,0:T(8,128)(2,1)} %copy.58, bf16[2,3,2176]{1,2,0:T(8,128)(2,1)S(1)} %copy.63, f32[2,2176]{1,0:T(2,128)} %get-tuple-element.58, f32[2,2176]{1,0:T(2,128)} %get-tuple-element.59, f32[2,2176]{1,0:T(2,128)} %get-tuple-element.60, ...), kind=kLoop, calls=%fused_computation.25 | loop fusion | flops 56819712 | bytes 6910976 | tf_op jit(solution)/shard_map/convert_element_type | solution.py:71
  49.2 1.2 copy-done.3
  51.0 2.1 %fusion.36 = f32[2,32,64,64]{3,2,1,0:T(8,128)} fusion(bf16[2,256,32,64]{1,3,2,0:T(8,128)(2,1)S(1)} %bitcast.106, f32[2,256,32]{1,2,0:T(8,128)S(1)} %copy-done.20, bf16[2,256,2176]{1,2,0:T(8,128)(2,1)S(1)} %get-tuple-element.17), kind=kOutput, calls=%fused_computation.58 | convolution fusion | flops 137363456 | bytes 3276800 | tf_op jit(solution)/shard_map/rshp,rsn->rhpn/dot_general | solution.py:102
  53.1 2.1 %reshape.144 = f32[2,32,4096]{2,1,0:T(8,128)S(1)} reshape(f32[2,32,64,64]{3,2,1,0:T(8,128)} %fusion.36) | data formatting | bytes 2097152 | tf_op jit(solution)/shard_map/reshape | solution.py:108
  55.3 1.0 fusion.54
  56.3 2.1 %collective-permute-start.7 = (bf16[2,32,4224]{2,1,0:T(8,128)(2,1)}, bf16[2,32,4224]{2,1,0:T(8,128)(2,1)}, u32[]{:S(2)}, u32[]{:S(2)}) collective-permute-start(bf16[2,32,4224]{2,1,0:T(8,128)(2,1)} %fusion.54), channel_id=1, source_target_pairs={{15,14},{13,12},{11,10},{9,8},{7,6},{5,4},{3,2},{1,0},{31,30},{29,... | collective-permute-start | bytes 1622024 | tf_op jit(solution)/shard_map/ppermute | solution.py:42
  59.2 1.3 copy-done.7
  60.5 2.1 %fusion.39 = f32[2,32,64,64]{3,2,1,0:T(8,128)} fusion(bf16[2,256,32,64]{1,3,2,0:T(8,128)(2,1)S(1)} %bitcast.109, f32[2,256,32]{1,2,0:T(8,128)S(1)} %get-tuple-element.36, bf16[2,256,2176]{1,2,0:T(8,128)(2,1)S(1)} %get-tuple-element.18), kind=kOutput, calls=%fused_computation.59 | convolution fusion | flops 137363456 | bytes 3276800 | tf_op jit(solution)/shard_map/rshp,rsn->rhpn/dot_general | solution.py:102
  62.6 2.1 %reshape.142 = f32[2,32,4096]{2,1,0:T(8,128)S(1)} reshape(f32[2,32,64,64]{3,2,1,0:T(8,128)} %fusion.39) | data formatting | bytes 2097152 | tf_op jit(solution)/shard_map/reshape | solution.py:108
  64.7 1.6 %fusion.87 = (bf16[2,32,4224]{2,1,0:T(8,128)(2,1)S(1)}, f32[2,32,4224]{2,1,0:T(8,128)S(1)}) fusion(f32[2,32,128]{2,1,0:T(8,128)S(1)} %broadcast_in_dim.44, f32[2,32,4096]{2,1,0:T(8,128)} %copy-done.2, pred[4224]{0:T(1024)(128)(4,1)S(1)} %iota_compare_fusion.4, bf16[2,32,4224]{2,1,0:T(8,128)(2,1)} %collective-permute-done.7, f32[2,32]{1,0:T(2,128)S(1)} %exp.80), kind=kLoop, calls=%fused_computation.171 | loop fusion | flops 1622016 | bytes 3248512 | tf_op jit(solution)/shard_map/convert_element_type | solution.py:42
  67.1 0.9 fusion.55
  68.0 1.4 collective-permute-start.1
  69.7 1.6 fusion.86
  71.2 1.5 collective-permute-start.9
  72.7 4.4 %convert_bitcast_fusion = f32[2,2048,256]{1,2,0:T(8,128)} fusion(bf16[2,256,1024]{2,1,0:T(8,128)(2,1)S(1)} %bitcast.113, bf16[1024,2048]{1,0:T(8,128)(2,1)S(1)} %copy-done.30), kind=kOutput, calls=%fused_computation.39 | convolution fusion | flops 2149580800 | bytes 9437184 | tf_op jit(solution)/shard_map/rtd,de->ret/dot_general | solution.py:134
  77.1 5.4 %copy.65 = f32[2,2048,256]{2,1,0:T(8,128)} copy(f32[2,2048,256]{1,2,0:T(8,128)} %convert_bitcast_fusion) | data formatting | bytes 8388608 | tf_op jit(solution)/shard_map/transpose | solution.py:167
  82.5 0.8 slice_reduce_fusion
  83.4 1.9 %fusion.90 = (bf16[2,32,4224]{2,1,0:T(8,128)(2,1)S(1)}, f32[2,32,4224]{2,1,0:T(8,128)S(1)}, bf16[2,32,4224]{2,1,0:T(8,128)(2,1)S(1)}) fusion(f32[2,32,128]{2,1,0:T(8,128)S(1)} %broadcast_in_dim.40, f32[2,32,4096]{2,1,0:T(8,128)S(1)} %reshape.142, pred[4224]{0:T(1024)(128)(4,1)S(1)} %iota_compare_fusion.4, bf16[2,32,4224]{2,1,0:T(8,128)(2,1)} %collective-permute-done.1, ...), kind=kLoop, calls=%fused_computation.174 | loop fusion | flops 2973696 | bytes 5411456 | tf_op jit(solution)/shard_map/convert_element_type | solution.py:42
  85.3 5.6 %collective-permute-start.2 = (bf16[2,32,4224]{2,1,0:T(8,128)(2,1)S(1)}, bf16[2,32,4224]{2,1,0:T(8,128)(2,1)S(1)}, u32[]{:S(2)}, u32[]{:S(2)}) collective-permute-start(bf16[2,32,4224]{2,1,0:T(8,128)(2,1)S(1)} %get-tuple-element.15), channel_id=1, source_target_pairs={{1,3},{3,1},{5,7},{7,5},{9,11},{11,9},{13,15},{15,13},{17,19},{19,... | collective-permute-start | bytes 1622024 | tf_op jit(solution)/shard_map/ppermute | solution.py:42
  91.7 1.1 convert_element_type.201
  93.0 4.7 %collective-permute-done.2 = bf16[2,32,4224]{2,1,0:T(8,128)(2,1)S(1)} collective-permute-done((bf16[2,32,4224]{2,1,0:T(8,128)(2,1)S(1)}, bf16[2,32,4224]{2,1,0:T(8,128)(2,1)S(1)}, u32[]{:S(2)}, u32[]{:S(2)}) %collective-permute-start.2) | collective-permute-done | bytes 540704 | tf_op jit(solution)/shard_map/ppermute | solution.py:42
  97.9 1.8 %fusion.85 = (bf16[2,32,4224]{2,1,0:T(8,128)(2,1)S(1)}, f32[2,32,4224]{2,1,0:T(8,128)S(1)}, bf16[2,32,4224]{2,1,0:T(8,128)(2,1)S(1)}, f32[2,32,4224]{2,1,0:T(8,128)S(1)}) fusion(bf16[2,32,4224]{2,1,0:T(8,128)(2,1)S(1)} %copy-done.12, f32[2,32]{1,0:T(2,128)S(1)} %slice_reduce_fusion.3, bf16[2,32,4224]{2,1,0:T(8,128)(2,1)} %collective-permute-done.9, ...), kind=kLoop, calls=%fused_computation.169 | loop fusion | flops 5406720 | bytes 6493314 | tf_op jit(solution)/shard_map/convert_element_type | solution.py:42
  99.7 3.7 %collective-permute-start.3 = (bf16[2,32,4224]{2,1,0:T(8,128)(2,1)S(1)}, bf16[2,32,4224]{2,1,0:T(8,128)(2,1)S(1)}, u32[]{:S(2)}, u32[]{:S(2)}) collective-permute-start(bf16[2,32,4224]{2,1,0:T(8,128)(2,1)S(1)} %get-tuple-element.43), channel_id=1, source_target_pairs={{1,5},{3,7},{5,9},{7,11},{9,13},{11,15},{17,21},{19,23},{21,25},{2... | collective-permute-start | bytes 1622024 | tf_op jit(solution)/shard_map/ppermute | solution.py:42
  103.4 1.1 fusion.68
  104.7 5.0 %collective-permute-done.3 = bf16[2,32,4224]{2,1,0:T(8,128)(2,1)S(1)} collective-permute-done((bf16[2,32,4224]{2,1,0:T(8,128)(2,1)S(1)}, bf16[2,32,4224]{2,1,0:T(8,128)(2,1)S(1)}, u32[]{:S(2)}, u32[]{:S(2)}) %collective-permute-start.3) | collective-permute-done | bytes 540704 | tf_op jit(solution)/shard_map/ppermute | solution.py:42
  109.9 5.8 %collective-permute-start.4 = (bf16[2,32,4224]{2,1,0:T(8,128)(2,1)S(1)}, bf16[2,32,4224]{2,1,0:T(8,128)(2,1)S(1)}, u32[]{:S(2)}, u32[]{:S(2)}) collective-permute-start(bf16[2,32,4224]{2,1,0:T(8,128)(2,1)S(1)} %add_convert_fusion.1), channel_id=1, source_target_pairs={{1,9},{3,11},{5,13},{7,15},{17,25},{19,27},{21,29},{23,31},{33,41}... | collective-permute-start | bytes 1622024 | tf_op jit(solution)/shard_map/ppermute | solution.py:42
  115.7 5.8 %fusion.1 = f32[2,32,64,256]{3,2,1,0:T(8,128)} fusion(f32[2,32,256]{2,1,0:T(8,128)S(1)} %copy-done.17, f32[2,256,256]{2,1,0:T(8,128)S(1)} %fusion.68, pred[256,256]{1,0:T(8,128)(4,1)S(1)} %iota_compare_fusion, bf16[2,256,32,64]{1,3,2,0:T(8,128)(2,1)S(1)} %bitcast.107, f32[2,256,32]{1,2,0:T(8,128)S(1)} %get-tuple-element.40), kind=kOutput, calls=%fused_computation.3 | convolution fusion | flops 556793856 | bytes 7012352 | tf_op jit(solution)/shard_map/rhts,rshp->rthp/dot_general | solution.py:98
  121.8 1.4 collective-permute-start.11
  123.8 3.3 %collective-permute-start.5 = (bf16[2,32,4224]{2,1,0:T(8,128)(2,1)S(1)}, bf16[2,32,4224]{2,1,0:T(8,128)(2,1)S(1)}, u32[]{:S(2)}, u32[]{:S(2)}) collective-permute-start(bf16[2,32,4224]{2,1,0:T(8,128)(2,1)S(1)} %get-tuple-element.11), channel_id=1, source_target_pairs={{1,0},{3,2},{5,4},{7,6},{9,8},{11,10},{13,12},{15,14},{17,16},{19,... | collective-permute-start | bytes 1622024 | tf_op jit(solution)/shard_map/ppermute | solution.py:42
  127.1 5.7 %fusion = f32[2,32,64,256]{3,2,1,0:T(8,128)} fusion(f32[2,32,256]{2,1,0:T(8,128)S(1)} %fusion.58, f32[2,256,256]{2,1,0:T(8,128)S(1)} %fusion.73, pred[256,256]{1,0:T(8,128)(4,1)S(1)} %iota_compare_fusion.1, bf16[2,256,32,64]{1,3,2,0:T(8,128)(2,1)S(1)} %bitcast.110, f32[2,256,32]{1,2,0:T(8,128)S(1)} %get-tuple-element.39), kind=kOutput, calls=%fused_computation.2 | convolution fusion | flops 556793856 | bytes 7012352 | tf_op jit(solution)/shard_map/rhts,rshp->rthp/dot_general | solution.py:98
  132.9 1.1 convert_element_type.197
  134.0 1.1 convert_element_type.178
  135.3 1.5 fusion.51
  136.8 3.1 %reshape.145 = f32[2,32,64,64]{3,2,1,0:T(8,128)} reshape(f32[2,32,4096]{2,1,0:T(8,128)} %get-tuple-element.46) | data formatting | bytes 2097152 | tf_op jit(solution)/shard_map/reshape | solution.py:118
  139.9 2.2 %reshape.143 = f32[2,32,64,64]{3,2,1,0:T(8,128)} reshape(f32[2,32,4096]{2,1,0:T(8,128)S(1)} %get-tuple-element.47) | data formatting | bytes 2097152 | tf_op jit(solution)/shard_map/reshape | solution.py:118
  142.1 3.5 %fusion.63 = f32[2,256,32,64]{1,3,2,0:T(8,128)S(1)} fusion(f32[2,32,64,64]{3,2,1,0:T(8,128)} %reshape.143, bf16[2,256,2176]{1,2,0:T(8,128)(2,1)S(1)} %get-tuple-element.18), kind=kOutput, calls=%fused_computation.115 | convolution fusion | flops 805306368 | bytes 5308416 | tf_op jit(solution)/shard_map/rtn,rhpn->rthp/dot_general | solution.py:119
  145.7 7.3 %multiply_reduce_fusion = (f32[2,256]{1,0:T(2,128)S(1)}, f32[2,256,32,64]{1,3,2,0:T(8,128)S(1)}) fusion(f32[2,256,32,64]{1,3,2,0:T(8,128)} %bitcast.115, f32[2,256,32]{1,2,0:T(8,128)S(1)} %copy-done.22, f32[2,32,64,64]{3,2,1,0:T(8,128)S(1)} %copy-done.15, bf16[2,256,2176]{1,2,0:T(8,128)(2,1)} %copy-done.3, bf16[2,256,32,64]{1,3,2,0:T(8,128)(2,1)S(1)} %bitcast.108, ...), kind=kOutput, calls=%fused_computation.41 | convolution fusion | flops 824180224 | bytes 26413568 | tf_op jit(solution)/shard_map/rtn,rhpn->rthp/dot_general | solution.py:119
  153.1 2.4 %fusion.42 = bf16[2,256,1024]{2,1,0:T(8,128)(2,1)S(1)} fusion(bf16[2,256,1024]{2,1,0:T(8,128)(2,1)S(1)} %bitcast.114, bf16[32,64,1024,1]{2,1,0,3:T(8,128)(2,1)S(1)} %bitcast.112, f32[2,256,32,64]{1,3,2,0:T(8,128)S(1)} %get-tuple-element.55, f32[32,64]{1,0:T(8,128)S(1)} %mul.438, f32[2,256]{1,0:T(2,128)S(1)} %add_rsqrt_fusion), kind=kOutput, calls=%fused_computation.61 | convolution fusion | flops 2152202240 | bytes 10496000 | tf_op jit(solution)/shard_map/rthp,hpd->rtd/dot_general | solution.py:175
  155.7 2.0 %copy.66 = bf16[256,2,1024]{2,1,0:T(2,128)(2,1)} copy(bf16[256,2,1024]{2,0,1:T(8,128)(2,1)S(1)} %pad_maximum_fusion.5) | data formatting | bytes 2097152 | tf_op jit(solution)/shard_map/stack | solution.py:184
  (129 shorter events, 11.7 us)
Async XLA Ops:
  0.0 17.5 %copy-start = (bf16[1024,32]{0,1:T(8,128)(2,1)S(1)}, bf16[1024,32]{0,1:T(8,128)(2,1)}, u32[]{:S(2)}) copy-start(bf16[1024,32]{0,1:T(8,128)(2,1)} %param.14) | copy-start | bytes 196612
  0.0 3.8 %copy-start.29 = (bf16[1024,2176]{1,0:T(8,128)(2,1)S(1)}, bf16[1024,2176]{1,0:T(8,128)(2,1)}, u32[]{:S(2)}) copy-start(bf16[1024,2176]{1,0:T(8,128)(2,1)} %param.13) | copy-start | bytes 13369348
  7.2 10.2 %copy-start.19 = (f32[2,4,2176]{2,1,0:T(4,128)S(1)}, f32[2,4,2176]{2,1,0:T(4,128)}, u32[]{:S(2)}) copy-start(f32[2,4,2176]{2,1,0:T(4,128)} %param.17) | copy-start | bytes 208900
  7.2 10.2 %copy-start.27 = (f32[2,32]{1,0:T(2,128)S(1)}, f32[2,32]{1,0:T(2,128)}, u32[]{:S(2)}) copy-start(f32[2,32]{1,0:T(2,128)} %param.16) | copy-start | bytes 772
  7.2 10.7 %copy-start.26 = (f32[2,32]{1,0:T(2,128)S(1)}, f32[2,32]{1,0:T(2,128)}, u32[]{:S(2)}) copy-start(f32[2,32]{1,0:T(2,128)} %param.15) | copy-start | bytes 772
  7.3 18.6 %collective-permute-start.6 = (bf16[2,3,2176]{2,0,1:T(2,128)(2,1)S(1)}, bf16[2,3,2176]{2,0,1:T(2,128)(2,1)}, u32[]{:S(2)}, u32[]{:S(2)}) collective-permute-start(bf16[2,3,2176]{2,0,1:T(2,128)(2,1)S(1)} %copy.83), channel_id=1, source_target_pairs={{1,0},{2,1},{3,2},{4,3},{5,4},{6,5},{7,6},{8,7},{9,8},{10,9},{11,1... | collective-permute-start | bytes 78344 | tf_op jit(solution)/shard_map/ppermute | solution.py:20
  11.4 7.8 %copy-start.21 = (f32[2,2176]{1,0:T(2,128)S(1)}, f32[2,2176]{1,0:T(2,128)}, u32[]{:S(2)}) copy-start(f32[2,2176]{1,0:T(2,128)} %param.18) | copy-start | bytes 52228
  11.4 15.9 %collective-permute-start = (bf16[2,3,2176]{2,0,1:T(2,128)(2,1)}, bf16[2,3,2176]{2,0,1:T(2,128)(2,1)}, u32[]{:S(2)}, u32[]{:S(2)}) collective-permute-start(bf16[2,3,2176]{2,0,1:T(2,128)(2,1)} %copy.82), channel_id=1, source_target_pairs={{0,1},{1,2},{2,3},{3,4},{4,5},{5,6},{6,7},{7,8},{8,9},{9,10},{10,1... | collective-permute-start | bytes 78344 | tf_op jit(solution)/shard_map/ppermute | solution.py:20
  18.4 6.9 %copy-start.16 = (f32[2,32,256]{2,1,0:T(8,128)}, f32[2,32,256]{2,1,0:T(8,128)S(1)}, u32[]{:S(2)}) copy-start(f32[2,32,256]{2,1,0:T(8,128)S(1)} %fusion.56) | copy-start | bytes 196612
  22.9 100.5 %copy-start.18 = (pred[4224]{0:T(1024)(128)(4,1)}, pred[4224]{0:T(1024)(128)(4,1)S(1)}, u32[]{:S(2)}) copy-start(pred[4224]{0:T(1024)(128)(4,1)S(1)} %iota_compare_fusion.4) | copy-start | bytes 12676
  49.0 1.4 copy-start.3
  49.0 2.0 %copy-start.20 = (f32[2,256,32]{1,2,0:T(8,128)S(1)}, f32[2,256,32]{1,2,0:T(8,128)}, u32[]{:S(2)}) copy-start(f32[2,256,32]{1,2,0:T(8,128)} %get-tuple-element.38) | copy-start | bytes 196612
  49.2 1.8 %copy-start.4 = (bf16[2,256,2048]{1,2,0:T(8,128)(2,1)}, bf16[2,256,2048]{1,2,0:T(8,128)(2,1)S(1)}, u32[]{:S(2)}) copy-start(bf16[2,256,2048]{1,2,0:T(8,128)(2,1)S(1)} %slice.233) | copy-start | bytes 6291460
  55.2 4.0 %copy-start.2 = (f32[2,32,4096]{2,1,0:T(8,128)}, f32[2,32,4096]{2,1,0:T(8,128)S(1)}, u32[]{:S(2)}) copy-start(f32[2,32,4096]{2,1,0:T(8,128)S(1)} %reshape.144) | copy-start | bytes 3145732
  56.3 8.5 %collective-permute-start.7 = (bf16[2,32,4224]{2,1,0:T(8,128)(2,1)}, bf16[2,32,4224]{2,1,0:T(8,128)(2,1)}, u32[]{:S(2)}, u32[]{:S(2)}) collective-permute-start(bf16[2,32,4224]{2,1,0:T(8,128)(2,1)} %fusion.54), channel_id=1, source_target_pairs={{15,14},{13,12},{11,10},{9,8},{7,6},{5,4},{3,2},{1,0},{31,30},{29,... | collective-permute-start | bytes 1622024 | tf_op jit(solution)/shard_map/ppermute | solution.py:42
  59.2 1.4 copy-start.7
  64.7 2.3 %copy-start.24 = (f32[2,32]{1,0:T(2,128)S(1)}, f32[2,32]{1,0:T(2,128)}, u32[]{:S(2)}) copy-start(f32[2,32]{1,0:T(2,128)} %exp.73) | copy-start | bytes 772
  66.3 3.2 %collective-permute-start.8 = (bf16[2,32,4224]{2,1,0:T(8,128)(2,1)S(1)}, bf16[2,32,4224]{2,1,0:T(8,128)(2,1)S(1)}, u32[]{:S(2)}, u32[]{:S(2)}) collective-permute-start(bf16[2,32,4224]{2,1,0:T(8,128)(2,1)S(1)} %get-tuple-element.9), channel_id=1, source_target_pairs={{14,12},{12,14},{10,8},{8,10},{6,4},{4,6},{2,0},{0,2},{30,28},{28,... | collective-permute-start | bytes 1622024 | tf_op jit(solution)/shard_map/ppermute | solution.py:42
  67.1 5.6 %copy-start.30 = (bf16[1024,2048]{1,0:T(8,128)(2,1)S(1)}, bf16[1024,2048]{1,0:T(8,128)(2,1)}, u32[]{:S(2)}) copy-start(bf16[1024,2048]{1,0:T(8,128)(2,1)} %param.12) | copy-start | bytes 12582916
  68.0 15.4 %collective-permute-start.1 = (bf16[2,32,4224]{2,1,0:T(8,128)(2,1)}, bf16[2,32,4224]{2,1,0:T(8,128)(2,1)}, u32[]{:S(2)}, u32[]{:S(2)}) collective-permute-start(bf16[2,32,4224]{2,1,0:T(8,128)(2,1)} %fusion.55), channel_id=1, source_target_pairs={{0,1},{2,3},{4,5},{6,7},{8,9},{10,11},{12,13},{14,15},{16,17},{18,... | collective-permute-start | bytes 1622024 | tf_op jit(solution)/shard_map/ppermute | solution.py:42
  69.5 3.2 %copy-start.13 = (bf16[512,1024]{1,0:T(8,128)(2,1)S(1)}, bf16[512,1024]{1,0:T(8,128)(2,1)}, u32[]{:S(2)}) copy-start(bf16[512,1024]{1,0:T(8,128)(2,1)} %pad_maximum_fusion.4) | copy-start | bytes 3145732
  69.5 1.7 %copy-start.11 = (bf16[2,32,4224]{2,1,0:T(8,128)(2,1)}, bf16[2,32,4224]{2,1,0:T(8,128)(2,1)S(1)}, u32[]{:S(2)}) copy-start(bf16[2,32,4224]{2,1,0:T(8,128)(2,1)S(1)} %collective-permute-done.8) | copy-start | bytes 1622020
  71.2 12.1 %collective-permute-start.9 = (bf16[2,32,4224]{2,1,0:T(8,128)(2,1)}, bf16[2,32,4224]{2,1,0:T(8,128)(2,1)}, u32[]{:S(2)}, u32[]{:S(2)}) collective-permute-start(bf16[2,32,4224]{2,1,0:T(8,128)(2,1)} %get-tuple-element.7), channel_id=1, source_target_pairs={{14,10},{12,8},{10,6},{8,4},{6,2},{4,0},{30,26},{28,24},{26,22},{2... | collective-permute-start | bytes 1622024 | tf_op jit(solution)/shard_map/ppermute | solution.py:42
  77.1 5.4 %copy-start.25 = (f32[2048]{0:T(1024)S(1)}, f32[2048]{0:T(1024)}, u32[]{:S(2)}) copy-start(f32[2048]{0:T(1024)} %param.20) | copy-start | bytes 24580
  83.4 8.3 %copy-start.28 = (f32[2,32]{1,0:T(2,128)S(1)}, f32[2,32]{1,0:T(2,128)}, u32[]{:S(2)}) copy-start(f32[2,32]{1,0:T(2,128)} %param.19) | copy-start | bytes 772
  85.3 12.5 %copy-start.12 = (bf16[2,32,4224]{2,1,0:T(8,128)(2,1)S(1)}, bf16[2,32,4224]{2,1,0:T(8,128)(2,1)}, u32[]{:S(2)}) copy-start(bf16[2,32,4224]{2,1,0:T(8,128)(2,1)} %copy-done.11) | copy-start | bytes 1622020
  85.3 12.4 %collective-permute-start.2 = (bf16[2,32,4224]{2,1,0:T(8,128)(2,1)S(1)}, bf16[2,32,4224]{2,1,0:T(8,128)(2,1)S(1)}, u32[]{:S(2)}, u32[]{:S(2)}) collective-permute-start(bf16[2,32,4224]{2,1,0:T(8,128)(2,1)S(1)} %get-tuple-element.15), channel_id=1, source_target_pairs={{1,3},{3,1},{5,7},{7,5},{9,11},{11,9},{13,15},{15,13},{17,19},{19,... | collective-permute-start | bytes 1622024 | tf_op jit(solution)/shard_map/ppermute | solution.py:42
  91.0 6.9 %collective-permute-start.10 = (bf16[2,32,4224]{2,1,0:T(8,128)(2,1)S(1)}, bf16[2,32,4224]{2,1,0:T(8,128)(2,1)S(1)}, u32[]{:S(2)}, u32[]{:S(2)}) collective-permute-start(bf16[2,32,4224]{2,1,0:T(8,128)(2,1)S(1)} %get-tuple-element.45), channel_id=1, source_target_pairs={{14,6},{12,4},{10,2},{8,0},{30,22},{28,20},{26,18},{24,16},{46,38}... | collective-permute-start | bytes 1622024 | tf_op jit(solution)/shard_map/ppermute | solution.py:42
  99.7 16.0 %copy-start.5 = (bf16[2,256,2048]{1,2,0:T(8,128)(2,1)S(1)}, bf16[2,256,2048]{1,2,0:T(8,128)(2,1)}, u32[]{:S(2)}) copy-start(bf16[2,256,2048]{1,2,0:T(8,128)(2,1)} %copy-done.4) | copy-start | bytes 6291460
  99.7 16.0 %copy-start.17 = (f32[2,32,256]{2,1,0:T(8,128)S(1)}, f32[2,32,256]{2,1,0:T(8,128)}, u32[]{:S(2)}) copy-start(f32[2,32,256]{2,1,0:T(8,128)} %copy-done.16) | copy-start | bytes 196612
  99.7 10.0 %collective-permute-start.3 = (bf16[2,32,4224]{2,1,0:T(8,128)(2,1)S(1)}, bf16[2,32,4224]{2,1,0:T(8,128)(2,1)S(1)}, u32[]{:S(2)}, u32[]{:S(2)}) collective-permute-start(bf16[2,32,4224]{2,1,0:T(8,128)(2,1)S(1)} %get-tuple-element.43), channel_id=1, source_target_pairs={{1,5},{3,7},{5,9},{7,11},{9,13},{11,15},{17,21},{19,23},{21,25},{2... | collective-permute-start | bytes 1622024 | tf_op jit(solution)/shard_map/ppermute | solution.py:42
  109.9 13.5 %collective-permute-start.4 = (bf16[2,32,4224]{2,1,0:T(8,128)(2,1)S(1)}, bf16[2,32,4224]{2,1,0:T(8,128)(2,1)S(1)}, u32[]{:S(2)}, u32[]{:S(2)}) collective-permute-start(bf16[2,32,4224]{2,1,0:T(8,128)(2,1)S(1)} %add_convert_fusion.1), channel_id=1, source_target_pairs={{1,9},{3,11},{5,13},{7,15},{17,25},{19,27},{21,29},{23,31},{33,41}... | collective-permute-start | bytes 1622024 | tf_op jit(solution)/shard_map/ppermute | solution.py:42
  121.8 5.4 %copy-start.8 = (bf16[2,256,2048]{1,2,0:T(8,128)(2,1)S(1)}, bf16[2,256,2048]{1,2,0:T(8,128)(2,1)}, u32[]{:S(2)}) copy-start(bf16[2,256,2048]{1,2,0:T(8,128)(2,1)} %copy-done.7) | copy-start | bytes 6291460
  121.8 13.5 %collective-permute-start.11 = (bf16[2,32,4224]{2,1,0:T(8,128)(2,1)S(1)}, bf16[2,32,4224]{2,1,0:T(8,128)(2,1)S(1)}, u32[]{:S(2)}, u32[]{:S(2)}) collective-permute-start(bf16[2,32,4224]{2,1,0:T(8,128)(2,1)S(1)} %get-tuple-element.5), channel_id=1, source_target_pairs={{14,15},{12,13},{10,11},{8,9},{6,7},{4,5},{2,3},{0,1},{30,31},{28,... | collective-permute-start | bytes 1622024 | tf_op jit(solution)/shard_map/ppermute | solution.py:42
  123.8 11.5 %collective-permute-start.5 = (bf16[2,32,4224]{2,1,0:T(8,128)(2,1)S(1)}, bf16[2,32,4224]{2,1,0:T(8,128)(2,1)S(1)}, u32[]{:S(2)}, u32[]{:S(2)}) collective-permute-start(bf16[2,32,4224]{2,1,0:T(8,128)(2,1)S(1)} %get-tuple-element.11), channel_id=1, source_target_pairs={{1,0},{3,2},{5,4},{7,6},{9,8},{11,10},{13,12},{15,14},{17,16},{19,... | collective-permute-start | bytes 1622024 | tf_op jit(solution)/shard_map/ppermute | solution.py:42
  132.9 2.4 %slice-start = ((pred[4224]{0:T(1024)(128)(4,1)}), pred[4096]{0:T(1024)(128)(4,1)S(1)}, s32[]{:S(2)}) async-start(pred[4224]{0:T(1024)(128)(4,1)} %copy-done.18), calls=%async_computation | async-start | bytes 8192 | tf_op jit(solution)/shard_map/slice | solution.py:58
  139.9 5.8 %copy-start.23 = (f32[2,256,32]{1,2,0:T(8,128)S(1)}, f32[2,256,32]{1,2,0:T(8,128)}, u32[]{:S(2)}) copy-start(f32[2,256,32]{1,2,0:T(8,128)} %get-tuple-element.35) | copy-start | bytes 196612
  142.1 3.6 %copy-start.6 = (bf16[2,256,2048]{1,2,0:T(8,128)(2,1)S(1)}, bf16[2,256,2048]{1,2,0:T(8,128)(2,1)}, u32[]{:S(2)}) copy-start(bf16[2,256,2048]{1,2,0:T(8,128)(2,1)} %copy-done.4) | copy-start | bytes 6291460
  142.1 3.6 %copy-start.9 = (bf16[2,256,2048]{1,2,0:T(8,128)(2,1)S(1)}, bf16[2,256,2048]{1,2,0:T(8,128)(2,1)}, u32[]{:S(2)}) copy-start(bf16[2,256,2048]{1,2,0:T(8,128)(2,1)} %copy-done.7) | copy-start | bytes 6291460
  142.1 3.6 %copy-start.15 = (f32[2,32,64,64]{3,2,1,0:T(8,128)S(1)}, f32[2,32,64,64]{3,2,1,0:T(8,128)}, u32[]{:S(2)}) copy-start(f32[2,32,64,64]{3,2,1,0:T(8,128)} %reshape.145) | copy-start | bytes 3145732
  142.1 3.6 %copy-start.22 = (f32[2,256,32]{1,2,0:T(8,128)S(1)}, f32[2,256,32]{1,2,0:T(8,128)}, u32[]{:S(2)}) copy-start(f32[2,256,32]{1,2,0:T(8,128)} %get-tuple-element.37) | copy-start | bytes 196612
  145.7 7.4 %copy-start.10 = (bf16[2048,1024]{1,0:T(8,128)(2,1)S(1)}, bf16[2048,1024]{1,0:T(8,128)(2,1)}, u32[]{:S(2)}) copy-start(bf16[2048,1024]{1,0:T(8,128)(2,1)} %param.21) | copy-start | bytes 12582916
  145.7 7.4 %copy-start.14 = (bf16[512,1024]{1,0:T(8,128)(2,1)S(1)}, bf16[512,1024]{1,0:T(8,128)(2,1)}, u32[]{:S(2)}) copy-start(bf16[512,1024]{1,0:T(8,128)(2,1)} %pad_maximum_fusion.4) | copy-start | bytes 3145732
  155.5 2.2 %copy-start.1 = (bf16[1024,32]{0,1:T(8,128)(2,1)S(1)}, bf16[1024,32]{0,1:T(8,128)(2,1)}, u32[]{:S(2)}) copy-start(bf16[1024,32]{0,1:T(8,128)(2,1)} %param.14) | copy-start | bytes 196612

commit v8 on v7

--- a/solution.py
+++ b/solution.py
@@ -61,13 +61,14 @@
 def group_terms(window, dt_raw, dt_shift, log_rate, weights, offset, skip_heads, falling):
     runs, length = dt_raw.shape[0], dt_raw.shape[1]
     heads = dt_raw.shape[2]
+    window = window.astype(jnp.float32)
     if falling:
         taps = [window[:, K - 1 - k : K - 1 - k + length] for k in range(K)]
     else:
         taps = [window[:, k : k + length] for k in range(K)]
-    total = offset[:, None, :] + weights[:, 0][:, None, :] * taps[0].astype(jnp.float32)
+    total = offset[:, None, :] + weights[:, 0][:, None, :] * taps[0]
     for k in range(1, K):
-        total = total + weights[:, k][:, None, :] * taps[k].astype(jnp.float32)
+        total = total + weights[:, k][:, None, :] * taps[k]
     conv = jax.nn.silu(total).astype(jnp.bfloat16)
     inner = conv.shape[2] - 2 * NS
     head_size = inner // heads

time: 159 us -> 164 us (1.031)
  other arithmetic: 37.4 us -> 45.6 us
    convert_element_type x0 -> x1, other arithmetic: none -> 4.63 us  [group_terms(): window = window.astype(jnp.float32)]
    convert_element_type x1 -> x2, other arithmetic: 19.5 us -> 22.9 us  [group_terms(): conv = jax.nn.silu(total).astype(jnp.bfloat16)]
    unnamed x68 -> x90, local copies, waits for them, and re-layouts: 6.44 us -> 6.45 us
  transfers between devices with their start and end apart: 12 -> 12, of which waited for: 2 -> 2; matrix products, arithmetic and copies ran while one was open for 30% -> 39% of each run, Pallas kernels for 0% -> 0%
where the time goes in v8:
time: 164 us; the launch traced here: 163 us
  other arithmetic  45.6 us (28%)
  matrix products  37.8 us (23%)
  local copies, waits for them, and re-layouts  34.9 us (21%)
  starting transfers between devices  34.6 us (21%)
  waiting for transfers between devices  9.67 us (6%)
    ppermute x10, starting transfers between devices, send(): moved = lax.ppermute(value.astype(jnp.bfloat16), 'ctx', pairs)  26.2 us
    convert_element_type x2, other arithmetic, group_terms(): conv = jax.nn.silu(total).astype(jnp.bfloat16)  22.9 us
    dot_general x2, matrix products, group_terms(): jnp.einsum('rhts,rshp->rthp', mixing, scaled, preferred_element_type=jnp....  11.5 us
    dot_general x2, matrix products, finish(): jnp.einsum('rtn,rhpn->rthp', reads.astype(jnp.float32), entering, precisi...  10.9 us
    ppermute x10, waiting for transfers between devices, send(): moved = lax.ppermute(value.astype(jnp.bfloat16), 'ctx', pairs)  9.66 us
    convert_element_type x8, other arithmetic, send(): moved = lax.ppermute(value.astype(jnp.bfloat16), 'ctx', pairs)  9.48 us
    ppermute x2, starting transfers between devices, shifted(): return lax.ppermute(value, 'ctx', pairs)  8.37 us
    unnamed x90, local copies, waits for them, and re-layouts  6.45 us
  transfers between devices with their start and end apart: 12, of which 2 were waited for; matrix products, arithmetic and copies ran while one was open for 39% of the time, Pallas kernels for 0%

profile of v8, /device:TPU:1, one launch (start us, length us, event | category | flops | bytes accessed | tf_op | source)
XLA Modules:
  0.0 163.4 jit_solution(17948738471607494611)
XLA Ops:
  0.0 3.4 %fusion.94 = (bf16[256,1,1024]{2,1,0:T(2,128)(2,1)S(1)}, bf16[256,1,1024]{2,1,0:T(2,128)(2,1)S(1)}) fusion(bf16[256,2,1024]{2,1,0:T(2,128)(2,1)} %param.11), kind=kLoop, calls=%fused_computation.176 | loop fusion | bytes 2097152 | tf_op jit(solution)/shard_map/slice | solution.py:134
  3.8 3.4 %convolution_convert_fusion = bf16[512,2176]{1,0:T(8,128)(2,1)S(1)} fusion(bf16[1024,2176]{1,0:T(8,128)(2,1)S(1)} %copy-done.40, bf16[256,1024]{1,0:T(8,128)(2,1)S(1)} %get-tuple-element.56, bf16[256,1024]{1,0:T(8,128)(2,1)S(1)} %get-tuple-element.57), kind=kOutput, calls=%fused_computation.20 | convolution fusion | flops 2284912640 | bytes 7733248 | tf_op jit(solution)/shard_map/dot_general | solution.py:138
  7.3 3.4 %collective-permute-start.6 = (bf16[2,3,2176]{2,0,1:T(2,128)(2,1)S(1)}, bf16[2,3,2176]{2,0,1:T(2,128)(2,1)}, u32[]{:S(2)}, u32[]{:S(2)}) collective-permute-start(bf16[2,3,2176]{2,0,1:T(2,128)(2,1)S(1)} %copy.79), channel_id=1, source_target_pairs={{1,0},{2,1},{3,2},{4,3},{5,4},{6,5},{7,6},{8,7},{9,8},{10,9},{11,1... | collective-permute-start | bytes 78344 | tf_op jit(solution)/shard_map/ppermute | solution.py:20
  11.4 5.0 %collective-permute-start = (bf16[2,3,2176]{2,0,1:T(2,128)(2,1)}, bf16[2,3,2176]{2,0,1:T(2,128)(2,1)}, u32[]{:S(2)}, u32[]{:S(2)}) collective-permute-start(bf16[2,3,2176]{2,0,1:T(2,128)(2,1)} %copy.78), channel_id=1, source_target_pairs={{0,1},{1,2},{2,3},{3,4},{4,5},{5,6},{6,7},{7,8},{8,9},{9,10},{10,1... | collective-permute-start | bytes 78344 | tf_op jit(solution)/shard_map/ppermute | solution.py:20
  16.3 1.0 pad_maximum_fusion.2
  18.5 0.7 bitcast_exponential_fusion
  23.6 3.0 %copy.55 = bf16[2,256,2176]{1,2,0:T(8,128)(2,1)S(1)} copy(bf16[2,256,2176]{2,1,0:T(8,128)(2,1)} %bitcast.117) | data formatting | bytes 4456448 | tf_op jit(solution)/shard_map/reshape | solution.py:139
  26.7 1.4 copy.59
  28.1 2.2 %copy.54 = bf16[2,3,2176]{1,2,0:T(8,128)(2,1)} copy(bf16[2,3,2176]{2,0,1:T(2,128)(2,1)} %collective-permute-done) | data formatting | bytes 52224 | tf_op jit(solution)/shard_map/ppermute | solution.py:20
  30.3 4.6 %maximum_convert_fusion.1 = (f32[2,259,2176]{1,2,0:T(8,128)S(1)}, f32[2,259,2176]{1,2,0:T(8,128)}) fusion(bf16[2,3,2176]{1,2,0:T(8,128)(2,1)S(1)} %copy.59, bf16[2,256,2176]{1,2,0:T(8,128)(2,1)S(1)} %copy.55, bf16[2,3,2176]{1,2,0:T(8,128)(2,1)} %copy.54), kind=kLoop, calls=%fused_computation.55 | loop fusion | flops 9017344 | bytes 11297792 | tf_op jit(solution)/shard_map/convert_element_type | solution.py:64
  35.0 7.3 %multiply_convert_fusion.4 = bf16[2,256,2176]{1,2,0:T(8,128)(2,1)S(1)} fusion(f32[2,259,2176]{1,2,0:T(8,128)S(1)} %get-tuple-element.17, f32[2,2176]{1,0:T(2,128)S(1)} %copy-done.29, f32[2,2176]{1,0:T(2,128)S(1)} %copy-done.30, f32[2,2176]{1,0:T(2,128)S(1)} %copy-done.31, f32[2,2176]{1,0:T(2,128)S(1)} %copy-done.32, f32[2,2176]{1,0:T(2,128)S(1)} %copy-done.33), kind=kLoop, calls=%fused_computation.37 | loop fusion | flops 14483456 | bytes 20141056 | tf_op jit(solution)/shard_map/convert_element_type | solution.py:72
  42.5 1.2 copy-done.3
  45.7 1.1 fusion.56
  46.8 2.1 %collective-permute-start.7 = (bf16[2,32,4224]{2,1,0:T(8,128)(2,1)}, bf16[2,32,4224]{2,1,0:T(8,128)(2,1)}, u32[]{:S(2)}, u32[]{:S(2)}) collective-permute-start(bf16[2,32,4224]{2,1,0:T(8,128)(2,1)} %fusion.56), channel_id=1, source_target_pairs={{15,14},{13,12},{11,10},{9,8},{7,6},{5,4},{3,2},{1,0},{31,30},{29,... | collective-permute-start | bytes 1622024 | tf_op jit(solution)/shard_map/ppermute | solution.py:42
  48.9 15.7 %multiply_convert_fusion.5 = bf16[2,256,2176]{1,2,0:T(8,128)(2,1)S(1)} fusion(f32[2,259,2176]{1,2,0:T(8,128)} %get-tuple-element.18, f32[2,2176]{1,0:T(2,128)S(1)} %copy-done.25, f32[2,2176]{1,0:T(2,128)S(1)} %copy-done.26, f32[2,2176]{1,0:T(2,128)S(1)} %copy-done.27, f32[2,2176]{1,0:T(2,128)S(1)} %copy-done.28, f32[2,2176]{1,0:T(2,128)S(1)} %copy-done.24), kind=kLoop, calls=%fused_computation.38 | loop fusion | flops 14483456 | bytes 20141056 | tf_op jit(solution)/shard_map/convert_element_type | solution.py:72
  64.8 1.3 copy-done.7
  66.1 2.1 %fusion.41 = f32[2,32,64,64]{3,2,1,0:T(8,128)} fusion(bf16[2,256,32,64]{1,3,2,0:T(8,128)(2,1)S(1)} %bitcast.109, f32[2,256,32]{1,2,0:T(8,128)S(1)} %copy-done.21, bf16[2,256,2176]{1,2,0:T(8,128)(2,1)S(1)} %multiply_convert_fusion.5), kind=kOutput, calls=%fused_computation.59 | convolution fusion | flops 137363456 | bytes 3276800 | tf_op jit(solution)/shard_map/rshp,rsn->rhpn/dot_general | solution.py:103
  68.2 2.1 %reshape.142 = f32[2,32,4096]{2,1,0:T(8,128)S(1)} reshape(f32[2,32,64,64]{3,2,1,0:T(8,128)} %fusion.41) | data formatting | bytes 2097152 | tf_op jit(solution)/shard_map/reshape | solution.py:109
  70.3 1.6 fusion.89
  72.7 0.9 fusion.57
  73.6 1.4 collective-permute-start.1
  75.3 1.6 fusion.88
  76.8 1.5 collective-permute-start.9
  78.3 4.4 %convert_bitcast_fusion = f32[2,2048,256]{1,2,0:T(8,128)} fusion(bf16[2,256,1024]{2,1,0:T(8,128)(2,1)S(1)} %bitcast.113, bf16[1024,2048]{1,0:T(8,128)(2,1)S(1)} %copy-done.41), kind=kOutput, calls=%fused_computation.51 | convolution fusion | flops 2149580800 | bytes 9437184 | tf_op jit(solution)/shard_map/rtd,de->ret/dot_general | solution.py:135
  82.7 5.4 %copy.61 = f32[2,2048,256]{2,1,0:T(8,128)} copy(f32[2,2048,256]{1,2,0:T(8,128)} %convert_bitcast_fusion) | data formatting | bytes 8388608 | tf_op jit(solution)/shard_map/transpose | solution.py:168
  88.2 0.8 slice_reduce_fusion
  89.0 1.9 %fusion.92 = (bf16[2,32,4224]{2,1,0:T(8,128)(2,1)S(1)}, f32[2,32,4224]{2,1,0:T(8,128)S(1)}, bf16[2,32,4224]{2,1,0:T(8,128)(2,1)S(1)}) fusion(f32[2,32,128]{2,1,0:T(8,128)S(1)} %broadcast_in_dim.40, f32[2,32,4096]{2,1,0:T(8,128)S(1)} %reshape.142, pred[4224]{0:T(1024)(128)(4,1)S(1)} %iota_compare_fusion.4, bf16[2,32,4224]{2,1,0:T(8,128)(2,1)} %collective-permute-done.1, ...), kind=kLoop, calls=%fused_computation.174 | loop fusion | flops 2973696 | bytes 5411456 | tf_op jit(solution)/shard_map/convert_element_type | solution.py:42
  91.0 5.6 %collective-permute-start.2 = (bf16[2,32,4224]{2,1,0:T(8,128)(2,1)S(1)}, bf16[2,32,4224]{2,1,0:T(8,128)(2,1)S(1)}, u32[]{:S(2)}, u32[]{:S(2)}) collective-permute-start(bf16[2,32,4224]{2,1,0:T(8,128)(2,1)S(1)} %get-tuple-element.15), channel_id=1, source_target_pairs={{1,3},{3,1},{5,7},{7,5},{9,11},{11,9},{13,15},{15,13},{17,19},{19,... | collective-permute-start | bytes 1622024 | tf_op jit(solution)/shard_map/ppermute | solution.py:42
  97.4 1.1 convert_element_type.180
  98.7 4.7 %collective-permute-done.2 = bf16[2,32,4224]{2,1,0:T(8,128)(2,1)S(1)} collective-permute-done((bf16[2,32,4224]{2,1,0:T(8,128)(2,1)S(1)}, bf16[2,32,4224]{2,1,0:T(8,128)(2,1)S(1)}, u32[]{:S(2)}, u32[]{:S(2)}) %collective-permute-start.2) | collective-permute-done | bytes 540704 | tf_op jit(solution)/shard_map/ppermute | solution.py:42
  103.5 1.8 %fusion.87 = (bf16[2,32,4224]{2,1,0:T(8,128)(2,1)S(1)}, f32[2,32,4224]{2,1,0:T(8,128)S(1)}, bf16[2,32,4224]{2,1,0:T(8,128)(2,1)S(1)}, f32[2,32,4224]{2,1,0:T(8,128)S(1)}) fusion(bf16[2,32,4224]{2,1,0:T(8,128)(2,1)S(1)} %copy-done.12, f32[2,32]{1,0:T(2,128)S(1)} %slice_reduce_fusion.3, bf16[2,32,4224]{2,1,0:T(8,128)(2,1)} %collective-permute-done.9, ...), kind=kLoop, calls=%fused_computation.169 | loop fusion | flops 5406720 | bytes 6493314 | tf_op jit(solution)/shard_map/convert_element_type | solution.py:42
  105.3 3.7 %collective-permute-start.3 = (bf16[2,32,4224]{2,1,0:T(8,128)(2,1)S(1)}, bf16[2,32,4224]{2,1,0:T(8,128)(2,1)S(1)}, u32[]{:S(2)}, u32[]{:S(2)}) collective-permute-start(bf16[2,32,4224]{2,1,0:T(8,128)(2,1)S(1)} %get-tuple-element.43), channel_id=1, source_target_pairs={{1,5},{3,7},{5,9},{7,11},{9,13},{11,15},{17,21},{19,23},{21,25},{2... | collective-permute-start | bytes 1622024 | tf_op jit(solution)/shard_map/ppermute | solution.py:42
  109.1 1.1 fusion.70
  110.3 5.0 %collective-permute-done.3 = bf16[2,32,4224]{2,1,0:T(8,128)(2,1)S(1)} collective-permute-done((bf16[2,32,4224]{2,1,0:T(8,128)(2,1)S(1)}, bf16[2,32,4224]{2,1,0:T(8,128)(2,1)S(1)}, u32[]{:S(2)}, u32[]{:S(2)}) %collective-permute-start.3) | collective-permute-done | bytes 540704 | tf_op jit(solution)/shard_map/ppermute | solution.py:42
  115.5 5.8 %collective-permute-start.4 = (bf16[2,32,4224]{2,1,0:T(8,128)(2,1)S(1)}, bf16[2,32,4224]{2,1,0:T(8,128)(2,1)S(1)}, u32[]{:S(2)}, u32[]{:S(2)}) collective-permute-start(bf16[2,32,4224]{2,1,0:T(8,128)(2,1)S(1)} %add_convert_fusion.1), channel_id=1, source_target_pairs={{1,9},{3,11},{5,13},{7,15},{17,25},{19,27},{21,29},{23,31},{33,41}... | collective-permute-start | bytes 1622024 | tf_op jit(solution)/shard_map/ppermute | solution.py:42
  121.3 5.8 %fusion.1 = f32[2,32,64,256]{3,2,1,0:T(8,128)} fusion(f32[2,32,256]{2,1,0:T(8,128)S(1)} %copy-done.18, f32[2,256,256]{2,1,0:T(8,128)S(1)} %fusion.70, pred[256,256]{1,0:T(8,128)(4,1)S(1)} %iota_compare_fusion, bf16[2,256,32,64]{1,3,2,0:T(8,128)(2,1)S(1)} %bitcast.107, f32[2,256,32]{1,2,0:T(8,128)S(1)} %get-tuple-element.40), kind=kOutput, calls=%fused_computation.3 | convolution fusion | flops 556793856 | bytes 7012352 | tf_op jit(solution)/shard_map/rhts,rshp->rthp/dot_general | solution.py:99
  127.4 1.4 collective-permute-start.11
  129.4 3.3 %collective-permute-start.5 = (bf16[2,32,4224]{2,1,0:T(8,128)(2,1)S(1)}, bf16[2,32,4224]{2,1,0:T(8,128)(2,1)S(1)}, u32[]{:S(2)}, u32[]{:S(2)}) collective-permute-start(bf16[2,32,4224]{2,1,0:T(8,128)(2,1)S(1)} %get-tuple-element.11), channel_id=1, source_target_pairs={{1,0},{3,2},{5,4},{7,6},{9,8},{11,10},{13,12},{15,14},{17,16},{19,... | collective-permute-start | bytes 1622024 | tf_op jit(solution)/shard_map/ppermute | solution.py:42
  132.8 5.7 %fusion = f32[2,32,64,256]{3,2,1,0:T(8,128)} fusion(f32[2,32,256]{2,1,0:T(8,128)S(1)} %fusion.60, f32[2,256,256]{2,1,0:T(8,128)S(1)} %fusion.75, pred[256,256]{1,0:T(8,128)(4,1)S(1)} %iota_compare_fusion.1, bf16[2,256,32,64]{1,3,2,0:T(8,128)(2,1)S(1)} %bitcast.110, f32[2,256,32]{1,2,0:T(8,128)S(1)} %get-tuple-element.39), kind=kOutput, calls=%fused_computation.2 | convolution fusion | flops 556793856 | bytes 7012352 | tf_op jit(solution)/shard_map/rhts,rshp->rthp/dot_general | solution.py:99
  138.5 1.1 convert_element_type.176
  139.6 1.1 convert_element_type.159
  140.9 1.4 fusion.53
  142.4 3.1 %reshape.145 = f32[2,32,64,64]{3,2,1,0:T(8,128)} reshape(f32[2,32,4096]{2,1,0:T(8,128)} %get-tuple-element.46) | data formatting | bytes 2097152 | tf_op jit(solution)/shard_map/reshape | solution.py:119
  145.5 2.2 %reshape.143 = f32[2,32,64,64]{3,2,1,0:T(8,128)} reshape(f32[2,32,4096]{2,1,0:T(8,128)S(1)} %get-tuple-element.47) | data formatting | bytes 2097152 | tf_op jit(solution)/shard_map/reshape | solution.py:119
  147.7 3.5 %fusion.65 = f32[2,256,32,64]{1,3,2,0:T(8,128)S(1)} fusion(f32[2,32,64,64]{3,2,1,0:T(8,128)} %reshape.143, bf16[2,256,2176]{1,2,0:T(8,128)(2,1)S(1)} %multiply_convert_fusion.5), kind=kOutput, calls=%fused_computation.115 | convolution fusion | flops 805306368 | bytes 5308416 | tf_op jit(solution)/shard_map/rtn,rhpn->rthp/dot_general | solution.py:120
  151.3 7.3 %multiply_reduce_fusion = (f32[2,256]{1,0:T(2,128)S(1)}, f32[2,256,32,64]{1,3,2,0:T(8,128)S(1)}) fusion(f32[2,256,32,64]{1,3,2,0:T(8,128)} %bitcast.115, f32[2,256,32]{1,2,0:T(8,128)S(1)} %copy-done.34, f32[2,32,64,64]{3,2,1,0:T(8,128)S(1)} %copy-done.16, bf16[2,256,2176]{1,2,0:T(8,128)(2,1)} %copy-done.3, bf16[2,256,32,64]{1,3,2,0:T(8,128)(2,1)S(1)} %bitcast.108, ...), kind=kOutput, calls=%fused_computation.53 | convolution fusion | flops 824180224 | bytes 26413568 | tf_op jit(solution)/shard_map/rtn,rhpn->rthp/dot_general | solution.py:120
  158.7 2.4 %fusion.44 = bf16[2,256,1024]{2,1,0:T(8,128)(2,1)S(1)} fusion(bf16[2,256,1024]{2,1,0:T(8,128)(2,1)S(1)} %bitcast.114, bf16[32,64,1024,1]{2,1,0,3:T(8,128)(2,1)S(1)} %bitcast.112, f32[2,256,32,64]{1,3,2,0:T(8,128)S(1)} %get-tuple-element.55, f32[32,64]{1,0:T(8,128)S(1)} %mul.438, f32[2,256]{1,0:T(2,128)S(1)} %add_rsqrt_fusion), kind=kOutput, calls=%fused_computation.61 | convolution fusion | flops 2152202240 | bytes 10496000 | tf_op jit(solution)/shard_map/rthp,hpd->rtd/dot_general | solution.py:176
  161.3 2.0 %copy.62 = bf16[256,2,1024]{2,1,0:T(2,128)(2,1)} copy(bf16[256,2,1024]{2,0,1:T(8,128)(2,1)S(1)} %pad_maximum_fusion.3) | data formatting | bytes 2097152 | tf_op jit(solution)/shard_map/stack | solution.py:185
  (153 shorter events, 12.6 us)
Async XLA Ops:
  0.0 17.5 %copy-start = (bf16[1024,32]{0,1:T(8,128)(2,1)S(1)}, bf16[1024,32]{0,1:T(8,128)(2,1)}, u32[]{:S(2)}) copy-start(bf16[1024,32]{0,1:T(8,128)(2,1)} %param.14) | copy-start | bytes 196612
  0.0 3.8 %copy-start.40 = (bf16[1024,2176]{1,0:T(8,128)(2,1)S(1)}, bf16[1024,2176]{1,0:T(8,128)(2,1)}, u32[]{:S(2)}) copy-start(bf16[1024,2176]{1,0:T(8,128)(2,1)} %param.13) | copy-start | bytes 13369348
  7.2 10.7 %copy-start.15 = (bf16[512,2176]{1,0:T(8,128)(2,1)}, bf16[512,2176]{1,0:T(8,128)(2,1)S(1)}, u32[]{:S(2)}) copy-start(bf16[512,2176]{1,0:T(8,128)(2,1)S(1)} %convolution_convert_fusion) | copy-start | bytes 6684676
  7.2 10.2 %copy-start.38 = (f32[2,32]{1,0:T(2,128)S(1)}, f32[2,32]{1,0:T(2,128)}, u32[]{:S(2)}) copy-start(f32[2,32]{1,0:T(2,128)} %param.16) | copy-start | bytes 772
  7.2 10.2 %copy-start.20 = (f32[2,4,2176]{2,1,0:T(4,128)S(1)}, f32[2,4,2176]{2,1,0:T(4,128)}, u32[]{:S(2)}) copy-start(f32[2,4,2176]{2,1,0:T(4,128)} %param.17) | copy-start | bytes 208900
  7.2 10.7 %copy-start.37 = (f32[2,32]{1,0:T(2,128)S(1)}, f32[2,32]{1,0:T(2,128)}, u32[]{:S(2)}) copy-start(f32[2,32]{1,0:T(2,128)} %param.15) | copy-start | bytes 772
  7.3 19.4 %collective-permute-start.6 = (bf16[2,3,2176]{2,0,1:T(2,128)(2,1)S(1)}, bf16[2,3,2176]{2,0,1:T(2,128)(2,1)}, u32[]{:S(2)}, u32[]{:S(2)}) collective-permute-start(bf16[2,3,2176]{2,0,1:T(2,128)(2,1)S(1)} %copy.79), channel_id=1, source_target_pairs={{1,0},{2,1},{3,2},{4,3},{5,4},{6,5},{7,6},{8,7},{9,8},{10,9},{11,1... | collective-permute-start | bytes 78344 | tf_op jit(solution)/shard_map/ppermute | solution.py:20
  11.4 7.9 %copy-start.23 = (f32[2,2176]{1,0:T(2,128)S(1)}, f32[2,2176]{1,0:T(2,128)}, u32[]{:S(2)}) copy-start(f32[2,2176]{1,0:T(2,128)} %param.18) | copy-start | bytes 52228
  11.4 16.7 %collective-permute-start = (bf16[2,3,2176]{2,0,1:T(2,128)(2,1)}, bf16[2,3,2176]{2,0,1:T(2,128)(2,1)}, u32[]{:S(2)}, u32[]{:S(2)}) collective-permute-start(bf16[2,3,2176]{2,0,1:T(2,128)(2,1)} %copy.78), channel_id=1, source_target_pairs={{0,1},{1,2},{2,3},{3,4},{4,5},{5,6},{6,7},{7,8},{8,9},{9,10},{10,1... | collective-permute-start | bytes 78344 | tf_op jit(solution)/shard_map/ppermute | solution.py:20
  18.4 5.2 %copy-start.17 = (f32[2,32,256]{2,1,0:T(8,128)}, f32[2,32,256]{2,1,0:T(8,128)S(1)}, u32[]{:S(2)}) copy-start(f32[2,32,256]{2,1,0:T(8,128)S(1)} %fusion.58) | copy-start | bytes 196612
  23.6 105.4 %copy-start.19 = (pred[4224]{0:T(1024)(128)(4,1)}, pred[4224]{0:T(1024)(128)(4,1)S(1)}, u32[]{:S(2)}) copy-start(pred[4224]{0:T(1024)(128)(4,1)S(1)} %iota_compare_fusion.4) | copy-start | bytes 12676
  30.3 4.7 %copy-start.29 = (f32[2,2176]{1,0:T(2,128)S(1)}, f32[2,2176]{1,0:T(2,128)}, u32[]{:S(2)}) copy-start(f32[2,2176]{1,0:T(2,128)} %get-tuple-element.58) | copy-start | bytes 52228
  30.3 4.7 %copy-start.30 = (f32[2,2176]{1,0:T(2,128)S(1)}, f32[2,2176]{1,0:T(2,128)}, u32[]{:S(2)}) copy-start(f32[2,2176]{1,0:T(2,128)} %get-tuple-element.59) | copy-start | bytes 52228
  30.3 4.7 %copy-start.31 = (f32[2,2176]{1,0:T(2,128)S(1)}, f32[2,2176]{1,0:T(2,128)}, u32[]{:S(2)}) copy-start(f32[2,2176]{1,0:T(2,128)} %get-tuple-element.60) | copy-start | bytes 52228
  30.3 4.7 %copy-start.32 = (f32[2,2176]{1,0:T(2,128)S(1)}, f32[2,2176]{1,0:T(2,128)}, u32[]{:S(2)}) copy-start(f32[2,2176]{1,0:T(2,128)} %get-tuple-element.61) | copy-start | bytes 52228
  30.3 4.7 %copy-start.33 = (f32[2,2176]{1,0:T(2,128)S(1)}, f32[2,2176]{1,0:T(2,128)}, u32[]{:S(2)}) copy-start(f32[2,2176]{1,0:T(2,128)} %pad_maximum_fusion.5) | copy-start | bytes 52228
  45.0 4.0 %copy-start.24 = (f32[2,2176]{1,0:T(2,128)S(1)}, f32[2,2176]{1,0:T(2,128)}, u32[]{:S(2)}) copy-start(f32[2,2176]{1,0:T(2,128)} %param.18) | copy-start | bytes 52228
  45.0 3.9 %copy-start.25 = (f32[2,2176]{1,0:T(2,128)S(1)}, f32[2,2176]{1,0:T(2,128)}, u32[]{:S(2)}) copy-start(f32[2,2176]{1,0:T(2,128)} %get-tuple-element.62) | copy-start | bytes 52228
  45.0 3.9 %copy-start.26 = (f32[2,2176]{1,0:T(2,128)S(1)}, f32[2,2176]{1,0:T(2,128)}, u32[]{:S(2)}) copy-start(f32[2,2176]{1,0:T(2,128)} %get-tuple-element.63) | copy-start | bytes 52228
  45.0 3.9 %copy-start.27 = (f32[2,2176]{1,0:T(2,128)S(1)}, f32[2,2176]{1,0:T(2,128)}, u32[]{:S(2)}) copy-start(f32[2,2176]{1,0:T(2,128)} %get-tuple-element.64) | copy-start | bytes 52228
  45.0 3.9 %copy-start.28 = (f32[2,2176]{1,0:T(2,128)S(1)}, f32[2,2176]{1,0:T(2,128)}, u32[]{:S(2)}) copy-start(f32[2,2176]{1,0:T(2,128)} %get-tuple-element.65) | copy-start | bytes 52228
  45.7 3.2 %copy-start.2 = (f32[2,32,4096]{2,1,0:T(8,128)}, f32[2,32,4096]{2,1,0:T(8,128)S(1)}, u32[]{:S(2)}) copy-start(f32[2,32,4096]{2,1,0:T(8,128)S(1)} %reshape.144) | copy-start | bytes 3145732
  46.8 23.5 %collective-permute-start.7 = (bf16[2,32,4224]{2,1,0:T(8,128)(2,1)}, bf16[2,32,4224]{2,1,0:T(8,128)(2,1)}, u32[]{:S(2)}, u32[]{:S(2)}) collective-permute-start(bf16[2,32,4224]{2,1,0:T(8,128)(2,1)} %fusion.56), channel_id=1, source_target_pairs={{15,14},{13,12},{11,10},{9,8},{7,6},{5,4},{3,2},{1,0},{31,30},{29,... | collective-permute-start | bytes 1622024 | tf_op jit(solution)/shard_map/ppermute | solution.py:42
  71.9 3.2 %collective-permute-start.8 = (bf16[2,32,4224]{2,1,0:T(8,128)(2,1)S(1)}, bf16[2,32,4224]{2,1,0:T(8,128)(2,1)S(1)}, u32[]{:S(2)}, u32[]{:S(2)}) collective-permute-start(bf16[2,32,4224]{2,1,0:T(8,128)(2,1)S(1)} %get-tuple-element.9), channel_id=1, source_target_pairs={{14,12},{12,14},{10,8},{8,10},{6,4},{4,6},{2,0},{0,2},{30,28},{28,... | collective-permute-start | bytes 1622024 | tf_op jit(solution)/shard_map/ppermute | solution.py:42
  72.7 5.6 %copy-start.41 = (bf16[1024,2048]{1,0:T(8,128)(2,1)S(1)}, bf16[1024,2048]{1,0:T(8,128)(2,1)}, u32[]{:S(2)}) copy-start(bf16[1024,2048]{1,0:T(8,128)(2,1)} %param.12) | copy-start | bytes 12582916
  73.6 15.4 %collective-permute-start.1 = (bf16[2,32,4224]{2,1,0:T(8,128)(2,1)}, bf16[2,32,4224]{2,1,0:T(8,128)(2,1)}, u32[]{:S(2)}, u32[]{:S(2)}) collective-permute-start(bf16[2,32,4224]{2,1,0:T(8,128)(2,1)} %fusion.57), channel_id=1, source_target_pairs={{0,1},{2,3},{4,5},{6,7},{8,9},{10,11},{12,13},{14,15},{16,17},{18,... | collective-permute-start | bytes 1622024 | tf_op jit(solution)/shard_map/ppermute | solution.py:42
  75.1 3.2 %copy-start.13 = (bf16[512,1024]{1,0:T(8,128)(2,1)S(1)}, bf16[512,1024]{1,0:T(8,128)(2,1)}, u32[]{:S(2)}) copy-start(bf16[512,1024]{1,0:T(8,128)(2,1)} %pad_maximum_fusion.2) | copy-start | bytes 3145732
  76.8 12.2 %collective-permute-start.9 = (bf16[2,32,4224]{2,1,0:T(8,128)(2,1)}, bf16[2,32,4224]{2,1,0:T(8,128)(2,1)}, u32[]{:S(2)}, u32[]{:S(2)}) collective-permute-start(bf16[2,32,4224]{2,1,0:T(8,128)(2,1)} %get-tuple-element.7), channel_id=1, source_target_pairs={{14,10},{12,8},{10,6},{8,4},{6,2},{4,0},{30,26},{28,24},{26,22},{2... | collective-permute-start | bytes 1622024 | tf_op jit(solution)/shard_map/ppermute | solution.py:42
  82.7 5.4 %copy-start.36 = (f32[2048]{0:T(1024)S(1)}, f32[2048]{0:T(1024)}, u32[]{:S(2)}) copy-start(f32[2048]{0:T(1024)} %param.20) | copy-start | bytes 24580
  89.0 8.3 %copy-start.39 = (f32[2,32]{1,0:T(2,128)S(1)}, f32[2,32]{1,0:T(2,128)}, u32[]{:S(2)}) copy-start(f32[2,32]{1,0:T(2,128)} %param.19) | copy-start | bytes 772
  91.0 12.5 %copy-start.12 = (bf16[2,32,4224]{2,1,0:T(8,128)(2,1)S(1)}, bf16[2,32,4224]{2,1,0:T(8,128)(2,1)}, u32[]{:S(2)}) copy-start(bf16[2,32,4224]{2,1,0:T(8,128)(2,1)} %copy-done.11) | copy-start | bytes 1622020
  91.0 12.4 %collective-permute-start.2 = (bf16[2,32,4224]{2,1,0:T(8,128)(2,1)S(1)}, bf16[2,32,4224]{2,1,0:T(8,128)(2,1)S(1)}, u32[]{:S(2)}, u32[]{:S(2)}) collective-permute-start(bf16[2,32,4224]{2,1,0:T(8,128)(2,1)S(1)} %get-tuple-element.15), channel_id=1, source_target_pairs={{1,3},{3,1},{5,7},{7,5},{9,11},{11,9},{13,15},{15,13},{17,19},{19,... | collective-permute-start | bytes 1622024 | tf_op jit(solution)/shard_map/ppermute | solution.py:42
  96.6 6.9 %collective-permute-start.10 = (bf16[2,32,4224]{2,1,0:T(8,128)(2,1)S(1)}, bf16[2,32,4224]{2,1,0:T(8,128)(2,1)S(1)}, u32[]{:S(2)}, u32[]{:S(2)}) collective-permute-start(bf16[2,32,4224]{2,1,0:T(8,128)(2,1)S(1)} %get-tuple-element.45), channel_id=1, source_target_pairs={{14,6},{12,4},{10,2},{8,0},{30,22},{28,20},{26,18},{24,16},{46,38}... | collective-permute-start | bytes 1622024 | tf_op jit(solution)/shard_map/ppermute | solution.py:42
  105.3 16.0 %copy-start.5 = (bf16[2,256,2048]{1,2,0:T(8,128)(2,1)S(1)}, bf16[2,256,2048]{1,2,0:T(8,128)(2,1)}, u32[]{:S(2)}) copy-start(bf16[2,256,2048]{1,2,0:T(8,128)(2,1)} %copy-done.4) | copy-start | bytes 6291460
  105.3 16.0 %copy-start.18 = (f32[2,32,256]{2,1,0:T(8,128)S(1)}, f32[2,32,256]{2,1,0:T(8,128)}, u32[]{:S(2)}) copy-start(f32[2,32,256]{2,1,0:T(8,128)} %copy-done.17) | copy-start | bytes 196612
  105.3 10.0 %collective-permute-start.3 = (bf16[2,32,4224]{2,1,0:T(8,128)(2,1)S(1)}, bf16[2,32,4224]{2,1,0:T(8,128)(2,1)S(1)}, u32[]{:S(2)}, u32[]{:S(2)}) collective-permute-start(bf16[2,32,4224]{2,1,0:T(8,128)(2,1)S(1)} %get-tuple-element.43), channel_id=1, source_target_pairs={{1,5},{3,7},{5,9},{7,11},{9,13},{11,15},{17,21},{19,23},{21,25},{2... | collective-permute-start | bytes 1622024 | tf_op jit(solution)/shard_map/ppermute | solution.py:42
  115.5 13.5 %collective-permute-start.4 = (bf16[2,32,4224]{2,1,0:T(8,128)(2,1)S(1)}, bf16[2,32,4224]{2,1,0:T(8,128)(2,1)S(1)}, u32[]{:S(2)}, u32[]{:S(2)}) collective-permute-start(bf16[2,32,4224]{2,1,0:T(8,128)(2,1)S(1)} %add_convert_fusion.1), channel_id=1, source_target_pairs={{1,9},{3,11},{5,13},{7,15},{17,25},{19,27},{21,29},{23,31},{33,41}... | collective-permute-start | bytes 1622024 | tf_op jit(solution)/shard_map/ppermute | solution.py:42
  127.4 5.4 %copy-start.8 = (bf16[2,256,2048]{1,2,0:T(8,128)(2,1)S(1)}, bf16[2,256,2048]{1,2,0:T(8,128)(2,1)}, u32[]{:S(2)}) copy-start(bf16[2,256,2048]{1,2,0:T(8,128)(2,1)} %copy-done.7) | copy-start | bytes 6291460
  127.4 13.5 %collective-permute-start.11 = (bf16[2,32,4224]{2,1,0:T(8,128)(2,1)S(1)}, bf16[2,32,4224]{2,1,0:T(8,128)(2,1)S(1)}, u32[]{:S(2)}, u32[]{:S(2)}) collective-permute-start(bf16[2,32,4224]{2,1,0:T(8,128)(2,1)S(1)} %get-tuple-element.5), channel_id=1, source_target_pairs={{14,15},{12,13},{10,11},{8,9},{6,7},{4,5},{2,3},{0,1},{30,31},{28,... | collective-permute-start | bytes 1622024 | tf_op jit(solution)/shard_map/ppermute | solution.py:42
  129.4 11.5 %collective-permute-start.5 = (bf16[2,32,4224]{2,1,0:T(8,128)(2,1)S(1)}, bf16[2,32,4224]{2,1,0:T(8,128)(2,1)S(1)}, u32[]{:S(2)}, u32[]{:S(2)}) collective-permute-start(bf16[2,32,4224]{2,1,0:T(8,128)(2,1)S(1)} %get-tuple-element.11), channel_id=1, source_target_pairs={{1,0},{3,2},{5,4},{7,6},{9,8},{11,10},{13,12},{15,14},{17,16},{19,... | collective-permute-start | bytes 1622024 | tf_op jit(solution)/shard_map/ppermute | solution.py:42
  138.5 2.4 %slice-start = ((pred[4224]{0:T(1024)(128)(4,1)}), pred[4096]{0:T(1024)(128)(4,1)S(1)}, s32[]{:S(2)}) async-start(pred[4224]{0:T(1024)(128)(4,1)} %copy-done.19), calls=%async_computation | async-start | bytes 8192 | tf_op jit(solution)/shard_map/slice | solution.py:58
  145.5 5.7 %copy-start.35 = (f32[2,256,32]{1,2,0:T(8,128)S(1)}, f32[2,256,32]{1,2,0:T(8,128)}, u32[]{:S(2)}) copy-start(f32[2,256,32]{1,2,0:T(8,128)} %get-tuple-element.35) | copy-start | bytes 196612
  147.7 3.6 %copy-start.6 = (bf16[2,256,2048]{1,2,0:T(8,128)(2,1)S(1)}, bf16[2,256,2048]{1,2,0:T(8,128)(2,1)}, u32[]{:S(2)}) copy-start(bf16[2,256,2048]{1,2,0:T(8,128)(2,1)} %copy-done.4) | copy-start | bytes 6291460
  147.7 3.6 %copy-start.9 = (bf16[2,256,2048]{1,2,0:T(8,128)(2,1)S(1)}, bf16[2,256,2048]{1,2,0:T(8,128)(2,1)}, u32[]{:S(2)}) copy-start(bf16[2,256,2048]{1,2,0:T(8,128)(2,1)} %copy-done.7) | copy-start | bytes 6291460
  147.7 3.6 %copy-start.16 = (f32[2,32,64,64]{3,2,1,0:T(8,128)S(1)}, f32[2,32,64,64]{3,2,1,0:T(8,128)}, u32[]{:S(2)}) copy-start(f32[2,32,64,64]{3,2,1,0:T(8,128)} %reshape.145) | copy-start | bytes 3145732
  147.7 3.6 %copy-start.34 = (f32[2,256,32]{1,2,0:T(8,128)S(1)}, f32[2,256,32]{1,2,0:T(8,128)}, u32[]{:S(2)}) copy-start(f32[2,256,32]{1,2,0:T(8,128)} %get-tuple-element.37) | copy-start | bytes 196612
  151.3 7.4 %copy-start.10 = (bf16[2048,1024]{1,0:T(8,128)(2,1)S(1)}, bf16[2048,1024]{1,0:T(8,128)(2,1)}, u32[]{:S(2)}) copy-start(bf16[2048,1024]{1,0:T(8,128)(2,1)} %param.21) | copy-start | bytes 12582916
  151.3 7.4 %copy-start.14 = (bf16[512,1024]{1,0:T(8,128)(2,1)S(1)}, bf16[512,1024]{1,0:T(8,128)(2,1)}, u32[]{:S(2)}) copy-start(bf16[512,1024]{1,0:T(8,128)(2,1)} %pad_maximum_fusion.2) | copy-start | bytes 3145732
  (7 other events, 11.9 us)

commit v9 on v7

--- a/solution.py
+++ b/solution.py
@@ -1,6 +1,8 @@
 import jax
 import jax.numpy as jnp
 from jax import lax
+from jax.experimental import pallas as pl
+from jax.experimental.pallas import tpu as pltpu
 from jax.sharding import PartitionSpec as P
 
 NS = 64
@@ -58,17 +60,51 @@
     return chained[..., : chained.shape[-1] - DECAY_LANES]
 
 
-def group_terms(window, dt_raw, dt_shift, log_rate, weights, offset, skip_heads, falling):
+def conv_kernel(x_ref, before_ref, after_ref, wr_ref, br_ref, wf_ref, bf_ref, rise_ref, fall_ref, pad):
+    length = x_ref.shape[1]
+    x = x_ref[0].astype(jnp.float32)
+    pad[pl.ds(0, K - 1), :] = before_ref[0].astype(jnp.float32)
+    pad[pl.ds(K - 1, length), :] = x
+    total = br_ref[0] + wr_ref[0, 0:1, :] * pad[pl.ds(0, length), :]
+    for k in range(1, K):
+        total = total + wr_ref[0, k : k + 1, :] * pad[pl.ds(k, length), :]
+    rise_ref[0] = jnp.transpose(jax.nn.silu(total)).astype(rise_ref.dtype)
+    pad[pl.ds(0, length), :] = x
+    pad[pl.ds(length, K - 1), :] = after_ref[0].astype(jnp.float32)
+    total = bf_ref[0] + wf_ref[0, 0:1, :] * pad[pl.ds(K - 1, length), :]
+    for k in range(1, K):
+        total = total + wf_ref[0, k : k + 1, :] * pad[pl.ds(K - 1 - k, length), :]
+    fall_ref[0] = jnp.transpose(jax.nn.silu(total)).astype(fall_ref.dtype)
+
+
+def convolve(projected, before, after, w_rise, b_rise, w_fall, b_fall):
+    runs, length, channels = projected.shape
+    lanes = 128
+    grid = (runs, channels // lanes)
+    rows = lambda r, c: (r, 0, c)
+    out_spec = pl.BlockSpec((1, lanes, length), lambda r, c: (r, c, 0))
+    rise, fall = pl.pallas_call(
+        conv_kernel,
+        grid=grid,
+        in_specs=[
+            pl.BlockSpec((1, length, lanes), rows),
+            pl.BlockSpec((1, K - 1, lanes), rows),
+            pl.BlockSpec((1, K - 1, lanes), rows),
+            pl.BlockSpec((1, K, lanes), rows),
+            pl.BlockSpec((1, 1, lanes), rows),
+            pl.BlockSpec((1, K, lanes), rows),
+            pl.BlockSpec((1, 1, lanes), rows),
+        ],
+        out_specs=[out_spec, out_spec],
+        out_shape=[jax.ShapeDtypeStruct((runs, channels, length), jnp.bfloat16)] * 2,
+        scratch_shapes=[pltpu.VMEM((length + 8, lanes), jnp.float32)],
+    )(projected, before, after, w_rise, b_rise[:, None, :], w_fall, b_fall[:, None, :])
+    return jnp.transpose(rise, (0, 2, 1)), jnp.transpose(fall, (0, 2, 1))
+
+
+def group_terms(conv, dt_raw, dt_shift, log_rate, skip_heads, falling):
     runs, length = dt_raw.shape[0], dt_raw.shape[1]
     heads = dt_raw.shape[2]
-    if falling:
-        taps = [window[:, K - 1 - k : K - 1 - k + length] for k in range(K)]
-    else:
-        taps = [window[:, k : k + length] for k in range(K)]
-    total = offset[:, None, :] + weights[:, 0][:, None, :] * taps[0].astype(jnp.float32)
-    for k in range(1, K):
-        total = total + weights[:, k][:, None, :] * taps[k].astype(jnp.float32)
-    conv = jax.nn.silu(total).astype(jnp.bfloat16)
     inner = conv.shape[2] - 2 * NS
     head_size = inner // heads
     values = conv[:, :, :inner].reshape(runs, length, heads, head_size)
@@ -140,25 +176,12 @@
     dt_raw = dt_raw.reshape(2, length, dt_raw.shape[1])
     before = shifted(projected[:, length - (K - 1) :], 1)
     after = shifted(projected[:, : K - 1], -1)
-    rising = group_terms(
-        jnp.concatenate([before, projected], axis=1),
-        dt_raw,
-        dt_bias,
-        decay_log,
-        conv_w,
-        conv_b,
-        skip_gain,
-        False,
-    )
+    conv_rise, conv_fall = convolve(
+        projected, before, after, conv_w, conv_b, swapped(conv_w), swapped(conv_b)
+    )
+    rising = group_terms(conv_rise, dt_raw, dt_bias, decay_log, skip_gain, False)
     falling = group_terms(
-        jnp.concatenate([projected, after], axis=1),
-        dt_raw,
-        swapped(dt_bias),
-        swapped(decay_log),
-        swapped(conv_w),
-        swapped(conv_b),
-        swapped(skip_gain),
-        True,
+        conv_fall, dt_raw, swapped(dt_bias), swapped(decay_log), swapped(skip_gain), True
     )
     rising_in = exclusive_chain(rising[3], 1)
     falling_in = exclusive_chain(falling[3], -1)

time: 159 us -> 151 us (0.950)
  other arithmetic: 37.4 us -> 10.5 us
  Pallas kernels: 0 us -> 21 us
  local copies, waits for them, and re-layouts: 36.3 us -> 29.2 us
  matrix products: 39.1 us -> 40.7 us
    pallas_call x0 -> x1, Pallas kernels: none -> 21 us  [convolve(): pl.pallas_call(conv_kernel, grid=grid, in_specs=[pl.BlockSpec((1, length,...]
    convert_element_type x1 -> x0, other arithmetic: 19.5 us -> none  [group_terms(): conv = jax.nn.silu(total).astype(jnp.bfloat16)]
    convert_element_type x8, other arithmetic: 9.37 us -> 5.25 us  [send(): moved = lax.ppermute(value.astype(jnp.bfloat16), 'ctx', pairs)]
    ppermute x2 -> x0, local copies, waits for them, and re-layouts: 3.57 us -> none  [shifted(): return lax.ppermute(value, 'ctx', pairs)]
    slice x2, local copies, waits for them, and re-layouts: 0.27 us -> 3.45 us  [group_terms(): values = conv[:, :, :inner].reshape(runs, length, heads, head_size)]
    reshape x1 -> x0, local copies, waits for them, and re-layouts: 2.46 us -> none  [body(): projected = projected.reshape(2, length, projected.shape[1])]
    reshape x2, local copies, waits for them, and re-layouts: 5.33 us -> 3.06 us  [finish(): entering.reshape(local.shape[0], local.shape[2], local.shape[3], NS)]
    convert_element_type x6, other arithmetic: 3.58 us -> 1.48 us  [send(): return moved.astype(jnp.float32)]
  transfers between devices with their start and end apart: 12 -> 12, of which waited for: 2 -> 2; matrix products, arithmetic and copies ran while one was open for 30% -> 27% of each run, Pallas kernels for 0% -> 0%
where the time goes in v9:
time: 151 us; the launch traced here: 149 us
  matrix products  40.7 us (27%)
  starting transfers between devices  36 us (24%)
  local copies, waits for them, and re-layouts  29.2 us (19%)
  Pallas kernels  21 us (14%)
  other arithmetic  10.5 us (7%)
  waiting for transfers between devices  10.5 us (7%)
    ppermute x10, starting transfers between devices, send(): moved = lax.ppermute(value.astype(jnp.bfloat16), 'ctx', pairs)  27.7 us
    pallas_call x1, Pallas kernels, convolve(): pl.pallas_call(conv_kernel, grid=grid, in_specs=[pl.BlockSpec((1, length,...  21 us
    dot_general x2, matrix products, group_terms(): jnp.einsum('rhts,rshp->rthp', mixing, scaled, preferred_element_type=jnp....  11.4 us
    ppermute x10, waiting for transfers between devices, send(): moved = lax.ppermute(value.astype(jnp.bfloat16), 'ctx', pairs)  10.5 us
    dot_general x2, matrix products, finish(): jnp.einsum('rtn,rhpn->rthp', reads.astype(jnp.float32), entering, precisi...  10.1 us
    ppermute x2, starting transfers between devices, shifted(): return lax.ppermute(value, 'ctx', pairs)  8.38 us
    dot_general x2, matrix products, group_terms(): jnp.einsum('rshp,rsn->rhpn', weighted, keys_in, preferred_element_type=jn...  5.75 us
    transpose x1, local copies, waits for them, and re-layouts, body(): jnp.transpose(gate.reshape(2, heads, head_size, length).astype(jnp.float3...  5.34 us
  transfers between devices with their start and end apart: 12, of which 2 were waited for; matrix products, arithmetic and copies ran while one was open for 27% of the time, Pallas kernels for 0%

profile of v9, /device:TPU:1, one launch (start us, length us, event | category | flops | bytes accessed | tf_op | source)
XLA Modules:
  0.0 148.7 jit_solution(14144270177629041645)
XLA Ops:
  0.0 3.4 %fusion.83 = (bf16[256,1,1024]{2,1,0:T(2,128)(2,1)S(1)}, bf16[256,1,1024]{2,1,0:T(2,128)(2,1)S(1)}) fusion(bf16[256,2,1024]{2,1,0:T(2,128)(2,1)} %param.11), kind=kLoop, calls=%fused_computation.139 | loop fusion | bytes 2097152 | tf_op jit(solution)/shard_map/slice | solution.py:169
  3.8 3.4 %convolution_convert_fusion = bf16[512,2176]{1,0:T(8,128)(2,1)S(1)} fusion(bf16[1024,2176]{1,0:T(8,128)(2,1)S(1)} %copy-done.26, bf16[256,1024]{1,0:T(8,128)(2,1)S(1)} %get-tuple-element.50, bf16[256,1024]{1,0:T(8,128)(2,1)S(1)} %get-tuple-element.51), kind=kOutput, calls=%fused_computation.20 | convolution fusion | flops 2284912640 | bytes 7733248 | tf_op jit(solution)/shard_map/dot_general | solution.py:173
  7.3 6.3 %collective-permute-start = (bf16[2,3,2176]{2,1,0:T(4,128)(2,1)S(1)}, bf16[2,3,2176]{2,1,0:T(4,128)(2,1)S(1)}, u32[]{:S(2)}, u32[]{:S(2)}) collective-permute-start(bf16[2,3,2176]{2,1,0:T(4,128)(2,1)S(1)} %get-tuple-element.22), channel_id=1, source_target_pairs={{0,1},{1,2},{2,3},{3,4},{4,5},{5,6},{6,7},{7,8},{8,9},{9,10},{10,1... | collective-permute-start | bytes 78344 | tf_op jit(solution)/shard_map/ppermute | solution.py:22
  13.6 2.1 %collective-permute-start.1 = (bf16[2,3,2176]{2,1,0:T(4,128)(2,1)S(1)}, bf16[2,3,2176]{2,1,0:T(4,128)(2,1)S(1)}, u32[]{:S(2)}, u32[]{:S(2)}) collective-permute-start(bf16[2,3,2176]{2,1,0:T(4,128)(2,1)S(1)} %get-tuple-element.21), channel_id=1, source_target_pairs={{1,0},{2,1},{3,2},{4,3},{5,4},{6,5},{7,6},{8,7},{9,8},{10,9},{11,1... | collective-permute-start | bytes 78344 | tf_op jit(solution)/shard_map/ppermute | solution.py:22
  15.7 1.0 pad_maximum_fusion.2
  17.8 0.6 bitcast_exponential_fusion
  18.9 0.6 pad_maximum_fusion.4.wf_ref
  19.6 0.6 broadcast_in_dim.43.br_ref
  20.2 0.6 broadcast_in_dim.44.bf_ref
  22.1 21.0 %shard_map.109 = (bf16[2,2176,256]{2,1,0:T(8,128)(2,1)}, bf16[2,2176,256]{2,1,0:T(8,128)(2,1)}) custom-call(bf16[2,256,2176]{2,1,0:T(8,128)(2,1)} %bitcast.107, bf16[2,3,2176]{2,1,0:T(4,128)(2,1)} %copy-done.20, bf16[2,3,2176]{2,1,0:T(4,128)(2,1)} %copy-done.21, f32[2,4,2176]{2,1,0:T(4,128)} %wr_ref.1, f32[2,1,2176]{2,1,0:T(1,128)} %broadcast_in_dim.43.br_ref, ...), custom_call_target="tpu_custom_call" | custom-call | tf_op jit(solution)/shard_map/pallas_call | solution.py:86
  43.0 1.7 %slice.163 = bf16[2,256,2048]{1,2,0:T(8,128)(2,1)S(1)} slice(bf16[2,256,2176]{1,2,0:T(8,128)(2,1)} %bitcast.108), slice={[0:2], [0:256], [0:2048]} | slice | bytes 4194304 | tf_op jit(solution)/shard_map/slice | solution.py:110
  44.8 1.4 copy-done.2
  46.1 2.9 %fusion.30 = f32[2,32,64,64]{3,2,1,0:T(8,128)} fusion(bf16[2,256,32,64]{1,3,2,0:T(8,128)(2,1)S(1)} %bitcast.92, f32[2,256,32]{1,2,0:T(8,128)S(1)} %get-tuple-element.32, bf16[2,256,2176]{1,2,0:T(8,128)(2,1)} %bitcast.109), kind=kOutput, calls=%fused_computation.38 | convolution fusion | flops 137363456 | bytes 3276800 | tf_op jit(solution)/shard_map/rshp,rsn->rhpn/dot_general | solution.py:138
  49.0 2.1 %reshape.142 = f32[2,32,4096]{2,1,0:T(8,128)S(1)} reshape(f32[2,32,64,64]{3,2,1,0:T(8,128)} %fusion.30) | data formatting | bytes 2097152 | tf_op jit(solution)/shard_map/reshape | solution.py:144
  51.3 1.3 collective-permute-start.7
  52.6 0.6 bitcast_exponential_fusion.1
  53.2 1.7 %slice.150 = bf16[2,256,2048]{1,2,0:T(8,128)(2,1)S(1)} slice(bf16[2,256,2176]{1,2,0:T(8,128)(2,1)} %bitcast.102), slice={[0:2], [0:256], [0:2048]} | slice | bytes 4194304 | tf_op jit(solution)/shard_map/slice | solution.py:110
  55.0 1.3 copy-done.5
  56.3 2.9 %fusion.33 = f32[2,32,64,64]{3,2,1,0:T(8,128)} fusion(bf16[2,256,32,64]{1,3,2,0:T(8,128)(2,1)S(1)} %bitcast.95, f32[2,256,32]{1,2,0:T(8,128)S(1)} %get-tuple-element.30, bf16[2,256,2176]{1,2,0:T(8,128)(2,1)} %bitcast.103), kind=kOutput, calls=%fused_computation.39 | convolution fusion | flops 137363456 | bytes 3276800 | tf_op jit(solution)/shard_map/rshp,rsn->rhpn/dot_general | solution.py:138
  59.2 2.1 %reshape.140 = f32[2,32,4096]{2,1,0:T(8,128)S(1)} reshape(f32[2,32,64,64]{3,2,1,0:T(8,128)} %fusion.33) | data formatting | bytes 2097152 | tf_op jit(solution)/shard_map/reshape | solution.py:144
  62.1 0.7 collective-permute-start.8
  62.9 0.9 fusion.49
  63.8 1.4 collective-permute-start.2
  65.5 1.2 fusion.77
  66.7 0.7 collective-permute-start.9
  67.4 4.4 %convert_bitcast_fusion = f32[2,2048,256]{1,2,0:T(8,128)} fusion(bf16[2,256,1024]{2,1,0:T(8,128)(2,1)S(1)} %bitcast.99, bf16[1024,2048]{1,0:T(8,128)(2,1)S(1)} %copy-done.27), kind=kOutput, calls=%fused_computation.33 | convolution fusion | flops 2149580800 | bytes 9437184 | tf_op jit(solution)/shard_map/rtd,de->ret/dot_general | solution.py:170
  71.8 5.3 %copy.41 = f32[2,2048,256]{2,1,0:T(8,128)} copy(f32[2,2048,256]{1,2,0:T(8,128)} %convert_bitcast_fusion) | data formatting | bytes 8388608 | tf_op jit(solution)/shard_map/transpose | solution.py:190
  77.3 1.4 fusion.81
  78.7 5.9 %collective-permute-start.3 = (bf16[2,32,4224]{2,1,0:T(8,128)(2,1)S(1)}, bf16[2,32,4224]{2,1,0:T(8,128)(2,1)S(1)}, u32[]{:S(2)}, u32[]{:S(2)}) collective-permute-start(bf16[2,32,4224]{2,1,0:T(8,128)(2,1)S(1)} %get-tuple-element.19), channel_id=1, source_target_pairs={{1,3},{3,1},{5,7},{7,5},{9,11},{11,9},{13,15},{15,13},{17,19},{19,... | collective-permute-start | bytes 1622024 | tf_op jit(solution)/shard_map/ppermute | solution.py:44
  84.6 0.9 collective-permute-start.10
  85.8 5.5 %collective-permute-done.3 = bf16[2,32,4224]{2,1,0:T(8,128)(2,1)S(1)} collective-permute-done((bf16[2,32,4224]{2,1,0:T(8,128)(2,1)S(1)}, bf16[2,32,4224]{2,1,0:T(8,128)(2,1)S(1)}, u32[]{:S(2)}, u32[]{:S(2)}) %collective-permute-start.3) | collective-permute-done | bytes 540704 | tf_op jit(solution)/shard_map/ppermute | solution.py:44
  91.5 0.8 fusion.76
  92.3 4.6 %collective-permute-start.4 = (bf16[2,32,4224]{2,1,0:T(8,128)(2,1)S(1)}, bf16[2,32,4224]{2,1,0:T(8,128)(2,1)S(1)}, u32[]{:S(2)}, u32[]{:S(2)}) collective-permute-start(bf16[2,32,4224]{2,1,0:T(8,128)(2,1)S(1)} %get-tuple-element.37), channel_id=1, source_target_pairs={{1,5},{3,7},{5,9},{7,11},{9,13},{11,15},{17,21},{19,23},{21,25},{2... | collective-permute-start | bytes 1622024 | tf_op jit(solution)/shard_map/ppermute | solution.py:44
  97.0 1.1 fusion.62
  98.2 5.0 %collective-permute-done.4 = bf16[2,32,4224]{2,1,0:T(8,128)(2,1)S(1)} collective-permute-done((bf16[2,32,4224]{2,1,0:T(8,128)(2,1)S(1)}, bf16[2,32,4224]{2,1,0:T(8,128)(2,1)S(1)}, u32[]{:S(2)}, u32[]{:S(2)}) %collective-permute-start.4) | collective-permute-done | bytes 540704 | tf_op jit(solution)/shard_map/ppermute | solution.py:44
  103.4 7.5 %collective-permute-start.5 = (bf16[2,32,4224]{2,1,0:T(8,128)(2,1)S(1)}, bf16[2,32,4224]{2,1,0:T(8,128)(2,1)S(1)}, u32[]{:S(2)}, u32[]{:S(2)}) collective-permute-start(bf16[2,32,4224]{2,1,0:T(8,128)(2,1)S(1)} %add_convert_fusion.1), channel_id=1, source_target_pairs={{1,9},{3,11},{5,13},{7,15},{17,25},{19,27},{21,29},{23,31},{33,41}... | collective-permute-start | bytes 1622024 | tf_op jit(solution)/shard_map/ppermute | solution.py:44
  110.9 5.7 %fusion.1 = f32[2,32,64,256]{3,2,1,0:T(8,128)} fusion(f32[2,32,256]{2,1,0:T(8,128)S(1)} %fusion.50, f32[2,256,256]{2,1,0:T(8,128)S(1)} %fusion.62, pred[256,256]{1,0:T(8,128)(4,1)S(1)} %iota_compare_fusion, bf16[2,256,32,64]{1,3,2,0:T(8,128)(2,1)S(1)} %bitcast.93, f32[2,256,32]{1,2,0:T(8,128)S(1)} %get-tuple-element.34), kind=kOutput, calls=%fused_computation.3 | convolution fusion | flops 556793856 | bytes 7012352 | tf_op jit(solution)/shard_map/rhts,rshp->rthp/dot_general | solution.py:134
  116.7 1.1 fusion.67
  117.8 1.4 collective-permute-start.11
  119.8 3.2 %collective-permute-start.6 = (bf16[2,32,4224]{2,1,0:T(8,128)(2,1)S(1)}, bf16[2,32,4224]{2,1,0:T(8,128)(2,1)S(1)}, u32[]{:S(2)}, u32[]{:S(2)}) collective-permute-start(bf16[2,32,4224]{2,1,0:T(8,128)(2,1)S(1)} %get-tuple-element.15), channel_id=1, source_target_pairs={{1,0},{3,2},{5,4},{7,6},{9,8},{11,10},{13,12},{15,14},{17,16},{19,... | collective-permute-start | bytes 1622024 | tf_op jit(solution)/shard_map/ppermute | solution.py:44
  123.1 5.7 %fusion = f32[2,32,64,256]{3,2,1,0:T(8,128)} fusion(f32[2,32,256]{2,1,0:T(8,128)S(1)} %fusion.52, f32[2,256,256]{2,1,0:T(8,128)S(1)} %fusion.67, pred[256,256]{1,0:T(8,128)(4,1)S(1)} %iota_compare_fusion.1, bf16[2,256,32,64]{1,3,2,0:T(8,128)(2,1)S(1)} %bitcast.96, f32[2,256,32]{1,2,0:T(8,128)S(1)} %get-tuple-element.33), kind=kOutput, calls=%fused_computation.2 | convolution fusion | flops 556793856 | bytes 7012352 | tf_op jit(solution)/shard_map/rhts,rshp->rthp/dot_general | solution.py:134
  128.9 1.1 convert_element_type.145
  130.6 2.2 %reshape.143 = f32[2,32,64,64]{3,2,1,0:T(8,128)} reshape(f32[2,32,4096]{2,1,0:T(8,128)S(1)} %get-tuple-element.40) | data formatting | bytes 2097152 | tf_op jit(solution)/shard_map/reshape | solution.py:154
  132.9 0.8 reshape.141
  133.7 2.8 %fusion.57 = f32[2,256,32,64]{1,3,2,0:T(8,128)S(1)} fusion(f32[2,32,64,64]{3,2,1,0:T(8,128)S(1)} %reshape.141, bf16[2,256,2176]{1,2,0:T(8,128)(2,1)} %bitcast.105), kind=kOutput, calls=%fused_computation.90 | convolution fusion | flops 805306368 | bytes 5308416 | tf_op jit(solution)/shard_map/rtn,rhpn->rthp/dot_general | solution.py:155
  136.6 7.3 %multiply_reduce_fusion = (f32[2,256]{1,0:T(2,128)S(1)}, f32[2,256,32,64]{1,3,2,0:T(8,128)S(1)}) fusion(f32[2,256,32,64]{1,3,2,0:T(8,128)} %bitcast.101, f32[2,256,32]{1,2,0:T(8,128)S(1)} %copy-done.18, f32[2,32,64,64]{3,2,1,0:T(8,128)S(1)} %copy-done.14, bf16[2,256,2176]{1,2,0:T(8,128)(2,1)} %bitcast.111, bf16[2,256,32,64]{1,3,2,0:T(8,128)(2,1)S(1)} %bitcast.94, ...), kind=kOutput, calls=%fused_computation.35 | convolution fusion | flops 824180224 | bytes 26413568 | tf_op jit(solution)/shard_map/rtn,rhpn->rthp/dot_general | solution.py:155
  144.0 2.4 %fusion.36 = bf16[2,256,1024]{2,1,0:T(8,128)(2,1)S(1)} fusion(bf16[2,256,1024]{2,1,0:T(8,128)(2,1)S(1)} %bitcast.100, bf16[32,64,1024,1]{2,1,0,3:T(8,128)(2,1)S(1)} %bitcast.98, f32[2,256,32,64]{1,3,2,0:T(8,128)S(1)} %get-tuple-element.49, f32[32,64]{1,0:T(8,128)S(1)} %mul.325, f32[2,256]{1,0:T(2,128)S(1)} %add_rsqrt_fusion), kind=kOutput, calls=%fused_computation.41 | convolution fusion | flops 2152202240 | bytes 10496000 | tf_op jit(solution)/shard_map/rthp,hpd->rtd/dot_general | solution.py:198
  146.6 2.0 %copy.42 = bf16[256,2,1024]{2,1,0:T(2,128)(2,1)} copy(bf16[256,2,1024]{2,0,1:T(8,128)(2,1)S(1)} %pad_maximum_fusion.3) | data formatting | bytes 2097152 | tf_op jit(solution)/shard_map/stack | solution.py:207
  (115 shorter events, 6.9 us)
Async XLA Ops:
  0.0 16.8 %copy-start = (bf16[1024,32]{0,1:T(8,128)(2,1)S(1)}, bf16[1024,32]{0,1:T(8,128)(2,1)}, u32[]{:S(2)}) copy-start(bf16[1024,32]{0,1:T(8,128)(2,1)} %param.14) | copy-start | bytes 196612
  0.0 3.8 %copy-start.26 = (bf16[1024,2176]{1,0:T(8,128)(2,1)S(1)}, bf16[1024,2176]{1,0:T(8,128)(2,1)}, u32[]{:S(2)}) copy-start(bf16[1024,2176]{1,0:T(8,128)(2,1)} %param.13) | copy-start | bytes 13369348
  7.2 10.2 %copy-start.11 = (bf16[512,2176]{1,0:T(8,128)(2,1)}, bf16[512,2176]{1,0:T(8,128)(2,1)S(1)}, u32[]{:S(2)}) copy-start(bf16[512,2176]{1,0:T(8,128)(2,1)S(1)} %convolution_convert_fusion) | copy-start | bytes 6684676
  7.2 9.5 %copy-start.24 = (f32[2,32]{1,0:T(2,128)S(1)}, f32[2,32]{1,0:T(2,128)}, u32[]{:S(2)}) copy-start(f32[2,32]{1,0:T(2,128)} %param.16) | copy-start | bytes 772
  7.2 10.0 %copy-start.23 = (f32[2,32]{1,0:T(2,128)S(1)}, f32[2,32]{1,0:T(2,128)}, u32[]{:S(2)}) copy-start(f32[2,32]{1,0:T(2,128)} %param.15) | copy-start | bytes 772
  7.3 13.6 %collective-permute-start = (bf16[2,3,2176]{2,1,0:T(4,128)(2,1)S(1)}, bf16[2,3,2176]{2,1,0:T(4,128)(2,1)S(1)}, u32[]{:S(2)}, u32[]{:S(2)}) collective-permute-start(bf16[2,3,2176]{2,1,0:T(4,128)(2,1)S(1)} %get-tuple-element.22), channel_id=1, source_target_pairs={{0,1},{1,2},{2,3},{3,4},{4,5},{5,6},{6,7},{7,8},{8,9},{9,10},{10,1... | collective-permute-start | bytes 78344 | tf_op jit(solution)/shard_map/ppermute | solution.py:22
  13.6 4.8 %copy-start.16 = (f32[2,4,2176]{2,1,0:T(4,128)S(1)}, f32[2,4,2176]{2,1,0:T(4,128)}, u32[]{:S(2)}) copy-start(f32[2,4,2176]{2,1,0:T(4,128)} %wr_ref.1) | copy-start | bytes 208900
  13.6 4.8 %copy-start.17 = (f32[2,2176]{1,0:T(2,128)S(1)}, f32[2,2176]{1,0:T(2,128)}, u32[]{:S(2)}) copy-start(f32[2,2176]{1,0:T(2,128)} %param.18) | copy-start | bytes 52228
  13.6 7.2 %collective-permute-start.1 = (bf16[2,3,2176]{2,1,0:T(4,128)(2,1)S(1)}, bf16[2,3,2176]{2,1,0:T(4,128)(2,1)S(1)}, u32[]{:S(2)}, u32[]{:S(2)}) collective-permute-start(bf16[2,3,2176]{2,1,0:T(4,128)(2,1)S(1)} %get-tuple-element.21), channel_id=1, source_target_pairs={{1,0},{2,1},{3,2},{4,3},{5,4},{6,5},{7,6},{8,7},{9,8},{10,9},{11,1... | collective-permute-start | bytes 78344 | tf_op jit(solution)/shard_map/ppermute | solution.py:22
  19.6 99.8 %copy-start.15 = (pred[4224]{0:T(1024)(128)(4,1)}, pred[4224]{0:T(1024)(128)(4,1)S(1)}, u32[]{:S(2)}) copy-start(pred[4224]{0:T(1024)(128)(4,1)S(1)} %iota_compare_fusion.4) | copy-start | bytes 12676
  20.8 0.6 copy-start.20
  21.4 0.6 copy-start.21
  44.8 1.4 copy-start.2
  51.3 10.0 %collective-permute-start.7 = (bf16[2,32,4224]{2,1,0:T(8,128)(2,1)S(1)}, bf16[2,32,4224]{2,1,0:T(8,128)(2,1)S(1)}, u32[]{:S(2)}, u32[]{:S(2)}) collective-permute-start(bf16[2,32,4224]{2,1,0:T(8,128)(2,1)S(1)} %fusion.48), channel_id=1, source_target_pairs={{15,14},{13,12},{11,10},{9,8},{7,6},{5,4},{3,2},{1,0},{31,30},{29,... | collective-permute-start | bytes 1622024 | tf_op jit(solution)/shard_map/ppermute | solution.py:44
  55.0 1.3 copy-start.5
  61.3 0.8 copy-start.12
  62.1 3.2 %collective-permute-start.8 = (bf16[2,32,4224]{2,1,0:T(8,128)(2,1)S(1)}, bf16[2,32,4224]{2,1,0:T(8,128)(2,1)S(1)}, u32[]{:S(2)}, u32[]{:S(2)}) collective-permute-start(bf16[2,32,4224]{2,1,0:T(8,128)(2,1)S(1)} %get-tuple-element.13), channel_id=1, source_target_pairs={{14,12},{12,14},{10,8},{8,10},{6,4},{4,6},{2,0},{0,2},{30,28},{28,... | collective-permute-start | bytes 1622024 | tf_op jit(solution)/shard_map/ppermute | solution.py:44
  62.9 4.5 %copy-start.27 = (bf16[1024,2048]{1,0:T(8,128)(2,1)S(1)}, bf16[1024,2048]{1,0:T(8,128)(2,1)}, u32[]{:S(2)}) copy-start(bf16[1024,2048]{1,0:T(8,128)(2,1)} %param.12) | copy-start | bytes 12582916
  63.8 13.5 %collective-permute-start.2 = (bf16[2,32,4224]{2,1,0:T(8,128)(2,1)}, bf16[2,32,4224]{2,1,0:T(8,128)(2,1)}, u32[]{:S(2)}, u32[]{:S(2)}) collective-permute-start(bf16[2,32,4224]{2,1,0:T(8,128)(2,1)} %fusion.49), channel_id=1, source_target_pairs={{0,1},{2,3},{4,5},{6,7},{8,9},{10,11},{12,13},{14,15},{16,17},{18,... | collective-permute-start | bytes 1622024 | tf_op jit(solution)/shard_map/ppermute | solution.py:44
  65.3 2.1 %copy-start.9 = (bf16[512,1024]{1,0:T(8,128)(2,1)S(1)}, bf16[512,1024]{1,0:T(8,128)(2,1)}, u32[]{:S(2)}) copy-start(bf16[512,1024]{1,0:T(8,128)(2,1)} %pad_maximum_fusion.2) | copy-start | bytes 3145732
  66.7 10.6 %collective-permute-start.9 = (bf16[2,32,4224]{2,1,0:T(8,128)(2,1)}, bf16[2,32,4224]{2,1,0:T(8,128)(2,1)S(1)}, u32[]{:S(2)}, u32[]{:S(2)}) collective-permute-start(bf16[2,32,4224]{2,1,0:T(8,128)(2,1)} %get-tuple-element.11), channel_id=1, source_target_pairs={{14,10},{12,8},{10,6},{8,4},{6,2},{4,0},{30,26},{28,24},{26,22},{2... | collective-permute-start | bytes 1622024 | tf_op jit(solution)/shard_map/ppermute | solution.py:44
  71.8 5.3 %copy-start.22 = (f32[2048]{0:T(1024)S(1)}, f32[2048]{0:T(1024)}, u32[]{:S(2)}) copy-start(f32[2048]{0:T(1024)} %param.20) | copy-start | bytes 24580
  77.3 8.3 %copy-start.25 = (f32[2,32]{1,0:T(2,128)S(1)}, f32[2,32]{1,0:T(2,128)}, u32[]{:S(2)}) copy-start(f32[2,32]{1,0:T(2,128)} %param.19) | copy-start | bytes 772
  78.7 12.6 %collective-permute-start.3 = (bf16[2,32,4224]{2,1,0:T(8,128)(2,1)S(1)}, bf16[2,32,4224]{2,1,0:T(8,128)(2,1)S(1)}, u32[]{:S(2)}, u32[]{:S(2)}) collective-permute-start(bf16[2,32,4224]{2,1,0:T(8,128)(2,1)S(1)} %get-tuple-element.19), channel_id=1, source_target_pairs={{1,3},{3,1},{5,7},{7,5},{9,11},{11,9},{13,15},{15,13},{17,19},{19,... | collective-permute-start | bytes 1622024 | tf_op jit(solution)/shard_map/ppermute | solution.py:44
  84.6 6.9 %collective-permute-start.10 = (bf16[2,32,4224]{2,1,0:T(8,128)(2,1)S(1)}, bf16[2,32,4224]{2,1,0:T(8,128)(2,1)S(1)}, u32[]{:S(2)}, u32[]{:S(2)}) collective-permute-start(bf16[2,32,4224]{2,1,0:T(8,128)(2,1)S(1)} %get-tuple-element.39), channel_id=1, source_target_pairs={{14,6},{12,4},{10,2},{8,0},{30,22},{28,20},{26,18},{24,16},{46,38}... | collective-permute-start | bytes 1622024 | tf_op jit(solution)/shard_map/ppermute | solution.py:44
  92.3 18.7 %copy-start.3 = (bf16[2,256,2048]{1,2,0:T(8,128)(2,1)S(1)}, bf16[2,256,2048]{1,2,0:T(8,128)(2,1)}, u32[]{:S(2)}) copy-start(bf16[2,256,2048]{1,2,0:T(8,128)(2,1)} %copy-done.2) | copy-start | bytes 6291460
  92.3 10.9 %collective-permute-start.4 = (bf16[2,32,4224]{2,1,0:T(8,128)(2,1)S(1)}, bf16[2,32,4224]{2,1,0:T(8,128)(2,1)S(1)}, u32[]{:S(2)}, u32[]{:S(2)}) collective-permute-start(bf16[2,32,4224]{2,1,0:T(8,128)(2,1)S(1)} %get-tuple-element.37), channel_id=1, source_target_pairs={{1,5},{3,7},{5,9},{7,11},{9,13},{11,15},{17,21},{19,23},{21,25},{2... | collective-permute-start | bytes 1622024 | tf_op jit(solution)/shard_map/ppermute | solution.py:44
  103.4 16.0 %collective-permute-start.5 = (bf16[2,32,4224]{2,1,0:T(8,128)(2,1)S(1)}, bf16[2,32,4224]{2,1,0:T(8,128)(2,1)S(1)}, u32[]{:S(2)}, u32[]{:S(2)}) collective-permute-start(bf16[2,32,4224]{2,1,0:T(8,128)(2,1)S(1)} %add_convert_fusion.1), channel_id=1, source_target_pairs={{1,9},{3,11},{5,13},{7,15},{17,25},{19,27},{21,29},{23,31},{33,41}... | collective-permute-start | bytes 1622024 | tf_op jit(solution)/shard_map/ppermute | solution.py:44
  117.8 5.3 %copy-start.6 = (bf16[2,256,2048]{1,2,0:T(8,128)(2,1)S(1)}, bf16[2,256,2048]{1,2,0:T(8,128)(2,1)}, u32[]{:S(2)}) copy-start(bf16[2,256,2048]{1,2,0:T(8,128)(2,1)} %copy-done.5) | copy-start | bytes 6291460
  117.8 12.4 %collective-permute-start.11 = (bf16[2,32,4224]{2,1,0:T(8,128)(2,1)S(1)}, bf16[2,32,4224]{2,1,0:T(8,128)(2,1)S(1)}, u32[]{:S(2)}, u32[]{:S(2)}) collective-permute-start(bf16[2,32,4224]{2,1,0:T(8,128)(2,1)S(1)} %get-tuple-element.9), channel_id=1, source_target_pairs={{14,15},{12,13},{10,11},{8,9},{6,7},{4,5},{2,3},{0,1},{30,31},{28,... | collective-permute-start | bytes 1622024 | tf_op jit(solution)/shard_map/ppermute | solution.py:44
  119.8 9.0 %copy-start.13 = (bf16[2,32,4224]{2,1,0:T(8,128)(2,1)S(1)}, bf16[2,32,4224]{2,1,0:T(8,128)(2,1)}, u32[]{:S(2)}) copy-start(bf16[2,32,4224]{2,1,0:T(8,128)(2,1)} %copy-done.12) | copy-start | bytes 1622020
  119.8 10.3 %collective-permute-start.6 = (bf16[2,32,4224]{2,1,0:T(8,128)(2,1)S(1)}, bf16[2,32,4224]{2,1,0:T(8,128)(2,1)S(1)}, u32[]{:S(2)}, u32[]{:S(2)}) collective-permute-start(bf16[2,32,4224]{2,1,0:T(8,128)(2,1)S(1)} %get-tuple-element.15), channel_id=1, source_target_pairs={{1,0},{3,2},{5,4},{7,6},{9,8},{11,10},{13,12},{15,14},{17,16},{19,... | collective-permute-start | bytes 1622024 | tf_op jit(solution)/shard_map/ppermute | solution.py:44
  128.8 1.4 slice-start
  132.9 3.7 %copy-start.19 = (f32[2,256,32]{1,2,0:T(8,128)S(1)}, f32[2,256,32]{1,2,0:T(8,128)}, u32[]{:S(2)}) copy-start(f32[2,256,32]{1,2,0:T(8,128)} %get-tuple-element.29) | copy-start | bytes 196612
  133.7 2.8 %copy-start.4 = (bf16[2,256,2048]{1,2,0:T(8,128)(2,1)S(1)}, bf16[2,256,2048]{1,2,0:T(8,128)(2,1)}, u32[]{:S(2)}) copy-start(bf16[2,256,2048]{1,2,0:T(8,128)(2,1)} %copy-done.2) | copy-start | bytes 6291460
  133.7 2.8 %copy-start.7 = (bf16[2,256,2048]{1,2,0:T(8,128)(2,1)S(1)}, bf16[2,256,2048]{1,2,0:T(8,128)(2,1)}, u32[]{:S(2)}) copy-start(bf16[2,256,2048]{1,2,0:T(8,128)(2,1)} %copy-done.5) | copy-start | bytes 6291460
  133.7 2.9 %copy-start.14 = (f32[2,32,64,64]{3,2,1,0:T(8,128)S(1)}, f32[2,32,64,64]{3,2,1,0:T(8,128)}, u32[]{:S(2)}) copy-start(f32[2,32,64,64]{3,2,1,0:T(8,128)} %reshape.143) | copy-start | bytes 3145732
  133.7 2.9 %copy-start.18 = (f32[2,256,32]{1,2,0:T(8,128)S(1)}, f32[2,256,32]{1,2,0:T(8,128)}, u32[]{:S(2)}) copy-start(f32[2,256,32]{1,2,0:T(8,128)} %get-tuple-element.31) | copy-start | bytes 196612
  136.6 7.4 %copy-start.8 = (bf16[2048,1024]{1,0:T(8,128)(2,1)S(1)}, bf16[2048,1024]{1,0:T(8,128)(2,1)}, u32[]{:S(2)}) copy-start(bf16[2048,1024]{1,0:T(8,128)(2,1)} %param.21) | copy-start | bytes 12582916
  136.6 7.4 %copy-start.10 = (bf16[512,1024]{1,0:T(8,128)(2,1)S(1)}, bf16[512,1024]{1,0:T(8,128)(2,1)}, u32[]{:S(2)}) copy-start(bf16[512,1024]{1,0:T(8,128)(2,1)} %pad_maximum_fusion.2) | copy-start | bytes 3145732
  146.5 2.2 %copy-start.1 = (bf16[1024,32]{0,1:T(8,128)(2,1)S(1)}, bf16[1024,32]{0,1:T(8,128)(2,1)}, u32[]{:S(2)}) copy-start(bf16[1024,32]{0,1:T(8,128)(2,1)} %param.14) | copy-start | bytes 196612

commit v10 on v9

--- a/solution.py
+++ b/solution.py
@@ -79,7 +79,7 @@
 
 def convolve(projected, before, after, w_rise, b_rise, w_fall, b_fall):
     runs, length, channels = projected.shape
-    lanes = 128
+    lanes = channels
     grid = (runs, channels // lanes)
     rows = lambda r, c: (r, 0, c)
     out_spec = pl.BlockSpec((1, lanes, length), lambda r, c: (r, c, 0))

time: 151 us -> 138 us (0.914); the launches traced: 149 us -> 138 us
  Pallas kernels: 21 us -> 9.66 us
    pallas_call x1, Pallas kernels: 21 us -> 9.66 us  [convolve(): pl.pallas_call(conv_kernel, grid=grid, in_specs=[pl.BlockSpec((1, length,...]
  transfers between devices with their start and end apart: 12 -> 12, of which waited for: 2 -> 2; matrix products, arithmetic and copies ran while one was open for 27% -> 30% of each run, Pallas kernels for 0% -> 0%
where the time goes in v10:
time: 138 us
  matrix products  40.7 us (29%)
  starting transfers between devices  36.1 us (26%)
  local copies, waits for them, and re-layouts  29.2 us (21%)
  waiting for transfers between devices  10.7 us (8%)
  other arithmetic  10.5 us (8%)
  Pallas kernels  9.66 us (7%)
    ppermute x10, starting transfers between devices, send(): moved = lax.ppermute(value.astype(jnp.bfloat16), 'ctx', pairs)  27.7 us
    dot_general x2, matrix products, group_terms(): jnp.einsum('rhts,rshp->rthp', mixing, scaled, preferred_element_type=jnp....  11.4 us
    ppermute x10, waiting for transfers between devices, send(): moved = lax.ppermute(value.astype(jnp.bfloat16), 'ctx', pairs)  10.7 us
    dot_general x2, matrix products, finish(): jnp.einsum('rtn,rhpn->rthp', reads.astype(jnp.float32), entering, precisi...  10.1 us
    pallas_call x1, Pallas kernels, convolve(): pl.pallas_call(conv_kernel, grid=grid, in_specs=[pl.BlockSpec((1, length,...  9.66 us
    ppermute x2, starting transfers between devices, shifted(): return lax.ppermute(value, 'ctx', pairs)  8.38 us
    dot_general x2, matrix products, group_terms(): jnp.einsum('rshp,rsn->rhpn', weighted, keys_in, preferred_element_type=jn...  5.74 us
    transpose x1, local copies, waits for them, and re-layouts, body(): jnp.transpose(gate.reshape(2, heads, head_size, length).astype(jnp.float3...  5.34 us
  transfers between devices with their start and end apart: 12, of which 2 were waited for; matrix products, arithmetic and copies ran while one was open for 30% of the time, Pallas kernels for 0%

profile of v10, /device:TPU:1, one launch (start us, length us, event | category | flops | bytes accessed | tf_op | source)
XLA Modules:
  0.0 137.6 jit_solution(15927077093515104798)
XLA Ops:
  0.0 3.4 %fusion.83 = (bf16[256,1,1024]{2,1,0:T(2,128)(2,1)S(1)}, bf16[256,1,1024]{2,1,0:T(2,128)(2,1)S(1)}) fusion(bf16[256,2,1024]{2,1,0:T(2,128)(2,1)} %param.11), kind=kLoop, calls=%fused_computation.139 | loop fusion | bytes 2097152 | tf_op jit(solution)/shard_map/slice | solution.py:169
  3.8 3.4 %convolution_convert_fusion = bf16[512,2176]{1,0:T(8,128)(2,1)S(1)} fusion(bf16[1024,2176]{1,0:T(8,128)(2,1)S(1)} %copy-done.26, bf16[256,1024]{1,0:T(8,128)(2,1)S(1)} %get-tuple-element.50, bf16[256,1024]{1,0:T(8,128)(2,1)S(1)} %get-tuple-element.51), kind=kOutput, calls=%fused_computation.20 | convolution fusion | flops 2284912640 | bytes 7733248 | tf_op jit(solution)/shard_map/dot_general | solution.py:173
  7.3 6.3 %collective-permute-start = (bf16[2,3,2176]{2,1,0:T(4,128)(2,1)S(1)}, bf16[2,3,2176]{2,1,0:T(4,128)(2,1)S(1)}, u32[]{:S(2)}, u32[]{:S(2)}) collective-permute-start(bf16[2,3,2176]{2,1,0:T(4,128)(2,1)S(1)} %get-tuple-element.22), channel_id=1, source_target_pairs={{0,1},{1,2},{2,3},{3,4},{4,5},{5,6},{6,7},{7,8},{8,9},{9,10},{10,1... | collective-permute-start | bytes 78344 | tf_op jit(solution)/shard_map/ppermute | solution.py:22
  13.6 2.1 %collective-permute-start.1 = (bf16[2,3,2176]{2,1,0:T(4,128)(2,1)S(1)}, bf16[2,3,2176]{2,1,0:T(4,128)(2,1)S(1)}, u32[]{:S(2)}, u32[]{:S(2)}) collective-permute-start(bf16[2,3,2176]{2,1,0:T(4,128)(2,1)S(1)} %get-tuple-element.21), channel_id=1, source_target_pairs={{1,0},{2,1},{3,2},{4,3},{5,4},{6,5},{7,6},{8,7},{9,8},{10,9},{11,1... | collective-permute-start | bytes 78344 | tf_op jit(solution)/shard_map/ppermute | solution.py:22
  15.7 1.0 pad_maximum_fusion.2
  17.8 0.6 bitcast_exponential_fusion
  18.9 0.6 pad_maximum_fusion.4.wf_ref
  19.6 0.6 broadcast_in_dim.43.br_ref
  20.2 0.6 broadcast_in_dim.44.bf_ref
  22.1 9.7 %shard_map.109 = (bf16[2,2176,256]{2,1,0:T(8,128)(2,1)}, bf16[2,2176,256]{2,1,0:T(8,128)(2,1)}) custom-call(bf16[2,256,2176]{2,1,0:T(8,128)(2,1)} %bitcast.107, bf16[2,3,2176]{2,1,0:T(4,128)(2,1)} %copy-done.20, bf16[2,3,2176]{2,1,0:T(4,128)(2,1)} %copy-done.21, f32[2,4,2176]{2,1,0:T(4,128)} %wr_ref.1, f32[2,1,2176]{2,1,0:T(1,128)} %broadcast_in_dim.43.br_ref, ...), custom_call_target="tpu_custom_call" | custom-call | tf_op jit(solution)/shard_map/pallas_call | solution.py:86
  31.7 1.7 %slice.163 = bf16[2,256,2048]{1,2,0:T(8,128)(2,1)S(1)} slice(bf16[2,256,2176]{1,2,0:T(8,128)(2,1)} %bitcast.108), slice={[0:2], [0:256], [0:2048]} | slice | bytes 4194304 | tf_op jit(solution)/shard_map/slice | solution.py:110
  33.5 1.4 copy-done.2
  34.8 2.9 %fusion.30 = f32[2,32,64,64]{3,2,1,0:T(8,128)} fusion(bf16[2,256,32,64]{1,3,2,0:T(8,128)(2,1)S(1)} %bitcast.92, f32[2,256,32]{1,2,0:T(8,128)S(1)} %get-tuple-element.32, bf16[2,256,2176]{1,2,0:T(8,128)(2,1)} %bitcast.109), kind=kOutput, calls=%fused_computation.38 | convolution fusion | flops 137363456 | bytes 3276800 | tf_op jit(solution)/shard_map/rshp,rsn->rhpn/dot_general | solution.py:138
  37.7 2.1 %reshape.142 = f32[2,32,4096]{2,1,0:T(8,128)S(1)} reshape(f32[2,32,64,64]{3,2,1,0:T(8,128)} %fusion.30) | data formatting | bytes 2097152 | tf_op jit(solution)/shard_map/reshape | solution.py:144
  39.9 1.3 collective-permute-start.7
  41.3 0.6 bitcast_exponential_fusion.1
  41.9 1.7 %slice.150 = bf16[2,256,2048]{1,2,0:T(8,128)(2,1)S(1)} slice(bf16[2,256,2176]{1,2,0:T(8,128)(2,1)} %bitcast.102), slice={[0:2], [0:256], [0:2048]} | slice | bytes 4194304 | tf_op jit(solution)/shard_map/slice | solution.py:110
  43.7 1.3 copy-done.5
  45.0 2.9 %fusion.33 = f32[2,32,64,64]{3,2,1,0:T(8,128)} fusion(bf16[2,256,32,64]{1,3,2,0:T(8,128)(2,1)S(1)} %bitcast.95, f32[2,256,32]{1,2,0:T(8,128)S(1)} %get-tuple-element.30, bf16[2,256,2176]{1,2,0:T(8,128)(2,1)} %bitcast.103), kind=kOutput, calls=%fused_computation.39 | convolution fusion | flops 137363456 | bytes 3276800 | tf_op jit(solution)/shard_map/rshp,rsn->rhpn/dot_general | solution.py:138
  47.8 2.1 %reshape.140 = f32[2,32,4096]{2,1,0:T(8,128)S(1)} reshape(f32[2,32,64,64]{3,2,1,0:T(8,128)} %fusion.33) | data formatting | bytes 2097152 | tf_op jit(solution)/shard_map/reshape | solution.py:144
  50.8 0.7 collective-permute-start.8
  51.5 0.9 fusion.49
  52.5 1.6 %collective-permute-start.2 = (bf16[2,32,4224]{2,1,0:T(8,128)(2,1)}, bf16[2,32,4224]{2,1,0:T(8,128)(2,1)}, u32[]{:S(2)}, u32[]{:S(2)}) collective-permute-start(bf16[2,32,4224]{2,1,0:T(8,128)(2,1)} %fusion.49), channel_id=1, source_target_pairs={{0,1},{2,3},{4,5},{6,7},{8,9},{10,11},{12,13},{14,15},{16,17},{18,... | collective-permute-start | bytes 1622024 | tf_op jit(solution)/shard_map/ppermute | solution.py:44
  54.3 1.2 fusion.77
  55.5 0.7 collective-permute-start.9
  56.2 4.4 %convert_bitcast_fusion = f32[2,2048,256]{1,2,0:T(8,128)} fusion(bf16[2,256,1024]{2,1,0:T(8,128)(2,1)S(1)} %bitcast.99, bf16[1024,2048]{1,0:T(8,128)(2,1)S(1)} %copy-done.27), kind=kOutput, calls=%fused_computation.33 | convolution fusion | flops 2149580800 | bytes 9437184 | tf_op jit(solution)/shard_map/rtd,de->ret/dot_general | solution.py:170
  60.6 5.3 %copy.41 = f32[2,2048,256]{2,1,0:T(8,128)} copy(f32[2,2048,256]{1,2,0:T(8,128)} %convert_bitcast_fusion) | data formatting | bytes 8388608 | tf_op jit(solution)/shard_map/transpose | solution.py:190
  66.1 1.4 %fusion.81 = (bf16[2,32,4224]{2,1,0:T(8,128)(2,1)S(1)}, f32[2,32,4224]{2,1,0:T(8,128)S(1)}, bf16[2,32,4224]{2,1,0:T(8,128)(2,1)S(1)}) fusion(f32[2,32,128]{2,1,0:T(8,128)S(1)} %broadcast_in_dim.82, f32[2,32,4096]{2,1,0:T(8,128)S(1)} %reshape.140, pred[4224]{0:T(1024)(128)(4,1)S(1)} %iota_compare_fusion.4, bf16[2,32,4224]{2,1,0:T(8,128)(2,1)} %collective-permute-done.2, ...), kind=kLoop, calls=%fused_computation.137 | loop fusion | flops 2973696 | bytes 5411456 | tf_op jit(solution)/shard_map/convert_element_type | solution.py:44
  67.6 5.9 %collective-permute-start.3 = (bf16[2,32,4224]{2,1,0:T(8,128)(2,1)S(1)}, bf16[2,32,4224]{2,1,0:T(8,128)(2,1)S(1)}, u32[]{:S(2)}, u32[]{:S(2)}) collective-permute-start(bf16[2,32,4224]{2,1,0:T(8,128)(2,1)S(1)} %get-tuple-element.19), channel_id=1, source_target_pairs={{1,3},{3,1},{5,7},{7,5},{9,11},{11,9},{13,15},{15,13},{17,19},{19,... | collective-permute-start | bytes 1622024 | tf_op jit(solution)/shard_map/ppermute | solution.py:44
  73.5 0.7 collective-permute-start.10
  74.5 5.7 %collective-permute-done.3 = bf16[2,32,4224]{2,1,0:T(8,128)(2,1)S(1)} collective-permute-done((bf16[2,32,4224]{2,1,0:T(8,128)(2,1)S(1)}, bf16[2,32,4224]{2,1,0:T(8,128)(2,1)S(1)}, u32[]{:S(2)}, u32[]{:S(2)}) %collective-permute-start.3) | collective-permute-done | bytes 540704 | tf_op jit(solution)/shard_map/ppermute | solution.py:44
  80.4 0.8 fusion.76
  81.1 4.6 %collective-permute-start.4 = (bf16[2,32,4224]{2,1,0:T(8,128)(2,1)S(1)}, bf16[2,32,4224]{2,1,0:T(8,128)(2,1)S(1)}, u32[]{:S(2)}, u32[]{:S(2)}) collective-permute-start(bf16[2,32,4224]{2,1,0:T(8,128)(2,1)S(1)} %get-tuple-element.37), channel_id=1, source_target_pairs={{1,5},{3,7},{5,9},{7,11},{9,13},{11,15},{17,21},{19,23},{21,25},{2... | collective-permute-start | bytes 1622024 | tf_op jit(solution)/shard_map/ppermute | solution.py:44
  85.8 1.1 fusion.62
  87.1 5.0 %collective-permute-done.4 = bf16[2,32,4224]{2,1,0:T(8,128)(2,1)S(1)} collective-permute-done((bf16[2,32,4224]{2,1,0:T(8,128)(2,1)S(1)}, bf16[2,32,4224]{2,1,0:T(8,128)(2,1)S(1)}, u32[]{:S(2)}, u32[]{:S(2)}) %collective-permute-start.4) | collective-permute-done | bytes 540704 | tf_op jit(solution)/shard_map/ppermute | solution.py:44
  92.3 7.3 %collective-permute-start.5 = (bf16[2,32,4224]{2,1,0:T(8,128)(2,1)S(1)}, bf16[2,32,4224]{2,1,0:T(8,128)(2,1)S(1)}, u32[]{:S(2)}, u32[]{:S(2)}) collective-permute-start(bf16[2,32,4224]{2,1,0:T(8,128)(2,1)S(1)} %add_convert_fusion.1), channel_id=1, source_target_pairs={{1,9},{3,11},{5,13},{7,15},{17,25},{19,27},{21,29},{23,31},{33,41}... | collective-permute-start | bytes 1622024 | tf_op jit(solution)/shard_map/ppermute | solution.py:44
  99.6 5.7 %fusion.1 = f32[2,32,64,256]{3,2,1,0:T(8,128)} fusion(f32[2,32,256]{2,1,0:T(8,128)S(1)} %fusion.50, f32[2,256,256]{2,1,0:T(8,128)S(1)} %fusion.62, pred[256,256]{1,0:T(8,128)(4,1)S(1)} %iota_compare_fusion, bf16[2,256,32,64]{1,3,2,0:T(8,128)(2,1)S(1)} %bitcast.93, f32[2,256,32]{1,2,0:T(8,128)S(1)} %get-tuple-element.34), kind=kOutput, calls=%fused_computation.3 | convolution fusion | flops 556793856 | bytes 7012352 | tf_op jit(solution)/shard_map/rhts,rshp->rthp/dot_general | solution.py:134
  105.3 1.1 fusion.67
  106.5 1.4 %collective-permute-start.11 = (bf16[2,32,4224]{2,1,0:T(8,128)(2,1)S(1)}, bf16[2,32,4224]{2,1,0:T(8,128)(2,1)S(1)}, u32[]{:S(2)}, u32[]{:S(2)}) collective-permute-start(bf16[2,32,4224]{2,1,0:T(8,128)(2,1)S(1)} %get-tuple-element.9), channel_id=1, source_target_pairs={{14,15},{12,13},{10,11},{8,9},{6,7},{4,5},{2,3},{0,1},{30,31},{28,... | collective-permute-start | bytes 1622024 | tf_op jit(solution)/shard_map/ppermute | solution.py:44
  108.5 3.4 %collective-permute-start.6 = (bf16[2,32,4224]{2,1,0:T(8,128)(2,1)S(1)}, bf16[2,32,4224]{2,1,0:T(8,128)(2,1)S(1)}, u32[]{:S(2)}, u32[]{:S(2)}) collective-permute-start(bf16[2,32,4224]{2,1,0:T(8,128)(2,1)S(1)} %get-tuple-element.15), channel_id=1, source_target_pairs={{1,0},{3,2},{5,4},{7,6},{9,8},{11,10},{13,12},{15,14},{17,16},{19,... | collective-permute-start | bytes 1622024 | tf_op jit(solution)/shard_map/ppermute | solution.py:44
  112.0 5.7 %fusion = f32[2,32,64,256]{3,2,1,0:T(8,128)} fusion(f32[2,32,256]{2,1,0:T(8,128)S(1)} %fusion.52, f32[2,256,256]{2,1,0:T(8,128)S(1)} %fusion.67, pred[256,256]{1,0:T(8,128)(4,1)S(1)} %iota_compare_fusion.1, bf16[2,256,32,64]{1,3,2,0:T(8,128)(2,1)S(1)} %bitcast.96, f32[2,256,32]{1,2,0:T(8,128)S(1)} %get-tuple-element.33), kind=kOutput, calls=%fused_computation.2 | convolution fusion | flops 556793856 | bytes 7012352 | tf_op jit(solution)/shard_map/rhts,rshp->rthp/dot_general | solution.py:134
  117.8 1.1 convert_element_type.145
  119.6 2.2 %reshape.143 = f32[2,32,64,64]{3,2,1,0:T(8,128)} reshape(f32[2,32,4096]{2,1,0:T(8,128)S(1)} %get-tuple-element.40) | data formatting | bytes 2097152 | tf_op jit(solution)/shard_map/reshape | solution.py:154
  121.8 0.8 reshape.141
  122.7 2.8 %fusion.57 = f32[2,256,32,64]{1,3,2,0:T(8,128)S(1)} fusion(f32[2,32,64,64]{3,2,1,0:T(8,128)S(1)} %reshape.141, bf16[2,256,2176]{1,2,0:T(8,128)(2,1)} %bitcast.105), kind=kOutput, calls=%fused_computation.90 | convolution fusion | flops 805306368 | bytes 5308416 | tf_op jit(solution)/shard_map/rtn,rhpn->rthp/dot_general | solution.py:155
  125.5 7.3 %multiply_reduce_fusion = (f32[2,256]{1,0:T(2,128)S(1)}, f32[2,256,32,64]{1,3,2,0:T(8,128)S(1)}) fusion(f32[2,256,32,64]{1,3,2,0:T(8,128)} %bitcast.101, f32[2,256,32]{1,2,0:T(8,128)S(1)} %copy-done.18, f32[2,32,64,64]{3,2,1,0:T(8,128)S(1)} %copy-done.14, bf16[2,256,2176]{1,2,0:T(8,128)(2,1)} %bitcast.111, bf16[2,256,32,64]{1,3,2,0:T(8,128)(2,1)S(1)} %bitcast.94, ...), kind=kOutput, calls=%fused_computation.35 | convolution fusion | flops 824180224 | bytes 26413568 | tf_op jit(solution)/shard_map/rtn,rhpn->rthp/dot_general | solution.py:155
  132.9 2.4 %fusion.36 = bf16[2,256,1024]{2,1,0:T(8,128)(2,1)S(1)} fusion(bf16[2,256,1024]{2,1,0:T(8,128)(2,1)S(1)} %bitcast.100, bf16[32,64,1024,1]{2,1,0,3:T(8,128)(2,1)S(1)} %bitcast.98, f32[2,256,32,64]{1,3,2,0:T(8,128)S(1)} %get-tuple-element.49, f32[32,64]{1,0:T(8,128)S(1)} %mul.325, f32[2,256]{1,0:T(2,128)S(1)} %add_rsqrt_fusion), kind=kOutput, calls=%fused_computation.41 | convolution fusion | flops 2152202240 | bytes 10496000 | tf_op jit(solution)/shard_map/rthp,hpd->rtd/dot_general | solution.py:198
  135.5 2.0 %copy.42 = bf16[256,2,1024]{2,1,0:T(2,128)(2,1)} copy(bf16[256,2,1024]{2,0,1:T(8,128)(2,1)S(1)} %pad_maximum_fusion.3) | data formatting | bytes 2097152 | tf_op jit(solution)/shard_map/stack | solution.py:207
  (115 shorter events, 6.9 us)
Async XLA Ops:
  0.0 16.8 %copy-start = (bf16[1024,32]{0,1:T(8,128)(2,1)S(1)}, bf16[1024,32]{0,1:T(8,128)(2,1)}, u32[]{:S(2)}) copy-start(bf16[1024,32]{0,1:T(8,128)(2,1)} %param.14) | copy-start | bytes 196612
  0.0 3.8 %copy-start.26 = (bf16[1024,2176]{1,0:T(8,128)(2,1)S(1)}, bf16[1024,2176]{1,0:T(8,128)(2,1)}, u32[]{:S(2)}) copy-start(bf16[1024,2176]{1,0:T(8,128)(2,1)} %param.13) | copy-start | bytes 13369348
  7.2 10.2 %copy-start.11 = (bf16[512,2176]{1,0:T(8,128)(2,1)}, bf16[512,2176]{1,0:T(8,128)(2,1)S(1)}, u32[]{:S(2)}) copy-start(bf16[512,2176]{1,0:T(8,128)(2,1)S(1)} %convolution_convert_fusion) | copy-start | bytes 6684676
  7.2 9.5 %copy-start.24 = (f32[2,32]{1,0:T(2,128)S(1)}, f32[2,32]{1,0:T(2,128)}, u32[]{:S(2)}) copy-start(f32[2,32]{1,0:T(2,128)} %param.16) | copy-start | bytes 772
  7.2 10.0 %copy-start.23 = (f32[2,32]{1,0:T(2,128)S(1)}, f32[2,32]{1,0:T(2,128)}, u32[]{:S(2)}) copy-start(f32[2,32]{1,0:T(2,128)} %param.15) | copy-start | bytes 772
  7.3 13.6 %collective-permute-start = (bf16[2,3,2176]{2,1,0:T(4,128)(2,1)S(1)}, bf16[2,3,2176]{2,1,0:T(4,128)(2,1)S(1)}, u32[]{:S(2)}, u32[]{:S(2)}) collective-permute-start(bf16[2,3,2176]{2,1,0:T(4,128)(2,1)S(1)} %get-tuple-element.22), channel_id=1, source_target_pairs={{0,1},{1,2},{2,3},{3,4},{4,5},{5,6},{6,7},{7,8},{8,9},{9,10},{10,1... | collective-permute-start | bytes 78344 | tf_op jit(solution)/shard_map/ppermute | solution.py:22
  13.6 4.8 %copy-start.16 = (f32[2,4,2176]{2,1,0:T(4,128)S(1)}, f32[2,4,2176]{2,1,0:T(4,128)}, u32[]{:S(2)}) copy-start(f32[2,4,2176]{2,1,0:T(4,128)} %wr_ref.1) | copy-start | bytes 208900
  13.6 4.8 %copy-start.17 = (f32[2,2176]{1,0:T(2,128)S(1)}, f32[2,2176]{1,0:T(2,128)}, u32[]{:S(2)}) copy-start(f32[2,2176]{1,0:T(2,128)} %param.18) | copy-start | bytes 52228
  13.6 7.2 %collective-permute-start.1 = (bf16[2,3,2176]{2,1,0:T(4,128)(2,1)S(1)}, bf16[2,3,2176]{2,1,0:T(4,128)(2,1)S(1)}, u32[]{:S(2)}, u32[]{:S(2)}) collective-permute-start(bf16[2,3,2176]{2,1,0:T(4,128)(2,1)S(1)} %get-tuple-element.21), channel_id=1, source_target_pairs={{1,0},{2,1},{3,2},{4,3},{5,4},{6,5},{7,6},{8,7},{9,8},{10,9},{11,1... | collective-permute-start | bytes 78344 | tf_op jit(solution)/shard_map/ppermute | solution.py:22
  19.6 88.5 %copy-start.15 = (pred[4224]{0:T(1024)(128)(4,1)}, pred[4224]{0:T(1024)(128)(4,1)S(1)}, u32[]{:S(2)}) copy-start(pred[4224]{0:T(1024)(128)(4,1)S(1)} %iota_compare_fusion.4) | copy-start | bytes 12676
  20.8 0.6 copy-start.20
  21.4 0.6 copy-start.21
  33.4 1.4 copy-start.2
  39.9 10.0 %collective-permute-start.7 = (bf16[2,32,4224]{2,1,0:T(8,128)(2,1)S(1)}, bf16[2,32,4224]{2,1,0:T(8,128)(2,1)S(1)}, u32[]{:S(2)}, u32[]{:S(2)}) collective-permute-start(bf16[2,32,4224]{2,1,0:T(8,128)(2,1)S(1)} %fusion.48), channel_id=1, source_target_pairs={{15,14},{13,12},{11,10},{9,8},{7,6},{5,4},{3,2},{1,0},{31,30},{29,... | collective-permute-start | bytes 1622024 | tf_op jit(solution)/shard_map/ppermute | solution.py:44
  43.6 1.3 copy-start.5
  50.0 0.8 copy-start.12
  50.8 3.4 %collective-permute-start.8 = (bf16[2,32,4224]{2,1,0:T(8,128)(2,1)S(1)}, bf16[2,32,4224]{2,1,0:T(8,128)(2,1)S(1)}, u32[]{:S(2)}, u32[]{:S(2)}) collective-permute-start(bf16[2,32,4224]{2,1,0:T(8,128)(2,1)S(1)} %get-tuple-element.13), channel_id=1, source_target_pairs={{14,12},{12,14},{10,8},{8,10},{6,4},{4,6},{2,0},{0,2},{30,28},{28,... | collective-permute-start | bytes 1622024 | tf_op jit(solution)/shard_map/ppermute | solution.py:44
  51.5 4.7 %copy-start.27 = (bf16[1024,2048]{1,0:T(8,128)(2,1)S(1)}, bf16[1024,2048]{1,0:T(8,128)(2,1)}, u32[]{:S(2)}) copy-start(bf16[1024,2048]{1,0:T(8,128)(2,1)} %param.12) | copy-start | bytes 12582916
  52.5 13.6 %collective-permute-start.2 = (bf16[2,32,4224]{2,1,0:T(8,128)(2,1)}, bf16[2,32,4224]{2,1,0:T(8,128)(2,1)}, u32[]{:S(2)}, u32[]{:S(2)}) collective-permute-start(bf16[2,32,4224]{2,1,0:T(8,128)(2,1)} %fusion.49), channel_id=1, source_target_pairs={{0,1},{2,3},{4,5},{6,7},{8,9},{10,11},{12,13},{14,15},{16,17},{18,... | collective-permute-start | bytes 1622024 | tf_op jit(solution)/shard_map/ppermute | solution.py:44
  54.2 2.1 %copy-start.9 = (bf16[512,1024]{1,0:T(8,128)(2,1)S(1)}, bf16[512,1024]{1,0:T(8,128)(2,1)}, u32[]{:S(2)}) copy-start(bf16[512,1024]{1,0:T(8,128)(2,1)} %pad_maximum_fusion.2) | copy-start | bytes 3145732
  55.5 10.6 %collective-permute-start.9 = (bf16[2,32,4224]{2,1,0:T(8,128)(2,1)}, bf16[2,32,4224]{2,1,0:T(8,128)(2,1)S(1)}, u32[]{:S(2)}, u32[]{:S(2)}) collective-permute-start(bf16[2,32,4224]{2,1,0:T(8,128)(2,1)} %get-tuple-element.11), channel_id=1, source_target_pairs={{14,10},{12,8},{10,6},{8,4},{6,2},{4,0},{30,26},{28,24},{26,22},{2... | collective-permute-start | bytes 1622024 | tf_op jit(solution)/shard_map/ppermute | solution.py:44
  60.6 5.3 %copy-start.22 = (f32[2048]{0:T(1024)S(1)}, f32[2048]{0:T(1024)}, u32[]{:S(2)}) copy-start(f32[2048]{0:T(1024)} %param.20) | copy-start | bytes 24580
  66.1 8.1 %copy-start.25 = (f32[2,32]{1,0:T(2,128)S(1)}, f32[2,32]{1,0:T(2,128)}, u32[]{:S(2)}) copy-start(f32[2,32]{1,0:T(2,128)} %param.19) | copy-start | bytes 772
  67.6 12.6 %collective-permute-start.3 = (bf16[2,32,4224]{2,1,0:T(8,128)(2,1)S(1)}, bf16[2,32,4224]{2,1,0:T(8,128)(2,1)S(1)}, u32[]{:S(2)}, u32[]{:S(2)}) collective-permute-start(bf16[2,32,4224]{2,1,0:T(8,128)(2,1)S(1)} %get-tuple-element.19), channel_id=1, source_target_pairs={{1,3},{3,1},{5,7},{7,5},{9,11},{11,9},{13,15},{15,13},{17,19},{19,... | collective-permute-start | bytes 1622024 | tf_op jit(solution)/shard_map/ppermute | solution.py:44
  73.5 6.9 %collective-permute-start.10 = (bf16[2,32,4224]{2,1,0:T(8,128)(2,1)S(1)}, bf16[2,32,4224]{2,1,0:T(8,128)(2,1)S(1)}, u32[]{:S(2)}, u32[]{:S(2)}) collective-permute-start(bf16[2,32,4224]{2,1,0:T(8,128)(2,1)S(1)} %get-tuple-element.39), channel_id=1, source_target_pairs={{14,6},{12,4},{10,2},{8,0},{30,22},{28,20},{26,18},{24,16},{46,38}... | collective-permute-start | bytes 1622024 | tf_op jit(solution)/shard_map/ppermute | solution.py:44
  81.1 18.5 %copy-start.3 = (bf16[2,256,2048]{1,2,0:T(8,128)(2,1)S(1)}, bf16[2,256,2048]{1,2,0:T(8,128)(2,1)}, u32[]{:S(2)}) copy-start(bf16[2,256,2048]{1,2,0:T(8,128)(2,1)} %copy-done.2) | copy-start | bytes 6291460
  81.1 10.9 %collective-permute-start.4 = (bf16[2,32,4224]{2,1,0:T(8,128)(2,1)S(1)}, bf16[2,32,4224]{2,1,0:T(8,128)(2,1)S(1)}, u32[]{:S(2)}, u32[]{:S(2)}) collective-permute-start(bf16[2,32,4224]{2,1,0:T(8,128)(2,1)S(1)} %get-tuple-element.37), channel_id=1, source_target_pairs={{1,5},{3,7},{5,9},{7,11},{9,13},{11,15},{17,21},{19,23},{21,25},{2... | collective-permute-start | bytes 1622024 | tf_op jit(solution)/shard_map/ppermute | solution.py:44
  92.3 15.8 %collective-permute-start.5 = (bf16[2,32,4224]{2,1,0:T(8,128)(2,1)S(1)}, bf16[2,32,4224]{2,1,0:T(8,128)(2,1)S(1)}, u32[]{:S(2)}, u32[]{:S(2)}) collective-permute-start(bf16[2,32,4224]{2,1,0:T(8,128)(2,1)S(1)} %add_convert_fusion.1), channel_id=1, source_target_pairs={{1,9},{3,11},{5,13},{7,15},{17,25},{19,27},{21,29},{23,31},{33,41}... | collective-permute-start | bytes 1622024 | tf_op jit(solution)/shard_map/ppermute | solution.py:44
  106.5 5.5 %copy-start.6 = (bf16[2,256,2048]{1,2,0:T(8,128)(2,1)S(1)}, bf16[2,256,2048]{1,2,0:T(8,128)(2,1)}, u32[]{:S(2)}) copy-start(bf16[2,256,2048]{1,2,0:T(8,128)(2,1)} %copy-done.5) | copy-start | bytes 6291460
  106.5 12.6 %collective-permute-start.11 = (bf16[2,32,4224]{2,1,0:T(8,128)(2,1)S(1)}, bf16[2,32,4224]{2,1,0:T(8,128)(2,1)S(1)}, u32[]{:S(2)}, u32[]{:S(2)}) collective-permute-start(bf16[2,32,4224]{2,1,0:T(8,128)(2,1)S(1)} %get-tuple-element.9), channel_id=1, source_target_pairs={{14,15},{12,13},{10,11},{8,9},{6,7},{4,5},{2,3},{0,1},{30,31},{28,... | collective-permute-start | bytes 1622024 | tf_op jit(solution)/shard_map/ppermute | solution.py:44
  108.5 9.2 %copy-start.13 = (bf16[2,32,4224]{2,1,0:T(8,128)(2,1)S(1)}, bf16[2,32,4224]{2,1,0:T(8,128)(2,1)}, u32[]{:S(2)}) copy-start(bf16[2,32,4224]{2,1,0:T(8,128)(2,1)} %copy-done.12) | copy-start | bytes 1622020
  108.5 10.6 %collective-permute-start.6 = (bf16[2,32,4224]{2,1,0:T(8,128)(2,1)S(1)}, bf16[2,32,4224]{2,1,0:T(8,128)(2,1)S(1)}, u32[]{:S(2)}, u32[]{:S(2)}) collective-permute-start(bf16[2,32,4224]{2,1,0:T(8,128)(2,1)S(1)} %get-tuple-element.15), channel_id=1, source_target_pairs={{1,0},{3,2},{5,4},{7,6},{9,8},{11,10},{13,12},{15,14},{17,16},{19,... | collective-permute-start | bytes 1622024 | tf_op jit(solution)/shard_map/ppermute | solution.py:44
  117.7 1.4 %slice-start = ((pred[4224]{0:T(1024)(128)(4,1)}), pred[4096]{0:T(1024)(128)(4,1)S(1)}, s32[]{:S(2)}) async-start(pred[4224]{0:T(1024)(128)(4,1)} %copy-done.15), calls=%async_computation | async-start | bytes 8192 | tf_op jit(solution)/shard_map/slice | solution.py:60
  121.8 3.7 %copy-start.19 = (f32[2,256,32]{1,2,0:T(8,128)S(1)}, f32[2,256,32]{1,2,0:T(8,128)}, u32[]{:S(2)}) copy-start(f32[2,256,32]{1,2,0:T(8,128)} %get-tuple-element.29) | copy-start | bytes 196612
  122.6 2.8 %copy-start.4 = (bf16[2,256,2048]{1,2,0:T(8,128)(2,1)S(1)}, bf16[2,256,2048]{1,2,0:T(8,128)(2,1)}, u32[]{:S(2)}) copy-start(bf16[2,256,2048]{1,2,0:T(8,128)(2,1)} %copy-done.2) | copy-start | bytes 6291460
  122.6 2.8 %copy-start.7 = (bf16[2,256,2048]{1,2,0:T(8,128)(2,1)S(1)}, bf16[2,256,2048]{1,2,0:T(8,128)(2,1)}, u32[]{:S(2)}) copy-start(bf16[2,256,2048]{1,2,0:T(8,128)(2,1)} %copy-done.5) | copy-start | bytes 6291460
  122.6 2.9 %copy-start.14 = (f32[2,32,64,64]{3,2,1,0:T(8,128)S(1)}, f32[2,32,64,64]{3,2,1,0:T(8,128)}, u32[]{:S(2)}) copy-start(f32[2,32,64,64]{3,2,1,0:T(8,128)} %reshape.143) | copy-start | bytes 3145732
  122.6 2.9 %copy-start.18 = (f32[2,256,32]{1,2,0:T(8,128)S(1)}, f32[2,256,32]{1,2,0:T(8,128)}, u32[]{:S(2)}) copy-start(f32[2,256,32]{1,2,0:T(8,128)} %get-tuple-element.31) | copy-start | bytes 196612
  125.5 7.4 %copy-start.8 = (bf16[2048,1024]{1,0:T(8,128)(2,1)S(1)}, bf16[2048,1024]{1,0:T(8,128)(2,1)}, u32[]{:S(2)}) copy-start(bf16[2048,1024]{1,0:T(8,128)(2,1)} %param.21) | copy-start | bytes 12582916
  125.5 7.4 %copy-start.10 = (bf16[512,1024]{1,0:T(8,128)(2,1)S(1)}, bf16[512,1024]{1,0:T(8,128)(2,1)}, u32[]{:S(2)}) copy-start(bf16[512,1024]{1,0:T(8,128)(2,1)} %pad_maximum_fusion.2) | copy-start | bytes 3145732
  135.4 2.2 %copy-start.1 = (bf16[1024,32]{0,1:T(8,128)(2,1)S(1)}, bf16[1024,32]{0,1:T(8,128)(2,1)}, u32[]{:S(2)}) copy-start(bf16[1024,32]{0,1:T(8,128)(2,1)} %param.14) | copy-start | bytes 196612

commit v11 on v10

--- a/solution.py
+++ b/solution.py
@@ -152,9 +152,11 @@
 
 def finish(local, cum, reads, entering):
     entering = entering.reshape(local.shape[0], local.shape[2], local.shape[3], NS)
+    high = entering.astype(jnp.bfloat16)
+    low = (entering - high.astype(jnp.float32)).astype(jnp.bfloat16)
     product = jnp.einsum(
-        "rtn,rhpn->rthp", reads.astype(jnp.float32), entering, precision=lax.Precision.HIGHEST
-    )
+        "rtn,rhpn->rthp", reads, high, preferred_element_type=jnp.float32
+    ) + jnp.einsum("rtn,rhpn->rthp", reads, low, preferred_element_type=jnp.float32)
     return local + product * jnp.exp(cum)[..., None]
 
 

time: 138 us -> 157 us (1.14)
  the two profiles are of different devices: /device:TPU:1 before, /device:TPU:110 now
where the time goes in v11:
time: 157 us; the launch traced here: 156 us
  matrix products  53.4 us (34%)
  starting transfers between devices  38.5 us (25%)
  local copies, waits for them, and re-layouts  30.8 us (20%)
  other arithmetic  12.4 us (8%)
  waiting for transfers between devices  10.1 us (6%)
  Pallas kernels  9.64 us (6%)
    ppermute x10, starting transfers between devices, send(): moved = lax.ppermute(value.astype(jnp.bfloat16), 'ctx', pairs)  30.4 us
    dot_general x2, matrix products, group_terms(): jnp.einsum('rhts,rshp->rthp', mixing, scaled, preferred_element_type=jnp....  19 us
    ppermute x10, waiting for transfers between devices, send(): moved = lax.ppermute(value.astype(jnp.bfloat16), 'ctx', pairs)  10 us
    pallas_call x1, Pallas kernels, convolve(): pl.pallas_call(conv_kernel, grid=grid, in_specs=[pl.BlockSpec((1, length,...  9.64 us
    ppermute x2, starting transfers between devices, shifted(): return lax.ppermute(value, 'ctx', pairs)  8.1 us
    dot_general x2, matrix products, finish(): jnp.einsum('rtn,rhpn->rthp', reads, low, preferred_element_type=jnp.float32)  7.18 us
    dot_general x2, matrix products, finish(): jnp.einsum('rtn,rhpn->rthp', reads, high, preferred_element_type=jnp.floa...  6.98 us
    convert_element_type x8, other arithmetic, send(): moved = lax.ppermute(value.astype(jnp.bfloat16), 'ctx', pairs)  6.01 us
  transfers between devices with their start and end apart: 12, of which 3 were waited for; matrix products, arithmetic and copies ran while one was open for 23% of the time, Pallas kernels for 0%

profile of v11, /device:TPU:110, one launch (start us, length us, event | category | flops | bytes accessed | tf_op | source)
XLA Modules:
  0.0 155.6 jit_solution(16255852568429090661)
XLA Ops:
  0.0 3.4 %fusion.94 = (bf16[256,1,1024]{2,1,0:T(2,128)(2,1)S(1)}, bf16[256,1,1024]{2,1,0:T(2,128)(2,1)S(1)}) fusion(bf16[256,2,1024]{2,1,0:T(2,128)(2,1)} %param.11), kind=kLoop, calls=%fused_computation.152 | loop fusion | bytes 2097152 | tf_op jit(solution)/shard_map/slice | solution.py:171
  3.9 3.4 %convolution_convert_fusion = bf16[512,2176]{1,0:T(8,128)(2,1)S(1)} fusion(bf16[1024,2176]{1,0:T(8,128)(2,1)S(1)} %copy-done.31, bf16[256,1024]{1,0:T(8,128)(2,1)S(1)} %get-tuple-element.50, bf16[256,1024]{1,0:T(8,128)(2,1)S(1)} %get-tuple-element.51), kind=kOutput, calls=%fused_computation.20 | convolution fusion | flops 2284912640 | bytes 7733248 | tf_op jit(solution)/shard_map/dot_general | solution.py:175
  7.4 2.1 %collective-permute-start = (bf16[2,3,2176]{2,1,0:T(4,128)(2,1)S(1)}, bf16[2,3,2176]{2,1,0:T(4,128)(2,1)S(1)}, u32[]{:S(2)}, u32[]{:S(2)}) collective-permute-start(bf16[2,3,2176]{2,1,0:T(4,128)(2,1)S(1)} %get-tuple-element.22), channel_id=1, source_target_pairs={{0,1},{1,2},{2,3},{3,4},{4,5},{5,6},{6,7},{7,8},{8,9},{9,10},{10,1... | collective-permute-start | bytes 78344 | tf_op jit(solution)/shard_map/ppermute | solution.py:22
  9.4 6.0 %collective-permute-start.1 = (bf16[2,3,2176]{2,1,0:T(4,128)(2,1)S(1)}, bf16[2,3,2176]{2,1,0:T(4,128)(2,1)S(1)}, u32[]{:S(2)}, u32[]{:S(2)}) collective-permute-start(bf16[2,3,2176]{2,1,0:T(4,128)(2,1)S(1)} %get-tuple-element.21), channel_id=1, source_target_pairs={{1,0},{2,1},{3,2},{4,3},{5,4},{6,5},{7,6},{8,7},{9,8},{10,9},{11,1... | collective-permute-start | bytes 78344 | tf_op jit(solution)/shard_map/ppermute | solution.py:22
  17.7 0.6 pad_maximum_fusion.4.wf_ref
  20.9 9.6 %shard_map.109 = (bf16[2,2176,256]{2,1,0:T(8,128)(2,1)}, bf16[2,2176,256]{2,1,0:T(8,128)(2,1)}) custom-call(bf16[2,256,2176]{2,1,0:T(8,128)(2,1)} %bitcast.112, bf16[2,3,2176]{2,1,0:T(4,128)(2,1)} %copy-done.25, bf16[2,3,2176]{2,1,0:T(4,128)(2,1)} %copy-done.26, f32[2,4,2176]{2,1,0:T(4,128)} %wr_ref.1, f32[2,1,2176]{2,1,0:T(1,128)} %broadcast_in_dim.43.br_ref, ...), custom_call_target="tpu_custom_call" | custom-call | tf_op jit(solution)/shard_map/pallas_call | solution.py:86
  30.5 1.7 %slice.150 = bf16[2,256,2048]{1,2,0:T(8,128)(2,1)S(1)} slice(bf16[2,256,2176]{1,2,0:T(8,128)(2,1)} %bitcast.101), slice={[0:2], [0:256], [0:2048]} | slice | bytes 4194304 | tf_op jit(solution)/shard_map/slice | solution.py:110
  32.2 1.4 copy-done.2
  33.6 2.9 %fusion.33 = f32[2,32,64,64]{3,2,1,0:T(8,128)} fusion(bf16[2,256,32,64]{1,3,2,0:T(8,128)(2,1)S(1)} %bitcast.92, f32[2,256,32]{1,2,0:T(8,128)S(1)} %get-tuple-element.30, bf16[2,256,2176]{1,2,0:T(8,128)(2,1)} %bitcast.102), kind=kOutput, calls=%fused_computation.39 | convolution fusion | flops 137363456 | bytes 3276800 | tf_op jit(solution)/shard_map/rshp,rsn->rhpn/dot_general | solution.py:138
  36.5 2.1 %reshape.140 = f32[2,32,4096]{2,1,0:T(8,128)S(1)} reshape(f32[2,32,64,64]{3,2,1,0:T(8,128)} %fusion.33) | data formatting | bytes 2097152 | tf_op jit(solution)/shard_map/reshape | solution.py:144
  38.7 1.3 collective-permute-start.2
  40.1 0.6 bitcast_exponential_fusion
  40.7 1.7 %slice.163 = bf16[2,256,2048]{1,2,0:T(8,128)(2,1)S(1)} slice(bf16[2,256,2176]{1,2,0:T(8,128)(2,1)} %bitcast.106), slice={[0:2], [0:256], [0:2048]} | slice | bytes 4194304 | tf_op jit(solution)/shard_map/slice | solution.py:110
  42.5 1.3 copy-done.5
  43.8 2.9 %fusion.30 = f32[2,32,64,64]{3,2,1,0:T(8,128)} fusion(bf16[2,256,32,64]{1,3,2,0:T(8,128)(2,1)S(1)} %bitcast.95, f32[2,256,32]{1,2,0:T(8,128)S(1)} %get-tuple-element.32, bf16[2,256,2176]{1,2,0:T(8,128)(2,1)} %bitcast.107), kind=kOutput, calls=%fused_computation.38 | convolution fusion | flops 137363456 | bytes 3276800 | tf_op jit(solution)/shard_map/rshp,rsn->rhpn/dot_general | solution.py:138
  46.6 2.1 %reshape.142 = f32[2,32,4096]{2,1,0:T(8,128)S(1)} reshape(f32[2,32,64,64]{3,2,1,0:T(8,128)} %fusion.30) | data formatting | bytes 2097152 | tf_op jit(solution)/shard_map/reshape | solution.py:144
  49.0 0.7 collective-permute-start.3
  49.9 1.5 collective-permute-start.7
  52.0 0.7 collective-permute-start.4
  52.8 0.9 collective-permute-done.7
  53.7 1.6 %fusion.92 = (bf16[2,32,4224]{2,1,0:T(8,128)(2,1)}, f32[2,32,4224]{2,1,0:T(8,128)}, bf16[2,32,4224]{2,1,0:T(8,128)(2,1)}) fusion(f32[2,32,128]{2,1,0:T(8,128)S(1)} %broadcast_in_dim.85, f32[2,32,4096]{2,1,0:T(8,128)S(1)} %reshape.142, pred[4224]{0:T(1024)(128)(4,1)S(1)} %iota_compare_fusion.4, bf16[2,32,4224]{2,1,0:T(8,128)(2,1)S(1)} %collective-permute-done.7, ...), kind=kLoop, calls=%fused_computation.150 | loop fusion | flops 2973696 | bytes 5411456 | tf_op jit(solution)/shard_map/convert_element_type | solution.py:44
  55.3 3.5 %collective-permute-start.8 = (bf16[2,32,4224]{2,1,0:T(8,128)(2,1)}, bf16[2,32,4224]{2,1,0:T(8,128)(2,1)S(1)}, u32[]{:S(2)}, u32[]{:S(2)}) collective-permute-start(bf16[2,32,4224]{2,1,0:T(8,128)(2,1)} %get-tuple-element.19), channel_id=1, source_target_pairs={{14,12},{12,14},{10,8},{8,10},{6,4},{4,6},{2,0},{0,2},{30,28},{28,... | collective-permute-start | bytes 1622024 | tf_op jit(solution)/shard_map/ppermute | solution.py:44
  58.9 1.5 collective-permute-start.5
  60.4 1.3 pad_maximum_fusion.2
  61.8 1.3 slice_reduce_fusion.2
  63.2 5.1 %collective-permute-done.8 = bf16[2,32,4224]{2,1,0:T(8,128)(2,1)S(1)} collective-permute-done((bf16[2,32,4224]{2,1,0:T(8,128)(2,1)}, bf16[2,32,4224]{2,1,0:T(8,128)(2,1)S(1)}, u32[]{:S(2)}, u32[]{:S(2)}) %collective-permute-start.8) | collective-permute-done | bytes 540704 | tf_op jit(solution)/shard_map/ppermute | solution.py:44
  68.5 3.0 %fusion.87 = (bf16[2,32,4224]{2,1,0:T(8,128)(2,1)}, f32[2,32,4224]{2,1,0:T(8,128)}, bf16[2,32,4224]{2,1,0:T(8,128)(2,1)}, f32[2,32,4224]{2,1,0:T(8,128)S(1)}) fusion(bf16[2,32,4224]{2,1,0:T(8,128)(2,1)S(1)} %collective-permute-done.3, f32[2,32]{1,0:T(2,128)S(1)} %slice_reduce_fusion.9, bf16[2,32,4224]{2,1,0:T(8,128)(2,1)S(1)} %collective-permute-done.4, ...), kind=kLoop, calls=%fused_computation.145 | loop fusion | flops 5406720 | bytes 6493314 | tf_op jit(solution)/shard_map/convert_element_type | solution.py:44
  71.5 3.6 %collective-permute-start.9 = (bf16[2,32,4224]{2,1,0:T(8,128)(2,1)}, bf16[2,32,4224]{2,1,0:T(8,128)(2,1)S(1)}, u32[]{:S(2)}, u32[]{:S(2)}) collective-permute-start(bf16[2,32,4224]{2,1,0:T(8,128)(2,1)} %get-tuple-element.37), channel_id=1, source_target_pairs={{14,10},{12,8},{10,6},{8,4},{6,2},{4,0},{30,26},{28,24},{26,22},{2... | collective-permute-start | bytes 1622024 | tf_op jit(solution)/shard_map/ppermute | solution.py:44
  75.1 4.4 %convert_bitcast_fusion = f32[2,2048,256]{1,2,0:T(8,128)} fusion(bf16[2,256,1024]{2,1,0:T(8,128)(2,1)S(1)} %bitcast.98, bf16[1024,2048]{1,0:T(8,128)(2,1)S(1)} %copy-done.32), kind=kOutput, calls=%fused_computation.33 | convolution fusion | flops 2149580800 | bytes 9437184 | tf_op jit(solution)/shard_map/rtd,de->ret/dot_general | solution.py:172
  79.5 5.3 %copy.41 = f32[2,2048,256]{2,1,0:T(8,128)} copy(f32[2,2048,256]{1,2,0:T(8,128)} %convert_bitcast_fusion) | data formatting | bytes 8388608 | tf_op jit(solution)/shard_map/transpose | solution.py:192
  85.0 0.7 iota_compare_fusion
  85.9 4.1 %collective-permute-start.10 = (bf16[2,32,4224]{2,1,0:T(8,128)(2,1)S(1)}, bf16[2,32,4224]{2,1,0:T(8,128)(2,1)S(1)}, u32[]{:S(2)}, u32[]{:S(2)}) collective-permute-start(bf16[2,32,4224]{2,1,0:T(8,128)(2,1)S(1)} %add_convert_fusion), channel_id=1, source_target_pairs={{14,6},{12,4},{10,2},{8,0},{30,22},{28,20},{26,18},{24,16},{46,38}... | collective-permute-start | bytes 1622024 | tf_op jit(solution)/shard_map/ppermute | solution.py:44
  90.1 1.1 fusion.74
  91.2 1.4 collective-permute-start.6
  92.8 4.0 %collective-permute-done.10 = bf16[2,32,4224]{2,1,0:T(8,128)(2,1)S(1)} collective-permute-done((bf16[2,32,4224]{2,1,0:T(8,128)(2,1)S(1)}, bf16[2,32,4224]{2,1,0:T(8,128)(2,1)S(1)}, u32[]{:S(2)}, u32[]{:S(2)}) %collective-permute-start.10) | collective-permute-done | bytes 540704 | tf_op jit(solution)/shard_map/ppermute | solution.py:44
  97.3 12.0 %collective-permute-start.11 = (bf16[2,32,4224]{2,1,0:T(8,128)(2,1)S(1)}, bf16[2,32,4224]{2,1,0:T(8,128)(2,1)S(1)}, u32[]{:S(2)}, u32[]{:S(2)}) collective-permute-start(bf16[2,32,4224]{2,1,0:T(8,128)(2,1)S(1)} %get-tuple-element.15), channel_id=1, source_target_pairs={{14,15},{12,13},{10,11},{8,9},{6,7},{4,5},{2,3},{0,1},{30,31},{28,... | collective-permute-start | bytes 1622024 | tf_op jit(solution)/shard_map/ppermute | solution.py:44
  109.3 5.8 %fusion = f32[2,32,64,256]{3,2,1,0:T(8,128)} fusion(f32[2,32,256]{2,1,0:T(8,128)S(1)} %fusion.60, f32[2,256,256]{2,1,0:T(8,128)S(1)} %fusion.74, pred[256,256]{1,0:T(8,128)(4,1)S(1)} %iota_compare_fusion.1, bf16[2,256,32,64]{1,3,2,0:T(8,128)(2,1)S(1)} %bitcast.93, f32[2,256,32]{1,2,0:T(8,128)S(1)} %get-tuple-element.34), kind=kOutput, calls=%fused_computation.2 | convolution fusion | flops 556793856 | bytes 7012352 | tf_op jit(solution)/shard_map/rhts,rshp->rthp/dot_general | solution.py:134
  115.1 2.0 %fusion.71 = f32[2,256,256]{2,1,0:T(8,128)} fusion(bf16[2,256,2176]{1,2,0:T(8,128)(2,1)} %bitcast.108), kind=kOutput, calls=%fused_computation.108 | convolution fusion | flops 16777216 | bytes 655360 | tf_op jit(solution)/shard_map/rtn,rsn->rts/dot_general | solution.py:130
  117.5 1.8 %fusion.49 = (f32[2,32,4096]{2,1,0:T(8,128)}, f32[2,32,4096]{2,1,0:T(8,128)}) fusion(f32[2,32,4224]{2,1,0:T(8,128)S(1)} %convert_element_type.161, f32[2,32,4224]{2,1,0:T(8,128)S(1)} %copy-done.9, bf16[2,32,4224]{2,1,0:T(8,128)(2,1)S(1)} %collective-permute-done.6, f32[2,32]{1,0:T(2,128)S(1)} %slice_reduce_fusion.10, pred[]{:T(512)S(6)} %eq.19, ...), kind=kLoop, calls=%fused_computation.70 | loop fusion | flops 2621440 | bytes 7344642 | tf_op jit(solution)/shard_map/jit(_where)/select_n | solution.py:59
  119.3 2.0 %reshape.143 = f32[2,32,64,64]{3,2,1,0:T(8,128)S(1)} reshape(f32[2,32,4096]{2,1,0:T(8,128)} %get-tuple-element.41) | data formatting | bytes 2097152 | tf_op jit(solution)/shard_map/reshape | solution.py:154
  121.3 3.5 %fusion.53 = f32[2,256,32,64]{1,3,2,0:T(8,128)} fusion(f32[2,32,64,64]{3,2,1,0:T(8,128)S(1)} %reshape.143, bf16[2,256,2176]{1,2,0:T(8,128)(2,1)} %bitcast.109), kind=kOutput, calls=%fused_computation.81 | convolution fusion | flops 134479872 | bytes 5308416 | tf_op jit(solution)/shard_map/rtn,rhpn->rthp/dot_general | solution.py:157
  124.8 3.5 %fusion.45 = f32[2,256,32,64]{1,3,2,0:T(8,128)} fusion(f32[2,32,64,64]{3,2,1,0:T(8,128)S(1)} %reshape.143, bf16[2,256,2176]{1,2,0:T(8,128)(2,1)} %bitcast.110), kind=kOutput, calls=%fused_computation.63 | convolution fusion | flops 135266304 | bytes 5308416 | tf_op jit(solution)/shard_map/rtn,rhpn->rthp/dot_general | solution.py:159
  128.3 2.0 %reshape.141 = f32[2,32,64,64]{3,2,1,0:T(8,128)S(1)} reshape(f32[2,32,4096]{2,1,0:T(8,128)} %get-tuple-element.40) | data formatting | bytes 2097152 | tf_op jit(solution)/shard_map/reshape | solution.py:154
  130.3 3.5 %fusion.56 = f32[2,256,32,64]{1,3,2,0:T(8,128)} fusion(f32[2,32,64,64]{3,2,1,0:T(8,128)S(1)} %reshape.141, bf16[2,256,2176]{1,2,0:T(8,128)(2,1)} %bitcast.104), kind=kOutput, calls=%fused_computation.84 | convolution fusion | flops 134479872 | bytes 5308416 | tf_op jit(solution)/shard_map/rtn,rhpn->rthp/dot_general | solution.py:157
  133.8 3.7 %fusion.44 = f32[2,256,32,64]{1,3,2,0:T(8,128)} fusion(f32[2,32,64,64]{3,2,1,0:T(8,128)S(1)} %reshape.141, bf16[2,256,2176]{1,2,0:T(8,128)(2,1)} %bitcast.105), kind=kOutput, calls=%fused_computation.62 | convolution fusion | flops 135266304 | bytes 5308416 | tf_op jit(solution)/shard_map/rtn,rhpn->rthp/dot_general | solution.py:159
  137.5 13.2 %multiply_reduce_fusion = (f32[2,256]{1,0:T(2,128)S(1)}, f32[2,256,32,64]{1,3,2,0:T(8,128)S(1)}) fusion(f32[2,256,32,64]{1,3,2,0:T(8,128)} %bitcast.100, f32[2,256,32]{1,2,0:T(8,128)S(1)} %copy-done.24, f32[2,256,32,64]{1,3,2,0:T(8,128)} %fusion.53, f32[2,256,32,64]{1,3,2,0:T(8,128)} %fusion.45, bf16[2,256,32,64]{1,3,2,0:T(8,128)(2,1)S(1)} %bitcast.96, ...), kind=kOutput, calls=%fused_computation.35 | convolution fusion | flops 577764864 | bytes 34408960 | tf_op jit(solution)/shard_map/rhts,rshp->rthp/dot_general | solution.py:134
  150.8 2.5 %fusion.36 = bf16[2,256,1024]{2,1,0:T(8,128)(2,1)S(1)} fusion(bf16[2,256,1024]{2,1,0:T(8,128)(2,1)S(1)} %bitcast.99, bf16[32,64,1024,1]{2,1,0,3:T(8,128)(2,1)S(1)} %bitcast.97, f32[2,256,32,64]{1,3,2,0:T(8,128)S(1)} %get-tuple-element.49, f32[32,64]{1,0:T(8,128)S(1)} %mul.325, f32[2,256]{1,0:T(2,128)S(1)} %add_rsqrt_fusion), kind=kOutput, calls=%fused_computation.41 | convolution fusion | flops 2152202240 | bytes 10496000 | tf_op jit(solution)/shard_map/rthp,hpd->rtd/dot_general | solution.py:200
  153.5 2.0 %copy.42 = bf16[256,2,1024]{2,1,0:T(2,128)(2,1)} copy(bf16[256,2,1024]{2,0,1:T(8,128)(2,1)S(1)} %pad_maximum_fusion.3) | data formatting | bytes 2097152 | tf_op jit(solution)/shard_map/stack | solution.py:209
  (127 shorter events, 8.1 us)
Async XLA Ops:
  0.0 15.5 %copy-start = (bf16[1024,32]{0,1:T(8,128)(2,1)S(1)}, bf16[1024,32]{0,1:T(8,128)(2,1)}, u32[]{:S(2)}) copy-start(bf16[1024,32]{0,1:T(8,128)(2,1)} %param.14) | copy-start | bytes 196612
  0.0 3.8 %copy-start.31 = (bf16[1024,2176]{1,0:T(8,128)(2,1)S(1)}, bf16[1024,2176]{1,0:T(8,128)(2,1)}, u32[]{:S(2)}) copy-start(bf16[1024,2176]{1,0:T(8,128)(2,1)} %param.13) | copy-start | bytes 13369348
  3.8 11.7 %copy-start.15 = (bf16[256,1024]{1,0:T(8,128)(2,1)}, bf16[256,1024]{1,0:T(8,128)(2,1)S(1)}, u32[]{:S(2)}) copy-start(bf16[256,1024]{1,0:T(8,128)(2,1)S(1)} %get-tuple-element.50) | copy-start | bytes 1572868
  3.8 11.7 %copy-start.16 = (bf16[256,1024]{1,0:T(8,128)(2,1)}, bf16[256,1024]{1,0:T(8,128)(2,1)S(1)}, u32[]{:S(2)}) copy-start(bf16[256,1024]{1,0:T(8,128)(2,1)S(1)} %get-tuple-element.51) | copy-start | bytes 1572868
  3.9 11.6 %copy-start.29 = (f32[2,32]{1,0:T(2,128)S(1)}, f32[2,32]{1,0:T(2,128)}, u32[]{:S(2)}) copy-start(f32[2,32]{1,0:T(2,128)} %param.16) | copy-start | bytes 772
  3.9 12.1 %copy-start.28 = (f32[2,32]{1,0:T(2,128)S(1)}, f32[2,32]{1,0:T(2,128)}, u32[]{:S(2)}) copy-start(f32[2,32]{1,0:T(2,128)} %param.15) | copy-start | bytes 772
  7.3 12.3 %copy-start.12 = (bf16[512,2176]{1,0:T(8,128)(2,1)}, bf16[512,2176]{1,0:T(8,128)(2,1)S(1)}, u32[]{:S(2)}) copy-start(bf16[512,2176]{1,0:T(8,128)(2,1)S(1)} %convolution_convert_fusion) | copy-start | bytes 6684676
  7.3 9.7 %copy-start.20 = (f32[2,4,2176]{2,1,0:T(4,128)S(1)}, f32[2,4,2176]{2,1,0:T(4,128)}, u32[]{:S(2)}) copy-start(f32[2,4,2176]{2,1,0:T(4,128)} %wr_ref.1) | copy-start | bytes 208900
  7.3 9.7 %copy-start.21 = (f32[2,2176]{1,0:T(2,128)S(1)}, f32[2,2176]{1,0:T(2,128)}, u32[]{:S(2)}) copy-start(f32[2,2176]{1,0:T(2,128)} %param.18) | copy-start | bytes 52228
  7.4 12.3 %collective-permute-start = (bf16[2,3,2176]{2,1,0:T(4,128)(2,1)S(1)}, bf16[2,3,2176]{2,1,0:T(4,128)(2,1)S(1)}, u32[]{:S(2)}, u32[]{:S(2)}) collective-permute-start(bf16[2,3,2176]{2,1,0:T(4,128)(2,1)S(1)} %get-tuple-element.22), channel_id=1, source_target_pairs={{0,1},{1,2},{2,3},{3,4},{4,5},{5,6},{6,7},{7,8},{8,9},{9,10},{10,1... | collective-permute-start | bytes 78344 | tf_op jit(solution)/shard_map/ppermute | solution.py:22
  9.4 10.2 %collective-permute-start.1 = (bf16[2,3,2176]{2,1,0:T(4,128)(2,1)S(1)}, bf16[2,3,2176]{2,1,0:T(4,128)(2,1)S(1)}, u32[]{:S(2)}, u32[]{:S(2)}) collective-permute-start(bf16[2,3,2176]{2,1,0:T(4,128)(2,1)S(1)} %get-tuple-element.21), channel_id=1, source_target_pairs={{1,0},{2,1},{3,2},{4,3},{5,4},{6,5},{7,6},{8,7},{9,8},{10,9},{11,1... | collective-permute-start | bytes 78344 | tf_op jit(solution)/shard_map/ppermute | solution.py:22
  18.4 78.5 %copy-start.19 = (pred[4224]{0:T(1024)(128)(4,1)}, pred[4224]{0:T(1024)(128)(4,1)S(1)}, u32[]{:S(2)}) copy-start(pred[4224]{0:T(1024)(128)(4,1)S(1)} %iota_compare_fusion.4) | copy-start | bytes 12676
  19.6 0.6 copy-start.25
  20.2 0.6 copy-start.26
  32.2 1.4 copy-start.2
  38.7 10.0 %collective-permute-start.2 = (bf16[2,32,4224]{2,1,0:T(8,128)(2,1)S(1)}, bf16[2,32,4224]{2,1,0:T(8,128)(2,1)S(1)}, u32[]{:S(2)}, u32[]{:S(2)}) collective-permute-start(bf16[2,32,4224]{2,1,0:T(8,128)(2,1)S(1)} %fusion.51), channel_id=1, source_target_pairs={{0,1},{2,3},{4,5},{6,7},{8,9},{10,11},{12,13},{14,15},{16,17},{18,... | collective-permute-start | bytes 1622024 | tf_op jit(solution)/shard_map/ppermute | solution.py:44
  42.4 1.3 copy-start.5
  48.8 1.1 copy-start.13
  49.0 2.4 %collective-permute-start.3 = (bf16[2,32,4224]{2,1,0:T(8,128)(2,1)S(1)}, bf16[2,32,4224]{2,1,0:T(8,128)(2,1)S(1)}, u32[]{:S(2)}, u32[]{:S(2)}) collective-permute-start(bf16[2,32,4224]{2,1,0:T(8,128)(2,1)S(1)} %get-tuple-element.13), channel_id=1, source_target_pairs={{1,3},{3,1},{5,7},{7,5},{9,11},{11,9},{13,15},{15,13},{17,19},{19,... | collective-permute-start | bytes 1622024 | tf_op jit(solution)/shard_map/ppermute | solution.py:44
  49.9 3.8 %collective-permute-start.7 = (bf16[2,32,4224]{2,1,0:T(8,128)(2,1)S(1)}, bf16[2,32,4224]{2,1,0:T(8,128)(2,1)S(1)}, u32[]{:S(2)}, u32[]{:S(2)}) collective-permute-start(bf16[2,32,4224]{2,1,0:T(8,128)(2,1)S(1)} %fusion.50), channel_id=1, source_target_pairs={{15,14},{13,12},{11,10},{9,8},{7,6},{5,4},{3,2},{1,0},{31,30},{29,... | collective-permute-start | bytes 1622024 | tf_op jit(solution)/shard_map/ppermute | solution.py:44
  52.0 1.7 %collective-permute-start.4 = (bf16[2,32,4224]{2,1,0:T(8,128)(2,1)S(1)}, bf16[2,32,4224]{2,1,0:T(8,128)(2,1)S(1)}, u32[]{:S(2)}, u32[]{:S(2)}) collective-permute-start(bf16[2,32,4224]{2,1,0:T(8,128)(2,1)S(1)} %get-tuple-element.11), channel_id=1, source_target_pairs={{1,5},{3,7},{5,9},{7,11},{9,13},{11,15},{17,21},{19,23},{21,25},{2... | collective-permute-start | bytes 1622024 | tf_op jit(solution)/shard_map/ppermute | solution.py:44
  55.3 13.0 %collective-permute-start.8 = (bf16[2,32,4224]{2,1,0:T(8,128)(2,1)}, bf16[2,32,4224]{2,1,0:T(8,128)(2,1)S(1)}, u32[]{:S(2)}, u32[]{:S(2)}) collective-permute-start(bf16[2,32,4224]{2,1,0:T(8,128)(2,1)} %get-tuple-element.19), channel_id=1, source_target_pairs={{14,12},{12,14},{10,8},{8,10},{6,4},{4,6},{2,0},{0,2},{30,28},{28,... | collective-permute-start | bytes 1622024 | tf_op jit(solution)/shard_map/ppermute | solution.py:44
  58.9 9.6 %collective-permute-start.5 = (bf16[2,32,4224]{2,1,0:T(8,128)(2,1)}, bf16[2,32,4224]{2,1,0:T(8,128)(2,1)}, u32[]{:S(2)}, u32[]{:S(2)}) collective-permute-start(bf16[2,32,4224]{2,1,0:T(8,128)(2,1)} %get-tuple-element.39), channel_id=1, source_target_pairs={{1,9},{3,11},{5,13},{7,15},{17,25},{19,27},{21,29},{23,31},{33,41}... | collective-permute-start | bytes 1622024 | tf_op jit(solution)/shard_map/ppermute | solution.py:44
  61.6 13.5 %copy-start.10 = (bf16[512,1024]{1,0:T(8,128)(2,1)}, bf16[512,1024]{1,0:T(8,128)(2,1)S(1)}, u32[]{:S(2)}) copy-start(bf16[512,1024]{1,0:T(8,128)(2,1)S(1)} %pad_maximum_fusion.2) | copy-start | bytes 3145732
  61.7 6.8 %copy-start.8 = (f32[2,32,4224]{2,1,0:T(8,128)S(1)}, f32[2,32,4224]{2,1,0:T(8,128)}, u32[]{:S(2)}) copy-start(f32[2,32,4224]{2,1,0:T(8,128)} %get-tuple-element.20) | copy-start | bytes 3244036
  68.5 6.7 %copy-start.32 = (bf16[1024,2048]{1,0:T(8,128)(2,1)S(1)}, bf16[1024,2048]{1,0:T(8,128)(2,1)}, u32[]{:S(2)}) copy-start(bf16[1024,2048]{1,0:T(8,128)(2,1)} %param.12) | copy-start | bytes 12582916
  71.5 14.2 %collective-permute-start.9 = (bf16[2,32,4224]{2,1,0:T(8,128)(2,1)}, bf16[2,32,4224]{2,1,0:T(8,128)(2,1)S(1)}, u32[]{:S(2)}, u32[]{:S(2)}) collective-permute-start(bf16[2,32,4224]{2,1,0:T(8,128)(2,1)} %get-tuple-element.37), channel_id=1, source_target_pairs={{14,10},{12,8},{10,6},{8,4},{6,2},{4,0},{30,26},{28,24},{26,22},{2... | collective-permute-start | bytes 1622024 | tf_op jit(solution)/shard_map/ppermute | solution.py:44
  79.5 5.3 %copy-start.27 = (f32[2048]{0:T(1024)S(1)}, f32[2048]{0:T(1024)}, u32[]{:S(2)}) copy-start(f32[2048]{0:T(1024)} %param.20) | copy-start | bytes 24580
  79.5 6.1 %copy-start.30 = (f32[2,32]{1,0:T(2,128)S(1)}, f32[2,32]{1,0:T(2,128)}, u32[]{:S(2)}) copy-start(f32[2,32]{1,0:T(2,128)} %param.19) | copy-start | bytes 772
  84.9 6.3 %copy-start.17 = (bf16[2,32,4224]{2,1,0:T(8,128)(2,1)S(1)}, bf16[2,32,4224]{2,1,0:T(8,128)(2,1)}, u32[]{:S(2)}) copy-start(bf16[2,32,4224]{2,1,0:T(8,128)(2,1)} %get-tuple-element.9) | copy-start | bytes 1622020
  85.9 10.9 %collective-permute-start.10 = (bf16[2,32,4224]{2,1,0:T(8,128)(2,1)S(1)}, bf16[2,32,4224]{2,1,0:T(8,128)(2,1)S(1)}, u32[]{:S(2)}, u32[]{:S(2)}) collective-permute-start(bf16[2,32,4224]{2,1,0:T(8,128)(2,1)S(1)} %add_convert_fusion), channel_id=1, source_target_pairs={{14,6},{12,4},{10,2},{8,0},{30,22},{28,20},{26,18},{24,16},{46,38}... | collective-permute-start | bytes 1622024 | tf_op jit(solution)/shard_map/ppermute | solution.py:44
  91.2 18.1 %copy-start.3 = (bf16[2,256,2048]{1,2,0:T(8,128)(2,1)S(1)}, bf16[2,256,2048]{1,2,0:T(8,128)(2,1)}, u32[]{:S(2)}) copy-start(bf16[2,256,2048]{1,2,0:T(8,128)(2,1)} %copy-done.2) | copy-start | bytes 6291460
  91.2 26.2 %collective-permute-start.6 = (bf16[2,32,4224]{2,1,0:T(8,128)(2,1)S(1)}, bf16[2,32,4224]{2,1,0:T(8,128)(2,1)S(1)}, u32[]{:S(2)}, u32[]{:S(2)}) collective-permute-start(bf16[2,32,4224]{2,1,0:T(8,128)(2,1)S(1)} %copy-done.17), channel_id=1, source_target_pairs={{1,0},{3,2},{5,4},{7,6},{9,8},{11,10},{13,12},{15,14},{17,16},{19,... | collective-permute-start | bytes 1622024 | tf_op jit(solution)/shard_map/ppermute | solution.py:44
  97.3 19.9 %copy-start.14 = (bf16[2,32,4224]{2,1,0:T(8,128)(2,1)S(1)}, bf16[2,32,4224]{2,1,0:T(8,128)(2,1)}, u32[]{:S(2)}) copy-start(bf16[2,32,4224]{2,1,0:T(8,128)(2,1)} %copy-done.13) | copy-start | bytes 1622020
  97.3 20.2 %collective-permute-start.11 = (bf16[2,32,4224]{2,1,0:T(8,128)(2,1)S(1)}, bf16[2,32,4224]{2,1,0:T(8,128)(2,1)S(1)}, u32[]{:S(2)}, u32[]{:S(2)}) collective-permute-start(bf16[2,32,4224]{2,1,0:T(8,128)(2,1)S(1)} %get-tuple-element.15), channel_id=1, source_target_pairs={{14,15},{12,13},{10,11},{8,9},{6,7},{4,5},{2,3},{0,1},{30,31},{28,... | collective-permute-start | bytes 1622024 | tf_op jit(solution)/shard_map/ppermute | solution.py:44
  115.1 2.4 %copy-start.9 = (f32[2,32,4224]{2,1,0:T(8,128)S(1)}, f32[2,32,4224]{2,1,0:T(8,128)}, u32[]{:S(2)}) copy-start(f32[2,32,4224]{2,1,0:T(8,128)} %get-tuple-element.10) | copy-start | bytes 3244036
  115.1 2.4 %slice-start = ((pred[4224]{0:T(1024)(128)(4,1)}), pred[4096]{0:T(1024)(128)(4,1)S(1)}, s32[]{:S(2)}) async-start(pred[4224]{0:T(1024)(128)(4,1)} %copy-done.19), calls=%async_computation | async-start | bytes 8192 | tf_op jit(solution)/shard_map/slice | solution.py:60
  133.7 3.7 %copy-start.4 = (bf16[2,256,2048]{1,2,0:T(8,128)(2,1)S(1)}, bf16[2,256,2048]{1,2,0:T(8,128)(2,1)}, u32[]{:S(2)}) copy-start(bf16[2,256,2048]{1,2,0:T(8,128)(2,1)} %copy-done.2) | copy-start | bytes 6291460
  133.7 3.7 %copy-start.6 = (bf16[2,256,2048]{1,2,0:T(8,128)(2,1)S(1)}, bf16[2,256,2048]{1,2,0:T(8,128)(2,1)}, u32[]{:S(2)}) copy-start(bf16[2,256,2048]{1,2,0:T(8,128)(2,1)} %copy-done.5) | copy-start | bytes 6291460
  133.7 3.7 %copy-start.18 = (f32[2,256,256]{2,1,0:T(8,128)S(1)}, f32[2,256,256]{2,1,0:T(8,128)}, u32[]{:S(2)}) copy-start(f32[2,256,256]{2,1,0:T(8,128)} %fusion.71) | copy-start | bytes 1572868
  133.7 3.8 %copy-start.22 = (pred[256,256]{1,0:T(8,128)(4,1)S(1)}, pred[256,256]{1,0:T(8,128)(4,1)}, u32[]{:S(2)}) copy-start(pred[256,256]{1,0:T(8,128)(4,1)} %iota_compare_fusion) | copy-start | bytes 196612
  133.7 3.8 %copy-start.23 = (f32[2,256,32]{1,2,0:T(8,128)S(1)}, f32[2,256,32]{1,2,0:T(8,128)}, u32[]{:S(2)}) copy-start(f32[2,256,32]{1,2,0:T(8,128)} %get-tuple-element.29) | copy-start | bytes 196612
  133.7 3.8 %copy-start.24 = (f32[2,256,32]{1,2,0:T(8,128)S(1)}, f32[2,256,32]{1,2,0:T(8,128)}, u32[]{:S(2)}) copy-start(f32[2,256,32]{1,2,0:T(8,128)} %get-tuple-element.31) | copy-start | bytes 196612
  137.5 13.3 %copy-start.7 = (bf16[2048,1024]{1,0:T(8,128)(2,1)S(1)}, bf16[2048,1024]{1,0:T(8,128)(2,1)}, u32[]{:S(2)}) copy-start(bf16[2048,1024]{1,0:T(8,128)(2,1)} %param.21) | copy-start | bytes 12582916
  137.5 13.3 %copy-start.11 = (bf16[512,1024]{1,0:T(8,128)(2,1)S(1)}, bf16[512,1024]{1,0:T(8,128)(2,1)}, u32[]{:S(2)}) copy-start(bf16[512,1024]{1,0:T(8,128)(2,1)} %copy-done.10) | copy-start | bytes 3145732
  153.4 2.2 %copy-start.1 = (bf16[1024,32]{0,1:T(8,128)(2,1)S(1)}, bf16[1024,32]{0,1:T(8,128)(2,1)}, u32[]{:S(2)}) copy-start(bf16[1024,32]{0,1:T(8,128)(2,1)} %param.14) | copy-start | bytes 196612

commit v12 on v10

--- a/solution.py
+++ b/solution.py
@@ -7,7 +7,6 @@
 
 NS = 64
 K = 4
-Q = 256
 DECAY_LANES = 128
 
 
@@ -131,7 +130,9 @@
     mixing = (scores[:, None] * decay).astype(jnp.bfloat16)
     values32 = values.astype(jnp.float32)
     scaled = (values32 * step[..., None]).astype(jnp.bfloat16)
-    diagonal = jnp.einsum("rhts,rshp->rthp", mixing, scaled, preferred_element_type=jnp.float32)
+    diagonal = jnp.einsum(
+        "rhts,rshp->rthp", mixing, scaled, preferred_element_type=jnp.float32
+    )
     last = cum[:, 0] if falling else cum[:, -1]
     to_end = jnp.exp(last[:, None, :] - cum)
     weighted = (values32 * (step * to_end)[..., None]).astype(jnp.bfloat16)
@@ -209,6 +210,7 @@
 
 def solution(mesh):
     placed = (P(("dp", "ctx"), None, None), P(), P(), P(), P(), P(), P(), P(), P(), P(), P())
+
     return jax.shard_map(
         body, mesh=mesh, in_specs=placed, out_specs=P(("dp", "ctx"), None, None), check_vma=False
     )

time: 138 us -> 138 us (level)
  no operation moved by 1% of the time
where the time goes in v12:
time: 138 us
  matrix products  40.7 us (29%)
  starting transfers between devices  36.1 us (26%)
  local copies, waits for them, and re-layouts  29.2 us (21%)
  waiting for transfers between devices  10.7 us (8%)
  other arithmetic  10.5 us (8%)
  Pallas kernels  9.66 us (7%)
    ppermute x10, starting transfers between devices, send(): moved = lax.ppermute(value.astype(jnp.bfloat16), 'ctx', pairs)  27.7 us
    dot_general x2, matrix products, group_terms(): jnp.einsum('rhts,rshp->rthp', mixing, scaled, preferred_element_type=jnp....  11.4 us
    ppermute x10, waiting for transfers between devices, send(): moved = lax.ppermute(value.astype(jnp.bfloat16), 'ctx', pairs)  10.7 us
    dot_general x2, matrix products, finish(): jnp.einsum('rtn,rhpn->rthp', reads.astype(jnp.float32), entering, precisi...  10.1 us
    pallas_call x1, Pallas kernels, convolve(): pl.pallas_call(conv_kernel, grid=grid, in_specs=[pl.BlockSpec((1, length,...  9.66 us
    ppermute x2, starting transfers between devices, shifted(): return lax.ppermute(value, 'ctx', pairs)  8.38 us
    dot_general x2, matrix products, group_terms(): jnp.einsum('rshp,rsn->rhpn', weighted, keys_in, preferred_element_type=jn...  5.74 us
    transpose x1, local copies, waits for them, and re-layouts, body(): jnp.transpose(gate.reshape(2, heads, head_size, length).astype(jnp.float3...  5.34 us
  transfers between devices with their start and end apart: 12, of which 2 were waited for; matrix products, arithmetic and copies ran while one was open for 30% of the time, Pallas kernels for 0%

profile of v12, /device:TPU:1, one launch (start us, length us, event | category | flops | bytes accessed | tf_op | source)
XLA Modules:
  0.0 137.6 jit_solution(15927077093515104798)
XLA Ops:
  0.0 3.4 %fusion.83 = (bf16[256,1,1024]{2,1,0:T(2,128)(2,1)S(1)}, bf16[256,1,1024]{2,1,0:T(2,128)(2,1)S(1)}) fusion(bf16[256,2,1024]{2,1,0:T(2,128)(2,1)} %param.11), kind=kLoop, calls=%fused_computation.139 | loop fusion | bytes 2097152 | tf_op jit(solution)/shard_map/slice | solution.py:170
  3.8 3.4 %convolution_convert_fusion = bf16[512,2176]{1,0:T(8,128)(2,1)S(1)} fusion(bf16[1024,2176]{1,0:T(8,128)(2,1)S(1)} %copy-done.26, bf16[256,1024]{1,0:T(8,128)(2,1)S(1)} %get-tuple-element.50, bf16[256,1024]{1,0:T(8,128)(2,1)S(1)} %get-tuple-element.51), kind=kOutput, calls=%fused_computation.20 | convolution fusion | flops 2284912640 | bytes 7733248 | tf_op jit(solution)/shard_map/dot_general | solution.py:174
  7.3 6.3 %collective-permute-start = (bf16[2,3,2176]{2,1,0:T(4,128)(2,1)S(1)}, bf16[2,3,2176]{2,1,0:T(4,128)(2,1)S(1)}, u32[]{:S(2)}, u32[]{:S(2)}) collective-permute-start(bf16[2,3,2176]{2,1,0:T(4,128)(2,1)S(1)} %get-tuple-element.22), channel_id=1, source_target_pairs={{0,1},{1,2},{2,3},{3,4},{4,5},{5,6},{6,7},{7,8},{8,9},{9,10},{10,1... | collective-permute-start | bytes 78344 | tf_op jit(solution)/shard_map/ppermute | solution.py:21
  13.6 2.1 %collective-permute-start.1 = (bf16[2,3,2176]{2,1,0:T(4,128)(2,1)S(1)}, bf16[2,3,2176]{2,1,0:T(4,128)(2,1)S(1)}, u32[]{:S(2)}, u32[]{:S(2)}) collective-permute-start(bf16[2,3,2176]{2,1,0:T(4,128)(2,1)S(1)} %get-tuple-element.21), channel_id=1, source_target_pairs={{1,0},{2,1},{3,2},{4,3},{5,4},{6,5},{7,6},{8,7},{9,8},{10,9},{11,1... | collective-permute-start | bytes 78344 | tf_op jit(solution)/shard_map/ppermute | solution.py:21
  15.7 1.0 pad_maximum_fusion.2
  17.8 0.6 bitcast_exponential_fusion
  18.9 0.6 pad_maximum_fusion.4.wf_ref
  19.6 0.6 broadcast_in_dim.43.br_ref
  20.2 0.6 broadcast_in_dim.44.bf_ref
  22.1 9.7 %shard_map.109 = (bf16[2,2176,256]{2,1,0:T(8,128)(2,1)}, bf16[2,2176,256]{2,1,0:T(8,128)(2,1)}) custom-call(bf16[2,256,2176]{2,1,0:T(8,128)(2,1)} %bitcast.107, bf16[2,3,2176]{2,1,0:T(4,128)(2,1)} %copy-done.20, bf16[2,3,2176]{2,1,0:T(4,128)(2,1)} %copy-done.21, f32[2,4,2176]{2,1,0:T(4,128)} %wr_ref.1, f32[2,1,2176]{2,1,0:T(1,128)} %broadcast_in_dim.43.br_ref, ...), custom_call_target="tpu_custom_call" | custom-call | tf_op jit(solution)/shard_map/pallas_call | solution.py:85
  31.7 1.7 %slice.163 = bf16[2,256,2048]{1,2,0:T(8,128)(2,1)S(1)} slice(bf16[2,256,2176]{1,2,0:T(8,128)(2,1)} %bitcast.108), slice={[0:2], [0:256], [0:2048]} | slice | bytes 4194304 | tf_op jit(solution)/shard_map/slice | solution.py:109
  33.5 1.4 copy-done.2
  34.8 2.9 %fusion.30 = f32[2,32,64,64]{3,2,1,0:T(8,128)} fusion(bf16[2,256,32,64]{1,3,2,0:T(8,128)(2,1)S(1)} %bitcast.92, f32[2,256,32]{1,2,0:T(8,128)S(1)} %get-tuple-element.32, bf16[2,256,2176]{1,2,0:T(8,128)(2,1)} %bitcast.109), kind=kOutput, calls=%fused_computation.38 | convolution fusion | flops 137363456 | bytes 3276800 | tf_op jit(solution)/shard_map/rshp,rsn->rhpn/dot_general | solution.py:139
  37.7 2.1 %reshape.142 = f32[2,32,4096]{2,1,0:T(8,128)S(1)} reshape(f32[2,32,64,64]{3,2,1,0:T(8,128)} %fusion.30) | data formatting | bytes 2097152 | tf_op jit(solution)/shard_map/reshape | solution.py:145
  39.9 1.3 collective-permute-start.7
  41.3 0.6 bitcast_exponential_fusion.1
  41.9 1.7 %slice.150 = bf16[2,256,2048]{1,2,0:T(8,128)(2,1)S(1)} slice(bf16[2,256,2176]{1,2,0:T(8,128)(2,1)} %bitcast.102), slice={[0:2], [0:256], [0:2048]} | slice | bytes 4194304 | tf_op jit(solution)/shard_map/slice | solution.py:109
  43.7 1.3 copy-done.5
  45.0 2.9 %fusion.33 = f32[2,32,64,64]{3,2,1,0:T(8,128)} fusion(bf16[2,256,32,64]{1,3,2,0:T(8,128)(2,1)S(1)} %bitcast.95, f32[2,256,32]{1,2,0:T(8,128)S(1)} %get-tuple-element.30, bf16[2,256,2176]{1,2,0:T(8,128)(2,1)} %bitcast.103), kind=kOutput, calls=%fused_computation.39 | convolution fusion | flops 137363456 | bytes 3276800 | tf_op jit(solution)/shard_map/rshp,rsn->rhpn/dot_general | solution.py:139
  47.8 2.1 %reshape.140 = f32[2,32,4096]{2,1,0:T(8,128)S(1)} reshape(f32[2,32,64,64]{3,2,1,0:T(8,128)} %fusion.33) | data formatting | bytes 2097152 | tf_op jit(solution)/shard_map/reshape | solution.py:145
  50.8 0.7 collective-permute-start.8
  51.5 0.9 fusion.49
  52.5 1.6 %collective-permute-start.2 = (bf16[2,32,4224]{2,1,0:T(8,128)(2,1)}, bf16[2,32,4224]{2,1,0:T(8,128)(2,1)}, u32[]{:S(2)}, u32[]{:S(2)}) collective-permute-start(bf16[2,32,4224]{2,1,0:T(8,128)(2,1)} %fusion.49), channel_id=1, source_target_pairs={{0,1},{2,3},{4,5},{6,7},{8,9},{10,11},{12,13},{14,15},{16,17},{18,... | collective-permute-start | bytes 1622024 | tf_op jit(solution)/shard_map/ppermute | solution.py:43
  54.3 1.2 fusion.77
  55.5 0.7 collective-permute-start.9
  56.2 4.4 %convert_bitcast_fusion = f32[2,2048,256]{1,2,0:T(8,128)} fusion(bf16[2,256,1024]{2,1,0:T(8,128)(2,1)S(1)} %bitcast.99, bf16[1024,2048]{1,0:T(8,128)(2,1)S(1)} %copy-done.27), kind=kOutput, calls=%fused_computation.33 | convolution fusion | flops 2149580800 | bytes 9437184 | tf_op jit(solution)/shard_map/rtd,de->ret/dot_general | solution.py:171
  60.6 5.3 %copy.41 = f32[2,2048,256]{2,1,0:T(8,128)} copy(f32[2,2048,256]{1,2,0:T(8,128)} %convert_bitcast_fusion) | data formatting | bytes 8388608 | tf_op jit(solution)/shard_map/transpose | solution.py:191
  66.1 1.4 %fusion.81 = (bf16[2,32,4224]{2,1,0:T(8,128)(2,1)S(1)}, f32[2,32,4224]{2,1,0:T(8,128)S(1)}, bf16[2,32,4224]{2,1,0:T(8,128)(2,1)S(1)}) fusion(f32[2,32,128]{2,1,0:T(8,128)S(1)} %broadcast_in_dim.82, f32[2,32,4096]{2,1,0:T(8,128)S(1)} %reshape.140, pred[4224]{0:T(1024)(128)(4,1)S(1)} %iota_compare_fusion.4, bf16[2,32,4224]{2,1,0:T(8,128)(2,1)} %collective-permute-done.2, ...), kind=kLoop, calls=%fused_computation.137 | loop fusion | flops 2973696 | bytes 5411456 | tf_op jit(solution)/shard_map/convert_element_type | solution.py:43
  67.6 5.9 %collective-permute-start.3 = (bf16[2,32,4224]{2,1,0:T(8,128)(2,1)S(1)}, bf16[2,32,4224]{2,1,0:T(8,128)(2,1)S(1)}, u32[]{:S(2)}, u32[]{:S(2)}) collective-permute-start(bf16[2,32,4224]{2,1,0:T(8,128)(2,1)S(1)} %get-tuple-element.19), channel_id=1, source_target_pairs={{1,3},{3,1},{5,7},{7,5},{9,11},{11,9},{13,15},{15,13},{17,19},{19,... | collective-permute-start | bytes 1622024 | tf_op jit(solution)/shard_map/ppermute | solution.py:43
  73.5 0.7 collective-permute-start.10
  74.5 5.7 %collective-permute-done.3 = bf16[2,32,4224]{2,1,0:T(8,128)(2,1)S(1)} collective-permute-done((bf16[2,32,4224]{2,1,0:T(8,128)(2,1)S(1)}, bf16[2,32,4224]{2,1,0:T(8,128)(2,1)S(1)}, u32[]{:S(2)}, u32[]{:S(2)}) %collective-permute-start.3) | collective-permute-done | bytes 540704 | tf_op jit(solution)/shard_map/ppermute | solution.py:43
  80.4 0.8 fusion.76
  81.1 4.6 %collective-permute-start.4 = (bf16[2,32,4224]{2,1,0:T(8,128)(2,1)S(1)}, bf16[2,32,4224]{2,1,0:T(8,128)(2,1)S(1)}, u32[]{:S(2)}, u32[]{:S(2)}) collective-permute-start(bf16[2,32,4224]{2,1,0:T(8,128)(2,1)S(1)} %get-tuple-element.37), channel_id=1, source_target_pairs={{1,5},{3,7},{5,9},{7,11},{9,13},{11,15},{17,21},{19,23},{21,25},{2... | collective-permute-start | bytes 1622024 | tf_op jit(solution)/shard_map/ppermute | solution.py:43
  85.8 1.1 fusion.62
  87.1 5.0 %collective-permute-done.4 = bf16[2,32,4224]{2,1,0:T(8,128)(2,1)S(1)} collective-permute-done((bf16[2,32,4224]{2,1,0:T(8,128)(2,1)S(1)}, bf16[2,32,4224]{2,1,0:T(8,128)(2,1)S(1)}, u32[]{:S(2)}, u32[]{:S(2)}) %collective-permute-start.4) | collective-permute-done | bytes 540704 | tf_op jit(solution)/shard_map/ppermute | solution.py:43
  92.3 7.3 %collective-permute-start.5 = (bf16[2,32,4224]{2,1,0:T(8,128)(2,1)S(1)}, bf16[2,32,4224]{2,1,0:T(8,128)(2,1)S(1)}, u32[]{:S(2)}, u32[]{:S(2)}) collective-permute-start(bf16[2,32,4224]{2,1,0:T(8,128)(2,1)S(1)} %add_convert_fusion.1), channel_id=1, source_target_pairs={{1,9},{3,11},{5,13},{7,15},{17,25},{19,27},{21,29},{23,31},{33,41}... | collective-permute-start | bytes 1622024 | tf_op jit(solution)/shard_map/ppermute | solution.py:43
  99.6 5.7 %fusion.1 = f32[2,32,64,256]{3,2,1,0:T(8,128)} fusion(f32[2,32,256]{2,1,0:T(8,128)S(1)} %fusion.50, f32[2,256,256]{2,1,0:T(8,128)S(1)} %fusion.62, pred[256,256]{1,0:T(8,128)(4,1)S(1)} %iota_compare_fusion, bf16[2,256,32,64]{1,3,2,0:T(8,128)(2,1)S(1)} %bitcast.93, f32[2,256,32]{1,2,0:T(8,128)S(1)} %get-tuple-element.34), kind=kOutput, calls=%fused_computation.3 | convolution fusion | flops 556793856 | bytes 7012352 | tf_op jit(solution)/shard_map/rhts,rshp->rthp/dot_general | solution.py:133
  105.3 1.1 fusion.67
  106.5 1.4 %collective-permute-start.11 = (bf16[2,32,4224]{2,1,0:T(8,128)(2,1)S(1)}, bf16[2,32,4224]{2,1,0:T(8,128)(2,1)S(1)}, u32[]{:S(2)}, u32[]{:S(2)}) collective-permute-start(bf16[2,32,4224]{2,1,0:T(8,128)(2,1)S(1)} %get-tuple-element.9), channel_id=1, source_target_pairs={{14,15},{12,13},{10,11},{8,9},{6,7},{4,5},{2,3},{0,1},{30,31},{28,... | collective-permute-start | bytes 1622024 | tf_op jit(solution)/shard_map/ppermute | solution.py:43
  108.5 3.4 %collective-permute-start.6 = (bf16[2,32,4224]{2,1,0:T(8,128)(2,1)S(1)}, bf16[2,32,4224]{2,1,0:T(8,128)(2,1)S(1)}, u32[]{:S(2)}, u32[]{:S(2)}) collective-permute-start(bf16[2,32,4224]{2,1,0:T(8,128)(2,1)S(1)} %get-tuple-element.15), channel_id=1, source_target_pairs={{1,0},{3,2},{5,4},{7,6},{9,8},{11,10},{13,12},{15,14},{17,16},{19,... | collective-permute-start | bytes 1622024 | tf_op jit(solution)/shard_map/ppermute | solution.py:43
  112.0 5.7 %fusion = f32[2,32,64,256]{3,2,1,0:T(8,128)} fusion(f32[2,32,256]{2,1,0:T(8,128)S(1)} %fusion.52, f32[2,256,256]{2,1,0:T(8,128)S(1)} %fusion.67, pred[256,256]{1,0:T(8,128)(4,1)S(1)} %iota_compare_fusion.1, bf16[2,256,32,64]{1,3,2,0:T(8,128)(2,1)S(1)} %bitcast.96, f32[2,256,32]{1,2,0:T(8,128)S(1)} %get-tuple-element.33), kind=kOutput, calls=%fused_computation.2 | convolution fusion | flops 556793856 | bytes 7012352 | tf_op jit(solution)/shard_map/rhts,rshp->rthp/dot_general | solution.py:133
  117.8 1.1 convert_element_type.145
  119.6 2.2 %reshape.143 = f32[2,32,64,64]{3,2,1,0:T(8,128)} reshape(f32[2,32,4096]{2,1,0:T(8,128)S(1)} %get-tuple-element.40) | data formatting | bytes 2097152 | tf_op jit(solution)/shard_map/reshape | solution.py:155
  121.8 0.8 reshape.141
  122.7 2.8 %fusion.57 = f32[2,256,32,64]{1,3,2,0:T(8,128)S(1)} fusion(f32[2,32,64,64]{3,2,1,0:T(8,128)S(1)} %reshape.141, bf16[2,256,2176]{1,2,0:T(8,128)(2,1)} %bitcast.105), kind=kOutput, calls=%fused_computation.90 | convolution fusion | flops 805306368 | bytes 5308416 | tf_op jit(solution)/shard_map/rtn,rhpn->rthp/dot_general | solution.py:156
  125.5 7.3 %multiply_reduce_fusion = (f32[2,256]{1,0:T(2,128)S(1)}, f32[2,256,32,64]{1,3,2,0:T(8,128)S(1)}) fusion(f32[2,256,32,64]{1,3,2,0:T(8,128)} %bitcast.101, f32[2,256,32]{1,2,0:T(8,128)S(1)} %copy-done.18, f32[2,32,64,64]{3,2,1,0:T(8,128)S(1)} %copy-done.14, bf16[2,256,2176]{1,2,0:T(8,128)(2,1)} %bitcast.111, bf16[2,256,32,64]{1,3,2,0:T(8,128)(2,1)S(1)} %bitcast.94, ...), kind=kOutput, calls=%fused_computation.35 | convolution fusion | flops 824180224 | bytes 26413568 | tf_op jit(solution)/shard_map/rtn,rhpn->rthp/dot_general | solution.py:156
  132.9 2.4 %fusion.36 = bf16[2,256,1024]{2,1,0:T(8,128)(2,1)S(1)} fusion(bf16[2,256,1024]{2,1,0:T(8,128)(2,1)S(1)} %bitcast.100, bf16[32,64,1024,1]{2,1,0,3:T(8,128)(2,1)S(1)} %bitcast.98, f32[2,256,32,64]{1,3,2,0:T(8,128)S(1)} %get-tuple-element.49, f32[32,64]{1,0:T(8,128)S(1)} %mul.325, f32[2,256]{1,0:T(2,128)S(1)} %add_rsqrt_fusion), kind=kOutput, calls=%fused_computation.41 | convolution fusion | flops 2152202240 | bytes 10496000 | tf_op jit(solution)/shard_map/rthp,hpd->rtd/dot_general | solution.py:199
  135.5 2.0 %copy.42 = bf16[256,2,1024]{2,1,0:T(2,128)(2,1)} copy(bf16[256,2,1024]{2,0,1:T(8,128)(2,1)S(1)} %pad_maximum_fusion.3) | data formatting | bytes 2097152 | tf_op jit(solution)/shard_map/stack | solution.py:208
  (115 shorter events, 6.9 us)
Async XLA Ops:
  0.0 16.8 %copy-start = (bf16[1024,32]{0,1:T(8,128)(2,1)S(1)}, bf16[1024,32]{0,1:T(8,128)(2,1)}, u32[]{:S(2)}) copy-start(bf16[1024,32]{0,1:T(8,128)(2,1)} %param.14) | copy-start | bytes 196612
  0.0 3.8 %copy-start.26 = (bf16[1024,2176]{1,0:T(8,128)(2,1)S(1)}, bf16[1024,2176]{1,0:T(8,128)(2,1)}, u32[]{:S(2)}) copy-start(bf16[1024,2176]{1,0:T(8,128)(2,1)} %param.13) | copy-start | bytes 13369348
  7.2 10.2 %copy-start.11 = (bf16[512,2176]{1,0:T(8,128)(2,1)}, bf16[512,2176]{1,0:T(8,128)(2,1)S(1)}, u32[]{:S(2)}) copy-start(bf16[512,2176]{1,0:T(8,128)(2,1)S(1)} %convolution_convert_fusion) | copy-start | bytes 6684676
  7.2 9.5 %copy-start.24 = (f32[2,32]{1,0:T(2,128)S(1)}, f32[2,32]{1,0:T(2,128)}, u32[]{:S(2)}) copy-start(f32[2,32]{1,0:T(2,128)} %param.16) | copy-start | bytes 772
  7.2 10.0 %copy-start.23 = (f32[2,32]{1,0:T(2,128)S(1)}, f32[2,32]{1,0:T(2,128)}, u32[]{:S(2)}) copy-start(f32[2,32]{1,0:T(2,128)} %param.15) | copy-start | bytes 772
  7.3 13.6 %collective-permute-start = (bf16[2,3,2176]{2,1,0:T(4,128)(2,1)S(1)}, bf16[2,3,2176]{2,1,0:T(4,128)(2,1)S(1)}, u32[]{:S(2)}, u32[]{:S(2)}) collective-permute-start(bf16[2,3,2176]{2,1,0:T(4,128)(2,1)S(1)} %get-tuple-element.22), channel_id=1, source_target_pairs={{0,1},{1,2},{2,3},{3,4},{4,5},{5,6},{6,7},{7,8},{8,9},{9,10},{10,1... | collective-permute-start | bytes 78344 | tf_op jit(solution)/shard_map/ppermute | solution.py:21
  13.6 4.8 %copy-start.16 = (f32[2,4,2176]{2,1,0:T(4,128)S(1)}, f32[2,4,2176]{2,1,0:T(4,128)}, u32[]{:S(2)}) copy-start(f32[2,4,2176]{2,1,0:T(4,128)} %wr_ref.1) | copy-start | bytes 208900
  13.6 4.8 %copy-start.17 = (f32[2,2176]{1,0:T(2,128)S(1)}, f32[2,2176]{1,0:T(2,128)}, u32[]{:S(2)}) copy-start(f32[2,2176]{1,0:T(2,128)} %param.18) | copy-start | bytes 52228
  13.6 7.2 %collective-permute-start.1 = (bf16[2,3,2176]{2,1,0:T(4,128)(2,1)S(1)}, bf16[2,3,2176]{2,1,0:T(4,128)(2,1)S(1)}, u32[]{:S(2)}, u32[]{:S(2)}) collective-permute-start(bf16[2,3,2176]{2,1,0:T(4,128)(2,1)S(1)} %get-tuple-element.21), channel_id=1, source_target_pairs={{1,0},{2,1},{3,2},{4,3},{5,4},{6,5},{7,6},{8,7},{9,8},{10,9},{11,1... | collective-permute-start | bytes 78344 | tf_op jit(solution)/shard_map/ppermute | solution.py:21
  19.6 88.5 %copy-start.15 = (pred[4224]{0:T(1024)(128)(4,1)}, pred[4224]{0:T(1024)(128)(4,1)S(1)}, u32[]{:S(2)}) copy-start(pred[4224]{0:T(1024)(128)(4,1)S(1)} %iota_compare_fusion.4) | copy-start | bytes 12676
  20.8 0.6 copy-start.20
  21.4 0.6 copy-start.21
  33.4 1.4 copy-start.2
  39.9 10.0 %collective-permute-start.7 = (bf16[2,32,4224]{2,1,0:T(8,128)(2,1)S(1)}, bf16[2,32,4224]{2,1,0:T(8,128)(2,1)S(1)}, u32[]{:S(2)}, u32[]{:S(2)}) collective-permute-start(bf16[2,32,4224]{2,1,0:T(8,128)(2,1)S(1)} %fusion.48), channel_id=1, source_target_pairs={{15,14},{13,12},{11,10},{9,8},{7,6},{5,4},{3,2},{1,0},{31,30},{29,... | collective-permute-start | bytes 1622024 | tf_op jit(solution)/shard_map/ppermute | solution.py:43
  43.6 1.3 copy-start.5
  50.0 0.8 copy-start.12
  50.8 3.4 %collective-permute-start.8 = (bf16[2,32,4224]{2,1,0:T(8,128)(2,1)S(1)}, bf16[2,32,4224]{2,1,0:T(8,128)(2,1)S(1)}, u32[]{:S(2)}, u32[]{:S(2)}) collective-permute-start(bf16[2,32,4224]{2,1,0:T(8,128)(2,1)S(1)} %get-tuple-element.13), channel_id=1, source_target_pairs={{14,12},{12,14},{10,8},{8,10},{6,4},{4,6},{2,0},{0,2},{30,28},{28,... | collective-permute-start | bytes 1622024 | tf_op jit(solution)/shard_map/ppermute | solution.py:43
  51.5 4.7 %copy-start.27 = (bf16[1024,2048]{1,0:T(8,128)(2,1)S(1)}, bf16[1024,2048]{1,0:T(8,128)(2,1)}, u32[]{:S(2)}) copy-start(bf16[1024,2048]{1,0:T(8,128)(2,1)} %param.12) | copy-start | bytes 12582916
  52.5 13.6 %collective-permute-start.2 = (bf16[2,32,4224]{2,1,0:T(8,128)(2,1)}, bf16[2,32,4224]{2,1,0:T(8,128)(2,1)}, u32[]{:S(2)}, u32[]{:S(2)}) collective-permute-start(bf16[2,32,4224]{2,1,0:T(8,128)(2,1)} %fusion.49), channel_id=1, source_target_pairs={{0,1},{2,3},{4,5},{6,7},{8,9},{10,11},{12,13},{14,15},{16,17},{18,... | collective-permute-start | bytes 1622024 | tf_op jit(solution)/shard_map/ppermute | solution.py:43
  54.2 2.1 %copy-start.9 = (bf16[512,1024]{1,0:T(8,128)(2,1)S(1)}, bf16[512,1024]{1,0:T(8,128)(2,1)}, u32[]{:S(2)}) copy-start(bf16[512,1024]{1,0:T(8,128)(2,1)} %pad_maximum_fusion.2) | copy-start | bytes 3145732
  55.5 10.6 %collective-permute-start.9 = (bf16[2,32,4224]{2,1,0:T(8,128)(2,1)}, bf16[2,32,4224]{2,1,0:T(8,128)(2,1)S(1)}, u32[]{:S(2)}, u32[]{:S(2)}) collective-permute-start(bf16[2,32,4224]{2,1,0:T(8,128)(2,1)} %get-tuple-element.11), channel_id=1, source_target_pairs={{14,10},{12,8},{10,6},{8,4},{6,2},{4,0},{30,26},{28,24},{26,22},{2... | collective-permute-start | bytes 1622024 | tf_op jit(solution)/shard_map/ppermute | solution.py:43
  60.6 5.3 %copy-start.22 = (f32[2048]{0:T(1024)S(1)}, f32[2048]{0:T(1024)}, u32[]{:S(2)}) copy-start(f32[2048]{0:T(1024)} %param.20) | copy-start | bytes 24580
  66.1 8.1 %copy-start.25 = (f32[2,32]{1,0:T(2,128)S(1)}, f32[2,32]{1,0:T(2,128)}, u32[]{:S(2)}) copy-start(f32[2,32]{1,0:T(2,128)} %param.19) | copy-start | bytes 772
  67.6 12.6 %collective-permute-start.3 = (bf16[2,32,4224]{2,1,0:T(8,128)(2,1)S(1)}, bf16[2,32,4224]{2,1,0:T(8,128)(2,1)S(1)}, u32[]{:S(2)}, u32[]{:S(2)}) collective-permute-start(bf16[2,32,4224]{2,1,0:T(8,128)(2,1)S(1)} %get-tuple-element.19), channel_id=1, source_target_pairs={{1,3},{3,1},{5,7},{7,5},{9,11},{11,9},{13,15},{15,13},{17,19},{19,... | collective-permute-start | bytes 1622024 | tf_op jit(solution)/shard_map/ppermute | solution.py:43
  73.5 6.9 %collective-permute-start.10 = (bf16[2,32,4224]{2,1,0:T(8,128)(2,1)S(1)}, bf16[2,32,4224]{2,1,0:T(8,128)(2,1)S(1)}, u32[]{:S(2)}, u32[]{:S(2)}) collective-permute-start(bf16[2,32,4224]{2,1,0:T(8,128)(2,1)S(1)} %get-tuple-element.39), channel_id=1, source_target_pairs={{14,6},{12,4},{10,2},{8,0},{30,22},{28,20},{26,18},{24,16},{46,38}... | collective-permute-start | bytes 1622024 | tf_op jit(solution)/shard_map/ppermute | solution.py:43
  81.1 18.5 %copy-start.3 = (bf16[2,256,2048]{1,2,0:T(8,128)(2,1)S(1)}, bf16[2,256,2048]{1,2,0:T(8,128)(2,1)}, u32[]{:S(2)}) copy-start(bf16[2,256,2048]{1,2,0:T(8,128)(2,1)} %copy-done.2) | copy-start | bytes 6291460
  81.1 10.9 %collective-permute-start.4 = (bf16[2,32,4224]{2,1,0:T(8,128)(2,1)S(1)}, bf16[2,32,4224]{2,1,0:T(8,128)(2,1)S(1)}, u32[]{:S(2)}, u32[]{:S(2)}) collective-permute-start(bf16[2,32,4224]{2,1,0:T(8,128)(2,1)S(1)} %get-tuple-element.37), channel_id=1, source_target_pairs={{1,5},{3,7},{5,9},{7,11},{9,13},{11,15},{17,21},{19,23},{21,25},{2... | collective-permute-start | bytes 1622024 | tf_op jit(solution)/shard_map/ppermute | solution.py:43
  92.3 15.8 %collective-permute-start.5 = (bf16[2,32,4224]{2,1,0:T(8,128)(2,1)S(1)}, bf16[2,32,4224]{2,1,0:T(8,128)(2,1)S(1)}, u32[]{:S(2)}, u32[]{:S(2)}) collective-permute-start(bf16[2,32,4224]{2,1,0:T(8,128)(2,1)S(1)} %add_convert_fusion.1), channel_id=1, source_target_pairs={{1,9},{3,11},{5,13},{7,15},{17,25},{19,27},{21,29},{23,31},{33,41}... | collective-permute-start | bytes 1622024 | tf_op jit(solution)/shard_map/ppermute | solution.py:43
  106.5 5.5 %copy-start.6 = (bf16[2,256,2048]{1,2,0:T(8,128)(2,1)S(1)}, bf16[2,256,2048]{1,2,0:T(8,128)(2,1)}, u32[]{:S(2)}) copy-start(bf16[2,256,2048]{1,2,0:T(8,128)(2,1)} %copy-done.5) | copy-start | bytes 6291460
  106.5 12.6 %collective-permute-start.11 = (bf16[2,32,4224]{2,1,0:T(8,128)(2,1)S(1)}, bf16[2,32,4224]{2,1,0:T(8,128)(2,1)S(1)}, u32[]{:S(2)}, u32[]{:S(2)}) collective-permute-start(bf16[2,32,4224]{2,1,0:T(8,128)(2,1)S(1)} %get-tuple-element.9), channel_id=1, source_target_pairs={{14,15},{12,13},{10,11},{8,9},{6,7},{4,5},{2,3},{0,1},{30,31},{28,... | collective-permute-start | bytes 1622024 | tf_op jit(solution)/shard_map/ppermute | solution.py:43
  108.5 9.2 %copy-start.13 = (bf16[2,32,4224]{2,1,0:T(8,128)(2,1)S(1)}, bf16[2,32,4224]{2,1,0:T(8,128)(2,1)}, u32[]{:S(2)}) copy-start(bf16[2,32,4224]{2,1,0:T(8,128)(2,1)} %copy-done.12) | copy-start | bytes 1622020
  108.5 10.6 %collective-permute-start.6 = (bf16[2,32,4224]{2,1,0:T(8,128)(2,1)S(1)}, bf16[2,32,4224]{2,1,0:T(8,128)(2,1)S(1)}, u32[]{:S(2)}, u32[]{:S(2)}) collective-permute-start(bf16[2,32,4224]{2,1,0:T(8,128)(2,1)S(1)} %get-tuple-element.15), channel_id=1, source_target_pairs={{1,0},{3,2},{5,4},{7,6},{9,8},{11,10},{13,12},{15,14},{17,16},{19,... | collective-permute-start | bytes 1622024 | tf_op jit(solution)/shard_map/ppermute | solution.py:43
  117.7 1.4 %slice-start = ((pred[4224]{0:T(1024)(128)(4,1)}), pred[4096]{0:T(1024)(128)(4,1)S(1)}, s32[]{:S(2)}) async-start(pred[4224]{0:T(1024)(128)(4,1)} %copy-done.15), calls=%async_computation | async-start | bytes 8192 | tf_op jit(solution)/shard_map/slice | solution.py:59
  121.8 3.7 %copy-start.19 = (f32[2,256,32]{1,2,0:T(8,128)S(1)}, f32[2,256,32]{1,2,0:T(8,128)}, u32[]{:S(2)}) copy-start(f32[2,256,32]{1,2,0:T(8,128)} %get-tuple-element.29) | copy-start | bytes 196612
  122.6 2.8 %copy-start.4 = (bf16[2,256,2048]{1,2,0:T(8,128)(2,1)S(1)}, bf16[2,256,2048]{1,2,0:T(8,128)(2,1)}, u32[]{:S(2)}) copy-start(bf16[2,256,2048]{1,2,0:T(8,128)(2,1)} %copy-done.2) | copy-start | bytes 6291460
  122.6 2.8 %copy-start.7 = (bf16[2,256,2048]{1,2,0:T(8,128)(2,1)S(1)}, bf16[2,256,2048]{1,2,0:T(8,128)(2,1)}, u32[]{:S(2)}) copy-start(bf16[2,256,2048]{1,2,0:T(8,128)(2,1)} %copy-done.5) | copy-start | bytes 6291460
  122.6 2.9 %copy-start.14 = (f32[2,32,64,64]{3,2,1,0:T(8,128)S(1)}, f32[2,32,64,64]{3,2,1,0:T(8,128)}, u32[]{:S(2)}) copy-start(f32[2,32,64,64]{3,2,1,0:T(8,128)} %reshape.143) | copy-start | bytes 3145732
  122.6 2.9 %copy-start.18 = (f32[2,256,32]{1,2,0:T(8,128)S(1)}, f32[2,256,32]{1,2,0:T(8,128)}, u32[]{:S(2)}) copy-start(f32[2,256,32]{1,2,0:T(8,128)} %get-tuple-element.31) | copy-start | bytes 196612
  125.5 7.4 %copy-start.8 = (bf16[2048,1024]{1,0:T(8,128)(2,1)S(1)}, bf16[2048,1024]{1,0:T(8,128)(2,1)}, u32[]{:S(2)}) copy-start(bf16[2048,1024]{1,0:T(8,128)(2,1)} %param.21) | copy-start | bytes 12582916
  125.5 7.4 %copy-start.10 = (bf16[512,1024]{1,0:T(8,128)(2,1)S(1)}, bf16[512,1024]{1,0:T(8,128)(2,1)}, u32[]{:S(2)}) copy-start(bf16[512,1024]{1,0:T(8,128)(2,1)} %pad_maximum_fusion.2) | copy-start | bytes 3145732
  135.4 2.2 %copy-start.1 = (bf16[1024,32]{0,1:T(8,128)(2,1)S(1)}, bf16[1024,32]{0,1:T(8,128)(2,1)}, u32[]{:S(2)}) copy-start(bf16[1024,32]{0,1:T(8,128)(2,1)} %param.14) | copy-start | bytes 196612

commit v13 on v10

--- a/solution.py
+++ b/solution.py
@@ -153,7 +153,7 @@
 def finish(local, cum, reads, entering):
     entering = entering.reshape(local.shape[0], local.shape[2], local.shape[3], NS)
     product = jnp.einsum(
-        "rtn,rhpn->rthp", reads.astype(jnp.float32), entering, precision=lax.Precision.HIGHEST
+        "rtn,rhpn->rthp", reads.astype(jnp.float32), entering, precision=lax.Precision.HIGH
     )
     return local + product * jnp.exp(cum)[..., None]
 

time: 138 us -> 138 us (level)
  no operation moved by 1% of the time
where the time goes in v13:
time: 138 us; the launch traced here: 137 us
  matrix products  39.6 us (29%)
  starting transfers between devices  36.1 us (26%)
  local copies, waits for them, and re-layouts  29.7 us (22%)
  waiting for transfers between devices  10.7 us (8%)
  other arithmetic  10.5 us (8%)
  Pallas kernels  9.66 us (7%)
    ppermute x10, starting transfers between devices, send(): moved = lax.ppermute(value.astype(jnp.bfloat16), 'ctx', pairs)  27.7 us
    dot_general x2, matrix products, group_terms(): jnp.einsum('rhts,rshp->rthp', mixing, scaled, preferred_element_type=jnp....  11.4 us
    ppermute x10, waiting for transfers between devices, send(): moved = lax.ppermute(value.astype(jnp.bfloat16), 'ctx', pairs)  10.7 us
    pallas_call x1, Pallas kernels, convolve(): pl.pallas_call(conv_kernel, grid=grid, in_specs=[pl.BlockSpec((1, length,...  9.66 us
    dot_general x2, matrix products, finish(): jnp.einsum('rtn,rhpn->rthp', reads.astype(jnp.float32), entering, precisi...  9.01 us
    ppermute x2, starting transfers between devices, shifted(): return lax.ppermute(value, 'ctx', pairs)  8.38 us
    dot_general x2, matrix products, group_terms(): jnp.einsum('rshp,rsn->rhpn', weighted, keys_in, preferred_element_type=jn...  5.74 us
    transpose x1, local copies, waits for them, and re-layouts, body(): jnp.transpose(gate.reshape(2, heads, head_size, length).astype(jnp.float3...  5.34 us
  transfers between devices with their start and end apart: 12, of which 2 were waited for; matrix products, arithmetic and copies ran while one was open for 30% of the time, Pallas kernels for 0%

profile of v13, /device:TPU:1, one launch (start us, length us, event | category | flops | bytes accessed | tf_op | source)
XLA Modules:
  0.0 137.0 jit_solution(3855108538494497761)
XLA Ops:
  0.0 3.4 %fusion.83 = (bf16[256,1,1024]{2,1,0:T(2,128)(2,1)S(1)}, bf16[256,1,1024]{2,1,0:T(2,128)(2,1)S(1)}) fusion(bf16[256,2,1024]{2,1,0:T(2,128)(2,1)} %param.11), kind=kLoop, calls=%fused_computation.139 | loop fusion | bytes 2097152 | tf_op jit(solution)/shard_map/slice | solution.py:169
  3.8 3.4 %convolution_convert_fusion = bf16[512,2176]{1,0:T(8,128)(2,1)S(1)} fusion(bf16[1024,2176]{1,0:T(8,128)(2,1)S(1)} %copy-done.26, bf16[256,1024]{1,0:T(8,128)(2,1)S(1)} %get-tuple-element.50, bf16[256,1024]{1,0:T(8,128)(2,1)S(1)} %get-tuple-element.51), kind=kOutput, calls=%fused_computation.20 | convolution fusion | flops 2284912640 | bytes 7733248 | tf_op jit(solution)/shard_map/dot_general | solution.py:173
  7.3 6.3 %collective-permute-start = (bf16[2,3,2176]{2,1,0:T(4,128)(2,1)S(1)}, bf16[2,3,2176]{2,1,0:T(4,128)(2,1)S(1)}, u32[]{:S(2)}, u32[]{:S(2)}) collective-permute-start(bf16[2,3,2176]{2,1,0:T(4,128)(2,1)S(1)} %get-tuple-element.22), channel_id=1, source_target_pairs={{0,1},{1,2},{2,3},{3,4},{4,5},{5,6},{6,7},{7,8},{8,9},{9,10},{10,1... | collective-permute-start | bytes 78344 | tf_op jit(solution)/shard_map/ppermute | solution.py:22
  13.6 2.1 %collective-permute-start.1 = (bf16[2,3,2176]{2,1,0:T(4,128)(2,1)S(1)}, bf16[2,3,2176]{2,1,0:T(4,128)(2,1)S(1)}, u32[]{:S(2)}, u32[]{:S(2)}) collective-permute-start(bf16[2,3,2176]{2,1,0:T(4,128)(2,1)S(1)} %get-tuple-element.21), channel_id=1, source_target_pairs={{1,0},{2,1},{3,2},{4,3},{5,4},{6,5},{7,6},{8,7},{9,8},{10,9},{11,1... | collective-permute-start | bytes 78344 | tf_op jit(solution)/shard_map/ppermute | solution.py:22
  15.7 1.0 pad_maximum_fusion.2
  17.8 0.6 bitcast_exponential_fusion
  18.9 0.6 pad_maximum_fusion.4.wf_ref
  19.6 0.6 broadcast_in_dim.43.br_ref
  20.2 0.6 broadcast_in_dim.44.bf_ref
  22.1 9.7 %shard_map.109 = (bf16[2,2176,256]{2,1,0:T(8,128)(2,1)}, bf16[2,2176,256]{2,1,0:T(8,128)(2,1)}) custom-call(bf16[2,256,2176]{2,1,0:T(8,128)(2,1)} %bitcast.107, bf16[2,3,2176]{2,1,0:T(4,128)(2,1)} %copy-done.20, bf16[2,3,2176]{2,1,0:T(4,128)(2,1)} %copy-done.21, f32[2,4,2176]{2,1,0:T(4,128)} %wr_ref.1, f32[2,1,2176]{2,1,0:T(1,128)} %broadcast_in_dim.43.br_ref, ...), custom_call_target="tpu_custom_call" | custom-call | tf_op jit(solution)/shard_map/pallas_call | solution.py:86
  31.7 1.7 %slice.163 = bf16[2,256,2048]{1,2,0:T(8,128)(2,1)S(1)} slice(bf16[2,256,2176]{1,2,0:T(8,128)(2,1)} %bitcast.108), slice={[0:2], [0:256], [0:2048]} | slice | bytes 4194304 | tf_op jit(solution)/shard_map/slice | solution.py:110
  33.5 1.4 copy-done.2
  34.8 2.9 %fusion.30 = f32[2,32,64,64]{3,2,1,0:T(8,128)} fusion(bf16[2,256,32,64]{1,3,2,0:T(8,128)(2,1)S(1)} %bitcast.92, f32[2,256,32]{1,2,0:T(8,128)S(1)} %get-tuple-element.32, bf16[2,256,2176]{1,2,0:T(8,128)(2,1)} %bitcast.109), kind=kOutput, calls=%fused_computation.38 | convolution fusion | flops 137363456 | bytes 3276800 | tf_op jit(solution)/shard_map/rshp,rsn->rhpn/dot_general | solution.py:138
  37.7 2.1 %reshape.142 = f32[2,32,4096]{2,1,0:T(8,128)S(1)} reshape(f32[2,32,64,64]{3,2,1,0:T(8,128)} %fusion.30) | data formatting | bytes 2097152 | tf_op jit(solution)/shard_map/reshape | solution.py:144
  39.9 1.3 collective-permute-start.7
  41.3 0.6 bitcast_exponential_fusion.1
  41.9 1.7 %slice.150 = bf16[2,256,2048]{1,2,0:T(8,128)(2,1)S(1)} slice(bf16[2,256,2176]{1,2,0:T(8,128)(2,1)} %bitcast.102), slice={[0:2], [0:256], [0:2048]} | slice | bytes 4194304 | tf_op jit(solution)/shard_map/slice | solution.py:110
  43.7 1.3 copy-done.5
  45.0 2.9 %fusion.33 = f32[2,32,64,64]{3,2,1,0:T(8,128)} fusion(bf16[2,256,32,64]{1,3,2,0:T(8,128)(2,1)S(1)} %bitcast.95, f32[2,256,32]{1,2,0:T(8,128)S(1)} %get-tuple-element.30, bf16[2,256,2176]{1,2,0:T(8,128)(2,1)} %bitcast.103), kind=kOutput, calls=%fused_computation.39 | convolution fusion | flops 137363456 | bytes 3276800 | tf_op jit(solution)/shard_map/rshp,rsn->rhpn/dot_general | solution.py:138
  47.8 2.1 %reshape.140 = f32[2,32,4096]{2,1,0:T(8,128)S(1)} reshape(f32[2,32,64,64]{3,2,1,0:T(8,128)} %fusion.33) | data formatting | bytes 2097152 | tf_op jit(solution)/shard_map/reshape | solution.py:144
  50.8 0.7 collective-permute-start.8
  51.5 0.9 fusion.49
  52.5 1.6 %collective-permute-start.2 = (bf16[2,32,4224]{2,1,0:T(8,128)(2,1)}, bf16[2,32,4224]{2,1,0:T(8,128)(2,1)}, u32[]{:S(2)}, u32[]{:S(2)}) collective-permute-start(bf16[2,32,4224]{2,1,0:T(8,128)(2,1)} %fusion.49), channel_id=1, source_target_pairs={{0,1},{2,3},{4,5},{6,7},{8,9},{10,11},{12,13},{14,15},{16,17},{18,... | collective-permute-start | bytes 1622024 | tf_op jit(solution)/shard_map/ppermute | solution.py:44
  54.3 1.2 fusion.77
  55.5 0.7 collective-permute-start.9
  56.2 4.4 %convert_bitcast_fusion = f32[2,2048,256]{1,2,0:T(8,128)} fusion(bf16[2,256,1024]{2,1,0:T(8,128)(2,1)S(1)} %bitcast.99, bf16[1024,2048]{1,0:T(8,128)(2,1)S(1)} %copy-done.27), kind=kOutput, calls=%fused_computation.33 | convolution fusion | flops 2149580800 | bytes 9437184 | tf_op jit(solution)/shard_map/rtd,de->ret/dot_general | solution.py:170
  60.6 5.3 %copy.41 = f32[2,2048,256]{2,1,0:T(8,128)} copy(f32[2,2048,256]{1,2,0:T(8,128)} %convert_bitcast_fusion) | data formatting | bytes 8388608 | tf_op jit(solution)/shard_map/transpose | solution.py:190
  66.1 1.4 %fusion.81 = (bf16[2,32,4224]{2,1,0:T(8,128)(2,1)S(1)}, f32[2,32,4224]{2,1,0:T(8,128)S(1)}, bf16[2,32,4224]{2,1,0:T(8,128)(2,1)S(1)}) fusion(f32[2,32,128]{2,1,0:T(8,128)S(1)} %broadcast_in_dim.82, f32[2,32,4096]{2,1,0:T(8,128)S(1)} %reshape.140, pred[4224]{0:T(1024)(128)(4,1)S(1)} %iota_compare_fusion.4, bf16[2,32,4224]{2,1,0:T(8,128)(2,1)} %collective-permute-done.2, ...), kind=kLoop, calls=%fused_computation.137 | loop fusion | flops 2973696 | bytes 5411456 | tf_op jit(solution)/shard_map/convert_element_type | solution.py:44
  67.6 5.9 %collective-permute-start.3 = (bf16[2,32,4224]{2,1,0:T(8,128)(2,1)S(1)}, bf16[2,32,4224]{2,1,0:T(8,128)(2,1)S(1)}, u32[]{:S(2)}, u32[]{:S(2)}) collective-permute-start(bf16[2,32,4224]{2,1,0:T(8,128)(2,1)S(1)} %get-tuple-element.19), channel_id=1, source_target_pairs={{1,3},{3,1},{5,7},{7,5},{9,11},{11,9},{13,15},{15,13},{17,19},{19,... | collective-permute-start | bytes 1622024 | tf_op jit(solution)/shard_map/ppermute | solution.py:44
  73.5 0.7 collective-permute-start.10
  74.5 5.7 %collective-permute-done.3 = bf16[2,32,4224]{2,1,0:T(8,128)(2,1)S(1)} collective-permute-done((bf16[2,32,4224]{2,1,0:T(8,128)(2,1)S(1)}, bf16[2,32,4224]{2,1,0:T(8,128)(2,1)S(1)}, u32[]{:S(2)}, u32[]{:S(2)}) %collective-permute-start.3) | collective-permute-done | bytes 540704 | tf_op jit(solution)/shard_map/ppermute | solution.py:44
  80.4 0.8 fusion.76
  81.1 4.6 %collective-permute-start.4 = (bf16[2,32,4224]{2,1,0:T(8,128)(2,1)S(1)}, bf16[2,32,4224]{2,1,0:T(8,128)(2,1)S(1)}, u32[]{:S(2)}, u32[]{:S(2)}) collective-permute-start(bf16[2,32,4224]{2,1,0:T(8,128)(2,1)S(1)} %get-tuple-element.37), channel_id=1, source_target_pairs={{1,5},{3,7},{5,9},{7,11},{9,13},{11,15},{17,21},{19,23},{21,25},{2... | collective-permute-start | bytes 1622024 | tf_op jit(solution)/shard_map/ppermute | solution.py:44
  85.8 1.1 fusion.62
  87.1 5.0 %collective-permute-done.4 = bf16[2,32,4224]{2,1,0:T(8,128)(2,1)S(1)} collective-permute-done((bf16[2,32,4224]{2,1,0:T(8,128)(2,1)S(1)}, bf16[2,32,4224]{2,1,0:T(8,128)(2,1)S(1)}, u32[]{:S(2)}, u32[]{:S(2)}) %collective-permute-start.4) | collective-permute-done | bytes 540704 | tf_op jit(solution)/shard_map/ppermute | solution.py:44
  92.3 7.3 %collective-permute-start.5 = (bf16[2,32,4224]{2,1,0:T(8,128)(2,1)S(1)}, bf16[2,32,4224]{2,1,0:T(8,128)(2,1)S(1)}, u32[]{:S(2)}, u32[]{:S(2)}) collective-permute-start(bf16[2,32,4224]{2,1,0:T(8,128)(2,1)S(1)} %add_convert_fusion.1), channel_id=1, source_target_pairs={{1,9},{3,11},{5,13},{7,15},{17,25},{19,27},{21,29},{23,31},{33,41}... | collective-permute-start | bytes 1622024 | tf_op jit(solution)/shard_map/ppermute | solution.py:44
  99.6 5.7 %fusion.1 = f32[2,32,64,256]{3,2,1,0:T(8,128)} fusion(f32[2,32,256]{2,1,0:T(8,128)S(1)} %fusion.50, f32[2,256,256]{2,1,0:T(8,128)S(1)} %fusion.62, pred[256,256]{1,0:T(8,128)(4,1)S(1)} %iota_compare_fusion, bf16[2,256,32,64]{1,3,2,0:T(8,128)(2,1)S(1)} %bitcast.93, f32[2,256,32]{1,2,0:T(8,128)S(1)} %get-tuple-element.34), kind=kOutput, calls=%fused_computation.3 | convolution fusion | flops 556793856 | bytes 7012352 | tf_op jit(solution)/shard_map/rhts,rshp->rthp/dot_general | solution.py:134
  105.3 1.1 fusion.67
  106.5 1.4 %collective-permute-start.11 = (bf16[2,32,4224]{2,1,0:T(8,128)(2,1)S(1)}, bf16[2,32,4224]{2,1,0:T(8,128)(2,1)S(1)}, u32[]{:S(2)}, u32[]{:S(2)}) collective-permute-start(bf16[2,32,4224]{2,1,0:T(8,128)(2,1)S(1)} %get-tuple-element.9), channel_id=1, source_target_pairs={{14,15},{12,13},{10,11},{8,9},{6,7},{4,5},{2,3},{0,1},{30,31},{28,... | collective-permute-start | bytes 1622024 | tf_op jit(solution)/shard_map/ppermute | solution.py:44
  108.5 3.4 %collective-permute-start.6 = (bf16[2,32,4224]{2,1,0:T(8,128)(2,1)S(1)}, bf16[2,32,4224]{2,1,0:T(8,128)(2,1)S(1)}, u32[]{:S(2)}, u32[]{:S(2)}) collective-permute-start(bf16[2,32,4224]{2,1,0:T(8,128)(2,1)S(1)} %get-tuple-element.15), channel_id=1, source_target_pairs={{1,0},{3,2},{5,4},{7,6},{9,8},{11,10},{13,12},{15,14},{17,16},{19,... | collective-permute-start | bytes 1622024 | tf_op jit(solution)/shard_map/ppermute | solution.py:44
  112.0 5.7 %fusion = f32[2,32,64,256]{3,2,1,0:T(8,128)} fusion(f32[2,32,256]{2,1,0:T(8,128)S(1)} %fusion.52, f32[2,256,256]{2,1,0:T(8,128)S(1)} %fusion.67, pred[256,256]{1,0:T(8,128)(4,1)S(1)} %iota_compare_fusion.1, bf16[2,256,32,64]{1,3,2,0:T(8,128)(2,1)S(1)} %bitcast.96, f32[2,256,32]{1,2,0:T(8,128)S(1)} %get-tuple-element.33), kind=kOutput, calls=%fused_computation.2 | convolution fusion | flops 556793856 | bytes 7012352 | tf_op jit(solution)/shard_map/rhts,rshp->rthp/dot_general | solution.py:134
  117.8 1.1 convert_element_type.145
  119.6 2.2 %reshape.143 = f32[2,32,64,64]{3,2,1,0:T(8,128)} reshape(f32[2,32,4096]{2,1,0:T(8,128)S(1)} %get-tuple-element.40) | data formatting | bytes 2097152 | tf_op jit(solution)/shard_map/reshape | solution.py:154
  121.8 0.8 reshape.141
  122.7 2.2 %fusion.57 = f32[2,256,32,64]{1,3,2,0:T(8,128)S(1)} fusion(f32[2,32,64,64]{3,2,1,0:T(8,128)S(1)} %reshape.141, bf16[2,256,2176]{1,2,0:T(8,128)(2,1)} %bitcast.105), kind=kOutput, calls=%fused_computation.90 | convolution fusion | flops 402653184 | bytes 5308416 | tf_op jit(solution)/shard_map/rtn,rhpn->rthp/dot_general | solution.py:155
  125.5 6.8 %multiply_reduce_fusion = (f32[2,256]{1,0:T(2,128)S(1)}, f32[2,256,32,64]{1,3,2,0:T(8,128)S(1)}) fusion(f32[2,256,32,64]{1,3,2,0:T(8,128)} %bitcast.101, f32[2,256,32]{1,2,0:T(8,128)S(1)} %copy-done.18, f32[2,32,64,64]{3,2,1,0:T(8,128)S(1)} %copy-done.14, bf16[2,256,2176]{1,2,0:T(8,128)(2,1)} %bitcast.111, bf16[2,256,32,64]{1,3,2,0:T(8,128)(2,1)S(1)} %bitcast.94, ...), kind=kOutput, calls=%fused_computation.35 | convolution fusion | flops 421527040 | bytes 26413568 | tf_op jit(solution)/shard_map/rtn,rhpn->rthp/dot_general | solution.py:155
  132.3 2.4 %fusion.36 = bf16[2,256,1024]{2,1,0:T(8,128)(2,1)S(1)} fusion(bf16[2,256,1024]{2,1,0:T(8,128)(2,1)S(1)} %bitcast.100, bf16[32,64,1024,1]{2,1,0,3:T(8,128)(2,1)S(1)} %bitcast.98, f32[2,256,32,64]{1,3,2,0:T(8,128)S(1)} %get-tuple-element.49, f32[32,64]{1,0:T(8,128)S(1)} %mul.325, f32[2,256]{1,0:T(2,128)S(1)} %add_rsqrt_fusion), kind=kOutput, calls=%fused_computation.41 | convolution fusion | flops 2152202240 | bytes 10496000 | tf_op jit(solution)/shard_map/rthp,hpd->rtd/dot_general | solution.py:198
  135.0 2.0 %copy.42 = bf16[256,2,1024]{2,1,0:T(2,128)(2,1)} copy(bf16[256,2,1024]{2,0,1:T(8,128)(2,1)S(1)} %pad_maximum_fusion.3) | data formatting | bytes 2097152 | tf_op jit(solution)/shard_map/stack | solution.py:207
  (115 shorter events, 7.4 us)
Async XLA Ops:
  0.0 16.8 %copy-start = (bf16[1024,32]{0,1:T(8,128)(2,1)S(1)}, bf16[1024,32]{0,1:T(8,128)(2,1)}, u32[]{:S(2)}) copy-start(bf16[1024,32]{0,1:T(8,128)(2,1)} %param.14) | copy-start | bytes 196612
  0.0 3.8 %copy-start.26 = (bf16[1024,2176]{1,0:T(8,128)(2,1)S(1)}, bf16[1024,2176]{1,0:T(8,128)(2,1)}, u32[]{:S(2)}) copy-start(bf16[1024,2176]{1,0:T(8,128)(2,1)} %param.13) | copy-start | bytes 13369348
  7.2 10.2 %copy-start.11 = (bf16[512,2176]{1,0:T(8,128)(2,1)}, bf16[512,2176]{1,0:T(8,128)(2,1)S(1)}, u32[]{:S(2)}) copy-start(bf16[512,2176]{1,0:T(8,128)(2,1)S(1)} %convolution_convert_fusion) | copy-start | bytes 6684676
  7.2 9.5 %copy-start.24 = (f32[2,32]{1,0:T(2,128)S(1)}, f32[2,32]{1,0:T(2,128)}, u32[]{:S(2)}) copy-start(f32[2,32]{1,0:T(2,128)} %param.16) | copy-start | bytes 772
  7.2 10.0 %copy-start.23 = (f32[2,32]{1,0:T(2,128)S(1)}, f32[2,32]{1,0:T(2,128)}, u32[]{:S(2)}) copy-start(f32[2,32]{1,0:T(2,128)} %param.15) | copy-start | bytes 772
  7.3 13.6 %collective-permute-start = (bf16[2,3,2176]{2,1,0:T(4,128)(2,1)S(1)}, bf16[2,3,2176]{2,1,0:T(4,128)(2,1)S(1)}, u32[]{:S(2)}, u32[]{:S(2)}) collective-permute-start(bf16[2,3,2176]{2,1,0:T(4,128)(2,1)S(1)} %get-tuple-element.22), channel_id=1, source_target_pairs={{0,1},{1,2},{2,3},{3,4},{4,5},{5,6},{6,7},{7,8},{8,9},{9,10},{10,1... | collective-permute-start | bytes 78344 | tf_op jit(solution)/shard_map/ppermute | solution.py:22
  13.6 4.8 %copy-start.16 = (f32[2,4,2176]{2,1,0:T(4,128)S(1)}, f32[2,4,2176]{2,1,0:T(4,128)}, u32[]{:S(2)}) copy-start(f32[2,4,2176]{2,1,0:T(4,128)} %wr_ref.1) | copy-start | bytes 208900
  13.6 4.8 %copy-start.17 = (f32[2,2176]{1,0:T(2,128)S(1)}, f32[2,2176]{1,0:T(2,128)}, u32[]{:S(2)}) copy-start(f32[2,2176]{1,0:T(2,128)} %param.18) | copy-start | bytes 52228
  13.6 7.2 %collective-permute-start.1 = (bf16[2,3,2176]{2,1,0:T(4,128)(2,1)S(1)}, bf16[2,3,2176]{2,1,0:T(4,128)(2,1)S(1)}, u32[]{:S(2)}, u32[]{:S(2)}) collective-permute-start(bf16[2,3,2176]{2,1,0:T(4,128)(2,1)S(1)} %get-tuple-element.21), channel_id=1, source_target_pairs={{1,0},{2,1},{3,2},{4,3},{5,4},{6,5},{7,6},{8,7},{9,8},{10,9},{11,1... | collective-permute-start | bytes 78344 | tf_op jit(solution)/shard_map/ppermute | solution.py:22
  19.6 88.5 %copy-start.15 = (pred[4224]{0:T(1024)(128)(4,1)}, pred[4224]{0:T(1024)(128)(4,1)S(1)}, u32[]{:S(2)}) copy-start(pred[4224]{0:T(1024)(128)(4,1)S(1)} %iota_compare_fusion.4) | copy-start | bytes 12676
  20.8 0.6 copy-start.20
  21.4 0.6 copy-start.21
  33.4 1.4 copy-start.2
  39.9 10.0 %collective-permute-start.7 = (bf16[2,32,4224]{2,1,0:T(8,128)(2,1)S(1)}, bf16[2,32,4224]{2,1,0:T(8,128)(2,1)S(1)}, u32[]{:S(2)}, u32[]{:S(2)}) collective-permute-start(bf16[2,32,4224]{2,1,0:T(8,128)(2,1)S(1)} %fusion.48), channel_id=1, source_target_pairs={{15,14},{13,12},{11,10},{9,8},{7,6},{5,4},{3,2},{1,0},{31,30},{29,... | collective-permute-start | bytes 1622024 | tf_op jit(solution)/shard_map/ppermute | solution.py:44
  43.6 1.3 copy-start.5
  50.0 0.8 copy-start.12
  50.8 3.4 %collective-permute-start.8 = (bf16[2,32,4224]{2,1,0:T(8,128)(2,1)S(1)}, bf16[2,32,4224]{2,1,0:T(8,128)(2,1)S(1)}, u32[]{:S(2)}, u32[]{:S(2)}) collective-permute-start(bf16[2,32,4224]{2,1,0:T(8,128)(2,1)S(1)} %get-tuple-element.13), channel_id=1, source_target_pairs={{14,12},{12,14},{10,8},{8,10},{6,4},{4,6},{2,0},{0,2},{30,28},{28,... | collective-permute-start | bytes 1622024 | tf_op jit(solution)/shard_map/ppermute | solution.py:44
  51.5 4.7 %copy-start.27 = (bf16[1024,2048]{1,0:T(8,128)(2,1)S(1)}, bf16[1024,2048]{1,0:T(8,128)(2,1)}, u32[]{:S(2)}) copy-start(bf16[1024,2048]{1,0:T(8,128)(2,1)} %param.12) | copy-start | bytes 12582916
  52.5 13.6 %collective-permute-start.2 = (bf16[2,32,4224]{2,1,0:T(8,128)(2,1)}, bf16[2,32,4224]{2,1,0:T(8,128)(2,1)}, u32[]{:S(2)}, u32[]{:S(2)}) collective-permute-start(bf16[2,32,4224]{2,1,0:T(8,128)(2,1)} %fusion.49), channel_id=1, source_target_pairs={{0,1},{2,3},{4,5},{6,7},{8,9},{10,11},{12,13},{14,15},{16,17},{18,... | collective-permute-start | bytes 1622024 | tf_op jit(solution)/shard_map/ppermute | solution.py:44
  54.2 2.1 %copy-start.9 = (bf16[512,1024]{1,0:T(8,128)(2,1)S(1)}, bf16[512,1024]{1,0:T(8,128)(2,1)}, u32[]{:S(2)}) copy-start(bf16[512,1024]{1,0:T(8,128)(2,1)} %pad_maximum_fusion.2) | copy-start | bytes 3145732
  55.5 10.6 %collective-permute-start.9 = (bf16[2,32,4224]{2,1,0:T(8,128)(2,1)}, bf16[2,32,4224]{2,1,0:T(8,128)(2,1)S(1)}, u32[]{:S(2)}, u32[]{:S(2)}) collective-permute-start(bf16[2,32,4224]{2,1,0:T(8,128)(2,1)} %get-tuple-element.11), channel_id=1, source_target_pairs={{14,10},{12,8},{10,6},{8,4},{6,2},{4,0},{30,26},{28,24},{26,22},{2... | collective-permute-start | bytes 1622024 | tf_op jit(solution)/shard_map/ppermute | solution.py:44
  60.6 5.3 %copy-start.22 = (f32[2048]{0:T(1024)S(1)}, f32[2048]{0:T(1024)}, u32[]{:S(2)}) copy-start(f32[2048]{0:T(1024)} %param.20) | copy-start | bytes 24580
  66.1 8.1 %copy-start.25 = (f32[2,32]{1,0:T(2,128)S(1)}, f32[2,32]{1,0:T(2,128)}, u32[]{:S(2)}) copy-start(f32[2,32]{1,0:T(2,128)} %param.19) | copy-start | bytes 772
  67.6 12.6 %collective-permute-start.3 = (bf16[2,32,4224]{2,1,0:T(8,128)(2,1)S(1)}, bf16[2,32,4224]{2,1,0:T(8,128)(2,1)S(1)}, u32[]{:S(2)}, u32[]{:S(2)}) collective-permute-start(bf16[2,32,4224]{2,1,0:T(8,128)(2,1)S(1)} %get-tuple-element.19), channel_id=1, source_target_pairs={{1,3},{3,1},{5,7},{7,5},{9,11},{11,9},{13,15},{15,13},{17,19},{19,... | collective-permute-start | bytes 1622024 | tf_op jit(solution)/shard_map/ppermute | solution.py:44
  73.5 6.9 %collective-permute-start.10 = (bf16[2,32,4224]{2,1,0:T(8,128)(2,1)S(1)}, bf16[2,32,4224]{2,1,0:T(8,128)(2,1)S(1)}, u32[]{:S(2)}, u32[]{:S(2)}) collective-permute-start(bf16[2,32,4224]{2,1,0:T(8,128)(2,1)S(1)} %get-tuple-element.39), channel_id=1, source_target_pairs={{14,6},{12,4},{10,2},{8,0},{30,22},{28,20},{26,18},{24,16},{46,38}... | collective-permute-start | bytes 1622024 | tf_op jit(solution)/shard_map/ppermute | solution.py:44
  81.1 18.5 %copy-start.3 = (bf16[2,256,2048]{1,2,0:T(8,128)(2,1)S(1)}, bf16[2,256,2048]{1,2,0:T(8,128)(2,1)}, u32[]{:S(2)}) copy-start(bf16[2,256,2048]{1,2,0:T(8,128)(2,1)} %copy-done.2) | copy-start | bytes 6291460
  81.1 10.9 %collective-permute-start.4 = (bf16[2,32,4224]{2,1,0:T(8,128)(2,1)S(1)}, bf16[2,32,4224]{2,1,0:T(8,128)(2,1)S(1)}, u32[]{:S(2)}, u32[]{:S(2)}) collective-permute-start(bf16[2,32,4224]{2,1,0:T(8,128)(2,1)S(1)} %get-tuple-element.37), channel_id=1, source_target_pairs={{1,5},{3,7},{5,9},{7,11},{9,13},{11,15},{17,21},{19,23},{21,25},{2... | collective-permute-start | bytes 1622024 | tf_op jit(solution)/shard_map/ppermute | solution.py:44
  92.3 15.8 %collective-permute-start.5 = (bf16[2,32,4224]{2,1,0:T(8,128)(2,1)S(1)}, bf16[2,32,4224]{2,1,0:T(8,128)(2,1)S(1)}, u32[]{:S(2)}, u32[]{:S(2)}) collective-permute-start(bf16[2,32,4224]{2,1,0:T(8,128)(2,1)S(1)} %add_convert_fusion.1), channel_id=1, source_target_pairs={{1,9},{3,11},{5,13},{7,15},{17,25},{19,27},{21,29},{23,31},{33,41}... | collective-permute-start | bytes 1622024 | tf_op jit(solution)/shard_map/ppermute | solution.py:44
  106.5 5.5 %copy-start.6 = (bf16[2,256,2048]{1,2,0:T(8,128)(2,1)S(1)}, bf16[2,256,2048]{1,2,0:T(8,128)(2,1)}, u32[]{:S(2)}) copy-start(bf16[2,256,2048]{1,2,0:T(8,128)(2,1)} %copy-done.5) | copy-start | bytes 6291460
  106.5 12.6 %collective-permute-start.11 = (bf16[2,32,4224]{2,1,0:T(8,128)(2,1)S(1)}, bf16[2,32,4224]{2,1,0:T(8,128)(2,1)S(1)}, u32[]{:S(2)}, u32[]{:S(2)}) collective-permute-start(bf16[2,32,4224]{2,1,0:T(8,128)(2,1)S(1)} %get-tuple-element.9), channel_id=1, source_target_pairs={{14,15},{12,13},{10,11},{8,9},{6,7},{4,5},{2,3},{0,1},{30,31},{28,... | collective-permute-start | bytes 1622024 | tf_op jit(solution)/shard_map/ppermute | solution.py:44
  108.5 9.2 %copy-start.13 = (bf16[2,32,4224]{2,1,0:T(8,128)(2,1)S(1)}, bf16[2,32,4224]{2,1,0:T(8,128)(2,1)}, u32[]{:S(2)}) copy-start(bf16[2,32,4224]{2,1,0:T(8,128)(2,1)} %copy-done.12) | copy-start | bytes 1622020
  108.5 10.6 %collective-permute-start.6 = (bf16[2,32,4224]{2,1,0:T(8,128)(2,1)S(1)}, bf16[2,32,4224]{2,1,0:T(8,128)(2,1)S(1)}, u32[]{:S(2)}, u32[]{:S(2)}) collective-permute-start(bf16[2,32,4224]{2,1,0:T(8,128)(2,1)S(1)} %get-tuple-element.15), channel_id=1, source_target_pairs={{1,0},{3,2},{5,4},{7,6},{9,8},{11,10},{13,12},{15,14},{17,16},{19,... | collective-permute-start | bytes 1622024 | tf_op jit(solution)/shard_map/ppermute | solution.py:44
  117.7 1.4 %slice-start = ((pred[4224]{0:T(1024)(128)(4,1)}), pred[4096]{0:T(1024)(128)(4,1)S(1)}, s32[]{:S(2)}) async-start(pred[4224]{0:T(1024)(128)(4,1)} %copy-done.15), calls=%async_computation | async-start | bytes 8192 | tf_op jit(solution)/shard_map/slice | solution.py:60
  121.8 3.1 %copy-start.19 = (f32[2,256,32]{1,2,0:T(8,128)S(1)}, f32[2,256,32]{1,2,0:T(8,128)}, u32[]{:S(2)}) copy-start(f32[2,256,32]{1,2,0:T(8,128)} %get-tuple-element.29) | copy-start | bytes 196612
  122.6 2.3 %copy-start.4 = (bf16[2,256,2048]{1,2,0:T(8,128)(2,1)S(1)}, bf16[2,256,2048]{1,2,0:T(8,128)(2,1)}, u32[]{:S(2)}) copy-start(bf16[2,256,2048]{1,2,0:T(8,128)(2,1)} %copy-done.2) | copy-start | bytes 6291460
  122.6 2.3 %copy-start.7 = (bf16[2,256,2048]{1,2,0:T(8,128)(2,1)S(1)}, bf16[2,256,2048]{1,2,0:T(8,128)(2,1)}, u32[]{:S(2)}) copy-start(bf16[2,256,2048]{1,2,0:T(8,128)(2,1)} %copy-done.5) | copy-start | bytes 6291460
  122.6 2.9 %copy-start.14 = (f32[2,32,64,64]{3,2,1,0:T(8,128)S(1)}, f32[2,32,64,64]{3,2,1,0:T(8,128)}, u32[]{:S(2)}) copy-start(f32[2,32,64,64]{3,2,1,0:T(8,128)} %reshape.143) | copy-start | bytes 3145732
  122.6 2.9 %copy-start.18 = (f32[2,256,32]{1,2,0:T(8,128)S(1)}, f32[2,256,32]{1,2,0:T(8,128)}, u32[]{:S(2)}) copy-start(f32[2,256,32]{1,2,0:T(8,128)} %get-tuple-element.31) | copy-start | bytes 196612
  125.5 6.8 %copy-start.8 = (bf16[2048,1024]{1,0:T(8,128)(2,1)S(1)}, bf16[2048,1024]{1,0:T(8,128)(2,1)}, u32[]{:S(2)}) copy-start(bf16[2048,1024]{1,0:T(8,128)(2,1)} %param.21) | copy-start | bytes 12582916
  125.5 6.8 %copy-start.10 = (bf16[512,1024]{1,0:T(8,128)(2,1)S(1)}, bf16[512,1024]{1,0:T(8,128)(2,1)}, u32[]{:S(2)}) copy-start(bf16[512,1024]{1,0:T(8,128)(2,1)} %pad_maximum_fusion.2) | copy-start | bytes 3145732
  134.9 2.2 %copy-start.1 = (bf16[1024,32]{0,1:T(8,128)(2,1)S(1)}, bf16[1024,32]{0,1:T(8,128)(2,1)}, u32[]{:S(2)}) copy-start(bf16[1024,32]{0,1:T(8,128)(2,1)} %param.14) | copy-start | bytes 196612
